TPU v7x, 32 devices: a whole 2x2x4 slice. The times are simulated.
32 devices in a mesh: lat: 8 (over z, x), lon: 4 (over y, core).
Axes of the slice: x: 2, y: 2, z: 4, core: 2. Of those that a mesh axis runs over, the one named last changes fastest.
Arguments:
- heat_anomaly: float32 [75, 64, 512], P(None, 'lat', 'lon'), may hold values from -6 to 6
- brine_anomaly: float32 [75, 64, 512], P(None, 'lat', 'lon'), may hold values from -6 to 6
- eastward_current: float32 [75, 64, 512], P(None, 'lat', 'lon'), may hold values from -6 to 6
- northward_current: float32 [75, 64, 512], P(None, 'lat', 'lon'), may hold values from -6 to 6
- shoreline_indicator: int32 [64, 512], P('lat', 'lon'), may hold values from 0 to 1, as said below
- bottom_layer_index: int32 [64, 512], P('lat', 'lon'), may hold values from 1 to 75
- boundary_fluxes: float32 [4, 64, 512], P(None, 'lat', 'lon'), may hold values from -6 to 6
Outputs:
- next_temperature: float32 [75, 64, 512], P(None, 'lat', 'lon')
- next_salinity: float32 [75, 64, 512], P(None, 'lat', 'lon')
- next_zonal: float32 [75, 64, 512], P(None, 'lat', 'lon')
- next_merid: float32 [75, 64, 512], P(None, 'lat', 'lon')
Inputs may be any that keep to these rules, and one draw needn't show every extreme that they name: `shoreline_indicator`: 1 marks a sea column and 0 a land column. `bottom_layer_index`: the number of wet levels of a sea column; ignored on land.
All inputs are finite; a program needn't handle non-finite values.
Results may differ from a plain program's by a relative error of at most 0.0003.
Values sent between devices are 32-bit elements; how exact they have to be, the bound alone decides.
No kernel may reach another device: no remote copies, remote signals or barrier semaphores. Data moves between devices by JAX's collectives and lax.ppermute only.
A program may use at most 64 MiB of HBM per device.

v0:
```python
import jax
import jax.numpy as jnp
from jax import lax
from jax.sharding import PartitionSpec as P

courant = 0.25
time_step = 0.2
gravity = 0.2
coriolis = 0.5
thermal = 0.6
thermal_sq = 0.1
haline = 0.8
mix_back = 5.0
mix_conv = 60.0
strat_scale = 2.0
momentum_mix = 2.0
bottom_drag = 1.0
surface_gain = 0.5


def padded(block, sides, width, periodic):
    for axis, dim in sides:
        count = lax.axis_size(axis)
        forward = [(i, i + 1) for i in range(count - 1)]
        if periodic:
            forward.append((count - 1, 0))
        backward = [(target, source) for source, target in forward]
        low = lax.ppermute(
            lax.slice_in_dim(block, block.shape[dim] - width, None, axis=dim), axis, forward
        )
        high = lax.ppermute(lax.slice_in_dim(block, 0, width, axis=dim), axis, backward)
        block = jnp.concatenate([low, block, high], axis=dim)
    return block


def swapped(array, axis, stride):
    return lax.ppermute(array, axis, [(i, i ^ 1 << stride) for i in range(lax.axis_size(axis))])


def layer_thick(layered_profile):
    offsets = jnp.arange(layered_profile, dtype=jnp.float32) + 0.5
    return (0.5 + offsets / layered_profile, offsets / layered_profile)


def density(warmth, saltiness, depth_column):
    return -thermal * warmth * (1.0 + thermal_sq * warmth + depth_column) + haline * saltiness


def pressure(rho_cells, thickness):
    layer_load = rho_cells * thickness[:, None, None]
    return jnp.cumsum(layer_load, axis=0) - 0.5 * layer_load


def window(source, first, cell_count, axis_id):
    return lax.slice_in_dim(source, first, first + cell_count, axis=axis_id)


def flux_div(gridded_quantity, velocity, ocean_indicator, axis_id, cell_count):
    face_count = cell_count + 1
    face_vel = 0.5 * (
        window(velocity, 1, face_count, axis_id) + window(velocity, 2, face_count, axis_id)
    )
    face_vel = (
        face_vel
        * window(ocean_indicator, 1, face_count, axis_id)
        * window(ocean_indicator, 2, face_count, axis_id)
    )
    cell_before = window(gridded_quantity, 0, face_count, axis_id)
    cell_here = window(gridded_quantity, 1, face_count, axis_id)
    cell_after = window(gridded_quantity, 2, face_count, axis_id)
    cell_beyond = window(gridded_quantity, 3, face_count, axis_id)
    face_flux = (
        face_vel * 0.5 * (cell_here + cell_after)
        - (
            jnp.maximum(face_vel, 0.0) * (cell_after - 2.0 * cell_here + cell_before)
            + jnp.minimum(face_vel, 0.0) * (cell_beyond - 2.0 * cell_after + cell_here)
        )
        / 6.0
    )
    return window(face_flux, 1, cell_count, axis_id) - window(face_flux, 0, cell_count, axis_id)


def centred(pressure_field, axis_id, cell_count):
    return 0.5 * (
        window(pressure_field, 3, cell_count, axis_id)
        - window(pressure_field, 1, cell_count, axis_id)
    )


def wet_from(depth_plane, layered_profile):
    level_ids = jnp.arange(layered_profile, dtype=jnp.float32)[:, None, None]
    return (level_ids < depth_plane[None]).astype(jnp.float32)


def explicit_part(lon_padded, lat_padded, centre, turning_rate):
    layered_profile = centre.shape[0] - 1
    eastwest_sum = centre.shape[2]
    vertical_sum = centre.shape[3]
    thickness, depth_mid = layer_thick(layered_profile)
    depth_column = depth_mid[:, None, None]
    gridded_quantity = centre[:layered_profile]
    ocean_indicator = wet_from(centre[layered_profile, 0], layered_profile)
    lon_values = lon_padded[:layered_profile]
    lon_wet = wet_from(lon_padded[layered_profile, 0], layered_profile)
    lat_values = lat_padded[:layered_profile]
    lat_wet = wet_from(lat_padded[layered_profile, 0], layered_profile)
    div_x = flux_div(lon_values, lon_values[:, 2:3], lon_wet[:, None], 3, vertical_sum)
    div_y = flux_div(lat_values, lat_values[:, 3:4], lat_wet[:, None], 2, eastwest_sum)
    grad_x = centred(
        pressure(density(lon_values[:, 0], lon_values[:, 1], depth_column) * lon_wet, thickness),
        2,
        vertical_sum,
    )
    grad_y = centred(
        pressure(density(lat_values[:, 0], lat_values[:, 1], depth_column) * lat_wet, thickness),
        1,
        eastwest_sum,
    )
    advected = gridded_quantity - courant * (div_x + div_y)
    turning = turning_rate[None, :, None]
    zonal_new = advected[:, 2] + time_step * (turning * gridded_quantity[:, 3] - gravity * grad_x)
    merid_new = advected[:, 3] + time_step * (-turning * gridded_quantity[:, 2] - gravity * grad_y)
    stepped = (
        jnp.stack([advected[:, 0], advected[:, 1], zonal_new, merid_new], axis=1)
        * ocean_indicator[:, None]
    )
    return (stepped, ocean_indicator, thickness, depth_column)


def build_bands(stepped, ocean_indicator, depth_plane, forcing, thickness, depth_column):
    layered_profile = stepped.shape[0]
    rho_star = density(stepped[:, 0], stepped[:, 1], depth_column)
    spacing = (0.5 * (thickness[1:] + thickness[:-1]))[:, None, None]
    stratified = (rho_star[1:] - rho_star[:-1]) / spacing
    mixing = (mix_back + mix_conv * jax.nn.sigmoid(-stratified / strat_scale)) * ocean_indicator[1:]
    zero_plane = jnp.zeros_like(mixing[:1])
    upper_mix = jnp.concatenate([mixing, zero_plane], axis=0)
    lower_mix = jnp.concatenate([zero_plane, mixing], axis=0)
    channel_mix = jnp.array([1.0, 1.0, momentum_mix, momentum_mix], dtype=jnp.float32)[
        None, :, None, None
    ]
    channel_drag = jnp.array([0.0, 0.0, 1.0, 1.0], dtype=jnp.float32)[None, :, None, None]
    inverse = (1.0 / thickness)[:, None, None, None]
    lower_band = -lower_mix[:, None] * channel_mix * inverse
    upper_band = -upper_mix[:, None] * channel_mix * inverse
    level_ids = jnp.arange(layered_profile, dtype=jnp.float32)[:, None, None]
    floor_cells = (level_ids == depth_plane[None] - 1.0).astype(jnp.float32)
    centre_band = (
        1.0 - lower_band - upper_band + bottom_drag * floor_cells[:, None] * channel_drag * inverse
    )
    surface = forcing * ocean_indicator[0][None] * (surface_gain / thickness[0])
    right_side = jnp.concatenate([stepped[:1] + surface[None], stepped[1:]], axis=0)
    return (lower_band, centre_band, upper_band, right_side)


def thomas(lower_band, centre_band, upper_band, right_side):
    zero_plane = jnp.zeros_like(right_side[0])

    def forward(state_tuple, row_data):
        ratio_prev, scaled_prev = state_tuple
        lower_now, centre_now, upper_now, side_now = row_data
        pivot_now = centre_now - lower_now * ratio_prev
        ratio_now = upper_now / pivot_now
        scaled_now = (side_now - lower_now * scaled_prev) / pivot_now
        return ((ratio_now, scaled_now), (ratio_now, scaled_now))

    _, (ratios, scaled) = lax.scan(
        forward,
        (zero_plane, zero_plane),
        (lower_band, centre_band, upper_band, right_side),
        unroll=True,
    )

    def backward(next_value, row_data):
        ratio_now, scaled_now = row_data
        current = scaled_now - ratio_now * next_value
        return (current, current)

    _, solved = lax.scan(backward, zero_plane, (ratios, scaled), reverse=True, unroll=True)
    return solved


def on_device(
    heat_anomaly,
    brine_anomaly,
    eastward_current,
    northward_current,
    shoreline_indicator,
    bottom_layer_index,
    boundary_fluxes,
):
    layered_profile, eastwest_sum, vertical_sum = heat_anomaly.shape
    depth_int = shoreline_indicator * bottom_layer_index
    depth_plane = depth_int.astype(jnp.float32)
    ocean_indicator = wet_from(depth_plane, layered_profile)
    gridded_quantity = (
        jnp.stack([heat_anomaly, brine_anomaly, eastward_current, northward_current], axis=1)
        * ocean_indicator[:, None]
    )
    centre = jnp.concatenate(
        [
            gridded_quantity,
            jnp.broadcast_to(depth_plane[None, None], (1, 4, eastwest_sum, vertical_sum)),
        ],
        axis=0,
    )
    lon_padded = padded(centre, (("lon", 3),), 2, True)
    lat_padded = padded(centre, (("lat", 2),), 2, False)
    top_rows = centre[:, :, eastwest_sum - 2 :, :]
    lon_count = lax.axis_size("lon")
    partner = top_rows
    for bit_place in range(lon_count.bit_length() - 1):
        partner = swapped(partner, "lon", bit_place)
    fold_sign = jnp.array([1.0, 1.0, -1.0, -1.0], dtype=jnp.float32)[None, :, None, None]
    ghost = partner[:, :, ::-1, ::-1] * fold_sign
    is_north = lax.axis_index("lat") == lax.axis_size("lat") - 1
    north_rim = jnp.where(is_north, ghost, lat_padded[:, :, eastwest_sum + 2 :])
    lat_padded = jnp.concatenate([lat_padded[:, :, : eastwest_sum + 2], north_rim], axis=2)
    lat_ids = lax.axis_index("lat") * eastwest_sum + jnp.arange(eastwest_sum, dtype=jnp.int32)
    total_rows = eastwest_sum * lax.axis_size("lat")
    turning_rate = coriolis * (2.0 * (lat_ids.astype(jnp.float32) + 0.5) / total_rows - 1.0)
    stepped, wet_now, thickness, depth_column = explicit_part(
        lon_padded, lat_padded, centre, turning_rate
    )
    bands = build_bands(stepped, wet_now, depth_plane, boundary_fluxes, thickness, depth_column)
    solved = thomas(*bands)
    return (solved[:, 0], solved[:, 1], solved[:, 2], solved[:, 3])


def solution(mesh):
    in_specs = (
        P(None, "lat", "lon"),
        P(None, "lat", "lon"),
        P(None, "lat", "lon"),
        P(None, "lat", "lon"),
        P("lat", "lon"),
        P("lat", "lon"),
        P(None, "lat", "lon"),
    )
    out_specs = (
        P(None, "lat", "lon"),
        P(None, "lat", "lon"),
        P(None, "lat", "lon"),
        P(None, "lat", "lon"),
    )
    return jax.shard_map(
        on_device, mesh=mesh, in_specs=in_specs, out_specs=out_specs, check_vma=False
    )
```

profile of v0, /device:TPU:0, one launch (start us, length us, event | category | flops | bytes accessed | tf_op | source)
XLA Modules:
  0.0 48.2 jit_solution(13587551791958534259)
XLA Ops:
  0.6 0.7 %broadcast_add_fusion = (f32[8,128]{1,0:T(8,128)S(1)}, f32[8,128]{1,0:T(8,128)S(1)}) fusion(s32[8,128]{1,0:T(8,128)} %param.14, s32[8,128]{1,0:T(8,128)} %param.15), kind=kLoop, calls=%fused_computation.1025 | loop fusion | flops 3072 | bytes 16384 | tf_op jit(solution)/shard_map/sub | solution.py:147
  1.4 1.3 %maximum_multiply_fusion = f32[75,4,8,128]{3,2,0,1:T(8,128)S(1)} fusion(f32[75,1,8,128]{3,2,0,1:T(8,128)} %bitcast.3476, f32[75,1,8,128]{3,2,0,1:T(8,128)} %bitcast.3478, f32[75,1,8,128]{3,2,0,1:T(8,128)} %bitcast.3480, f32[75,1,8,128]{3,2,0,1:T(8,128)} %bitcast.3482, f32[75,8,128]{2,1,0:T(8,128)S(1)} %get-tuple-element.269), kind=kLoop, calls=%fused_computation.30 | loop fusion | flops 1228800 | bytes 2764800 | tf_op jit(solution)/shard_map/mul | solution.py:197
  2.7 1.0 %fusion.33 = (f32[76,4,2,128]{3,2,0,1:T(2,128)}, f32[76,4,2,128]{3,2,0,1:T(2,128)}) fusion(f32[75,4,8,128]{3,2,0,1:T(8,128)S(1)} %maximum_multiply_fusion, f32[1,4,8,128]{3,2,0,1:T(8,128)S(1)} %broadcast_in_dim.98), kind=kLoop, calls=%fused_computation.80 | loop fusion | flops 155648 | bytes 1867776 | tf_op jit(solution)/shard_map/concatenate | solution.py:200
  4.2 4.4 %collective-permute-start.2 = (f32[76,4,2,128]{3,2,0,1:T(2,128)}, f32[76,4,2,128]{3,2,0,1:T(2,128)S(1)}, u32[]{:S(2)}, u32[]{:S(2)}) collective-permute-start(f32[76,4,2,128]{3,2,0,1:T(2,128)} %get-tuple-element.254), channel_id=1, source_target_pairs={{0,4},{4,8},{8,12},{12,16},{16,20},{20,24},{24,28},{1,5},{5,9},{9,... | collective-permute-start | bytes 933896 | tf_op jit(solution)/shard_map/ppermute | solution.py:28
  8.6 1.3 %collective-permute-start.5 = (f32[76,4,2,128]{3,2,0,1:T(2,128)}, f32[76,4,2,128]{3,2,0,1:T(2,128)}, u32[]{:S(2)}, u32[]{:S(2)}) collective-permute-start(f32[76,4,2,128]{3,2,0,1:T(2,128)} %get-tuple-element.255), channel_id=1, source_target_pairs={{4,0},{8,4},{12,8},{16,12},{20,16},{24,20},{28,24},{5,1},{9,5},{13... | collective-permute-start | bytes 933896 | tf_op jit(solution)/shard_map/ppermute | solution.py:31
  9.9 1.5 %fusion.12 = (f32[76,4,8,2]{3,2,0,1:T(8,128)S(1)}, f32[76,4,8,2]{3,2,0,1:T(8,128)}) fusion(f32[1,4,8,128]{3,2,0,1:T(8,128)S(1)} %broadcast_in_dim.98, f32[75,4,8,128]{3,2,0,1:T(8,128)S(1)} %maximum_multiply_fusion), kind=kLoop, calls=%fused_computation.23 | loop fusion | flops 9728 | bytes 1284096 | tf_op jit(solution)/shard_map/concatenate | solution.py:200
  11.4 1.8 %copy.233 = f32[76,4,8,2]{0,2,3,1:T(8,128)S(1)} copy(f32[76,4,8,2]{3,2,0,1:T(8,128)} %get-tuple-element.251) | data formatting | bytes 38912 | tf_op jit(solution)/shard_map/slice | solution.py:31
  13.1 1.4 %collective-permute-start.1 = (f32[76,4,8,2]{0,2,3,1:T(8,128)S(1)}, f32[76,4,8,2]{0,2,3,1:T(8,128)S(1)}, u32[]{:S(2)}, u32[]{:S(2)}) collective-permute-start(f32[76,4,8,2]{0,2,3,1:T(8,128)S(1)} %copy.233), channel_id=1, source_target_pairs={{1,0},{2,1},{3,2},{0,3},{5,4},{6,5},{7,6},{4,7},{9,8},{10,9},{11,1... | collective-permute-start | bytes 58376 | tf_op jit(solution)/shard_map/ppermute | solution.py:31
  15.6 0.6 %add_multiply_fusion = f32[74]{0:T(128)} fusion(f32[75]{0:T(128)S(1)} %get-tuple-element.272), kind=kLoop, calls=%fused_computation.1026 | loop fusion | flops 148 | bytes 888 | tf_op jit(solution)/shard_map/mul | solution.py:133
  16.8 1.5 %collective-permute-done = f32[76,4,8,2]{0,2,3,1:T(8,128)S(1)} collective-permute-done((f32[76,4,8,2]{0,2,3,1:T(8,128)S(1)}, f32[76,4,8,2]{0,2,3,1:T(8,128)S(1)}, u32[]{:S(2)}, u32[]{:S(2)}) %collective-permute-start) | collective-permute-done | bytes 19488 | tf_op jit(solution)/shard_map/ppermute | solution.py:28
  18.9 1.6 %copy.234 = f32[76,4,8,2]{3,2,0,1:T(8,128)} copy(f32[76,4,8,2]{0,2,3,1:T(8,128)S(1)} %collective-permute-done.1) | data formatting | bytes 38912 | tf_op jit(solution)/shard_map/ppermute | solution.py:31
  20.5 0.9 %maximum_bitcast_fusion.3 = f32[8,132]{1,0:T(8,128)S(1)} fusion(f32[76,4,8,2]{3,2,0,1:T(8,128)} %copy.234, f32[76,4,8,2]{3,2,0,1:T(8,128)S(1)} %copy.232, f32[1,4,8,128]{3,2,0,1:T(8,128)S(1)} %broadcast_in_dim.98, f32[75,4,8,128]{3,2,0,1:T(8,128)S(1)} %maximum_multiply_fusion), kind=kLoop, calls=%fused_computation.1022 | loop fusion | flops 3168 | bytes 1288320 | tf_op jit(solution)/shard_map/lt | solution.py:92
  21.8 0.6 %multiply_bitcast_fusion.1 = (f32[75,8,129]{2,1,0:T(8,128)S(1)}, f32[75,1,8,129]{3,2,0,1:T(8,128)S(1)}) fusion(f32[75,1,8,132]{3,2,0,1:T(8,128)S(1)} %fusion.31, f32[76,4,8,2]{3,2,0,1:T(8,128)S(1)} %copy-done, f32[1,4,8,128]{3,2,0,1:T(8,128)S(1)} %broadcast_in_dim.98, f32[75,4,8,128]{3,2,0,1:T(8,128)S(1)} %maximum_multiply_fusion, f32[76,4,8,2]{3,2,0,1:T(8,128)S(1)} %copy.232), kind=kLoop, calls=%fused_computation.76 | loop fusion | flops 696600 | bytes 2522496 | tf_op jit(solution)/shard_map/mul | solution.py:73
  22.4 0.8 %maximum_maximum_fusion = (f32[76,4,8,130]{3,2,0,1:T(8,128)S(1)}, f32[76,4,8,130]{3,2,0,1:T(8,128)S(1)}) fusion(f32[1,4,8,128]{3,2,0,1:T(8,128)S(1)} %broadcast_in_dim.98, f32[75,4,8,128]{3,2,0,1:T(8,128)S(1)} %maximum_multiply_fusion, f32[76,4,8,2]{3,2,0,1:T(8,128)S(1)} %copy.232, f32[76,4,8,2]{3,2,0,1:T(8,128)S(1)} %copy-done), kind=kLoop, calls=%fused_computation | loop fusion | flops 1264640 | bytes 3813376 | tf_op jit(solution)/shard_map/concatenate | solution.py:32
  23.9 2.8 %fusion.10 = f32[75,4,8,129]{3,2,0,1:T(8,128)} fusion(f32[76,4,8,130]{3,2,0,1:T(8,128)S(1)} %get-tuple-element.249, f32[76,4,8,130]{3,2,0,1:T(8,128)S(1)} %get-tuple-element.248, f32[75,8,129]{2,1,0:T(8,128)S(1)} %get-tuple-element.261, f32[75,8,129]{2,1,0:T(8,128)S(1)} %get-tuple-element.260, f32[75,8,129]{2,1,0:T(8,128)S(1)} %get-tuple-element.242), kind=kLoop, calls=%fused_computation.17 | loop fusion | flops 4024800 | bytes 7120800 | tf_op jit(solution)/shard_map/sub | solution.py:73
  26.7 2.2 %multiply_subtract_fusion.1 = f32[75,8,132]{2,1,0:T(8,128)} fusion(f32[75]{0:T(128)S(1)} %copy-done.9, f32[76,4,8,2]{3,2,0,1:T(8,128)S(1)} %copy-done, f32[1,4,8,128]{3,2,0,1:T(8,128)S(1)} %broadcast_in_dim.98, f32[75,4,8,128]{3,2,0,1:T(8,128)S(1)} %maximum_multiply_fusion, f32[76,4,8,2]{3,2,0,1:T(8,128)S(1)} %copy.232, f32[75]{0:T(128)S(1)} %get-tuple-element.271, ...), kind=kOutput, calls=%fused_computation.68 | output fusion | flops 8553600 | bytes 1605720 | tf_op jit(solution)/shard_map/jit(cumsum)/reduce_window_sum | solution.py:51
  28.9 3.1 %collective-permute-done.4 = f32[76,4,2,128]{3,2,0,1:T(2,128)} collective-permute-done((f32[76,4,2,128]{3,2,0,1:T(2,128)}, f32[76,4,2,128]{3,2,0,1:T(2,128)}, u32[]{:S(2)}, u32[]{:S(2)}) %collective-permute-start.4) | collective-permute-done | bytes 311328 | tf_op jit(solution)/shard_map/ppermute | solution.py:37
  32.0 2.8 %rev.3 = f32[76,4,2,128]{3,2,0,1:T(2,128)S(1)} reverse(f32[76,4,2,128]{3,2,0,1:T(2,128)} %collective-permute-done.4), dimensions={2,3} | reverse | bytes 622592 | tf_op jit(solution)/shard_map/rev | solution.py:215
  34.8 1.2 %multiply_select_fusion = f32[76,4,2,128]{3,2,0,1:T(2,128)S(1)} fusion(f32[76,4,2,128]{3,2,0,1:T(2,128)} %collective-permute-done.5, f32[76,4,2,128]{3,2,0,1:T(2,128)S(1)} %rev.3, pred[]{:T(512)S(6)} %eq.18, f32[4]{0:T(128)S(1)} %copy-done.13), kind=kLoop, calls=%fused_computation.82 | loop fusion | flops 155648 | bytes 933905 | tf_op jit(solution)/shard_map/jit(_where)/select_n | solution.py:217
  37.0 1.4 %fusion.4 = f32[75,4,9,128]{3,2,0,1:T(8,128)S(1)} fusion(f32[76,4,10,128]{3,2,0,1:T(8,128)S(1)} %get-tuple-element.253, f32[76,4,10,128]{3,2,0,1:T(8,128)S(1)} %get-tuple-element.252, f32[75,9,128]{2,1,0:T(8,128)S(1)} %get-tuple-element.263, f32[75,9,128]{2,1,0:T(8,128)S(1)} %get-tuple-element.262, f32[75,9,128]{2,1,0:T(8,128)S(1)} %get-tuple-element.244), kind=kLoop, calls=%fused_computation.9 | loop fusion | flops 4492800 | bytes 7948800 | tf_op jit(solution)/shard_map/sub | solution.py:73
  39.5 0.6 %multiply_subtract_fusion = f32[75,12,128]{2,1,0:T(8,128)S(1)} fusion(f32[75]{0:T(128)S(1)} %copy-done.9, f32[76,4,2,128]{3,2,0,1:T(2,128)S(1)} %multiply_select_fusion, f32[1,4,8,128]{3,2,0,1:T(8,128)S(1)} %broadcast_in_dim.98, f32[75,4,8,128]{3,2,0,1:T(8,128)S(1)} %maximum_multiply_fusion, f32[76,4,2,128]{3,2,0,1:T(2,128)S(1)} %collective-permute-done.2, ...), kind=kOutput, calls=%fused_computation.66 | output fusion | flops 12441600 | bytes 2335320 | tf_op jit(solution)/shard_map/jit(cumsum)/reduce_window_sum | solution.py:51
  42.2 1.0 %multiply_multiply_fusion.1 = (f32[75,4,8,128]{3,2,1,0:T(8,128)S(1)}, f32[75,4,8,128]{3,2,1,0:T(8,128)S(1)}, f32[75,4,8,128]{3,2,1,0:T(8,128)S(1)}) fusion(f32[75]{0:T(128)S(1)} %copy-done.12, f32[4]{0:T(128)S(1)} %copy-done.11, f32[75,8,128]{2,1,0:T(8,128)S(1)} %get-tuple-element.268, f32[4]{0:T(128)S(1)} %copy-done.10, ...), kind=kLoop, calls=%fused_computation.34 | loop fusion | flops 2764800 | bytes 4608332 | tf_op jit(solution)/shard_map/mul | solution.py:144
  45.5 0.7 %constant_dynamic-update-slice_fusion.62 = (f32[75,4,8,128]{3,2,0,1:T(8,128)S(1)}, f32[1,4,8,128]{3,2,1,0:T(8,128)S(1)}, f32[1,4,8,128]{3,2,1,0:T(8,128)S(1)}, f...) fusion(f32[75,4,8,128]{3,2,0,1:T(8,128)S(1)} %constant_dynamic-, ...), kind=kLoop, calls=%fused_computation.186 | loop fusion | flops 1470464 | bytes 3915776
  47.1 1.0 %slice_bitcast_fusion = (f32[75,8,128]{2,1,0:T(8,128)}, f32[75,8,128]{2,1,0:T(8,128)}, f32[75,8,128]{2,1,0:T(8,128)}, f32[75,8,128]{2,1,0:T(8,128)}) fusion(f32[75,4,8,128]{3,2,0,1:T(8,128)S(1)} %constant_dynamic-update-slice_fusion), kind=kLoop, calls=%fused_computation.83 | loop fusion | bytes 2457600 | tf_op jit(solution)/shard_map/squeeze | solution.py:227
  (142 shorter events, 10.4 us)
Async XLA Ops:
  3.7 19.6 %collective-permute-start.3 = (f32[76,4,2,128]{3,2,0,1:T(2,128)}, f32[76,4,2,128]{3,2,0,1:T(2,128)}, u32[]{:S(2)}, u32[]{:S(2)}) collective-permute-start(f32[76,4,2,128]{3,2,0,1:T(2,128)} %get-tuple-element.254), channel_id=1, source_target_pairs={{0,1},{1,0},{2,3},{3,2},{4,5},{5,4},{6,7},{7,6},{8,9},{9,8},{10,11... | collective-permute-start | bytes 933896 | tf_op jit(solution)/shard_map/ppermute | solution.py:37
  4.2 31.8 %collective-permute-start.2 = (f32[76,4,2,128]{3,2,0,1:T(2,128)}, f32[76,4,2,128]{3,2,0,1:T(2,128)S(1)}, u32[]{:S(2)}, u32[]{:S(2)}) collective-permute-start(f32[76,4,2,128]{3,2,0,1:T(2,128)} %get-tuple-element.254), channel_id=1, source_target_pairs={{0,4},{4,8},{8,12},{12,16},{16,20},{20,24},{24,28},{1,5},{5,9},{9,... | collective-permute-start | bytes 933896 | tf_op jit(solution)/shard_map/ppermute | solution.py:28
  8.6 26.2 %collective-permute-start.5 = (f32[76,4,2,128]{3,2,0,1:T(2,128)}, f32[76,4,2,128]{3,2,0,1:T(2,128)}, u32[]{:S(2)}, u32[]{:S(2)}) collective-permute-start(f32[76,4,2,128]{3,2,0,1:T(2,128)} %get-tuple-element.255), channel_id=1, source_target_pairs={{4,0},{8,4},{12,8},{16,12},{20,16},{24,20},{28,24},{5,1},{9,5},{13... | collective-permute-start | bytes 933896 | tf_op jit(solution)/shard_map/ppermute | solution.py:31
  13.1 5.8 %collective-permute-start.1 = (f32[76,4,8,2]{0,2,3,1:T(8,128)S(1)}, f32[76,4,8,2]{0,2,3,1:T(8,128)S(1)}, u32[]{:S(2)}, u32[]{:S(2)}) collective-permute-start(f32[76,4,8,2]{0,2,3,1:T(8,128)S(1)} %copy.233), channel_id=1, source_target_pairs={{1,0},{2,1},{3,2},{0,3},{5,4},{6,5},{7,6},{4,7},{9,8},{10,9},{11,1... | collective-permute-start | bytes 58376 | tf_op jit(solution)/shard_map/ppermute | solution.py:31
  15.0 3.4 %collective-permute-start = (f32[76,4,8,2]{0,2,3,1:T(8,128)S(1)}, f32[76,4,8,2]{0,2,3,1:T(8,128)S(1)}, u32[]{:S(2)}, u32[]{:S(2)}) collective-permute-start(f32[76,4,8,2]{0,2,3,1:T(8,128)S(1)} %copy.231), channel_id=1, source_target_pairs={{0,1},{1,2},{2,3},{3,0},{4,5},{5,6},{6,7},{7,4},{8,9},{9,10},{10,1... | collective-permute-start | bytes 58376 | tf_op jit(solution)/shard_map/ppermute | solution.py:28
  15.0 1.8 %copy-start.8 = (f32[75]{0:T(128)}, f32[75]{0:T(128)S(1)}, u32[]{:S(2)}) copy-start(f32[75]{0:T(128)S(1)} %get-tuple-element.272) | copy-start | bytes 904
  20.5 1.3 %copy-start = (f32[76,4,8,2]{3,2,0,1:T(8,128)S(1)}, f32[76,4,8,2]{3,2,0,1:T(8,128)}, u32[]{:S(2)}) copy-start(f32[76,4,8,2]{3,2,0,1:T(8,128)} %copy.234) | copy-start | bytes 58372
  23.3 8.7 %collective-permute-start.4 = (f32[76,4,2,128]{3,2,0,1:T(2,128)}, f32[76,4,2,128]{3,2,0,1:T(2,128)}, u32[]{:S(2)}, u32[]{:S(2)}) collective-permute-start(f32[76,4,2,128]{3,2,0,1:T(2,128)} %collective-permute-done.3), channel_id=1, source_target_pairs={{0,2},{1,3},{2,0},{3,1},{4,6},{5,7},{6,4},{7,5},{8,10},{9,11},{10,... | collective-permute-start | bytes 933896 | tf_op jit(solution)/shard_map/ppermute | solution.py:37
  23.9 2.8 %copy-start.9 = (f32[75]{0:T(128)S(1)}, f32[75]{0:T(128)}, u32[]{:S(2)}) copy-start(f32[75]{0:T(128)} %copy-done.8) | copy-start | bytes 904
  26.7 8.1 %copy-start.13 = (f32[4]{0:T(128)S(1)}, f32[4]{0:T(128)}, u32[]{:S(2)}) copy-start(f32[4]{0:T(128)} %constant.43.clone) | copy-start | bytes 52
  36.9 1.7 %copy-start.1 = (f32[75,4,8,129]{3,2,0,1:T(8,128)S(1)}, f32[75,4,8,129]{3,2,0,1:T(8,128)}, u32[]{:S(2)}) copy-start(f32[75,4,8,129]{3,2,0,1:T(8,128)} %fusion.10) | copy-start | bytes 3715204
  37.0 1.7 %copy-start.3 = (f32[75,8,128]{2,1,0:T(8,128)S(1)}, f32[75,8,128]{2,1,0:T(8,128)}, u32[]{:S(2)}) copy-start(f32[75,8,128]{2,1,0:T(8,128)} %param.13) | copy-start | bytes 921604
  37.0 1.8 %copy-start.4 = (f32[75,8,128]{2,1,0:T(8,128)S(1)}, f32[75,8,128]{2,1,0:T(8,128)}, u32[]{:S(2)}) copy-start(f32[75,8,128]{2,1,0:T(8,128)} %param.12) | copy-start | bytes 921604
  37.0 1.9 %copy-start.5 = (f32[75,8,128]{2,1,0:T(8,128)S(1)}, f32[75,8,128]{2,1,0:T(8,128)}, u32[]{:S(2)}) copy-start(f32[75,8,128]{2,1,0:T(8,128)} %param.11) | copy-start | bytes 921604
  37.0 1.9 %copy-start.6 = (f32[75,8,128]{2,1,0:T(8,128)S(1)}, f32[75,8,128]{2,1,0:T(8,128)}, u32[]{:S(2)}) copy-start(f32[75,8,128]{2,1,0:T(8,128)} %param.10) | copy-start | bytes 921604
  39.5 1.1 %copy-start.2 = (f32[75,8,132]{2,1,0:T(8,128)S(1)}, f32[75,8,132]{2,1,0:T(8,128)}, u32[]{:S(2)}) copy-start(f32[75,8,132]{2,1,0:T(8,128)} %multiply_subtract_fusion.1) | copy-start | bytes 950404
  39.5 1.1 %copy-start.15 = (f32[8]{0:T(128)S(1)}, f32[8]{0:T(128)}, u32[]{:S(2)}) copy-start(f32[8]{0:T(128)} %get-tuple-element.273) | copy-start | bytes 100
  39.5 1.1 %copy-start.16 = (f32[8]{0:T(128)S(1)}, f32[8]{0:T(128)}, u32[]{:S(2)}) copy-start(f32[8]{0:T(128)} %get-tuple-element.274) | copy-start | bytes 100
  40.8 0.6 %copy-start.14 = (f32[74]{0:T(128)S(1)}, f32[74]{0:T(128)}, u32[]{:S(2)}) copy-start(f32[74]{0:T(128)} %add_multiply_fusion) | copy-start | bytes 892
  41.5 0.7 %copy-start.10 = (f32[4]{0:T(128)S(1)}, f32[4]{0:T(128)}, u32[]{:S(2)}) copy-start(f32[4]{0:T(128)} %constant.45.clone) | copy-start | bytes 52
  41.5 0.7 %copy-start.11 = (f32[4]{0:T(128)S(1)}, f32[4]{0:T(128)}, u32[]{:S(2)}) copy-start(f32[4]{0:T(128)} %constant.44.clone) | copy-start | bytes 52
  41.5 0.7 %copy-start.12 = (f32[75]{0:T(128)S(1)}, f32[75]{0:T(128)}, u32[]{:S(2)}) copy-start(f32[75]{0:T(128)} %broadcast_divide_fusion) | copy-start | bytes 904
  43.3 0.7 %copy-start.7 = (f32[4,8,128]{2,1,0:T(8,128)S(1)}, f32[4,8,128]{2,1,0:T(8,128)}, u32[]{:S(2)}) copy-start(f32[4,8,128]{2,1,0:T(8,128)} %param.16) | copy-start | bytes 49156
where the time goes:
time: 49 us; the launch traced here: 48.2 us
  other arithmetic  22.9 us (47%)
  local copies, waits for them, and re-layouts  10.9 us (22%)
  starting transfers between devices  8.13 us (17%)
  waiting for transfers between devices  4.68 us (10%)
  between operations  1.64 us (3%)
    ppermute x2, starting transfers between devices, padded(): lax.ppermute(lax.slice_in_dim(block, block.shape[dim] - width, None, axis...  4.44 us
    sub x2, other arithmetic, flux_div(): face_vel * 0.5 * (cell_here + cell_after)  4.17 us
    ppermute x2, waiting for transfers between devices, swapped(): lax.ppermute(array, axis, [(i, i ^ 1 << stride) for i in range(lax.axis_s...  3.14 us
    another operation x2, other arithmetic, pressure(): return jnp.cumsum(layer_load, axis=0) - 0.5 * layer_load  2.79 us
    rev x1, local copies, waits for them, and re-layouts, on_device(): ghost = partner[:, :, ::-1, ::-1] * fold_sign  2.76 us
    ppermute x2, starting transfers between devices, padded(): lax.ppermute(lax.slice_in_dim(block, 0, width, axis=dim), axis, backward)  2.67 us
    unnamed x71, local copies, waits for them, and re-layouts  2.66 us
    concatenate x2, other arithmetic, on_device(): jnp.concatenate([gridded_quantity, jnp.broadcast_to(depth_plane[None, Non...  2.46 us
  transfers between devices with their start and end apart: 6, of which 2 were waited for; matrix products, arithmetic and copies ran while one was open for 39% of the time, Pallas kernels for 0%

commit v1 on v0

v1 whole, which is shorter than its diff:
```python
import jax
import jax.numpy as jnp
from jax import lax
from jax.experimental import pallas as pl
from jax.experimental.pallas import tpu as pltpu
from jax.sharding import PartitionSpec as P

courant = 0.25
time_step = 0.2
gravity = 0.2
coriolis = 0.5
thermal = 0.6
thermal_sq = 0.1
haline = 0.8
mix_back = 5.0
mix_conv = 60.0
strat_scale = 2.0
momentum_mix = 2.0
bottom_drag = 1.0
surface_gain = 0.5


def density(warmth, saltiness, depth_column):
    return -thermal * warmth * (1.0 + thermal_sq * warmth + depth_column) + haline * saltiness


def face_flux(face_vel, before, here, after, beyond):
    return face_vel * 0.5 * (here + after) - (
        jnp.maximum(face_vel, 0.0) * (after - 2.0 * here + before)
        + jnp.minimum(face_vel, 0.0) * (beyond - 2.0 * after + here)
    ) * (1.0 / 6.0)


def step_kernel(
    h_ref, inv_h_ref, zmid_ref, inv_sp_ref,
    f_ref, dep_ref, flux_ref, t_ref, s_ref, u_ref, v_ref, elat_ref, elon_ref,
    o0_ref, o1_ref, o2_ref, o3_ref,
    star_scr, r_scr, rs_scr,
):
    layers = t_ref.shape[0]
    rows, cols = t_ref.shape[1], t_ref.shape[2]
    depth_plane = 4 * layers
    lane = lax.broadcasted_iota(jnp.int32, (rows, cols), 1)
    row = lax.broadcasted_iota(jnp.int32, (rows, cols), 0)

    def xs(v, e, s):
        if s == 1:
            return pltpu.roll(jnp.where(lane == 0, e, v), cols - 1, 1)
        if s == 2:
            return pltpu.roll(jnp.where(lane < 2, e, v), cols - 2, 1)
        if s == -1:
            return pltpu.roll(jnp.where(lane == cols - 1, e, v), 1, 1)
        return pltpu.roll(jnp.where(lane >= cols - 2, e, v), 2, 1)

    def ys(v, e, s):
        if s == 1:
            return pltpu.roll(jnp.where(row == 0, e, v), rows - 1, 0)
        if s == 2:
            return pltpu.roll(jnp.where(row < 2, e, v), rows - 2, 0)
        if s == -1:
            return pltpu.roll(jnp.where(row == rows - 1, e, v), 1, 0)
        return pltpu.roll(jnp.where(row >= rows - 2, e, v), 2, 0)

    dep = dep_ref[...]
    dep_xm = xs(dep, elon_ref[depth_plane], -1)
    dep_xp = xs(dep, elon_ref[depth_plane], 1)
    dep_ym = ys(dep, elat_ref[depth_plane], -1)
    dep_yp = ys(dep, elat_ref[depth_plane], 1)
    turning = f_ref[...]
    zero = jnp.zeros((rows, cols), jnp.float32)

    def explicit(k, carry):
        cum_xm, cum_xp, cum_ym, cum_yp = carry
        kf = k.astype(jnp.float32)
        h = h_ref[k]
        zmid = zmid_ref[k]
        w0 = (kf < dep).astype(jnp.float32)
        wxm = (kf < dep_xm).astype(jnp.float32)
        wxp = (kf < dep_xp).astype(jnp.float32)
        wym = (kf < dep_ym).astype(jnp.float32)
        wyp = (kf < dep_yp).astype(jnp.float32)
        q = [r[k] * w0 for r in (t_ref, s_ref, u_ref, v_ref)]
        ex = [elon_ref[c * layers + k] for c in range(4)]
        ey = [elat_ref[c * layers + k] for c in range(4)]
        xsh = {s: [xs(q[c], ex[c], s) for c in range(4)] for s in (-2, -1, 1, 2)}
        ysh = {s: [ys(q[c], ey[c], s) for c in range(4)] for s in (-2, -1, 1, 2)}
        a_r = 0.5 * (q[2] + xsh[1][2]) * w0 * wxp
        a_l = 0.5 * (xsh[-1][2] + q[2]) * wxm * w0
        b_r = 0.5 * (q[3] + ysh[1][3]) * w0 * wyp
        b_l = 0.5 * (ysh[-1][3] + q[3]) * wym * w0
        adv = []
        for c in range(4):
            div_x = face_flux(a_r, xsh[-1][c], q[c], xsh[1][c], xsh[2][c]) - face_flux(
                a_l, xsh[-2][c], xsh[-1][c], q[c], xsh[1][c]
            )
            div_y = face_flux(b_r, ysh[-1][c], q[c], ysh[1][c], ysh[2][c]) - face_flux(
                b_l, ysh[-2][c], ysh[-1][c], q[c], ysh[1][c]
            )
            adv.append(q[c] - courant * (div_x + div_y))
        load_xm = density(xsh[-1][0], xsh[-1][1], zmid) * wxm * h
        load_xp = density(xsh[1][0], xsh[1][1], zmid) * wxp * h
        load_ym = density(ysh[-1][0], ysh[-1][1], zmid) * wym * h
        load_yp = density(ysh[1][0], ysh[1][1], zmid) * wyp * h
        cum_xm = cum_xm + load_xm
        cum_xp = cum_xp + load_xp
        cum_ym = cum_ym + load_ym
        cum_yp = cum_yp + load_yp
        grad_x = 0.5 * ((cum_xp - 0.5 * load_xp) - (cum_xm - 0.5 * load_xm))
        grad_y = 0.5 * ((cum_yp - 0.5 * load_yp) - (cum_ym - 0.5 * load_ym))
        star0 = adv[0] * w0
        star1 = adv[1] * w0
        star2 = (adv[2] + time_step * (turning * q[3] - gravity * grad_x)) * w0
        star3 = (adv[3] + time_step * (-turning * q[2] - gravity * grad_y)) * w0
        for c, val in enumerate((star0, star1, star2, star3)):
            star_scr[c * layers + k] = val
        rs_scr[k] = density(star0, star1, zmid)
        return (cum_xm, cum_xp, cum_ym, cum_yp)

    lax.fori_loop(0, layers, explicit, (zero, zero, zero, zero), unroll=3)

    surface_scale = surface_gain * inv_h_ref[0]
    w_top = (0.0 < dep).astype(jnp.float32)
    for c in range(4):
        star_scr[c * layers] = star_scr[c * layers] + flux_ref[c] * w_top * surface_scale

    def forward(k, carry):
        mix_prev, r_a, r_b, s0, s1, s2, s3 = carry
        kf = k.astype(jnp.float32)
        inv_h = inv_h_ref[k]
        nxt = jnp.minimum(k + 1, layers - 1)
        stratified = (rs_scr[nxt] - rs_scr[k]) * inv_sp_ref[k]
        sig = 1.0 / (1.0 + jnp.exp(stratified * (1.0 / strat_scale)))
        w_next = (kf + 1.0 < dep).astype(jnp.float32)
        mix = (mix_back + mix_conv * sig) * w_next
        mix = jnp.where(k < layers - 1, mix, 0.0)
        low_a = -mix_prev * inv_h
        up_a = -mix * inv_h
        cen_a = 1.0 - low_a - up_a
        low_b = -mix_prev * momentum_mix * inv_h
        up_b = -mix * momentum_mix * inv_h
        floor = (kf == dep - 1.0).astype(jnp.float32)
        cen_b = 1.0 - low_b - up_b + bottom_drag * floor * inv_h
        inv_a = 1.0 / (cen_a - low_a * r_a)
        inv_b = 1.0 / (cen_b - low_b * r_b)
        r_a = up_a * inv_a
        r_b = up_b * inv_b
        r_scr[k] = r_a
        r_scr[layers + k] = r_b
        s0 = (star_scr[k] - low_a * s0) * inv_a
        s1 = (star_scr[layers + k] - low_a * s1) * inv_a
        s2 = (star_scr[2 * layers + k] - low_b * s2) * inv_b
        s3 = (star_scr[3 * layers + k] - low_b * s3) * inv_b
        star_scr[k] = s0
        star_scr[layers + k] = s1
        star_scr[2 * layers + k] = s2
        star_scr[3 * layers + k] = s3
        return (mix, r_a, r_b, s0, s1, s2, s3)

    lax.fori_loop(0, layers, forward, (zero,) * 7, unroll=3)

    def backward(i, carry):
        x0, x1, x2, x3 = carry
        k = layers - 1 - i
        r_a = r_scr[k]
        r_b = r_scr[layers + k]
        x0 = star_scr[k] - r_a * x0
        x1 = star_scr[layers + k] - r_a * x1
        x2 = star_scr[2 * layers + k] - r_b * x2
        x3 = star_scr[3 * layers + k] - r_b * x3
        o0_ref[k] = x0
        o1_ref[k] = x1
        o2_ref[k] = x2
        o3_ref[k] = x3
        return (x0, x1, x2, x3)

    lax.fori_loop(0, layers, backward, (zero,) * 4, unroll=3)


def on_device(
    heat_anomaly,
    brine_anomaly,
    eastward_current,
    northward_current,
    shoreline_indicator,
    bottom_layer_index,
    boundary_fluxes,
):
    layers, rows, cols = heat_anomaly.shape
    fields = (heat_anomaly, brine_anomaly, eastward_current, northward_current)
    depth_plane = (shoreline_indicator * bottom_layer_index).astype(jnp.float32)
    level_ids = jnp.arange(layers, dtype=jnp.float32)[:, None, None]

    def edge(row_slice, col_slice):
        d = depth_plane[row_slice, col_slice]
        wet = (level_ids < d[None]).astype(jnp.float32)
        parts = [x[:, row_slice, col_slice] * wet for x in fields]
        return jnp.concatenate(parts + [d[None]], axis=0)

    n_lat = lax.axis_size("lat")
    n_lon = lax.axis_size("lon")
    top = edge(slice(rows - 2, rows), slice(None))
    bottom = edge(slice(0, 2), slice(None))
    right = edge(slice(None), slice(cols - 2, cols))
    left = edge(slice(None), slice(0, 2))
    from_south = lax.ppermute(top, "lat", [(i, i + 1) for i in range(n_lat - 1)])
    from_north = lax.ppermute(bottom, "lat", [(i + 1, i) for i in range(n_lat - 1)])
    from_west = lax.ppermute(right, "lon", [(i, (i + 1) % n_lon) for i in range(n_lon)])
    from_east = lax.ppermute(left, "lon", [((i + 1) % n_lon, i) for i in range(n_lon)])
    last = (n_lat - 1) * n_lon
    from_fold = lax.ppermute(
        top, ("lat", "lon"), [(last + x, last + n_lon - 1 - x) for x in range(n_lon)]
    )
    planes = 4 * layers + 1
    fold_sign = jnp.concatenate(
        [jnp.ones((2 * layers,), jnp.float32), -jnp.ones((2 * layers,), jnp.float32),
         jnp.ones((1,), jnp.float32)]
    )[:, None, None]
    ghost = from_fold[:, ::-1, ::-1] * fold_sign
    is_north = lax.axis_index("lat") == n_lat - 1
    north_rows = jnp.where(is_north, ghost, from_north)
    edge_lat = jnp.concatenate(
        [north_rows, jnp.zeros((planes, rows - 4, cols), jnp.float32), from_south], axis=1
    )
    edge_lon = jnp.concatenate(
        [from_east, jnp.zeros((planes, rows, cols - 4), jnp.float32), from_west], axis=2
    )

    row_ids = lax.axis_index("lat") * rows + jnp.arange(rows, dtype=jnp.int32)
    total_rows = rows * n_lat
    turning_rate = coriolis * (2.0 * (row_ids.astype(jnp.float32) + 0.5) / total_rows - 1.0)
    turning_plane = jnp.broadcast_to(turning_rate[:, None], (rows, cols))

    offsets = jnp.arange(layers, dtype=jnp.float32) + 0.5
    thickness = 0.5 + offsets / layers
    zmid = offsets / layers
    inverse = 1.0 / thickness
    spacing = 0.5 * (thickness[1:] + thickness[:-1])
    inv_spacing = jnp.concatenate([1.0 / spacing, jnp.ones((1,), jnp.float32)])

    smem = pl.BlockSpec(memory_space=pltpu.SMEM)
    vmem = pl.BlockSpec(memory_space=pltpu.VMEM)
    plane = jax.ShapeDtypeStruct((layers, rows, cols), jnp.float32)
    outs = pl.pallas_call(
        step_kernel,
        out_shape=(plane,) * 4,
        in_specs=[smem] * 4 + [vmem] * 9,
        out_specs=(vmem,) * 4,
        scratch_shapes=[
            pltpu.VMEM((4 * layers, rows, cols), jnp.float32),
            pltpu.VMEM((2 * layers, rows, cols), jnp.float32),
            pltpu.VMEM((layers, rows, cols), jnp.float32),
        ],
    )(
        thickness, inverse, zmid, inv_spacing,
        turning_plane, depth_plane, boundary_fluxes,
        heat_anomaly, brine_anomaly, eastward_current, northward_current,
        edge_lat, edge_lon,
    )
    return tuple(outs)


def solution(mesh):
    in_specs = (
        P(None, "lat", "lon"),
        P(None, "lat", "lon"),
        P(None, "lat", "lon"),
        P(None, "lat", "lon"),
        P("lat", "lon"),
        P("lat", "lon"),
        P(None, "lat", "lon"),
    )
    out_specs = (
        P(None, "lat", "lon"),
        P(None, "lat", "lon"),
        P(None, "lat", "lon"),
        P(None, "lat", "lon"),
    )
    return jax.shard_map(
        on_device, mesh=mesh, in_specs=in_specs, out_specs=out_specs, check_vma=False
    )
```

time: 49 us -> 44.6 us (0.910)
  Pallas kernels: 0 us -> 9.2 us
  other arithmetic: 22.9 us -> 14.5 us
  waiting for transfers between devices: 4.68 us -> 1.26 us
  local copies, waits for them, and re-layouts: 10.9 us -> 8.83 us
  starting transfers between devices: 8.13 us -> 9.17 us
  between operations: 1.64 us -> 0.82 us
    pallas_call x0 -> x1, Pallas kernels: none -> 9.2 us  [on_device(): pl.pallas_call(step_kernel, out_shape=(plane,) * 4, in_specs=[smem] * 4 +...]
    sub x6 -> x0, other arithmetic: 5.87 us -> none  [the longest x2 4.17 us: flux_div(): face_vel * 0.5 * (cell_here + cell_after)]
    unnamed x37 -> x4, other arithmetic: 1.53 us -> 7.29 us
    mul x10 -> x3, other arithmetic: 4.89 us -> 0.16 us  [the longest x2 0.15 us: edge(): parts = [x[:, row_slice, col_slice] * wet for x in fields]]
    ppermute x6 -> x5, waiting for transfers between devices: 4.68 us -> 1.26 us  [the longest x1 1.25 us: on_device(): lax.ppermute(right, 'lon', [(i, (i + 1) % n_lon) for i in range(n_lon)])]
    another operation x3 -> x0, other arithmetic: 3.06 us -> none  [the longest x2 2.79 us: pressure(): return jnp.cumsum(layer_load, axis=0) - 0.5 * layer_load]
    slice x3 -> x8, local copies, waits for them, and re-layouts: 2.28 us -> 0.84 us  [the longest x4 0.6 us: edge(): parts = [x[:, row_slice, col_slice] * wet for x in fields]]
    squeeze x1 -> x0, local copies, waits for them, and re-layouts: 1.04 us -> none  [on_device(): return (solved[:, 0], solved[:, 1], solved[:, 2], solved[:, 3])]
  transfers between devices with their start and end apart: 6 -> 5, of which waited for: 2 -> 1; matrix products, arithmetic and copies ran while one was open for 39% -> 25% of each run, Pallas kernels for 0% -> 0%
where the time goes in v1:
time: 44.6 us; the launch traced here: 43.8 us
  other arithmetic  14.5 us (33%)
  Pallas kernels  9.2 us (21%)
  starting transfers between devices  9.17 us (21%)
  local copies, waits for them, and re-layouts  8.83 us (20%)
  waiting for transfers between devices  1.26 us (3%)
  between operations  0.82 us (2%)
    pallas_call x1, Pallas kernels, on_device(): pl.pallas_call(step_kernel, out_shape=(plane,) * 4, in_specs=[smem] * 4 +...  9.2 us
    unnamed x4, other arithmetic  7.29 us
    ppermute x1, starting transfers between devices, on_device(): lax.ppermute(top, 'lat', [(i, i + 1) for i in range(n_lat - 1)])  5.58 us
    rev x1, local copies, waits for them, and re-layouts, on_device(): ghost = from_fold[:, ::-1, ::-1] * fold_sign  2.92 us
    concatenate x1, other arithmetic, on_device(): jnp.concatenate([north_rows, jnp.zeros((planes, rows - 4, cols), jnp.floa...  2.3 us
    unnamed x22, local copies, waits for them, and re-layouts  2.13 us
    concatenate x1, other arithmetic, on_device(): jnp.concatenate([from_east, jnp.zeros((planes, rows, cols - 4), jnp.float...  1.45 us
    ppermute x1, starting transfers between devices, on_device(): lax.ppermute(bottom, 'lat', [(i + 1, i) for i in range(n_lat - 1)])  1.41 us
  transfers between devices with their start and end apart: 5, of which 1 were waited for; matrix products, arithmetic and copies ran while one was open for 25% of the time, Pallas kernels for 0%

profile of v1, /device:TPU:0, one launch (start us, length us, event | category | flops | bytes accessed | tf_op | source)
XLA Modules:
  0.0 43.8 jit_solution(8131618607233773906)
XLA Ops:
  0.6 0.8 %multiply_convert_fusion.dep_ref = f32[8,128]{1,0:T(8,128)S(1)} fusion(s32[8,128]{1,0:T(8,128)} %param.11, s32[8,128]{1,0:T(8,128)} %param.12), kind=kLoop, calls=%fused_computation.25 | loop fusion | flops 2048 | bytes 12288 | tf_op jit(solution)/shard_map/convert_element_type | solution.py:190
  1.4 1.8 %select_dynamic-update-slice_fusion.3 = (f32[301,2,128]{2,1,0:T(2,128)}, f32[301,2,128]{2,1,0:T(2,128)}) fusion(f32[75,8,128]{2,1,0:T(8,128)} %t_ref.1, f32[2,128]{1,0:T(2,128)S(1)} %get-tuple-element.24, f32[2,128]{1,0:T(2,128)S(1)} %get-tuple-element.25), kind=kLoop, calls=%fused_computation.6 | loop fusion | flops 76798 | bytes 309248
  3.2 1.8 %select_dynamic-update-slice_fusion.2 = (f32[301,2,128]{2,1,0:T(2,128)}, f32[301,2,128]{2,1,0:T(2,128)}) fusion(f32[301,2,128]{2,1,0:T(2,128)} %get-tuple-element.18, f32[75,8,128]{2,1,0:T(8,128)} %s_ref.1, f32[2,128]{1,0:T(2,128)S(1)} %get-tuple-element.24, f32[301,2,128]{2,1,0:T(2,128)} %get-tuple-element.19, f32[2,128]{1,0:T(2,128)S(1)} %get-tuple-element.25), kind=kLoop, calls=%fused_computation.5 | loop fusion | flops 76800 | bytes 309248
  5.1 1.8 %select_dynamic-update-slice_fusion.1 = (f32[301,2,128]{2,1,0:T(2,128)}, f32[301,2,128]{2,1,0:T(2,128)}) fusion(f32[301,2,128]{2,1,0:T(2,128)} %get-tuple-element.16, f32[75,8,128]{2,1,0:T(8,128)} %u_ref.1, f32[2,128]{1,0:T(2,128)S(1)} %get-tuple-element.24, f32[301,2,128]{2,1,0:T(2,128)} %get-tuple-element.17, f32[2,128]{1,0:T(2,128)S(1)} %get-tuple-element.25), kind=kLoop, calls=%fused_computation.4 | loop fusion | flops 76800 | bytes 309248
  6.9 1.8 %select_dynamic-update-slice_fusion = (f32[301,2,128]{2,1,0:T(2,128)}, f32[301,2,128]{2,1,0:T(2,128)}) fusion(f32[301,2,128]{2,1,0:T(2,128)} %get-tuple-element.14, f32[75,8,128]{2,1,0:T(8,128)} %v_ref.1, f32[2,128]{1,0:T(2,128)S(1)} %get-tuple-element.24, f32[301,2,128]{2,1,0:T(2,128)} %get-tuple-element.15, f32[2,128]{1,0:T(2,128)S(1)} %get-tuple-element.25), kind=kLoop, calls=%fused_computation.3 | loop fusion | flops 76800 | bytes 309248
  8.7 0.6 %constant_dynamic-update-slice_fusion.1 = (f32[301,2,128]{2,1,0:T(2,128)}, f32[301,2,128]{2,1,0:T(2,128)}) fusion(f32[301,2,128]{2,1,0:T(2,128)} %get-tuple-element.12, f32[8,128]{1,0:T(8,128)S(1)} %multiply_convert_fusion.dep_ref, f32[301,2,128]{2,1,0:T(2,128)} %get-tuple-element.13), kind=kLoop, calls=%fused_computation.14 | loop fusion | bytes 4096 | tf_op jit(solution)/shard_map/concatenate | solution.py:197
  9.3 1.4 %collective-permute-start = (f32[301,2,128]{2,1,0:T(2,128)}, f32[301,2,128]{2,1,0:T(2,128)}, u32[]{:S(2)}, u32[]{:S(2)}) collective-permute-start(f32[301,2,128]{2,1,0:T(2,128)} %get-tuple-element.23), channel_id=1, source_target_pairs={{28,31},{29,30},{30,29},{31,28}} | collective-permute-start | bytes 924680 | tf_op jit(solution)/shard_map/ppermute | solution.py:210
  10.7 5.6 %collective-permute-start.2 = (f32[301,2,128]{2,1,0:T(2,128)}, f32[301,2,128]{2,1,0:T(2,128)}, u32[]{:S(2)}, u32[]{:S(2)}) collective-permute-start(f32[301,2,128]{2,1,0:T(2,128)} %get-tuple-element.23), channel_id=1, source_target_pairs={{0,4},{4,8},{8,12},{12,16},{16,20},{20,24},{24,28},{1,5},{5,9},{9,... | collective-permute-start | bytes 924680 | tf_op jit(solution)/shard_map/ppermute | solution.py:205
  16.2 1.4 %collective-permute-start.1 = (f32[301,2,128]{2,1,0:T(2,128)}, f32[301,2,128]{2,1,0:T(2,128)}, u32[]{:S(2)}, u32[]{:S(2)}) collective-permute-start(f32[301,2,128]{2,1,0:T(2,128)} %get-tuple-element.22), channel_id=1, source_target_pairs={{4,0},{8,4},{12,8},{16,12},{20,16},{24,20},{28,24},{5,1},{9,5},{13... | collective-permute-start | bytes 924680 | tf_op jit(solution)/shard_map/ppermute | solution.py:206
  18.2 0.6 %copy-done.3 = f32[75,8,128]{2,1,0:T(8,128)S(1)} copy-done((f32[75,8,128]{2,1,0:T(8,128)S(1)}, f32[75,8,128]{2,1,0:T(8,128)}, u32[]{:S(2)}) %copy-start.3) | copy-done | bytes 307224
  19.3 0.2 copy.32
  19.5 0.2 copy.33
  20.1 0.7 %collective-permute-start.3 = (f32[301,8,2]{0,1,2:T(8,128)S(1)}, f32[301,8,2]{0,1,2:T(8,128)S(1)}, u32[]{:S(2)}, u32[]{:S(2)}) collective-permute-start(f32[301,8,2]{0,1,2:T(8,128)S(1)} %concatenate.25), channel_id=1, source_target_pairs={{1,0},{2,1},{3,2},{0,3},{5,4},{6,5},{7,6},{4,7},{9,8},{10,9},{11,1... | collective-permute-start | bytes 57800 | tf_op jit(solution)/shard_map/ppermute | solution.py:208
  22.0 0.5 %broadcast_divide_fusion.inv_h_ref = f32[75]{0:T(128)} fusion(), kind=kLoop, calls=%fused_computation.30 | loop fusion | flops 300 | bytes 300 | tf_op jit(solution)/shard_map/div | solution.py:236
  22.6 0.6 %pad_maximum_fusion.2 = (f32[75]{0:T(128)}, f32[75]{0:T(128)}) fusion(f32[1]{0:T(128)} %constant.43.clone.1, f32[74]{0:T(128)S(1)} %multiply_divide_fusion), kind=kLoop, calls=%fused_computation.26 | loop fusion | flops 225 | bytes 900 | tf_op jit(solution)/shard_map/concatenate | solution.py:238
  23.4 0.6 %copy.29 = f32[301,8,2]{2,1,0:T(8,128)S(1)} copy(f32[301,8,2]{0,1,2:T(8,128)S(1)} %collective-permute-done.3) | data formatting | bytes 38528 | tf_op jit(solution)/shard_map/ppermute | solution.py:208
  24.0 1.2 %collective-permute-done.4 = f32[301,8,2]{0,1,2:T(8,128)S(1)} collective-permute-done((f32[301,8,2]{0,1,2:T(8,128)S(1)}, f32[301,8,2]{0,1,2:T(8,128)S(1)}, u32[]{:S(2)}, u32[]{:S(2)}) %collective-permute-start.4) | collective-permute-done | bytes 19296 | tf_op jit(solution)/shard_map/ppermute | solution.py:207
  25.2 0.6 %copy.30 = f32[301,8,2]{2,1,0:T(8,128)S(1)} copy(f32[301,8,2]{0,1,2:T(8,128)S(1)} %collective-permute-done.4) | data formatting | bytes 38528 | tf_op jit(solution)/shard_map/ppermute | solution.py:207
  25.8 1.5 %pad_maximum_fusion.1.elon_ref = f32[301,8,128]{2,1,0:T(8,128)} fusion(f32[301,8,2]{2,1,0:T(8,128)S(1)} %copy.30, f32[301,8,2]{2,1,0:T(8,128)S(1)} %copy.29, f32[128]{0:T(128)S(1)} %pad.1.clone), kind=kLoop, calls=%fused_computation.1 | loop fusion | flops 616448 | bytes 1271936 | tf_op jit(solution)/shard_map/concatenate | solution.py:224
  27.3 2.9 %rev.3 = f32[301,2,128]{2,1,0:T(2,128)S(1)} reverse(f32[301,2,128]{2,1,0:T(2,128)} %collective-permute-done), dimensions={1,2} | reverse | bytes 616448 | tf_op jit(solution)/shard_map/rev | solution.py:218
  30.2 1.4 %multiply_select_fusion = f32[301,2,128]{2,1,0:T(2,128)S(1)} fusion(f32[301,2,128]{2,1,0:T(2,128)} %collective-permute-done.1, f32[301,2,128]{2,1,0:T(2,128)S(1)} %rev.3, pred[]{:T(512)S(6)} %eq.3, f32[301]{0:T(512)S(1)} %copy-done.5), kind=kLoop, calls=%fused_computation.2 | loop fusion | flops 154112 | bytes 925877 | tf_op jit(solution)/shard_map/jit(_where)/select_n | solution.py:220
  31.6 2.3 %pad_maximum_fusion.elat_ref = f32[301,8,128]{2,1,0:T(8,128)} fusion(f32[301,2,128]{2,1,0:T(2,128)} %collective-permute-done.2, f32[301,2,128]{2,1,0:T(2,128)S(1)} %multiply_select_fusion, f32[8]{0:T(128)S(1)} %pad.4.clone), kind=kLoop, calls=%fused_computation | loop fusion | flops 616448 | bytes 1849376 | tf_op jit(solution)/shard_map/concatenate | solution.py:221
  33.9 0.7 %broadcast_in_dim.14.f_ref = f32[8,128]{1,0:T(8,128)} broadcast(f32[8]{0:T(128)S(1)} %add_multiply_fusion), dimensions={0} | broadcast | bytes 4128 | tf_op jit(solution)/shard_map/broadcast_in_dim | solution.py:231
  34.6 9.2 %shard_map.102 = (f32[75,8,128]{2,1,0:T(8,128)}, f32[75,8,128]{2,1,0:T(8,128)}, f32[75,8,128]{2,1,0:T(8,128)}, f32[75,8,128]{2,1,0:T(8,128)}) custom-call(f32[75]{0:T(128)} %copy-done.6, f32[75]{0:T(128)} %broadcast_divide_fusion.inv_h_ref, f32[75]{0:T(128)} %get-tuple-element.35.zmid_ref, f32[75]{0:T(128)} %get-tuple-element.34.inv_sp_ref, ...), custom_call_target="tpu_custom_call" | custom-call | tf_op jit(solution)/shard_map/pallas_call | solution.py:243
  (45 shorter events, 2.8 us)
Async XLA Ops:
  0.6 17.1 %copy-start = (f32[75,8,128]{2,1,0:T(8,128)S(1)}, f32[75,8,128]{2,1,0:T(8,128)}, u32[]{:S(2)}) copy-start(f32[75,8,128]{2,1,0:T(8,128)} %t_ref.1) | copy-start | bytes 921604
  1.4 16.5 %copy-start.4 = (f32[8,128]{1,0:T(8,128)}, f32[8,128]{1,0:T(8,128)S(1)}, u32[]{:S(2)}) copy-start(f32[8,128]{1,0:T(8,128)S(1)} %multiply_convert_fusion.dep_ref) | copy-start | bytes 12292
  1.4 16.5 %copy-start.1 = (f32[75,8,128]{2,1,0:T(8,128)S(1)}, f32[75,8,128]{2,1,0:T(8,128)}, u32[]{:S(2)}) copy-start(f32[75,8,128]{2,1,0:T(8,128)} %s_ref.1) | copy-start | bytes 921604
  9.3 18.0 %collective-permute-start = (f32[301,2,128]{2,1,0:T(2,128)}, f32[301,2,128]{2,1,0:T(2,128)}, u32[]{:S(2)}, u32[]{:S(2)}) collective-permute-start(f32[301,2,128]{2,1,0:T(2,128)} %get-tuple-element.23), channel_id=1, source_target_pairs={{28,31},{29,30},{30,29},{31,28}} | collective-permute-start | bytes 924680 | tf_op jit(solution)/shard_map/ppermute | solution.py:210
  10.7 21.0 %collective-permute-start.2 = (f32[301,2,128]{2,1,0:T(2,128)}, f32[301,2,128]{2,1,0:T(2,128)}, u32[]{:S(2)}, u32[]{:S(2)}) collective-permute-start(f32[301,2,128]{2,1,0:T(2,128)} %get-tuple-element.23), channel_id=1, source_target_pairs={{0,4},{4,8},{8,12},{12,16},{16,20},{20,24},{24,28},{1,5},{5,9},{9,... | collective-permute-start | bytes 924680 | tf_op jit(solution)/shard_map/ppermute | solution.py:205
  16.2 1.8 %copy-start.2 = (f32[75,8,128]{2,1,0:T(8,128)S(1)}, f32[75,8,128]{2,1,0:T(8,128)}, u32[]{:S(2)}) copy-start(f32[75,8,128]{2,1,0:T(8,128)} %u_ref.1) | copy-start | bytes 921604
  16.2 14.0 %collective-permute-start.1 = (f32[301,2,128]{2,1,0:T(2,128)}, f32[301,2,128]{2,1,0:T(2,128)}, u32[]{:S(2)}, u32[]{:S(2)}) collective-permute-start(f32[301,2,128]{2,1,0:T(2,128)} %get-tuple-element.22), channel_id=1, source_target_pairs={{4,0},{8,4},{12,8},{16,12},{20,16},{24,20},{28,24},{5,1},{9,5},{13... | collective-permute-start | bytes 924680 | tf_op jit(solution)/shard_map/ppermute | solution.py:206
  17.9 1.0 %copy-start.3 = (f32[75,8,128]{2,1,0:T(8,128)S(1)}, f32[75,8,128]{2,1,0:T(8,128)}, u32[]{:S(2)}) copy-start(f32[75,8,128]{2,1,0:T(8,128)} %v_ref.1) | copy-start | bytes 921604
  20.1 3.3 %collective-permute-start.3 = (f32[301,8,2]{0,1,2:T(8,128)S(1)}, f32[301,8,2]{0,1,2:T(8,128)S(1)}, u32[]{:S(2)}, u32[]{:S(2)}) collective-permute-start(f32[301,8,2]{0,1,2:T(8,128)S(1)} %concatenate.25), channel_id=1, source_target_pairs={{1,0},{2,1},{3,2},{0,3},{5,4},{6,5},{7,6},{4,7},{9,8},{10,9},{11,1... | collective-permute-start | bytes 57800 | tf_op jit(solution)/shard_map/ppermute | solution.py:208
  21.9 3.3 %collective-permute-start.4 = (f32[301,8,2]{0,1,2:T(8,128)S(1)}, f32[301,8,2]{0,1,2:T(8,128)S(1)}, u32[]{:S(2)}, u32[]{:S(2)}) collective-permute-start(f32[301,8,2]{0,1,2:T(8,128)S(1)} %concatenate.26), channel_id=1, source_target_pairs={{0,1},{1,2},{2,3},{3,0},{4,5},{5,6},{6,7},{7,4},{8,9},{9,10},{10,1... | collective-permute-start | bytes 57800 | tf_op jit(solution)/shard_map/ppermute | solution.py:207
  22.0 3.8 %copy-start.6 = (f32[75]{0:T(128)}, f32[75]{0:T(128)S(1)}, u32[]{:S(2)}) copy-start(f32[75]{0:T(128)S(1)} %broadcast_add_fusion.h_ref) | copy-start | bytes 904
  25.8 4.4 %copy-start.5 = (f32[301]{0:T(512)S(1)}, f32[301]{0:T(512)}, u32[]{:S(2)}) copy-start(f32[301]{0:T(512)} %constant.51.clone.1) | copy-start | bytes 3616

commit v2 on v1

--- a/solution.py
+++ b/solution.py
@@ -1,3 +1,4 @@
+import numpy as np
 import jax
 import jax.numpy as jnp
 from jax import lax
@@ -19,6 +20,8 @@
 bottom_drag = 1.0
 surface_gain = 0.5
 
+GROUP = 15
+
 
 def density(warmth, saltiness, depth_column):
     return -thermal * warmth * (1.0 + thermal_sq * warmth + depth_column) + haline * saltiness
@@ -31,15 +34,80 @@
     ) * (1.0 / 6.0)
 
 
+def rolled(x, shift, axis):
+    shift %= x.shape[axis]
+    return x if shift == 0 else pltpu.roll(x, shift, axis)
+
+
+def pack_kernel(
+    last_ref, shore_ref, bottom_ref, t_ref, s_ref, u_ref, v_ref,
+    top_ref, bot_ref, fold_ref, right_ref, left_ref,
+):
+    layers, rows, cols = t_ref.shape
+    groups = layers // GROUP
+    lane = lax.broadcasted_iota(jnp.int32, (rows, cols), 1)
+    row = lax.broadcasted_iota(jnp.int32, (rows, cols), 0)
+    dep = (shore_ref[...] * bottom_ref[...]).astype(jnp.float32)
+    zero = jnp.zeros((rows, cols), jnp.float32)
+
+    def pack_rows(vals, first):
+        out = zero
+        for c, val in enumerate(vals):
+            out = jnp.where((row >> 1) == c, rolled(val, 2 * c - first, 0), out)
+        return out
+
+    def group_body(g, carry):
+        right = zero
+        left = zero
+        for j in range(GROUP):
+            k = g * GROUP + j
+            w = (k.astype(jnp.float32) < dep).astype(jnp.float32)
+            q = [r[k] * w for r in (t_ref, s_ref, u_ref, v_ref)]
+            top_ref[k] = pack_rows(q, rows - 2)
+            bot_ref[k] = pack_rows(q, 0)
+            for c in range(4):
+                m = j * 4 + c
+                slot = (lane >> 1) == m
+                right = jnp.where(slot, rolled(q[c], 2 * m - (cols - 2), 1), right)
+                left = jnp.where(slot, rolled(q[c], 2 * m, 1), left)
+        right_ref[g] = right
+        left_ref[g] = left
+        return carry
+
+    lax.fori_loop(0, groups, group_body, 0)
+    top_ref[layers] = pack_rows([dep], rows - 2)
+    bot_ref[layers] = pack_rows([dep], 0)
+    right_ref[groups] = jnp.where(lane < 2, rolled(dep, 2, 1), zero)
+    left_ref[groups] = jnp.where(lane < 2, dep, zero)
+
+    @pl.when(last_ref[0] == 1)
+    def _():
+        sign = jnp.where(row < 4, 1.0, -1.0)
+        masks = [(lane & (1 << b)) != 0 for b in range(7)]
+
+        def fold_body(k, carry):
+            tile = top_ref[k]
+            swapped = jnp.where((row & 1) == 0, rolled(tile, -1, 0), rolled(tile, 1, 0)) * sign
+            for b in range(7):
+                swapped = jnp.where(
+                    masks[b], rolled(swapped, 1 << b, 1), rolled(swapped, -(1 << b), 1)
+                )
+            fold_ref[k] = swapped
+            return carry
+
+        lax.fori_loop(0, layers + 1, fold_body, 0)
+
+
 def step_kernel(
-    h_ref, inv_h_ref, zmid_ref, inv_sp_ref,
-    f_ref, dep_ref, flux_ref, t_ref, s_ref, u_ref, v_ref, elat_ref, elon_ref,
+    lat_ref, h_ref, inv_h_ref, zmid_ref, inv_sp_ref,
+    shore_ref, bottom_ref, flux_ref, t_ref, s_ref, u_ref, v_ref,
+    south_ref, north_ref, fold_ref, west_ref, east_ref,
     o0_ref, o1_ref, o2_ref, o3_ref,
     star_scr, r_scr, rs_scr,
 ):
     layers = t_ref.shape[0]
     rows, cols = t_ref.shape[1], t_ref.shape[2]
-    depth_plane = 4 * layers
+    groups = layers // GROUP
     lane = lax.broadcasted_iota(jnp.int32, (rows, cols), 1)
     row = lax.broadcasted_iota(jnp.int32, (rows, cols), 0)
 
@@ -61,15 +129,33 @@
             return pltpu.roll(jnp.where(row == rows - 1, e, v), 1, 0)
         return pltpu.roll(jnp.where(row >= rows - 2, e, v), 2, 0)
 
-    dep = dep_ref[...]
-    dep_xm = xs(dep, elon_ref[depth_plane], -1)
-    dep_xp = xs(dep, elon_ref[depth_plane], 1)
-    dep_ym = ys(dep, elat_ref[depth_plane], -1)
-    dep_yp = ys(dep, elat_ref[depth_plane], 1)
-    turning = f_ref[...]
+    def lat_edge(tile_n, tile_s, c):
+        return jnp.where(row < 4, rolled(tile_n, -2 * c, 0), rolled(tile_s, rows - 2 - 2 * c, 0))
+
+    def lon_edge(tile_e, tile_w, m):
+        return jnp.where(lane < 64, rolled(tile_e, -2 * m, 1), rolled(tile_w, cols - 2 - 2 * m, 1))
+
+    dep = (shore_ref[...] * bottom_ref[...]).astype(jnp.float32)
+    dep_lat = lat_edge(north_ref[layers] + fold_ref[layers], south_ref[layers], 0)
+    dep_lon = lon_edge(east_ref[groups], west_ref[groups], 0)
+    dep_xm = xs(dep, dep_lon, -1)
+    dep_xp = xs(dep, dep_lon, 1)
+    dep_ym = ys(dep, dep_lat, -1)
+    dep_yp = ys(dep, dep_lat, 1)
+    total_rows = rows * lat_ref[1]
+    row_ids = (lat_ref[0] * rows + row).astype(jnp.float32)
+    turning = coriolis * (2.0 * (row_ids + 0.5) / total_rows.astype(jnp.float32) - 1.0)
     zero = jnp.zeros((rows, cols), jnp.float32)
 
-    def explicit(k, carry):
+    def explicit_group(g, carry):
+        tile_e = east_ref[g]
+        tile_w = west_ref[g]
+        for j in range(GROUP):
+            k = g * GROUP + j
+            carry = explicit(k, j, tile_e, tile_w, carry)
+        return carry
+
+    def explicit(k, j, tile_e, tile_w, carry):
         cum_xm, cum_xp, cum_ym, cum_yp = carry
         kf = k.astype(jnp.float32)
         h = h_ref[k]
@@ -80,8 +166,10 @@
         wym = (kf < dep_ym).astype(jnp.float32)
         wyp = (kf < dep_yp).astype(jnp.float32)
         q = [r[k] * w0 for r in (t_ref, s_ref, u_ref, v_ref)]
-        ex = [elon_ref[c * layers + k] for c in range(4)]
-        ey = [elat_ref[c * layers + k] for c in range(4)]
+        tile_n = north_ref[k] + fold_ref[k]
+        tile_s = south_ref[k]
+        ey = [lat_edge(tile_n, tile_s, c) for c in range(4)]
+        ex = [lon_edge(tile_e, tile_w, j * 4 + c) for c in range(4)]
         xsh = {s: [xs(q[c], ex[c], s) for c in range(4)] for s in (-2, -1, 1, 2)}
         ysh = {s: [ys(q[c], ey[c], s) for c in range(4)] for s in (-2, -1, 1, 2)}
         a_r = 0.5 * (q[2] + xsh[1][2]) * w0 * wxp
@@ -116,7 +204,7 @@
         rs_scr[k] = density(star0, star1, zmid)
         return (cum_xm, cum_xp, cum_ym, cum_yp)
 
-    lax.fori_loop(0, layers, explicit, (zero, zero, zero, zero), unroll=3)
+    lax.fori_loop(0, groups, explicit_group, (zero, zero, zero, zero))
 
     surface_scale = surface_gain * inv_h_ref[0]
     w_top = (0.0 < dep).astype(jnp.float32)
@@ -176,6 +264,16 @@
     lax.fori_loop(0, layers, backward, (zero,) * 4, unroll=3)
 
 
+def level_tables(layers):
+    offsets = np.arange(layers, dtype=np.float32) + np.float32(0.5)
+    zmid = offsets / np.float32(layers)
+    thickness = np.float32(0.5) + zmid
+    inverse = np.float32(1.0) / thickness
+    spacing = np.float32(0.5) * (thickness[1:] + thickness[:-1])
+    inv_spacing = np.concatenate([np.float32(1.0) / spacing, np.ones((1,), np.float32)])
+    return [jnp.asarray(t.astype(np.float32)) for t in (thickness, inverse, zmid, inv_spacing)]
+
+
 def on_device(
     heat_anomaly,
     brine_anomaly,
@@ -187,63 +285,38 @@
 ):
     layers, rows, cols = heat_anomaly.shape
     fields = (heat_anomaly, brine_anomaly, eastward_current, northward_current)
-    depth_plane = (shoreline_indicator * bottom_layer_index).astype(jnp.float32)
-    level_ids = jnp.arange(layers, dtype=jnp.float32)[:, None, None]
-
-    def edge(row_slice, col_slice):
-        d = depth_plane[row_slice, col_slice]
-        wet = (level_ids < d[None]).astype(jnp.float32)
-        parts = [x[:, row_slice, col_slice] * wet for x in fields]
-        return jnp.concatenate(parts + [d[None]], axis=0)
-
+    groups = layers // GROUP
     n_lat = lax.axis_size("lat")
     n_lon = lax.axis_size("lon")
-    top = edge(slice(rows - 2, rows), slice(None))
-    bottom = edge(slice(0, 2), slice(None))
-    right = edge(slice(None), slice(cols - 2, cols))
-    left = edge(slice(None), slice(0, 2))
+    lat_idx = lax.axis_index("lat").astype(jnp.int32)
+    is_last = (lat_idx == n_lat - 1).astype(jnp.int32).reshape(1)
+    lat_info = jnp.stack([lat_idx, jnp.int32(n_lat)])
+
+    smem = pl.BlockSpec(memory_space=pltpu.SMEM)
+    vmem = pl.BlockSpec(memory_space=pltpu.VMEM)
+    row_tiles = jax.ShapeDtypeStruct((layers + 1, rows, cols), jnp.float32)
+    col_tiles = jax.ShapeDtypeStruct((groups + 1, rows, cols), jnp.float32)
+    top, bot, fold, right, left = pl.pallas_call(
+        pack_kernel,
+        out_shape=(row_tiles, row_tiles, row_tiles, col_tiles, col_tiles),
+        in_specs=[smem] + [vmem] * 6,
+        out_specs=(vmem,) * 5,
+    )(is_last, shoreline_indicator, bottom_layer_index, *fields)
+
     from_south = lax.ppermute(top, "lat", [(i, i + 1) for i in range(n_lat - 1)])
-    from_north = lax.ppermute(bottom, "lat", [(i + 1, i) for i in range(n_lat - 1)])
+    from_north = lax.ppermute(bot, "lat", [(i + 1, i) for i in range(n_lat - 1)])
     from_west = lax.ppermute(right, "lon", [(i, (i + 1) % n_lon) for i in range(n_lon)])
     from_east = lax.ppermute(left, "lon", [((i + 1) % n_lon, i) for i in range(n_lon)])
     last = (n_lat - 1) * n_lon
     from_fold = lax.ppermute(
-        top, ("lat", "lon"), [(last + x, last + n_lon - 1 - x) for x in range(n_lon)]
-    )
-    planes = 4 * layers + 1
-    fold_sign = jnp.concatenate(
-        [jnp.ones((2 * layers,), jnp.float32), -jnp.ones((2 * layers,), jnp.float32),
-         jnp.ones((1,), jnp.float32)]
-    )[:, None, None]
-    ghost = from_fold[:, ::-1, ::-1] * fold_sign
-    is_north = lax.axis_index("lat") == n_lat - 1
-    north_rows = jnp.where(is_north, ghost, from_north)
-    edge_lat = jnp.concatenate(
-        [north_rows, jnp.zeros((planes, rows - 4, cols), jnp.float32), from_south], axis=1
-    )
-    edge_lon = jnp.concatenate(
-        [from_east, jnp.zeros((planes, rows, cols - 4), jnp.float32), from_west], axis=2
-    )
-
-    row_ids = lax.axis_index("lat") * rows + jnp.arange(rows, dtype=jnp.int32)
-    total_rows = rows * n_lat
-    turning_rate = coriolis * (2.0 * (row_ids.astype(jnp.float32) + 0.5) / total_rows - 1.0)
-    turning_plane = jnp.broadcast_to(turning_rate[:, None], (rows, cols))
-
-    offsets = jnp.arange(layers, dtype=jnp.float32) + 0.5
-    thickness = 0.5 + offsets / layers
-    zmid = offsets / layers
-    inverse = 1.0 / thickness
-    spacing = 0.5 * (thickness[1:] + thickness[:-1])
-    inv_spacing = jnp.concatenate([1.0 / spacing, jnp.ones((1,), jnp.float32)])
-
-    smem = pl.BlockSpec(memory_space=pltpu.SMEM)
-    vmem = pl.BlockSpec(memory_space=pltpu.VMEM)
+        fold, ("lat", "lon"), [(last + x, last + n_lon - 1 - x) for x in range(n_lon)]
+    )
+
     plane = jax.ShapeDtypeStruct((layers, rows, cols), jnp.float32)
     outs = pl.pallas_call(
         step_kernel,
         out_shape=(plane,) * 4,
-        in_specs=[smem] * 4 + [vmem] * 9,
+        in_specs=[smem] * 5 + [vmem] * 12,
         out_specs=(vmem,) * 4,
         scratch_shapes=[
             pltpu.VMEM((4 * layers, rows, cols), jnp.float32),
@@ -251,10 +324,9 @@
             pltpu.VMEM((layers, rows, cols), jnp.float32),
         ],
     )(
-        thickness, inverse, zmid, inv_spacing,
-        turning_plane, depth_plane, boundary_fluxes,
-        heat_anomaly, brine_anomaly, eastward_current, northward_current,
-        edge_lat, edge_lon,
+        lat_info, *level_tables(layers),
+        shoreline_indicator, bottom_layer_index, boundary_fluxes, *fields,
+        from_south, from_north, from_fold, from_west, from_east,
     )
     return tuple(outs)
 

time: 44.6 us -> 71.4 us (1.60)
  the two profiles are of different devices: /device:TPU:0 before, /device:TPU:27 now
where the time goes in v2:
time: 71.4 us; the launch traced here: 71.2 us
  Pallas kernels  50.6 us (71%)
  starting transfers between devices  10.1 us (14%)
  waiting for transfers between devices  7.57 us (11%)
  local copies, waits for them, and re-layouts  1.52 us (2%)
    pallas_call x1, Pallas kernels, on_device(): pl.pallas_call(pack_kernel, out_shape=(row_tiles, row_tiles, row_tiles, c...  40 us
    pallas_call x1, Pallas kernels, on_device(): pl.pallas_call(step_kernel, out_shape=(plane,) * 4, in_specs=[smem] * 5 +...  10.7 us
    ppermute x1, waiting for transfers between devices, on_device(): lax.ppermute(right, 'lon', [(i, (i + 1) % n_lon) for i in range(n_lon)])  6.14 us
    ppermute x1, starting transfers between devices, on_device(): lax.ppermute(fold, ('lat', 'lon'), [(last + x, last + n_lon - 1 - x) for...  4.27 us
    ppermute x1, starting transfers between devices, on_device(): lax.ppermute(bot, 'lat', [(i + 1, i) for i in range(n_lat - 1)])  4 us
    unnamed x10, local copies, waits for them, and re-layouts  1.52 us
  transfers between devices with their start and end apart: 5, of which 2 were waited for; matrix products, arithmetic and copies ran while one was open for 1% of the time, Pallas kernels for 0%

profile of v2, /device:TPU:27, one launch (start us, length us, event | category | flops | bytes accessed | tf_op | source)
XLA Modules:
  0.0 71.2 jit_solution(11315330979209708875)
XLA Ops:
  0.6 40.0 %shard_map.138 = (f32[76,8,128]{2,1,0:T(8,128)}, f32[76,8,128]{2,1,0:T(8,128)}, f32[76,8,128]{2,1,0:T(8,128)}, f32[6,8,128]{2,1,0:T(8,128)}, f32[6,8,128]{2,1,0:T(8,128)}) custom-call(s32[1]{0:T(128)} %bitcast.1.last_ref, s32[8,128]{1,0:T(8,128)} %shore_ref.3, s32[8,128]{1,0:T(8,128)} %bottom_ref.3, f32[75,8,128]{2,1,0:T(8,128)} %t_ref.3, ...), custom_call_target="tpu_custom_call" | custom-call | tf_op jit(solution)/shard_map/pallas_call | solution.py:299
  40.6 1.3 %collective-permute-start = (f32[76,8,128]{2,1,0:T(8,128)}, f32[76,8,128]{2,1,0:T(8,128)S(1)}, u32[]{:S(2)}, u32[]{:S(2)}) collective-permute-start(f32[76,8,128]{2,1,0:T(8,128)} %get-tuple-element.9), channel_id=1, source_target_pairs={{0,4},{4,8},{8,12},{12,16},{16,20},{20,24},{24,28},{1,5},{5,9},{9,... | collective-permute-start | bytes 933896 | tf_op jit(solution)/shard_map/ppermute | solution.py:306
  41.9 4.0 %collective-permute-start.1 = (f32[76,8,128]{2,1,0:T(8,128)}, f32[76,8,128]{2,1,0:T(8,128)S(1)}, u32[]{:S(2)}, u32[]{:S(2)}) collective-permute-start(f32[76,8,128]{2,1,0:T(8,128)} %get-tuple-element.10), channel_id=1, source_target_pairs={{4,0},{8,4},{12,8},{16,12},{20,16},{24,20},{28,24},{5,1},{9,5},{13... | collective-permute-start | bytes 933896 | tf_op jit(solution)/shard_map/ppermute | solution.py:307
  45.9 4.3 %collective-permute-start.2 = (f32[76,8,128]{2,1,0:T(8,128)}, f32[76,8,128]{2,1,0:T(8,128)S(1)}, u32[]{:S(2)}, u32[]{:S(2)}) collective-permute-start(f32[76,8,128]{2,1,0:T(8,128)} %get-tuple-element.11), channel_id=1, source_target_pairs={{28,31},{29,30},{30,29},{31,28}} | collective-permute-start | bytes 933896 | tf_op jit(solution)/shard_map/ppermute | solution.py:311
  50.2 0.1 collective-permute-start.3
  50.2 0.5 collective-permute-start.4
  50.7 0.6 pad_add_fusion.lat_ref
  51.4 6.1 %collective-permute-done.3.west_ref = f32[6,8,128]{2,1,0:T(8,128)S(1)} collective-permute-done((f32[6,8,128]{2,1,0:T(8,128)}, f32[6,8,128]{2,1,0:T(8,128)S(1)}, u32[]{:S(2)}, u32[]{:S(2)}) %collective-permute-start.3) | collective-permute-done | bytes 24608 | tf_op jit(solution)/shard_map/ppermute | solution.py:308
  57.5 0.0 copy-start.3
  57.5 1.4 %collective-permute-done.4.east_ref = f32[6,8,128]{2,1,0:T(8,128)S(1)} collective-permute-done((f32[6,8,128]{2,1,0:T(8,128)}, f32[6,8,128]{2,1,0:T(8,128)S(1)}, u32[]{:S(2)}, u32[]{:S(2)}) %collective-permute-start.4) | collective-permute-done | bytes 24608 | tf_op jit(solution)/shard_map/ppermute | solution.py:309
  59.0 0.0 copy-start.4
  59.0 0.0 collective-permute-done.south_ref
  59.0 0.0 copy-start
  59.0 0.0 collective-permute-done.1.north_ref
  59.0 0.0 copy-start.1
  59.0 0.0 collective-permute-done.2.fold_ref
  59.0 0.0 copy-done.3
  59.0 0.6 copy-done.4
  59.6 0.1 copy-done
  59.7 0.1 copy-done.1
  59.8 0.0 copy-start.2
  59.8 0.7 copy-done.2
  60.5 10.7 %shard_map.139 = (f32[75,8,128]{2,1,0:T(8,128)}, f32[75,8,128]{2,1,0:T(8,128)}, f32[75,8,128]{2,1,0:T(8,128)}, f32[75,8,128]{2,1,0:T(8,128)}) custom-call(s32[2]{0:T(128)} %pad_add_fusion.lat_ref, f32[75]{0:T(128)} %constant.18.clone.h_ref, f32[75]{0:T(128)} %constant.19.clone.inv_h_ref, f32[75]{0:T(128)} %constant.20.clone.zmid_ref, ...), custom_call_target="tpu_custom_call" | custom-call | tf_op jit(solution)/shard_map/pallas_call | solution.py:316
Async XLA Ops:
  40.6 18.4 %collective-permute-start = (f32[76,8,128]{2,1,0:T(8,128)}, f32[76,8,128]{2,1,0:T(8,128)S(1)}, u32[]{:S(2)}, u32[]{:S(2)}) collective-permute-start(f32[76,8,128]{2,1,0:T(8,128)} %get-tuple-element.9), channel_id=1, source_target_pairs={{0,4},{4,8},{8,12},{12,16},{16,20},{20,24},{24,28},{1,5},{5,9},{9,... | collective-permute-start | bytes 933896 | tf_op jit(solution)/shard_map/ppermute | solution.py:306
  41.9 17.1 %collective-permute-start.1 = (f32[76,8,128]{2,1,0:T(8,128)}, f32[76,8,128]{2,1,0:T(8,128)S(1)}, u32[]{:S(2)}, u32[]{:S(2)}) collective-permute-start(f32[76,8,128]{2,1,0:T(8,128)} %get-tuple-element.10), channel_id=1, source_target_pairs={{4,0},{8,4},{12,8},{16,12},{20,16},{24,20},{28,24},{5,1},{9,5},{13... | collective-permute-start | bytes 933896 | tf_op jit(solution)/shard_map/ppermute | solution.py:307
  45.9 13.1 %collective-permute-start.2 = (f32[76,8,128]{2,1,0:T(8,128)}, f32[76,8,128]{2,1,0:T(8,128)S(1)}, u32[]{:S(2)}, u32[]{:S(2)}) collective-permute-start(f32[76,8,128]{2,1,0:T(8,128)} %get-tuple-element.11), channel_id=1, source_target_pairs={{28,31},{29,30},{30,29},{31,28}} | collective-permute-start | bytes 933896 | tf_op jit(solution)/shard_map/ppermute | solution.py:311
  50.2 7.3 %collective-permute-start.3 = (f32[6,8,128]{2,1,0:T(8,128)}, f32[6,8,128]{2,1,0:T(8,128)S(1)}, u32[]{:S(2)}, u32[]{:S(2)}) collective-permute-start(f32[6,8,128]{2,1,0:T(8,128)} %get-tuple-element.12), channel_id=1, source_target_pairs={{0,1},{1,2},{2,3},{3,0},{4,5},{5,6},{6,7},{7,4},{8,9},{9,10},{10,1... | collective-permute-start | bytes 73736 | tf_op jit(solution)/shard_map/ppermute | solution.py:308
  50.2 8.7 %collective-permute-start.4 = (f32[6,8,128]{2,1,0:T(8,128)}, f32[6,8,128]{2,1,0:T(8,128)S(1)}, u32[]{:S(2)}, u32[]{:S(2)}) collective-permute-start(f32[6,8,128]{2,1,0:T(8,128)} %get-tuple-element.13), channel_id=1, source_target_pairs={{1,0},{2,1},{3,2},{0,3},{5,4},{6,5},{7,6},{4,7},{9,8},{10,9},{11,1... | collective-permute-start | bytes 73736 | tf_op jit(solution)/shard_map/ppermute | solution.py:309
  57.5 1.5 %copy-start.3 = (f32[6,8,128]{2,1,0:T(8,128)}, f32[6,8,128]{2,1,0:T(8,128)S(1)}, u32[]{:S(2)}) copy-start(f32[6,8,128]{2,1,0:T(8,128)S(1)} %collective-permute-done.3.west_ref) | copy-start | bytes 73732
  59.0 0.6 copy-start.4
  59.0 0.7 %copy-start = (f32[76,8,128]{2,1,0:T(8,128)}, f32[76,8,128]{2,1,0:T(8,128)S(1)}, u32[]{:S(2)}) copy-start(f32[76,8,128]{2,1,0:T(8,128)S(1)} %collective-permute-done.south_ref) | copy-start | bytes 933892
  59.0 0.8 %copy-start.1 = (f32[76,8,128]{2,1,0:T(8,128)}, f32[76,8,128]{2,1,0:T(8,128)S(1)}, u32[]{:S(2)}) copy-start(f32[76,8,128]{2,1,0:T(8,128)S(1)} %collective-permute-done.1.north_ref) | copy-start | bytes 933892
  59.8 0.7 copy-start.2

commit v3 on v2

--- a/solution.py
+++ b/solution.py
@@ -82,20 +82,20 @@
 
     @pl.when(last_ref[0] == 1)
     def _():
-        sign = jnp.where(row < 4, 1.0, -1.0)
-        masks = [(lane & (1 << b)) != 0 for b in range(7)]
-
-        def fold_body(k, carry):
-            tile = top_ref[k]
-            swapped = jnp.where((row & 1) == 0, rolled(tile, -1, 0), rolled(tile, 1, 0)) * sign
-            for b in range(7):
-                swapped = jnp.where(
-                    masks[b], rolled(swapped, 1 << b, 1), rolled(swapped, -(1 << b), 1)
-                )
-            fold_ref[k] = swapped
-            return carry
-
-        lax.fori_loop(0, layers + 1, fold_body, 0)
+        tiles = top_ref[...].reshape((layers + 1) * rows, cols)
+        tile_row = lax.broadcasted_iota(jnp.int32, tiles.shape, 0) % rows
+        sign = jnp.where(tile_row < 4, 1.0, -1.0)
+        swapped = jnp.where(
+            (tile_row & 1) == 0, rolled(tiles, -1, 0), rolled(tiles, 1, 0)
+        ) * sign
+        src_lane = lax.broadcasted_iota(jnp.int32, (cols, cols), 0)
+        dst_lane = lax.broadcasted_iota(jnp.int32, (cols, cols), 1)
+        reverse = (src_lane + dst_lane == cols - 1).astype(jnp.float32)
+        flipped = jnp.dot(
+            swapped, reverse, precision=lax.Precision.HIGHEST,
+            preferred_element_type=jnp.float32,
+        )
+        fold_ref[...] = flipped.reshape(layers + 1, rows, cols)
 
 
 def step_kernel(

time: 71.4 us -> 35.1 us (0.49)
  the two profiles are of different devices: /device:TPU:27 before, /device:TPU:0 now
where the time goes in v3:
time: 35.1 us; the launch traced here: 34.5 us
  Pallas kernels  13.9 us (40%)
  waiting for transfers between devices  9.13 us (26%)
  starting transfers between devices  8.61 us (25%)
  local copies, waits for them, and re-layouts  1.51 us (4%)
  between operations  0.7 us (2%)
  other arithmetic  0.65 us (2%)
    pallas_call x1, Pallas kernels, on_device(): pl.pallas_call(step_kernel, out_shape=(plane,) * 4, in_specs=[smem] * 5 +...  10.7 us
    ppermute x1, waiting for transfers between devices, on_device(): lax.ppermute(top, 'lat', [(i, i + 1) for i in range(n_lat - 1)])  8.05 us
    ppermute x1, starting transfers between devices, on_device(): lax.ppermute(top, 'lat', [(i, i + 1) for i in range(n_lat - 1)])  4.85 us
    pallas_call x1, Pallas kernels, on_device(): pl.pallas_call(pack_kernel, out_shape=(row_tiles, row_tiles, row_tiles, c...  3.21 us
    ppermute x1, starting transfers between devices, on_device(): lax.ppermute(left, 'lon', [((i + 1) % n_lon, i) for i in range(n_lon)])  1.73 us
    unnamed x10, local copies, waits for them, and re-layouts  1.51 us
    ppermute x1, starting transfers between devices, on_device(): lax.ppermute(bot, 'lat', [(i + 1, i) for i in range(n_lat - 1)])  1.29 us
    ppermute x1, waiting for transfers between devices, on_device(): lax.ppermute(right, 'lon', [(i, (i + 1) % n_lon) for i in range(n_lon)])  1.07 us
  transfers between devices with their start and end apart: 5, of which 2 were waited for; matrix products, arithmetic and copies ran while one was open for 2% of the time, Pallas kernels for 0%

profile of v3, /device:TPU:0, one launch (start us, length us, event | category | flops | bytes accessed | tf_op | source)
XLA Modules:
  0.0 34.5 jit_solution(14526446723596456861)
XLA Ops:
  0.6 3.2 %shard_map.138 = (f32[76,8,128]{2,1,0:T(8,128)}, f32[76,8,128]{2,1,0:T(8,128)}, f32[76,8,128]{2,1,0:T(8,128)}, f32[6,8,128]{2,1,0:T(8,128)}, f32[6,8,128]{2,1,0:T(8,128)}) custom-call(s32[1]{0:T(128)} %bitcast.1.last_ref, s32[8,128]{1,0:T(8,128)} %shore_ref.3, s32[8,128]{1,0:T(8,128)} %bottom_ref.3, f32[75,8,128]{2,1,0:T(8,128)} %t_ref.3, ...), custom_call_target="tpu_custom_call" | custom-call | tf_op jit(solution)/shard_map/pallas_call | solution.py:299
  3.8 4.8 %collective-permute-start = (f32[76,8,128]{2,1,0:T(8,128)}, f32[76,8,128]{2,1,0:T(8,128)S(1)}, u32[]{:S(2)}, u32[]{:S(2)}) collective-permute-start(f32[76,8,128]{2,1,0:T(8,128)} %get-tuple-element.9), channel_id=1, source_target_pairs={{0,4},{4,8},{8,12},{12,16},{16,20},{20,24},{24,28},{1,5},{5,9},{9,... | collective-permute-start | bytes 933896 | tf_op jit(solution)/shard_map/ppermute | solution.py:306
  8.7 1.3 %collective-permute-start.1 = (f32[76,8,128]{2,1,0:T(8,128)}, f32[76,8,128]{2,1,0:T(8,128)S(1)}, u32[]{:S(2)}, u32[]{:S(2)}) collective-permute-start(f32[76,8,128]{2,1,0:T(8,128)} %get-tuple-element.10), channel_id=1, source_target_pairs={{4,0},{8,4},{12,8},{16,12},{20,16},{24,20},{28,24},{5,1},{9,5},{13... | collective-permute-start | bytes 933896 | tf_op jit(solution)/shard_map/ppermute | solution.py:307
  10.0 0.7 %collective-permute-start.2 = (f32[76,8,128]{2,1,0:T(8,128)}, f32[76,8,128]{2,1,0:T(8,128)S(1)}, u32[]{:S(2)}, u32[]{:S(2)}) collective-permute-start(f32[76,8,128]{2,1,0:T(8,128)} %get-tuple-element.11), channel_id=1, source_target_pairs={{28,31},{29,30},{30,29},{31,28}} | collective-permute-start | bytes 933896 | tf_op jit(solution)/shard_map/ppermute | solution.py:311
  10.7 0.1 collective-permute-start.3
  10.8 1.7 %collective-permute-start.4 = (f32[6,8,128]{2,1,0:T(8,128)}, f32[6,8,128]{2,1,0:T(8,128)S(1)}, u32[]{:S(2)}, u32[]{:S(2)}) collective-permute-start(f32[6,8,128]{2,1,0:T(8,128)} %get-tuple-element.13), channel_id=1, source_target_pairs={{1,0},{2,1},{3,2},{0,3},{5,4},{6,5},{7,6},{4,7},{9,8},{10,9},{11,1... | collective-permute-start | bytes 73736 | tf_op jit(solution)/shard_map/ppermute | solution.py:309
  12.5 0.6 %pad_add_fusion.lat_ref = s32[2]{0:T(128)} fusion(s32[1]{0:T(128)} %constant.16.clone.1, s32[1]{0:T(128)} %bitcast), kind=kLoop, calls=%fused_computation | loop fusion | flops 2 | bytes 16 | tf_op jit(solution)/shard_map/stack | solution.py:293
  13.1 1.1 %collective-permute-done.3.west_ref = f32[6,8,128]{2,1,0:T(8,128)S(1)} collective-permute-done((f32[6,8,128]{2,1,0:T(8,128)}, f32[6,8,128]{2,1,0:T(8,128)S(1)}, u32[]{:S(2)}, u32[]{:S(2)}) %collective-permute-start.3) | collective-permute-done | bytes 24608 | tf_op jit(solution)/shard_map/ppermute | solution.py:308
  14.2 0.0 copy-start.3
  14.2 0.0 collective-permute-done.4.east_ref
  14.2 0.0 copy-start.4
  14.2 8.0 %collective-permute-done.south_ref = f32[76,8,128]{2,1,0:T(8,128)S(1)} collective-permute-done((f32[76,8,128]{2,1,0:T(8,128)}, f32[76,8,128]{2,1,0:T(8,128)S(1)}, u32[]{:S(2)}, u32[]{:S(2)}) %collective-permute-start) | collective-permute-done | bytes 311328 | tf_op jit(solution)/shard_map/ppermute | solution.py:306
  22.3 0.0 copy-start
  22.3 0.0 collective-permute-done.1.north_ref
  22.3 0.0 copy-start.1
  22.3 0.0 collective-permute-done.2.fold_ref
  22.3 0.0 copy-done.3
  22.3 0.0 copy-done.4
  22.3 0.7 %copy-done = f32[76,8,128]{2,1,0:T(8,128)} copy-done((f32[76,8,128]{2,1,0:T(8,128)}, f32[76,8,128]{2,1,0:T(8,128)S(1)}, u32[]{:S(2)}) %copy-start) | copy-done | bytes 311320
  23.0 0.1 copy-done.1
  23.1 0.0 copy-start.2
  23.1 0.7 %copy-done.2 = f32[76,8,128]{2,1,0:T(8,128)} copy-done((f32[76,8,128]{2,1,0:T(8,128)}, f32[76,8,128]{2,1,0:T(8,128)S(1)}, u32[]{:S(2)}) %copy-start.2) | copy-done | bytes 311320
  23.8 10.7 %shard_map.139 = (f32[75,8,128]{2,1,0:T(8,128)}, f32[75,8,128]{2,1,0:T(8,128)}, f32[75,8,128]{2,1,0:T(8,128)}, f32[75,8,128]{2,1,0:T(8,128)}) custom-call(s32[2]{0:T(128)} %pad_add_fusion.lat_ref, f32[75]{0:T(128)} %constant.18.clone.h_ref, f32[75]{0:T(128)} %constant.19.clone.inv_h_ref, f32[75]{0:T(128)} %constant.20.clone.zmid_ref, ...), custom_call_target="tpu_custom_call" | custom-call | tf_op jit(solution)/shard_map/pallas_call | solution.py:316
Async XLA Ops:
  3.8 18.4 %collective-permute-start = (f32[76,8,128]{2,1,0:T(8,128)}, f32[76,8,128]{2,1,0:T(8,128)S(1)}, u32[]{:S(2)}, u32[]{:S(2)}) collective-permute-start(f32[76,8,128]{2,1,0:T(8,128)} %get-tuple-element.9), channel_id=1, source_target_pairs={{0,4},{4,8},{8,12},{12,16},{16,20},{20,24},{24,28},{1,5},{5,9},{9,... | collective-permute-start | bytes 933896 | tf_op jit(solution)/shard_map/ppermute | solution.py:306
  8.7 13.6 %collective-permute-start.1 = (f32[76,8,128]{2,1,0:T(8,128)}, f32[76,8,128]{2,1,0:T(8,128)S(1)}, u32[]{:S(2)}, u32[]{:S(2)}) collective-permute-start(f32[76,8,128]{2,1,0:T(8,128)} %get-tuple-element.10), channel_id=1, source_target_pairs={{4,0},{8,4},{12,8},{16,12},{20,16},{24,20},{28,24},{5,1},{9,5},{13... | collective-permute-start | bytes 933896 | tf_op jit(solution)/shard_map/ppermute | solution.py:307
  10.0 12.3 %collective-permute-start.2 = (f32[76,8,128]{2,1,0:T(8,128)}, f32[76,8,128]{2,1,0:T(8,128)S(1)}, u32[]{:S(2)}, u32[]{:S(2)}) collective-permute-start(f32[76,8,128]{2,1,0:T(8,128)} %get-tuple-element.11), channel_id=1, source_target_pairs={{28,31},{29,30},{30,29},{31,28}} | collective-permute-start | bytes 933896 | tf_op jit(solution)/shard_map/ppermute | solution.py:311
  10.7 3.5 %collective-permute-start.3 = (f32[6,8,128]{2,1,0:T(8,128)}, f32[6,8,128]{2,1,0:T(8,128)S(1)}, u32[]{:S(2)}, u32[]{:S(2)}) collective-permute-start(f32[6,8,128]{2,1,0:T(8,128)} %get-tuple-element.12), channel_id=1, source_target_pairs={{0,1},{1,2},{2,3},{3,0},{4,5},{5,6},{6,7},{7,4},{8,9},{9,10},{10,1... | collective-permute-start | bytes 73736 | tf_op jit(solution)/shard_map/ppermute | solution.py:308
  10.8 3.5 %collective-permute-start.4 = (f32[6,8,128]{2,1,0:T(8,128)}, f32[6,8,128]{2,1,0:T(8,128)S(1)}, u32[]{:S(2)}, u32[]{:S(2)}) collective-permute-start(f32[6,8,128]{2,1,0:T(8,128)} %get-tuple-element.13), channel_id=1, source_target_pairs={{1,0},{2,1},{3,2},{0,3},{5,4},{6,5},{7,6},{4,7},{9,8},{10,9},{11,1... | collective-permute-start | bytes 73736 | tf_op jit(solution)/shard_map/ppermute | solution.py:309
  14.2 8.1 %copy-start.3 = (f32[6,8,128]{2,1,0:T(8,128)}, f32[6,8,128]{2,1,0:T(8,128)S(1)}, u32[]{:S(2)}) copy-start(f32[6,8,128]{2,1,0:T(8,128)S(1)} %collective-permute-done.3.west_ref) | copy-start | bytes 73732
  14.2 8.1 %copy-start.4 = (f32[6,8,128]{2,1,0:T(8,128)}, f32[6,8,128]{2,1,0:T(8,128)S(1)}, u32[]{:S(2)}) copy-start(f32[6,8,128]{2,1,0:T(8,128)S(1)} %collective-permute-done.4.east_ref) | copy-start | bytes 73732
  22.3 0.7 %copy-start = (f32[76,8,128]{2,1,0:T(8,128)}, f32[76,8,128]{2,1,0:T(8,128)S(1)}, u32[]{:S(2)}) copy-start(f32[76,8,128]{2,1,0:T(8,128)S(1)} %collective-permute-done.south_ref) | copy-start | bytes 933892
  22.3 0.8 %copy-start.1 = (f32[76,8,128]{2,1,0:T(8,128)}, f32[76,8,128]{2,1,0:T(8,128)S(1)}, u32[]{:S(2)}) copy-start(f32[76,8,128]{2,1,0:T(8,128)S(1)} %collective-permute-done.1.north_ref) | copy-start | bytes 933892
  23.1 0.7 %copy-start.2 = (f32[76,8,128]{2,1,0:T(8,128)}, f32[76,8,128]{2,1,0:T(8,128)S(1)}, u32[]{:S(2)}) copy-start(f32[76,8,128]{2,1,0:T(8,128)S(1)} %collective-permute-done.2.fold_ref) | copy-start | bytes 933892

commit v4 on v2

--- a/solution.py
+++ b/solution.py
@@ -39,13 +39,8 @@
     return x if shift == 0 else pltpu.roll(x, shift, axis)
 
 
-def pack_kernel(
-    last_ref, shore_ref, bottom_ref, t_ref, s_ref, u_ref, v_ref,
-    top_ref, bot_ref, fold_ref, right_ref, left_ref,
-):
+def pack_lat_kernel(shore_ref, bottom_ref, t_ref, s_ref, u_ref, v_ref, top_ref, bot_ref):
     layers, rows, cols = t_ref.shape
-    groups = layers // GROUP
-    lane = lax.broadcasted_iota(jnp.int32, (rows, cols), 1)
     row = lax.broadcasted_iota(jnp.int32, (rows, cols), 0)
     dep = (shore_ref[...] * bottom_ref[...]).astype(jnp.float32)
     zero = jnp.zeros((rows, cols), jnp.float32)
@@ -55,6 +50,46 @@
         for c, val in enumerate(vals):
             out = jnp.where((row >> 1) == c, rolled(val, 2 * c - first, 0), out)
         return out
+
+    def level_body(k, carry):
+        w = (k.astype(jnp.float32) < dep).astype(jnp.float32)
+        q = [r[k] * w for r in (t_ref, s_ref, u_ref, v_ref)]
+        top_ref[k] = pack_rows(q, rows - 2)
+        bot_ref[k] = pack_rows(q, 0)
+        return carry
+
+    lax.fori_loop(0, layers, level_body, 0, unroll=5)
+    top_ref[layers] = pack_rows([dep], rows - 2)
+    bot_ref[layers] = pack_rows([dep], 0)
+
+
+def pack_fold_kernel(last_ref, top_ref, fold_ref):
+    tiles_n, rows, cols = top_ref.shape
+
+    @pl.when(last_ref[0] == 1)
+    def _():
+        tiles = top_ref[...].reshape(tiles_n * rows, cols)
+        tile_row = lax.broadcasted_iota(jnp.int32, tiles.shape, 0) % rows
+        sign = jnp.where(tile_row < 4, 1.0, -1.0)
+        swapped = jnp.where(
+            (tile_row & 1) == 0, rolled(tiles, -1, 0), rolled(tiles, 1, 0)
+        ) * sign
+        src_lane = lax.broadcasted_iota(jnp.int32, (cols, cols), 0)
+        dst_lane = lax.broadcasted_iota(jnp.int32, (cols, cols), 1)
+        reverse = (src_lane + dst_lane == cols - 1).astype(jnp.float32)
+        flipped = jnp.dot(
+            swapped, reverse, precision=lax.Precision.HIGHEST,
+            preferred_element_type=jnp.float32,
+        )
+        fold_ref[...] = flipped.reshape(tiles_n, rows, cols)
+
+
+def pack_lon_kernel(shore_ref, bottom_ref, t_ref, s_ref, u_ref, v_ref, right_ref, left_ref):
+    layers, rows, cols = t_ref.shape
+    groups = layers // GROUP
+    lane = lax.broadcasted_iota(jnp.int32, (rows, cols), 1)
+    dep = (shore_ref[...] * bottom_ref[...]).astype(jnp.float32)
+    zero = jnp.zeros((rows, cols), jnp.float32)
 
     def group_body(g, carry):
         right = zero
@@ -63,8 +98,6 @@
             k = g * GROUP + j
             w = (k.astype(jnp.float32) < dep).astype(jnp.float32)
             q = [r[k] * w for r in (t_ref, s_ref, u_ref, v_ref)]
-            top_ref[k] = pack_rows(q, rows - 2)
-            bot_ref[k] = pack_rows(q, 0)
             for c in range(4):
                 m = j * 4 + c
                 slot = (lane >> 1) == m
@@ -75,27 +108,8 @@
         return carry
 
     lax.fori_loop(0, groups, group_body, 0)
-    top_ref[layers] = pack_rows([dep], rows - 2)
-    bot_ref[layers] = pack_rows([dep], 0)
     right_ref[groups] = jnp.where(lane < 2, rolled(dep, 2, 1), zero)
     left_ref[groups] = jnp.where(lane < 2, dep, zero)
-
-    @pl.when(last_ref[0] == 1)
-    def _():
-        sign = jnp.where(row < 4, 1.0, -1.0)
-        masks = [(lane & (1 << b)) != 0 for b in range(7)]
-
-        def fold_body(k, carry):
-            tile = top_ref[k]
-            swapped = jnp.where((row & 1) == 0, rolled(tile, -1, 0), rolled(tile, 1, 0)) * sign
-            for b in range(7):
-                swapped = jnp.where(
-                    masks[b], rolled(swapped, 1 << b, 1), rolled(swapped, -(1 << b), 1)
-                )
-            fold_ref[k] = swapped
-            return carry
-
-        lax.fori_loop(0, layers + 1, fold_body, 0)
 
 
 def step_kernel(
@@ -296,21 +310,32 @@
     vmem = pl.BlockSpec(memory_space=pltpu.VMEM)
     row_tiles = jax.ShapeDtypeStruct((layers + 1, rows, cols), jnp.float32)
     col_tiles = jax.ShapeDtypeStruct((groups + 1, rows, cols), jnp.float32)
-    top, bot, fold, right, left = pl.pallas_call(
-        pack_kernel,
-        out_shape=(row_tiles, row_tiles, row_tiles, col_tiles, col_tiles),
-        in_specs=[smem] + [vmem] * 6,
-        out_specs=(vmem,) * 5,
-    )(is_last, shoreline_indicator, bottom_layer_index, *fields)
-
+    top, bot = pl.pallas_call(
+        pack_lat_kernel,
+        out_shape=(row_tiles, row_tiles),
+        in_specs=[vmem] * 6,
+        out_specs=(vmem,) * 2,
+    )(shoreline_indicator, bottom_layer_index, *fields)
     from_south = lax.ppermute(top, "lat", [(i, i + 1) for i in range(n_lat - 1)])
     from_north = lax.ppermute(bot, "lat", [(i + 1, i) for i in range(n_lat - 1)])
-    from_west = lax.ppermute(right, "lon", [(i, (i + 1) % n_lon) for i in range(n_lon)])
-    from_east = lax.ppermute(left, "lon", [((i + 1) % n_lon, i) for i in range(n_lon)])
+    fold = pl.pallas_call(
+        pack_fold_kernel,
+        out_shape=row_tiles,
+        in_specs=[smem, vmem],
+        out_specs=vmem,
+    )(is_last, top)
     last = (n_lat - 1) * n_lon
     from_fold = lax.ppermute(
         fold, ("lat", "lon"), [(last + x, last + n_lon - 1 - x) for x in range(n_lon)]
     )
+    right, left = pl.pallas_call(
+        pack_lon_kernel,
+        out_shape=(col_tiles, col_tiles),
+        in_specs=[vmem] * 6,
+        out_specs=(vmem,) * 2,
+    )(shoreline_indicator, bottom_layer_index, *fields)
+    from_west = lax.ppermute(right, "lon", [(i, (i + 1) % n_lon) for i in range(n_lon)])
+    from_east = lax.ppermute(left, "lon", [((i + 1) % n_lon, i) for i in range(n_lon)])
 
     plane = jax.ShapeDtypeStruct((layers, rows, cols), jnp.float32)
     outs = pl.pallas_call(

time: 71.4 us -> 38.4 us (0.54)
  the two profiles are of different devices: /device:TPU:27 before, /device:TPU:25 now
where the time goes in v4:
time: 38.4 us; the launch traced here: 38.1 us
  Pallas kernels  17.7 us (46%)
  starting transfers between devices  9.11 us (24%)
  waiting for transfers between devices  8.59 us (22%)
  local copies, waits for them, and re-layouts  1.41 us (4%)
  between operations  0.71 us (2%)
  other arithmetic  0.61 us (2%)
    pallas_call x1, Pallas kernels, on_device(): pl.pallas_call(step_kernel, out_shape=(plane,) * 4, in_specs=[smem] * 5 +...  10.7 us
    ppermute x1, waiting for transfers between devices, on_device(): lax.ppermute(bot, 'lat', [(i + 1, i) for i in range(n_lat - 1)])  5.66 us
    ppermute x1, starting transfers between devices, on_device(): lax.ppermute(top, 'lat', [(i, i + 1) for i in range(n_lat - 1)])  4.93 us
    ppermute x1, starting transfers between devices, on_device(): lax.ppermute(bot, 'lat', [(i + 1, i) for i in range(n_lat - 1)])  3.01 us
    pallas_call x1, Pallas kernels, on_device(): pl.pallas_call(pack_lon_kernel, out_shape=(col_tiles, col_tiles), in_spec...  2.89 us
    ppermute x1, waiting for transfers between devices, on_device(): lax.ppermute(left, 'lon', [((i + 1) % n_lon, i) for i in range(n_lon)])  2.6 us
    pallas_call x1, Pallas kernels, on_device(): pl.pallas_call(pack_lat_kernel, out_shape=(row_tiles, row_tiles), in_spec...  2.4 us
    pallas_call x1, Pallas kernels, on_device(): pl.pallas_call(pack_fold_kernel, out_shape=row_tiles, in_specs=[smem, vme...  1.75 us
  transfers between devices with their start and end apart: 5, of which 3 were waited for; matrix products, arithmetic and copies ran while one was open for 2% of the time, Pallas kernels for 8%

profile of v4, /device:TPU:25, one launch (start us, length us, event | category | flops | bytes accessed | tf_op | source)
XLA Modules:
  0.0 38.1 jit_solution(14497765863723602697)
XLA Ops:
  0.6 2.4 %shard_map.138 = (f32[76,8,128]{2,1,0:T(8,128)}, f32[76,8,128]{2,1,0:T(8,128)}) custom-call(s32[8,128]{1,0:T(8,128)} %shore_ref.5, s32[8,128]{1,0:T(8,128)} %bottom_ref.5, f32[75,8,128]{2,1,0:T(8,128)} %t_ref.5, f32[75,8,128]{2,1,0:T(8,128)} %s_ref.5, f32[75,8,128]{2,1,0:T(8,128)} %u_ref.5, f32[75,8,128]{2,1,0:T(8,128)} %v_ref.5), custom_call_target="tpu_custom_call" | custom-call | tf_op jit(solution)/shard_map/pallas_call | solution.py:313
  3.0 0.0 copy-start.6
  3.0 0.0 copy-start
  3.0 1.8 %shard_map.139 = f32[76,8,128]{2,1,0:T(8,128)} custom-call(s32[1]{0:T(128)} %bitcast.1.last_ref, f32[76,8,128]{2,1,0:T(8,128)} %get-tuple-element.8.top_ref), custom_call_target="tpu_custom_call" | custom-call | tf_op jit(solution)/shard_map/pallas_call | solution.py:321
  4.8 0.7 %collective-permute-start.2 = (f32[76,8,128]{2,1,0:T(8,128)}, f32[76,8,128]{2,1,0:T(8,128)S(1)}, u32[]{:S(2)}, u32[]{:S(2)}) collective-permute-start(f32[76,8,128]{2,1,0:T(8,128)} %shard_map.139), channel_id=1, source_target_pairs={{28,31},{29,30},{30,29},{31,28}} | collective-permute-start | bytes 933896 | tf_op jit(solution)/shard_map/ppermute | solution.py:328
  5.5 0.0 copy-done.6
  5.5 3.0 %collective-permute-start.1 = (f32[76,8,128]{2,1,0:T(8,128)S(1)}, f32[76,8,128]{2,1,0:T(8,128)S(1)}, u32[]{:S(2)}, u32[]{:S(2)}) collective-permute-start(f32[76,8,128]{2,1,0:T(8,128)S(1)} %copy-done.6), channel_id=1, source_target_pairs={{4,0},{8,4},{12,8},{16,12},{20,16},{24,20},{28,24},{5,1},{9,5},{13... | collective-permute-start | bytes 933896 | tf_op jit(solution)/shard_map/ppermute | solution.py:320
  8.5 0.0 copy-done
  8.5 4.9 %collective-permute-start = (f32[76,8,128]{2,1,0:T(8,128)S(1)}, f32[76,8,128]{2,1,0:T(8,128)S(1)}, u32[]{:S(2)}, u32[]{:S(2)}) collective-permute-start(f32[76,8,128]{2,1,0:T(8,128)S(1)} %copy-done), channel_id=1, source_target_pairs={{0,4},{4,8},{8,12},{12,16},{16,20},{20,24},{24,28},{1,5},{5,9},{9,... | collective-permute-start | bytes 933896 | tf_op jit(solution)/shard_map/ppermute | solution.py:319
  13.4 2.9 %shard_map.140 = (f32[6,8,128]{2,1,0:T(8,128)}, f32[6,8,128]{2,1,0:T(8,128)}) custom-call(s32[8,128]{1,0:T(8,128)} %shore_ref.5, s32[8,128]{1,0:T(8,128)} %bottom_ref.5, f32[75,8,128]{2,1,0:T(8,128)} %t_ref.5, f32[75,8,128]{2,1,0:T(8,128)} %s_ref.5, f32[75,8,128]{2,1,0:T(8,128)} %u_ref.5, f32[75,8,128]{2,1,0:T(8,128)} %v_ref.5), custom_call_target="tpu_custom_call" | custom-call | tf_op jit(solution)/shard_map/pallas_call | solution.py:331
  16.3 0.3 collective-permute-start.3
  16.6 0.2 collective-permute-start.4
  16.8 0.6 %pad_add_fusion.lat_ref = s32[2]{0:T(128)} fusion(s32[1]{0:T(128)} %constant.16.clone.1, s32[1]{0:T(128)} %bitcast), kind=kLoop, calls=%fused_computation | loop fusion | flops 2 | bytes 16 | tf_op jit(solution)/shard_map/stack | solution.py:307
  17.5 0.3 collective-permute-done.3.west_ref
  17.8 2.6 %collective-permute-done.4.east_ref = f32[6,8,128]{2,1,0:T(8,128)S(1)} collective-permute-done((f32[6,8,128]{2,1,0:T(8,128)}, f32[6,8,128]{2,1,0:T(8,128)S(1)}, u32[]{:S(2)}, u32[]{:S(2)}) %collective-permute-start.4) | collective-permute-done | bytes 24608 | tf_op jit(solution)/shard_map/ppermute | solution.py:338
  20.4 0.0 collective-permute-done.2.fold_ref
  20.4 5.7 %collective-permute-done.1.north_ref = f32[76,8,128]{2,1,0:T(8,128)S(1)} collective-permute-done((f32[76,8,128]{2,1,0:T(8,128)S(1)}, f32[76,8,128]{2,1,0:T(8,128)S(1)}, u32[]{:S(2)}, u32[]{:S(2)}) %collective-permute-start.1) | collective-permute-done | bytes 311328 | tf_op jit(solution)/shard_map/ppermute | solution.py:320
  26.0 0.0 collective-permute-done.south_ref
  26.1 0.0 copy-done.4
  26.1 0.0 copy-done.5
  26.1 0.0 copy-done.1
  26.1 0.7 %copy-done.2 = f32[76,8,128]{2,1,0:T(8,128)} copy-done((f32[76,8,128]{2,1,0:T(8,128)}, f32[76,8,128]{2,1,0:T(8,128)S(1)}, u32[]{:S(2)}) %copy-start.2) | copy-done | bytes 311320
  26.8 0.7 %copy-done.3 = f32[76,8,128]{2,1,0:T(8,128)} copy-done((f32[76,8,128]{2,1,0:T(8,128)}, f32[76,8,128]{2,1,0:T(8,128)S(1)}, u32[]{:S(2)}) %copy-start.3) | copy-done | bytes 311320
  27.5 10.7 %shard_map.141 = (f32[75,8,128]{2,1,0:T(8,128)}, f32[75,8,128]{2,1,0:T(8,128)}, f32[75,8,128]{2,1,0:T(8,128)}, f32[75,8,128]{2,1,0:T(8,128)}) custom-call(s32[2]{0:T(128)} %pad_add_fusion.lat_ref, f32[75]{0:T(128)} %constant.18.clone.h_ref, f32[75]{0:T(128)} %constant.19.clone.inv_h_ref, f32[75]{0:T(128)} %constant.20.clone.zmid_ref, ...), custom_call_target="tpu_custom_call" | custom-call | tf_op jit(solution)/shard_map/pallas_call | solution.py:341
  (5 shorter events, 0.0 us)
Async XLA Ops:
  3.0 2.4 %copy-start.6 = (f32[76,8,128]{2,1,0:T(8,128)S(1)}, f32[76,8,128]{2,1,0:T(8,128)}, u32[]{:S(2)}) copy-start(f32[76,8,128]{2,1,0:T(8,128)} %get-tuple-element.9) | copy-start | bytes 933892
  3.0 5.5 %copy-start = (f32[76,8,128]{2,1,0:T(8,128)S(1)}, f32[76,8,128]{2,1,0:T(8,128)}, u32[]{:S(2)}) copy-start(f32[76,8,128]{2,1,0:T(8,128)} %get-tuple-element.8.top_ref) | copy-start | bytes 933892
  4.8 15.6 %collective-permute-start.2 = (f32[76,8,128]{2,1,0:T(8,128)}, f32[76,8,128]{2,1,0:T(8,128)S(1)}, u32[]{:S(2)}, u32[]{:S(2)}) collective-permute-start(f32[76,8,128]{2,1,0:T(8,128)} %shard_map.139), channel_id=1, source_target_pairs={{28,31},{29,30},{30,29},{31,28}} | collective-permute-start | bytes 933896 | tf_op jit(solution)/shard_map/ppermute | solution.py:328
  5.5 20.6 %collective-permute-start.1 = (f32[76,8,128]{2,1,0:T(8,128)S(1)}, f32[76,8,128]{2,1,0:T(8,128)S(1)}, u32[]{:S(2)}, u32[]{:S(2)}) collective-permute-start(f32[76,8,128]{2,1,0:T(8,128)S(1)} %copy-done.6), channel_id=1, source_target_pairs={{4,0},{8,4},{12,8},{16,12},{20,16},{24,20},{28,24},{5,1},{9,5},{13... | collective-permute-start | bytes 933896 | tf_op jit(solution)/shard_map/ppermute | solution.py:320
  8.5 17.5 %collective-permute-start = (f32[76,8,128]{2,1,0:T(8,128)S(1)}, f32[76,8,128]{2,1,0:T(8,128)S(1)}, u32[]{:S(2)}, u32[]{:S(2)}) collective-permute-start(f32[76,8,128]{2,1,0:T(8,128)S(1)} %copy-done), channel_id=1, source_target_pairs={{0,4},{4,8},{8,12},{12,16},{16,20},{20,24},{24,28},{1,5},{5,9},{9,... | collective-permute-start | bytes 933896 | tf_op jit(solution)/shard_map/ppermute | solution.py:319
  16.3 1.4 %collective-permute-start.3 = (f32[6,8,128]{2,1,0:T(8,128)}, f32[6,8,128]{2,1,0:T(8,128)S(1)}, u32[]{:S(2)}, u32[]{:S(2)}) collective-permute-start(f32[6,8,128]{2,1,0:T(8,128)} %get-tuple-element.10), channel_id=1, source_target_pairs={{0,1},{1,2},{2,3},{3,0},{4,5},{5,6},{6,7},{7,4},{8,9},{9,10},{10,1... | collective-permute-start | bytes 73736 | tf_op jit(solution)/shard_map/ppermute | solution.py:337
  16.6 3.8 %collective-permute-start.4 = (f32[6,8,128]{2,1,0:T(8,128)}, f32[6,8,128]{2,1,0:T(8,128)S(1)}, u32[]{:S(2)}, u32[]{:S(2)}) collective-permute-start(f32[6,8,128]{2,1,0:T(8,128)} %get-tuple-element.11), channel_id=1, source_target_pairs={{1,0},{2,1},{3,2},{0,3},{5,4},{6,5},{7,6},{4,7},{9,8},{10,9},{11,1... | collective-permute-start | bytes 73736 | tf_op jit(solution)/shard_map/ppermute | solution.py:338
  17.8 8.3 %copy-start.4 = (f32[6,8,128]{2,1,0:T(8,128)}, f32[6,8,128]{2,1,0:T(8,128)S(1)}, u32[]{:S(2)}) copy-start(f32[6,8,128]{2,1,0:T(8,128)S(1)} %collective-permute-done.3.west_ref) | copy-start | bytes 73732
  20.4 5.7 %copy-start.5 = (f32[6,8,128]{2,1,0:T(8,128)}, f32[6,8,128]{2,1,0:T(8,128)S(1)}, u32[]{:S(2)}) copy-start(f32[6,8,128]{2,1,0:T(8,128)S(1)} %collective-permute-done.4.east_ref) | copy-start | bytes 73732
  20.4 5.7 %copy-start.1 = (f32[76,8,128]{2,1,0:T(8,128)}, f32[76,8,128]{2,1,0:T(8,128)S(1)}, u32[]{:S(2)}) copy-start(f32[76,8,128]{2,1,0:T(8,128)S(1)} %collective-permute-done.2.fold_ref) | copy-start | bytes 933892
  26.0 0.7 %copy-start.2 = (f32[76,8,128]{2,1,0:T(8,128)}, f32[76,8,128]{2,1,0:T(8,128)S(1)}, u32[]{:S(2)}) copy-start(f32[76,8,128]{2,1,0:T(8,128)S(1)} %collective-permute-done.1.north_ref) | copy-start | bytes 933892
  26.8 0.7 %copy-start.3 = (f32[76,8,128]{2,1,0:T(8,128)}, f32[76,8,128]{2,1,0:T(8,128)S(1)}, u32[]{:S(2)}) copy-start(f32[76,8,128]{2,1,0:T(8,128)S(1)} %collective-permute-done.south_ref) | copy-start | bytes 933892

commit v5 on v3

--- a/solution.py
+++ b/solution.py
@@ -98,10 +98,68 @@
         fold_ref[...] = flipped.reshape(layers + 1, rows, cols)
 
 
+def xpart_kernel(
+    h_ref, zmid_ref, shore_ref, bottom_ref, t_ref, s_ref, u_ref, v_ref, west_ref, east_ref,
+    divx_ref, gradx_ref,
+):
+    layers, rows, cols = t_ref.shape
+    groups = layers // GROUP
+    lane = lax.broadcasted_iota(jnp.int32, (rows, cols), 1)
+
+    def xs(v, e, s):
+        if s == 1:
+            return pltpu.roll(jnp.where(lane == 0, e, v), cols - 1, 1)
+        if s == 2:
+            return pltpu.roll(jnp.where(lane < 2, e, v), cols - 2, 1)
+        if s == -1:
+            return pltpu.roll(jnp.where(lane == cols - 1, e, v), 1, 1)
+        return pltpu.roll(jnp.where(lane >= cols - 2, e, v), 2, 1)
+
+    def lon_edge(tile_e, tile_w, m):
+        return jnp.where(lane < 64, rolled(tile_e, -2 * m, 1), rolled(tile_w, cols - 2 - 2 * m, 1))
+
+    dep = (shore_ref[...] * bottom_ref[...]).astype(jnp.float32)
+    dep_lon = lon_edge(east_ref[groups], west_ref[groups], 0)
+    dep_xm = xs(dep, dep_lon, -1)
+    dep_xp = xs(dep, dep_lon, 1)
+    zero = jnp.zeros((rows, cols), jnp.float32)
+
+    def group_body(g, carry):
+        tile_e = east_ref[g]
+        tile_w = west_ref[g]
+        for j in range(GROUP):
+            cum_xm, cum_xp = carry
+            k = g * GROUP + j
+            kf = k.astype(jnp.float32)
+            h = h_ref[k]
+            zmid = zmid_ref[k]
+            w0 = (kf < dep).astype(jnp.float32)
+            wxm = (kf < dep_xm).astype(jnp.float32)
+            wxp = (kf < dep_xp).astype(jnp.float32)
+            q = [r[k] * w0 for r in (t_ref, s_ref, u_ref, v_ref)]
+            ex = [lon_edge(tile_e, tile_w, j * 4 + c) for c in range(4)]
+            xsh = {s: [xs(q[c], ex[c], s) for c in range(4)] for s in (-2, -1, 1, 2)}
+            a_r = 0.5 * (q[2] + xsh[1][2]) * w0 * wxp
+            a_l = 0.5 * (xsh[-1][2] + q[2]) * wxm * w0
+            for c in range(4):
+                divx_ref[c * layers + k] = face_flux(
+                    a_r, xsh[-1][c], q[c], xsh[1][c], xsh[2][c]
+                ) - face_flux(a_l, xsh[-2][c], xsh[-1][c], q[c], xsh[1][c])
+            load_xm = density(xsh[-1][0], xsh[-1][1], zmid) * wxm * h
+            load_xp = density(xsh[1][0], xsh[1][1], zmid) * wxp * h
+            cum_xm = cum_xm + load_xm
+            cum_xp = cum_xp + load_xp
+            gradx_ref[k] = 0.5 * ((cum_xp - 0.5 * load_xp) - (cum_xm - 0.5 * load_xm))
+            carry = (cum_xm, cum_xp)
+        return carry
+
+    lax.fori_loop(0, groups, group_body, (zero, zero))
+
+
 def step_kernel(
     lat_ref, h_ref, inv_h_ref, zmid_ref, inv_sp_ref,
     shore_ref, bottom_ref, flux_ref, t_ref, s_ref, u_ref, v_ref,
-    south_ref, north_ref, fold_ref, west_ref, east_ref,
+    south_ref, north_ref, fold_ref, divx_ref, gradx_ref,
     o0_ref, o1_ref, o2_ref, o3_ref,
     star_scr, r_scr, rs_scr,
 ):
@@ -111,15 +169,6 @@
     lane = lax.broadcasted_iota(jnp.int32, (rows, cols), 1)
     row = lax.broadcasted_iota(jnp.int32, (rows, cols), 0)
 
-    def xs(v, e, s):
-        if s == 1:
-            return pltpu.roll(jnp.where(lane == 0, e, v), cols - 1, 1)
-        if s == 2:
-            return pltpu.roll(jnp.where(lane < 2, e, v), cols - 2, 1)
-        if s == -1:
-            return pltpu.roll(jnp.where(lane == cols - 1, e, v), 1, 1)
-        return pltpu.roll(jnp.where(lane >= cols - 2, e, v), 2, 1)
-
     def ys(v, e, s):
         if s == 1:
             return pltpu.roll(jnp.where(row == 0, e, v), rows - 1, 0)
@@ -132,14 +181,8 @@
     def lat_edge(tile_n, tile_s, c):
         return jnp.where(row < 4, rolled(tile_n, -2 * c, 0), rolled(tile_s, rows - 2 - 2 * c, 0))
 
-    def lon_edge(tile_e, tile_w, m):
-        return jnp.where(lane < 64, rolled(tile_e, -2 * m, 1), rolled(tile_w, cols - 2 - 2 * m, 1))
-
     dep = (shore_ref[...] * bottom_ref[...]).astype(jnp.float32)
     dep_lat = lat_edge(north_ref[layers] + fold_ref[layers], south_ref[layers], 0)
-    dep_lon = lon_edge(east_ref[groups], west_ref[groups], 0)
-    dep_xm = xs(dep, dep_lon, -1)
-    dep_xp = xs(dep, dep_lon, 1)
     dep_ym = ys(dep, dep_lat, -1)
     dep_yp = ys(dep, dep_lat, 1)
     total_rows = rows * lat_ref[1]
@@ -147,53 +190,32 @@
     turning = coriolis * (2.0 * (row_ids + 0.5) / total_rows.astype(jnp.float32) - 1.0)
     zero = jnp.zeros((rows, cols), jnp.float32)
 
-    def explicit_group(g, carry):
-        tile_e = east_ref[g]
-        tile_w = west_ref[g]
-        for j in range(GROUP):
-            k = g * GROUP + j
-            carry = explicit(k, j, tile_e, tile_w, carry)
-        return carry
-
-    def explicit(k, j, tile_e, tile_w, carry):
-        cum_xm, cum_xp, cum_ym, cum_yp = carry
+    def explicit(k, carry):
+        cum_ym, cum_yp = carry
         kf = k.astype(jnp.float32)
         h = h_ref[k]
         zmid = zmid_ref[k]
         w0 = (kf < dep).astype(jnp.float32)
-        wxm = (kf < dep_xm).astype(jnp.float32)
-        wxp = (kf < dep_xp).astype(jnp.float32)
         wym = (kf < dep_ym).astype(jnp.float32)
         wyp = (kf < dep_yp).astype(jnp.float32)
         q = [r[k] * w0 for r in (t_ref, s_ref, u_ref, v_ref)]
         tile_n = north_ref[k] + fold_ref[k]
         tile_s = south_ref[k]
         ey = [lat_edge(tile_n, tile_s, c) for c in range(4)]
-        ex = [lon_edge(tile_e, tile_w, j * 4 + c) for c in range(4)]
-        xsh = {s: [xs(q[c], ex[c], s) for c in range(4)] for s in (-2, -1, 1, 2)}
         ysh = {s: [ys(q[c], ey[c], s) for c in range(4)] for s in (-2, -1, 1, 2)}
-        a_r = 0.5 * (q[2] + xsh[1][2]) * w0 * wxp
-        a_l = 0.5 * (xsh[-1][2] + q[2]) * wxm * w0
         b_r = 0.5 * (q[3] + ysh[1][3]) * w0 * wyp
         b_l = 0.5 * (ysh[-1][3] + q[3]) * wym * w0
         adv = []
         for c in range(4):
-            div_x = face_flux(a_r, xsh[-1][c], q[c], xsh[1][c], xsh[2][c]) - face_flux(
-                a_l, xsh[-2][c], xsh[-1][c], q[c], xsh[1][c]
-            )
             div_y = face_flux(b_r, ysh[-1][c], q[c], ysh[1][c], ysh[2][c]) - face_flux(
                 b_l, ysh[-2][c], ysh[-1][c], q[c], ysh[1][c]
             )
-            adv.append(q[c] - courant * (div_x + div_y))
-        load_xm = density(xsh[-1][0], xsh[-1][1], zmid) * wxm * h
-        load_xp = density(xsh[1][0], xsh[1][1], zmid) * wxp * h
+            adv.append(q[c] - courant * (divx_ref[c * layers + k] + div_y))
         load_ym = density(ysh[-1][0], ysh[-1][1], zmid) * wym * h
         load_yp = density(ysh[1][0], ysh[1][1], zmid) * wyp * h
-        cum_xm = cum_xm + load_xm
-        cum_xp = cum_xp + load_xp
         cum_ym = cum_ym + load_ym
         cum_yp = cum_yp + load_yp
-        grad_x = 0.5 * ((cum_xp - 0.5 * load_xp) - (cum_xm - 0.5 * load_xm))
+        grad_x = gradx_ref[k]
         grad_y = 0.5 * ((cum_yp - 0.5 * load_yp) - (cum_ym - 0.5 * load_ym))
         star0 = adv[0] * w0
         star1 = adv[1] * w0
@@ -202,9 +224,9 @@
         for c, val in enumerate((star0, star1, star2, star3)):
             star_scr[c * layers + k] = val
         rs_scr[k] = density(star0, star1, zmid)
-        return (cum_xm, cum_xp, cum_ym, cum_yp)
-
-    lax.fori_loop(0, groups, explicit_group, (zero, zero, zero, zero))
+        return (cum_ym, cum_yp)
+
+    lax.fori_loop(0, layers, explicit, (zero, zero), unroll=3)
 
     surface_scale = surface_gain * inv_h_ref[0]
     w_top = (0.0 < dep).astype(jnp.float32)
@@ -313,6 +335,13 @@
     )
 
     plane = jax.ShapeDtypeStruct((layers, rows, cols), jnp.float32)
+    tables = level_tables(layers)
+    divx, gradx = pl.pallas_call(
+        xpart_kernel,
+        out_shape=(jax.ShapeDtypeStruct((4 * layers, rows, cols), jnp.float32), plane),
+        in_specs=[smem] * 2 + [vmem] * 8,
+        out_specs=(vmem,) * 2,
+    )(tables[0], tables[2], shoreline_indicator, bottom_layer_index, *fields, from_west, from_east)
     outs = pl.pallas_call(
         step_kernel,
         out_shape=(plane,) * 4,
@@ -324,9 +353,9 @@
             pltpu.VMEM((layers, rows, cols), jnp.float32),
         ],
     )(
-        lat_info, *level_tables(layers),
+        lat_info, *tables,
         shoreline_indicator, bottom_layer_index, boundary_fluxes, *fields,
-        from_south, from_north, from_fold, from_west, from_east,
+        from_south, from_north, from_fold, divx, gradx,
     )
     return tuple(outs)
 

time: 35.1 us -> 40.5 us (1.15)
  the two profiles are of different devices: /device:TPU:0 before, /device:TPU:26 now
where the time goes in v5:
time: 40.5 us; the launch traced here: 40.3 us
  Pallas kernels  19.4 us (48%)
  starting transfers between devices  9.95 us (25%)
  waiting for transfers between devices  7.46 us (18%)
  local copies, waits for them, and re-layouts  2.11 us (5%)
  between operations  0.71 us (2%)
  other arithmetic  0.65 us (2%)
    pallas_call x1, Pallas kernels, on_device(): pl.pallas_call(xpart_kernel, out_shape=(jax.ShapeDtypeStruct((4 * layers,...  8.19 us
    pallas_call x1, Pallas kernels, on_device(): pl.pallas_call(step_kernel, out_shape=(plane,) * 4, in_specs=[smem] * 5 +...  7.5 us
    ppermute x1, waiting for transfers between devices, on_device(): lax.ppermute(right, 'lon', [(i, (i + 1) % n_lon) for i in range(n_lon)])  7.45 us
    ppermute x1, starting transfers between devices, on_device(): lax.ppermute(bot, 'lat', [(i + 1, i) for i in range(n_lat - 1)])  4.56 us
    pallas_call x1, Pallas kernels, on_device(): pl.pallas_call(pack_kernel, out_shape=(row_tiles, row_tiles, row_tiles, c...  3.69 us
    ppermute x1, starting transfers between devices, on_device(): lax.ppermute(fold, ('lat', 'lon'), [(last + x, last + n_lon - 1 - x) for...  2.31 us
    unnamed x10, local copies, waits for them, and re-layouts  2.11 us
    ppermute x1, starting transfers between devices, on_device(): lax.ppermute(right, 'lon', [(i, (i + 1) % n_lon) for i in range(n_lon)])  1.29 us
  transfers between devices with their start and end apart: 5, of which 1 were waited for; matrix products, arithmetic and copies ran while one was open for 2% of the time, Pallas kernels for 20%

profile of v5, /device:TPU:26, one launch (start us, length us, event | category | flops | bytes accessed | tf_op | source)
XLA Modules:
  0.0 40.3 jit_solution(13542545988904058679)
XLA Ops:
  0.6 3.7 %shard_map.138 = (f32[76,8,128]{2,1,0:T(8,128)}, f32[76,8,128]{2,1,0:T(8,128)}, f32[76,8,128]{2,1,0:T(8,128)}, f32[6,8,128]{2,1,0:T(8,128)}, f32[6,8,128]{2,1,0:T(8,128)}) custom-call(s32[1]{0:T(128)} %bitcast.1.last_ref, s32[8,128]{1,0:T(8,128)} %shore_ref.5, s32[8,128]{1,0:T(8,128)} %bottom_ref.5, f32[75,8,128]{2,1,0:T(8,128)} %t_ref.5, ...), custom_call_target="tpu_custom_call" | custom-call | tf_op jit(solution)/shard_map/pallas_call | solution.py:321
  4.3 1.3 %collective-permute-start = (f32[76,8,128]{2,1,0:T(8,128)}, f32[76,8,128]{2,1,0:T(8,128)S(1)}, u32[]{:S(2)}, u32[]{:S(2)}) collective-permute-start(f32[76,8,128]{2,1,0:T(8,128)} %get-tuple-element.11), channel_id=1, source_target_pairs={{0,4},{4,8},{8,12},{12,16},{16,20},{20,24},{24,28},{1,5},{5,9},{9,... | collective-permute-start | bytes 933896 | tf_op jit(solution)/shard_map/ppermute | solution.py:328
  5.6 4.6 %collective-permute-start.1 = (f32[76,8,128]{2,1,0:T(8,128)}, f32[76,8,128]{2,1,0:T(8,128)S(1)}, u32[]{:S(2)}, u32[]{:S(2)}) collective-permute-start(f32[76,8,128]{2,1,0:T(8,128)} %get-tuple-element.12), channel_id=1, source_target_pairs={{4,0},{8,4},{12,8},{16,12},{20,16},{24,20},{28,24},{5,1},{9,5},{13... | collective-permute-start | bytes 933896 | tf_op jit(solution)/shard_map/ppermute | solution.py:329
  10.2 2.3 %collective-permute-start.2 = (f32[76,8,128]{2,1,0:T(8,128)}, f32[76,8,128]{2,1,0:T(8,128)S(1)}, u32[]{:S(2)}, u32[]{:S(2)}) collective-permute-start(f32[76,8,128]{2,1,0:T(8,128)} %get-tuple-element.13), channel_id=1, source_target_pairs={{28,31},{29,30},{30,29},{31,28}} | collective-permute-start | bytes 933896 | tf_op jit(solution)/shard_map/ppermute | solution.py:333
  12.5 1.3 %collective-permute-start.3 = (f32[6,8,128]{2,1,0:T(8,128)}, f32[6,8,128]{2,1,0:T(8,128)S(1)}, u32[]{:S(2)}, u32[]{:S(2)}) collective-permute-start(f32[6,8,128]{2,1,0:T(8,128)} %get-tuple-element.14), channel_id=1, source_target_pairs={{0,1},{1,2},{2,3},{3,0},{4,5},{5,6},{6,7},{7,4},{8,9},{9,10},{10,1... | collective-permute-start | bytes 73736 | tf_op jit(solution)/shard_map/ppermute | solution.py:330
  13.8 0.5 %collective-permute-start.4 = (f32[6,8,128]{2,1,0:T(8,128)}, f32[6,8,128]{2,1,0:T(8,128)S(1)}, u32[]{:S(2)}, u32[]{:S(2)}) collective-permute-start(f32[6,8,128]{2,1,0:T(8,128)} %get-tuple-element.15), channel_id=1, source_target_pairs={{1,0},{2,1},{3,2},{0,3},{5,4},{6,5},{7,6},{4,7},{9,8},{10,9},{11,1... | collective-permute-start | bytes 73736 | tf_op jit(solution)/shard_map/ppermute | solution.py:331
  14.3 0.6 %pad_add_fusion.lat_ref = s32[2]{0:T(128)} fusion(s32[1]{0:T(128)} %constant.16.clone.1, s32[1]{0:T(128)} %bitcast), kind=kLoop, calls=%fused_computation | loop fusion | flops 2 | bytes 16 | tf_op jit(solution)/shard_map/stack | solution.py:315
  14.9 7.4 %collective-permute-done.3.west_ref = f32[6,8,128]{2,1,0:T(8,128)S(1)} collective-permute-done((f32[6,8,128]{2,1,0:T(8,128)}, f32[6,8,128]{2,1,0:T(8,128)S(1)}, u32[]{:S(2)}, u32[]{:S(2)}) %collective-permute-start.3) | collective-permute-done | bytes 24608 | tf_op jit(solution)/shard_map/ppermute | solution.py:330
  22.4 0.0 copy-start.3
  22.4 0.0 collective-permute-done.4.east_ref
  22.4 0.6 %copy-done.3 = f32[6,8,128]{2,1,0:T(8,128)} copy-done((f32[6,8,128]{2,1,0:T(8,128)}, f32[6,8,128]{2,1,0:T(8,128)S(1)}, u32[]{:S(2)}) %copy-start.3) | copy-done | bytes 24600
  23.0 0.0 copy-start.4
  23.0 0.6 %copy-done.4 = f32[6,8,128]{2,1,0:T(8,128)} copy-done((f32[6,8,128]{2,1,0:T(8,128)}, f32[6,8,128]{2,1,0:T(8,128)S(1)}, u32[]{:S(2)}) %copy-start.4) | copy-done | bytes 24600
  23.6 8.2 %shard_map.139 = (f32[300,8,128]{2,1,0:T(8,128)}, f32[75,8,128]{2,1,0:T(8,128)}) custom-call(f32[75]{0:T(128)} %constant.18.clone.h_ref, f32[75]{0:T(128)} %constant.20.clone.zmid_ref, s32[8,128]{1,0:T(8,128)} %shore_ref.5, s32[8,128]{1,0:T(8,128)} %bottom_ref.5, f32[75,8,128]{2,1,0:T(8,128)} %t_ref.5, f32[75,8,128]{2,1,0:T(8,128)} %s_ref.5, ...), custom_call_target="tpu_custom_call" | custom-call | tf_op jit(solution)/shard_map/pallas_call | solution.py:339
  31.8 0.0 collective-permute-done.south_ref
  31.8 0.0 copy-start
  31.8 0.0 collective-permute-done.1.north_ref
  31.8 0.0 copy-start.1
  31.8 0.0 collective-permute-done.2.fold_ref
  31.9 0.0 copy-start.2
  31.9 0.7 %copy-done = f32[76,8,128]{2,1,0:T(8,128)} copy-done((f32[76,8,128]{2,1,0:T(8,128)}, f32[76,8,128]{2,1,0:T(8,128)S(1)}, u32[]{:S(2)}) %copy-start) | copy-done | bytes 311320
  32.5 0.1 copy-done.1
  32.7 0.1 copy-done.2
  32.8 7.5 %shard_map.140 = (f32[75,8,128]{2,1,0:T(8,128)}, f32[75,8,128]{2,1,0:T(8,128)}, f32[75,8,128]{2,1,0:T(8,128)}, f32[75,8,128]{2,1,0:T(8,128)}) custom-call(s32[2]{0:T(128)} %pad_add_fusion.lat_ref, f32[75]{0:T(128)} %constant.18.clone.h_ref, f32[75]{0:T(128)} %constant.19.clone.inv_h_ref, f32[75]{0:T(128)} %constant.20.clone.zmid_ref, ...), custom_call_target="tpu_custom_call" | custom-call | tf_op jit(solution)/shard_map/pallas_call | solution.py:345
Async XLA Ops:
  4.3 27.5 %collective-permute-start = (f32[76,8,128]{2,1,0:T(8,128)}, f32[76,8,128]{2,1,0:T(8,128)S(1)}, u32[]{:S(2)}, u32[]{:S(2)}) collective-permute-start(f32[76,8,128]{2,1,0:T(8,128)} %get-tuple-element.11), channel_id=1, source_target_pairs={{0,4},{4,8},{8,12},{12,16},{16,20},{20,24},{24,28},{1,5},{5,9},{9,... | collective-permute-start | bytes 933896 | tf_op jit(solution)/shard_map/ppermute | solution.py:328
  5.6 26.2 %collective-permute-start.1 = (f32[76,8,128]{2,1,0:T(8,128)}, f32[76,8,128]{2,1,0:T(8,128)S(1)}, u32[]{:S(2)}, u32[]{:S(2)}) collective-permute-start(f32[76,8,128]{2,1,0:T(8,128)} %get-tuple-element.12), channel_id=1, source_target_pairs={{4,0},{8,4},{12,8},{16,12},{20,16},{24,20},{28,24},{5,1},{9,5},{13... | collective-permute-start | bytes 933896 | tf_op jit(solution)/shard_map/ppermute | solution.py:329
  10.2 21.7 %collective-permute-start.2 = (f32[76,8,128]{2,1,0:T(8,128)}, f32[76,8,128]{2,1,0:T(8,128)S(1)}, u32[]{:S(2)}, u32[]{:S(2)}) collective-permute-start(f32[76,8,128]{2,1,0:T(8,128)} %get-tuple-element.13), channel_id=1, source_target_pairs={{28,31},{29,30},{30,29},{31,28}} | collective-permute-start | bytes 933896 | tf_op jit(solution)/shard_map/ppermute | solution.py:333
  12.5 9.9 %collective-permute-start.3 = (f32[6,8,128]{2,1,0:T(8,128)}, f32[6,8,128]{2,1,0:T(8,128)S(1)}, u32[]{:S(2)}, u32[]{:S(2)}) collective-permute-start(f32[6,8,128]{2,1,0:T(8,128)} %get-tuple-element.14), channel_id=1, source_target_pairs={{0,1},{1,2},{2,3},{3,0},{4,5},{5,6},{6,7},{7,4},{8,9},{9,10},{10,1... | collective-permute-start | bytes 73736 | tf_op jit(solution)/shard_map/ppermute | solution.py:330
  13.8 8.6 %collective-permute-start.4 = (f32[6,8,128]{2,1,0:T(8,128)}, f32[6,8,128]{2,1,0:T(8,128)S(1)}, u32[]{:S(2)}, u32[]{:S(2)}) collective-permute-start(f32[6,8,128]{2,1,0:T(8,128)} %get-tuple-element.15), channel_id=1, source_target_pairs={{1,0},{2,1},{3,2},{0,3},{5,4},{6,5},{7,6},{4,7},{9,8},{10,9},{11,1... | collective-permute-start | bytes 73736 | tf_op jit(solution)/shard_map/ppermute | solution.py:331
  22.4 0.6 %copy-start.3 = (f32[6,8,128]{2,1,0:T(8,128)}, f32[6,8,128]{2,1,0:T(8,128)S(1)}, u32[]{:S(2)}) copy-start(f32[6,8,128]{2,1,0:T(8,128)S(1)} %collective-permute-done.3.west_ref) | copy-start | bytes 73732
  23.0 0.6 %copy-start.4 = (f32[6,8,128]{2,1,0:T(8,128)}, f32[6,8,128]{2,1,0:T(8,128)S(1)}, u32[]{:S(2)}) copy-start(f32[6,8,128]{2,1,0:T(8,128)S(1)} %collective-permute-done.4.east_ref) | copy-start | bytes 73732
  31.8 0.7 %copy-start = (f32[76,8,128]{2,1,0:T(8,128)}, f32[76,8,128]{2,1,0:T(8,128)S(1)}, u32[]{:S(2)}) copy-start(f32[76,8,128]{2,1,0:T(8,128)S(1)} %collective-permute-done.south_ref) | copy-start | bytes 933892
  31.8 0.8 %copy-start.1 = (f32[76,8,128]{2,1,0:T(8,128)}, f32[76,8,128]{2,1,0:T(8,128)S(1)}, u32[]{:S(2)}) copy-start(f32[76,8,128]{2,1,0:T(8,128)S(1)} %collective-permute-done.1.north_ref) | copy-start | bytes 933892
  31.9 0.9 %copy-start.2 = (f32[76,8,128]{2,1,0:T(8,128)}, f32[76,8,128]{2,1,0:T(8,128)S(1)}, u32[]{:S(2)}) copy-start(f32[76,8,128]{2,1,0:T(8,128)S(1)} %collective-permute-done.2.fold_ref) | copy-start | bytes 933892

commit v6 on v5

--- a/solution.py
+++ b/solution.py
@@ -330,6 +330,7 @@
     from_west = lax.ppermute(right, "lon", [(i, (i + 1) % n_lon) for i in range(n_lon)])
     from_east = lax.ppermute(left, "lon", [((i + 1) % n_lon, i) for i in range(n_lon)])
     last = (n_lat - 1) * n_lon
+    fold, from_west, from_east = lax.optimization_barrier((fold, from_west, from_east))
     from_fold = lax.ppermute(
         fold, ("lat", "lon"), [(last + x, last + n_lon - 1 - x) for x in range(n_lon)]
     )

time: 40.5 us -> 33.2 us (0.82)
  the two profiles are of different devices: /device:TPU:26 before, /device:TPU:27 now
where the time goes in v6:
time: 33.2 us; the launch traced here: 33 us
  Pallas kernels  19.4 us (58%)
  starting transfers between devices  11.3 us (34%)
  local copies, waits for them, and re-layouts  0.91 us (3%)
  between operations  0.74 us (2%)
  other arithmetic  0.65 us (2%)
    pallas_call x1, Pallas kernels, on_device(): pl.pallas_call(xpart_kernel, out_shape=(jax.ShapeDtypeStruct((4 * layers,...  8.19 us
    pallas_call x1, Pallas kernels, on_device(): pl.pallas_call(step_kernel, out_shape=(plane,) * 4, in_specs=[smem] * 5 +...  7.5 us
    ppermute x1, starting transfers between devices, on_device(): lax.ppermute(fold, ('lat', 'lon'), [(last + x, last + n_lon - 1 - x) for...  4.21 us
    ppermute x1, starting transfers between devices, on_device(): lax.ppermute(bot, 'lat', [(i + 1, i) for i in range(n_lat - 1)])  4 us
    pallas_call x1, Pallas kernels, on_device(): pl.pallas_call(pack_kernel, out_shape=(row_tiles, row_tiles, row_tiles, c...  3.69 us
    ppermute x1, starting transfers between devices, on_device(): lax.ppermute(right, 'lon', [(i, (i + 1) % n_lon) for i in range(n_lon)])  1.8 us
    ppermute x1, starting transfers between devices, on_device(): lax.ppermute(top, 'lat', [(i, i + 1) for i in range(n_lat - 1)])  1.28 us
    unnamed x10, local copies, waits for them, and re-layouts  0.91 us
  transfers between devices with their start and end apart: 5, of which 0 were waited for; matrix products, arithmetic and copies ran while one was open for 2% of the time, Pallas kernels for 25%

profile of v6, /device:TPU:27, one launch (start us, length us, event | category | flops | bytes accessed | tf_op | source)
XLA Modules:
  0.0 33.0 jit_solution(2888804109344610458)
XLA Ops:
  0.6 3.7 %shard_map.138 = (f32[76,8,128]{2,1,0:T(8,128)}, f32[76,8,128]{2,1,0:T(8,128)}, f32[76,8,128]{2,1,0:T(8,128)}, f32[6,8,128]{2,1,0:T(8,128)}, f32[6,8,128]{2,1,0:T(8,128)}) custom-call(s32[1]{0:T(128)} %bitcast.1.last_ref, s32[8,128]{1,0:T(8,128)} %shore_ref.5, s32[8,128]{1,0:T(8,128)} %bottom_ref.5, f32[75,8,128]{2,1,0:T(8,128)} %t_ref.5, ...), custom_call_target="tpu_custom_call" | custom-call | tf_op jit(solution)/shard_map/pallas_call | solution.py:321
  4.3 1.8 %collective-permute-start.2 = (f32[6,8,128]{2,1,0:T(8,128)}, f32[6,8,128]{2,1,0:T(8,128)S(1)}, u32[]{:S(2)}, u32[]{:S(2)}) collective-permute-start(f32[6,8,128]{2,1,0:T(8,128)} %get-tuple-element.17), channel_id=1, source_target_pairs={{0,1},{1,2},{2,3},{3,0},{4,5},{5,6},{6,7},{7,4},{8,9},{9,10},{10,1... | collective-permute-start | bytes 73736 | tf_op jit(solution)/shard_map/ppermute | solution.py:330
  6.1 0.0 collective-permute-start.3
  6.1 1.3 %collective-permute-start = (f32[76,8,128]{2,1,0:T(8,128)}, f32[76,8,128]{2,1,0:T(8,128)S(1)}, u32[]{:S(2)}, u32[]{:S(2)}) collective-permute-start(f32[76,8,128]{2,1,0:T(8,128)} %get-tuple-element.14), channel_id=1, source_target_pairs={{0,4},{4,8},{8,12},{12,16},{16,20},{20,24},{24,28},{1,5},{5,9},{9,... | collective-permute-start | bytes 933896 | tf_op jit(solution)/shard_map/ppermute | solution.py:328
  7.4 4.0 %collective-permute-start.1 = (f32[76,8,128]{2,1,0:T(8,128)}, f32[76,8,128]{2,1,0:T(8,128)S(1)}, u32[]{:S(2)}, u32[]{:S(2)}) collective-permute-start(f32[76,8,128]{2,1,0:T(8,128)} %get-tuple-element.15), channel_id=1, source_target_pairs={{4,0},{8,4},{12,8},{16,12},{20,16},{24,20},{28,24},{5,1},{9,5},{13... | collective-permute-start | bytes 933896 | tf_op jit(solution)/shard_map/ppermute | solution.py:329
  11.4 0.0 collective-permute-done.2.west_ref
  11.4 0.0 copy-start.3
  11.5 0.0 collective-permute-done.3.east_ref
  11.5 0.0 copy-start.4
  11.5 4.2 %collective-permute-start.4 = (f32[76,8,128]{2,1,0:T(8,128)}, f32[76,8,128]{2,1,0:T(8,128)S(1)}, u32[]{:S(2)}, u32[]{:S(2)}) collective-permute-start(f32[76,8,128]{2,1,0:T(8,128)} %get-tuple-element.19), channel_id=1, source_target_pairs={{28,31},{29,30},{30,29},{31,28}} | collective-permute-start | bytes 933896 | tf_op jit(solution)/shard_map/ppermute | solution.py:334
  15.7 0.7 %pad_add_fusion.lat_ref = s32[2]{0:T(128)} fusion(s32[1]{0:T(128)} %constant.16.clone.1, s32[1]{0:T(128)} %bitcast), kind=kLoop, calls=%fused_computation | loop fusion | flops 2 | bytes 16 | tf_op jit(solution)/shard_map/stack | solution.py:315
  16.3 0.0 copy-done.3
  16.3 0.0 copy-done.4
  16.4 8.2 %shard_map.139 = (f32[300,8,128]{2,1,0:T(8,128)}, f32[75,8,128]{2,1,0:T(8,128)}) custom-call(f32[75]{0:T(128)} %constant.18.clone.h_ref, f32[75]{0:T(128)} %constant.20.clone.zmid_ref, s32[8,128]{1,0:T(8,128)} %shore_ref.5, s32[8,128]{1,0:T(8,128)} %bottom_ref.5, f32[75,8,128]{2,1,0:T(8,128)} %t_ref.5, f32[75,8,128]{2,1,0:T(8,128)} %s_ref.5, ...), custom_call_target="tpu_custom_call" | custom-call | tf_op jit(solution)/shard_map/pallas_call | solution.py:340
  24.5 0.0 collective-permute-done.south_ref
  24.6 0.0 copy-start
  24.6 0.0 collective-permute-done.1.north_ref
  24.6 0.0 copy-start.1
  24.6 0.0 collective-permute-done.4.fold_ref
  24.6 0.0 copy-start.2
  24.6 0.7 %copy-done = f32[76,8,128]{2,1,0:T(8,128)} copy-done((f32[76,8,128]{2,1,0:T(8,128)}, f32[76,8,128]{2,1,0:T(8,128)S(1)}, u32[]{:S(2)}) %copy-start) | copy-done | bytes 311320
  25.3 0.1 copy-done.1
  25.4 0.1 copy-done.2
  25.5 7.5 %shard_map.140 = (f32[75,8,128]{2,1,0:T(8,128)}, f32[75,8,128]{2,1,0:T(8,128)}, f32[75,8,128]{2,1,0:T(8,128)}, f32[75,8,128]{2,1,0:T(8,128)}) custom-call(s32[2]{0:T(128)} %pad_add_fusion.lat_ref, f32[75]{0:T(128)} %constant.18.clone.h_ref, f32[75]{0:T(128)} %constant.19.clone.inv_h_ref, f32[75]{0:T(128)} %constant.20.clone.zmid_ref, ...), custom_call_target="tpu_custom_call" | custom-call | tf_op jit(solution)/shard_map/pallas_call | solution.py:346
Async XLA Ops:
  4.3 7.1 %collective-permute-start.2 = (f32[6,8,128]{2,1,0:T(8,128)}, f32[6,8,128]{2,1,0:T(8,128)S(1)}, u32[]{:S(2)}, u32[]{:S(2)}) collective-permute-start(f32[6,8,128]{2,1,0:T(8,128)} %get-tuple-element.17), channel_id=1, source_target_pairs={{0,1},{1,2},{2,3},{3,0},{4,5},{5,6},{6,7},{7,4},{8,9},{9,10},{10,1... | collective-permute-start | bytes 73736 | tf_op jit(solution)/shard_map/ppermute | solution.py:330
  6.1 5.3 %collective-permute-start.3 = (f32[6,8,128]{2,1,0:T(8,128)}, f32[6,8,128]{2,1,0:T(8,128)S(1)}, u32[]{:S(2)}, u32[]{:S(2)}) collective-permute-start(f32[6,8,128]{2,1,0:T(8,128)} %get-tuple-element.18), channel_id=1, source_target_pairs={{1,0},{2,1},{3,2},{0,3},{5,4},{6,5},{7,6},{4,7},{9,8},{10,9},{11,1... | collective-permute-start | bytes 73736 | tf_op jit(solution)/shard_map/ppermute | solution.py:331
  6.1 18.4 %collective-permute-start = (f32[76,8,128]{2,1,0:T(8,128)}, f32[76,8,128]{2,1,0:T(8,128)S(1)}, u32[]{:S(2)}, u32[]{:S(2)}) collective-permute-start(f32[76,8,128]{2,1,0:T(8,128)} %get-tuple-element.14), channel_id=1, source_target_pairs={{0,4},{4,8},{8,12},{12,16},{16,20},{20,24},{24,28},{1,5},{5,9},{9,... | collective-permute-start | bytes 933896 | tf_op jit(solution)/shard_map/ppermute | solution.py:328
  7.4 17.1 %collective-permute-start.1 = (f32[76,8,128]{2,1,0:T(8,128)}, f32[76,8,128]{2,1,0:T(8,128)S(1)}, u32[]{:S(2)}, u32[]{:S(2)}) collective-permute-start(f32[76,8,128]{2,1,0:T(8,128)} %get-tuple-element.15), channel_id=1, source_target_pairs={{4,0},{8,4},{12,8},{16,12},{20,16},{24,20},{28,24},{5,1},{9,5},{13... | collective-permute-start | bytes 933896 | tf_op jit(solution)/shard_map/ppermute | solution.py:329
  11.4 4.9 %copy-start.3 = (f32[6,8,128]{2,1,0:T(8,128)}, f32[6,8,128]{2,1,0:T(8,128)S(1)}, u32[]{:S(2)}) copy-start(f32[6,8,128]{2,1,0:T(8,128)S(1)} %collective-permute-done.2.west_ref) | copy-start | bytes 73732
  11.5 4.9 %copy-start.4 = (f32[6,8,128]{2,1,0:T(8,128)}, f32[6,8,128]{2,1,0:T(8,128)S(1)}, u32[]{:S(2)}) copy-start(f32[6,8,128]{2,1,0:T(8,128)S(1)} %collective-permute-done.3.east_ref) | copy-start | bytes 73732
  11.5 13.1 %collective-permute-start.4 = (f32[76,8,128]{2,1,0:T(8,128)}, f32[76,8,128]{2,1,0:T(8,128)S(1)}, u32[]{:S(2)}, u32[]{:S(2)}) collective-permute-start(f32[76,8,128]{2,1,0:T(8,128)} %get-tuple-element.19), channel_id=1, source_target_pairs={{28,31},{29,30},{30,29},{31,28}} | collective-permute-start | bytes 933896 | tf_op jit(solution)/shard_map/ppermute | solution.py:334
  24.6 0.7 %copy-start = (f32[76,8,128]{2,1,0:T(8,128)}, f32[76,8,128]{2,1,0:T(8,128)S(1)}, u32[]{:S(2)}) copy-start(f32[76,8,128]{2,1,0:T(8,128)S(1)} %collective-permute-done.south_ref) | copy-start | bytes 933892
  24.6 0.8 %copy-start.1 = (f32[76,8,128]{2,1,0:T(8,128)}, f32[76,8,128]{2,1,0:T(8,128)S(1)}, u32[]{:S(2)}) copy-start(f32[76,8,128]{2,1,0:T(8,128)S(1)} %collective-permute-done.1.north_ref) | copy-start | bytes 933892
  24.6 0.9 %copy-start.2 = (f32[76,8,128]{2,1,0:T(8,128)}, f32[76,8,128]{2,1,0:T(8,128)S(1)}, u32[]{:S(2)}) copy-start(f32[76,8,128]{2,1,0:T(8,128)S(1)} %collective-permute-done.4.fold_ref) | copy-start | bytes 933892

commit v7 on v6

--- a/solution.py
+++ b/solution.py
@@ -158,14 +158,32 @@
 
 def step_kernel(
     lat_ref, h_ref, inv_h_ref, zmid_ref, inv_sp_ref,
-    shore_ref, bottom_ref, flux_ref, t_ref, s_ref, u_ref, v_ref,
-    south_ref, north_ref, fold_ref, divx_ref, gradx_ref,
+    shore_ref, bottom_ref, flux_ref, t_hbm, s_hbm, u_hbm, v_hbm,
+    south_ref, north_ref, fold_ref, divx_hbm, gradx_hbm,
     o0_ref, o1_ref, o2_ref, o3_ref,
     star_scr, r_scr, rs_scr,
+    t_ref, s_ref, u_ref, v_ref, divx_ref, gradx_ref, sems,
 ):
     layers = t_ref.shape[0]
     rows, cols = t_ref.shape[1], t_ref.shape[2]
     groups = layers // GROUP
+
+    def chunk_copies(g):
+        span = pl.ds(g * GROUP, GROUP)
+        pairs = [(src.at[span], dst.at[span]) for src, dst in (
+            (t_hbm, t_ref), (s_hbm, s_ref), (u_hbm, u_ref), (v_hbm, v_ref),
+            (gradx_hbm, gradx_ref),
+        )]
+        for c in range(4):
+            plane_span = pl.ds(c * layers + g * GROUP, GROUP)
+            pairs.append((divx_hbm.at[plane_span], divx_ref.at[plane_span]))
+        return [
+            pltpu.make_async_copy(src, dst, sems.at[g, i]) for i, (src, dst) in enumerate(pairs)
+        ]
+
+    for g in range(groups):
+        for copy in chunk_copies(g):
+            copy.start()
     lane = lax.broadcasted_iota(jnp.int32, (rows, cols), 1)
     row = lax.broadcasted_iota(jnp.int32, (rows, cols), 0)
 
@@ -226,7 +244,11 @@
         rs_scr[k] = density(star0, star1, zmid)
         return (cum_ym, cum_yp)
 
-    lax.fori_loop(0, layers, explicit, (zero, zero), unroll=3)
+    carry = (zero, zero)
+    for g in range(groups):
+        for copy in chunk_copies(g):
+            copy.wait()
+        carry = lax.fori_loop(g * GROUP, (g + 1) * GROUP, explicit, carry, unroll=3)
 
     surface_scale = surface_gain * inv_h_ref[0]
     w_top = (0.0 < dep).astype(jnp.float32)
@@ -316,6 +338,7 @@
 
     smem = pl.BlockSpec(memory_space=pltpu.SMEM)
     vmem = pl.BlockSpec(memory_space=pltpu.VMEM)
+    anywhere = pl.BlockSpec(memory_space=pl.ANY)
     row_tiles = jax.ShapeDtypeStruct((layers + 1, rows, cols), jnp.float32)
     col_tiles = jax.ShapeDtypeStruct((groups + 1, rows, cols), jnp.float32)
     top, bot, fold, right, left = pl.pallas_call(
@@ -346,12 +369,16 @@
     outs = pl.pallas_call(
         step_kernel,
         out_shape=(plane,) * 4,
-        in_specs=[smem] * 5 + [vmem] * 12,
+        in_specs=[smem] * 5 + [vmem] * 3 + [anywhere] * 4 + [vmem] * 3 + [anywhere] * 2,
         out_specs=(vmem,) * 4,
         scratch_shapes=[
             pltpu.VMEM((4 * layers, rows, cols), jnp.float32),
             pltpu.VMEM((2 * layers, rows, cols), jnp.float32),
             pltpu.VMEM((layers, rows, cols), jnp.float32),
+        ] + [pltpu.VMEM((layers, rows, cols), jnp.float32)] * 4 + [
+            pltpu.VMEM((4 * layers, rows, cols), jnp.float32),
+            pltpu.VMEM((layers, rows, cols), jnp.float32),
+            pltpu.SemaphoreType.DMA((groups, 9)),
         ],
     )(
         lat_info, *tables,

time: 33.2 us -> 34 us (1.024)
  Pallas kernels: 19.4 us -> 20 us
    pallas_call x1, Pallas kernels: 7.5 us -> 8.16 us  [on_device(): pl.pallas_call(step_kernel, out_shape=(plane,) * 4, in_specs=[smem] * 5 +...]
  transfers between devices with their start and end apart: 5 -> 5, of which waited for: 0 -> 0; matrix products, arithmetic and copies ran while one was open for 2% -> 2% of each run, Pallas kernels for 25% -> 24%
where the time goes in v7:
time: 34 us; the launch traced here: 33.7 us
  Pallas kernels  20 us (59%)
  starting transfers between devices  11.3 us (33%)
  local copies, waits for them, and re-layouts  0.91 us (3%)
  between operations  0.74 us (2%)
  other arithmetic  0.65 us (2%)
    pallas_call x1, Pallas kernels, on_device(): pl.pallas_call(xpart_kernel, out_shape=(jax.ShapeDtypeStruct((4 * layers,...  8.19 us
    pallas_call x1, Pallas kernels, on_device(): pl.pallas_call(step_kernel, out_shape=(plane,) * 4, in_specs=[smem] * 5 +...  8.16 us
    ppermute x1, starting transfers between devices, on_device(): lax.ppermute(fold, ('lat', 'lon'), [(last + x, last + n_lon - 1 - x) for...  4.21 us
    ppermute x1, starting transfers between devices, on_device(): lax.ppermute(bot, 'lat', [(i + 1, i) for i in range(n_lat - 1)])  4 us
    pallas_call x1, Pallas kernels, on_device(): pl.pallas_call(pack_kernel, out_shape=(row_tiles, row_tiles, row_tiles, c...  3.69 us
    ppermute x1, starting transfers between devices, on_device(): lax.ppermute(right, 'lon', [(i, (i + 1) % n_lon) for i in range(n_lon)])  1.8 us
    ppermute x1, starting transfers between devices, on_device(): lax.ppermute(top, 'lat', [(i, i + 1) for i in range(n_lat - 1)])  1.28 us
    unnamed x10, local copies, waits for them, and re-layouts  0.91 us
  transfers between devices with their start and end apart: 5, of which 0 were waited for; matrix products, arithmetic and copies ran while one was open for 2% of the time, Pallas kernels for 24%

profile of v7, /device:TPU:27, one launch (start us, length us, event | category | flops | bytes accessed | tf_op | source)
XLA Modules:
  0.0 33.7 jit_solution(4426899292749355354)
XLA Ops:
  0.6 3.7 %shard_map.138 = (f32[76,8,128]{2,1,0:T(8,128)}, f32[76,8,128]{2,1,0:T(8,128)}, f32[76,8,128]{2,1,0:T(8,128)}, f32[6,8,128]{2,1,0:T(8,128)}, f32[6,8,128]{2,1,0:T(8,128)}) custom-call(s32[1]{0:T(128)} %bitcast.1.last_ref, s32[8,128]{1,0:T(8,128)} %shore_ref.5, s32[8,128]{1,0:T(8,128)} %bottom_ref.5, f32[75,8,128]{2,1,0:T(8,128)} %t_hbm.1, ...), custom_call_target="tpu_custom_call" | custom-call | tf_op jit(solution)/shard_map/pallas_call | solution.py:344
  4.3 1.8 %collective-permute-start.2 = (f32[6,8,128]{2,1,0:T(8,128)}, f32[6,8,128]{2,1,0:T(8,128)S(1)}, u32[]{:S(2)}, u32[]{:S(2)}) collective-permute-start(f32[6,8,128]{2,1,0:T(8,128)} %get-tuple-element.17), channel_id=1, source_target_pairs={{0,1},{1,2},{2,3},{3,0},{4,5},{5,6},{6,7},{7,4},{8,9},{9,10},{10,1... | collective-permute-start | bytes 73736 | tf_op jit(solution)/shard_map/ppermute | solution.py:353
  6.1 0.0 collective-permute-start.3
  6.1 1.3 %collective-permute-start = (f32[76,8,128]{2,1,0:T(8,128)}, f32[76,8,128]{2,1,0:T(8,128)S(1)}, u32[]{:S(2)}, u32[]{:S(2)}) collective-permute-start(f32[76,8,128]{2,1,0:T(8,128)} %get-tuple-element.14), channel_id=1, source_target_pairs={{0,4},{4,8},{8,12},{12,16},{16,20},{20,24},{24,28},{1,5},{5,9},{9,... | collective-permute-start | bytes 933896 | tf_op jit(solution)/shard_map/ppermute | solution.py:351
  7.4 4.0 %collective-permute-start.1 = (f32[76,8,128]{2,1,0:T(8,128)}, f32[76,8,128]{2,1,0:T(8,128)S(1)}, u32[]{:S(2)}, u32[]{:S(2)}) collective-permute-start(f32[76,8,128]{2,1,0:T(8,128)} %get-tuple-element.15), channel_id=1, source_target_pairs={{4,0},{8,4},{12,8},{16,12},{20,16},{24,20},{28,24},{5,1},{9,5},{13... | collective-permute-start | bytes 933896 | tf_op jit(solution)/shard_map/ppermute | solution.py:352
  11.4 0.0 collective-permute-done.2.west_ref
  11.4 0.0 copy-start.3
  11.5 0.0 collective-permute-done.3.east_ref
  11.5 0.0 copy-start.4
  11.5 4.2 %collective-permute-start.4 = (f32[76,8,128]{2,1,0:T(8,128)}, f32[76,8,128]{2,1,0:T(8,128)S(1)}, u32[]{:S(2)}, u32[]{:S(2)}) collective-permute-start(f32[76,8,128]{2,1,0:T(8,128)} %get-tuple-element.19), channel_id=1, source_target_pairs={{28,31},{29,30},{30,29},{31,28}} | collective-permute-start | bytes 933896 | tf_op jit(solution)/shard_map/ppermute | solution.py:357
  15.7 0.7 %pad_add_fusion.lat_ref = s32[2]{0:T(128)} fusion(s32[1]{0:T(128)} %constant.16.clone.1, s32[1]{0:T(128)} %bitcast), kind=kLoop, calls=%fused_computation | loop fusion | flops 2 | bytes 16 | tf_op jit(solution)/shard_map/stack | solution.py:337
  16.3 0.0 copy-done.3
  16.3 0.0 copy-done.4
  16.4 8.2 %shard_map.139 = (f32[300,8,128]{2,1,0:T(8,128)}, f32[75,8,128]{2,1,0:T(8,128)}) custom-call(f32[75]{0:T(128)} %constant.18.clone.h_ref, f32[75]{0:T(128)} %constant.20.clone.zmid_ref, s32[8,128]{1,0:T(8,128)} %shore_ref.5, s32[8,128]{1,0:T(8,128)} %bottom_ref.5, f32[75,8,128]{2,1,0:T(8,128)} %t_hbm.1, f32[75,8,128]{2,1,0:T(8,128)} %s_hbm.1, ...), custom_call_target="tpu_custom_call" | custom-call | tf_op jit(solution)/shard_map/pallas_call | solution.py:363
  24.5 0.0 collective-permute-done.south_ref
  24.6 0.0 copy-start
  24.6 0.0 collective-permute-done.1.north_ref
  24.6 0.0 copy-start.1
  24.6 0.0 collective-permute-done.4.fold_ref
  24.6 0.0 copy-start.2
  24.6 0.7 %copy-done = f32[76,8,128]{2,1,0:T(8,128)} copy-done((f32[76,8,128]{2,1,0:T(8,128)}, f32[76,8,128]{2,1,0:T(8,128)S(1)}, u32[]{:S(2)}) %copy-start) | copy-done | bytes 311320
  25.3 0.1 copy-done.1
  25.4 0.1 copy-done.2
  25.5 8.2 %shard_map.140 = (f32[75,8,128]{2,1,0:T(8,128)}, f32[75,8,128]{2,1,0:T(8,128)}, f32[75,8,128]{2,1,0:T(8,128)}, f32[75,8,128]{2,1,0:T(8,128)}) custom-call(s32[2]{0:T(128)} %pad_add_fusion.lat_ref, f32[75]{0:T(128)} %constant.18.clone.h_ref, f32[75]{0:T(128)} %constant.19.clone.inv_h_ref, f32[75]{0:T(128)} %constant.20.clone.zmid_ref, ...), custom_call_target="tpu_custom_call" | custom-call | tf_op jit(solution)/shard_map/pallas_call | solution.py:369
Async XLA Ops:
  4.3 7.1 %collective-permute-start.2 = (f32[6,8,128]{2,1,0:T(8,128)}, f32[6,8,128]{2,1,0:T(8,128)S(1)}, u32[]{:S(2)}, u32[]{:S(2)}) collective-permute-start(f32[6,8,128]{2,1,0:T(8,128)} %get-tuple-element.17), channel_id=1, source_target_pairs={{0,1},{1,2},{2,3},{3,0},{4,5},{5,6},{6,7},{7,4},{8,9},{9,10},{10,1... | collective-permute-start | bytes 73736 | tf_op jit(solution)/shard_map/ppermute | solution.py:353
  6.1 5.3 %collective-permute-start.3 = (f32[6,8,128]{2,1,0:T(8,128)}, f32[6,8,128]{2,1,0:T(8,128)S(1)}, u32[]{:S(2)}, u32[]{:S(2)}) collective-permute-start(f32[6,8,128]{2,1,0:T(8,128)} %get-tuple-element.18), channel_id=1, source_target_pairs={{1,0},{2,1},{3,2},{0,3},{5,4},{6,5},{7,6},{4,7},{9,8},{10,9},{11,1... | collective-permute-start | bytes 73736 | tf_op jit(solution)/shard_map/ppermute | solution.py:354
  6.1 18.4 %collective-permute-start = (f32[76,8,128]{2,1,0:T(8,128)}, f32[76,8,128]{2,1,0:T(8,128)S(1)}, u32[]{:S(2)}, u32[]{:S(2)}) collective-permute-start(f32[76,8,128]{2,1,0:T(8,128)} %get-tuple-element.14), channel_id=1, source_target_pairs={{0,4},{4,8},{8,12},{12,16},{16,20},{20,24},{24,28},{1,5},{5,9},{9,... | collective-permute-start | bytes 933896 | tf_op jit(solution)/shard_map/ppermute | solution.py:351
  7.4 17.1 %collective-permute-start.1 = (f32[76,8,128]{2,1,0:T(8,128)}, f32[76,8,128]{2,1,0:T(8,128)S(1)}, u32[]{:S(2)}, u32[]{:S(2)}) collective-permute-start(f32[76,8,128]{2,1,0:T(8,128)} %get-tuple-element.15), channel_id=1, source_target_pairs={{4,0},{8,4},{12,8},{16,12},{20,16},{24,20},{28,24},{5,1},{9,5},{13... | collective-permute-start | bytes 933896 | tf_op jit(solution)/shard_map/ppermute | solution.py:352
  11.4 4.9 %copy-start.3 = (f32[6,8,128]{2,1,0:T(8,128)}, f32[6,8,128]{2,1,0:T(8,128)S(1)}, u32[]{:S(2)}) copy-start(f32[6,8,128]{2,1,0:T(8,128)S(1)} %collective-permute-done.2.west_ref) | copy-start | bytes 73732
  11.5 4.9 %copy-start.4 = (f32[6,8,128]{2,1,0:T(8,128)}, f32[6,8,128]{2,1,0:T(8,128)S(1)}, u32[]{:S(2)}) copy-start(f32[6,8,128]{2,1,0:T(8,128)S(1)} %collective-permute-done.3.east_ref) | copy-start | bytes 73732
  11.5 13.1 %collective-permute-start.4 = (f32[76,8,128]{2,1,0:T(8,128)}, f32[76,8,128]{2,1,0:T(8,128)S(1)}, u32[]{:S(2)}, u32[]{:S(2)}) collective-permute-start(f32[76,8,128]{2,1,0:T(8,128)} %get-tuple-element.19), channel_id=1, source_target_pairs={{28,31},{29,30},{30,29},{31,28}} | collective-permute-start | bytes 933896 | tf_op jit(solution)/shard_map/ppermute | solution.py:357
  24.6 0.7 %copy-start = (f32[76,8,128]{2,1,0:T(8,128)}, f32[76,8,128]{2,1,0:T(8,128)S(1)}, u32[]{:S(2)}) copy-start(f32[76,8,128]{2,1,0:T(8,128)S(1)} %collective-permute-done.south_ref) | copy-start | bytes 933892
  24.6 0.8 %copy-start.1 = (f32[76,8,128]{2,1,0:T(8,128)}, f32[76,8,128]{2,1,0:T(8,128)S(1)}, u32[]{:S(2)}) copy-start(f32[76,8,128]{2,1,0:T(8,128)S(1)} %collective-permute-done.1.north_ref) | copy-start | bytes 933892
  24.6 0.9 %copy-start.2 = (f32[76,8,128]{2,1,0:T(8,128)}, f32[76,8,128]{2,1,0:T(8,128)S(1)}, u32[]{:S(2)}) copy-start(f32[76,8,128]{2,1,0:T(8,128)S(1)} %collective-permute-done.4.fold_ref) | copy-start | bytes 933892

commit v8 on v6

--- a/solution.py
+++ b/solution.py
@@ -226,7 +226,8 @@
         rs_scr[k] = density(star0, star1, zmid)
         return (cum_ym, cum_yp)
 
-    lax.fori_loop(0, layers, explicit, (zero, zero), unroll=3)
+    lag = 2
+    carry_e = lax.fori_loop(0, lag, explicit, (zero, zero))
 
     surface_scale = surface_gain * inv_h_ref[0]
     w_top = (0.0 < dep).astype(jnp.float32)
@@ -266,7 +267,12 @@
         star_scr[3 * layers + k] = s3
         return (mix, r_a, r_b, s0, s1, s2, s3)
 
-    lax.fori_loop(0, layers, forward, (zero,) * 7, unroll=3)
+    def fused(k, carry):
+        carry_e, carry_f = carry
+        return (explicit(k, carry_e), forward(k - lag, carry_f))
+
+    _, carry_f = lax.fori_loop(lag, layers, fused, (carry_e, (zero,) * 7), unroll=3)
+    lax.fori_loop(layers - lag, layers, forward, carry_f)
 
     def backward(i, carry):
         x0, x1, x2, x3 = carry

time: 33.2 us -> 33.1 us (level)
  no operation moved by 1% of the time
where the time goes in v8:
time: 33.1 us; the launch traced here: 32.9 us
  Pallas kernels  19.2 us (58%)
  starting transfers between devices  11.3 us (34%)
  local copies, waits for them, and re-layouts  0.91 us (3%)
  between operations  0.74 us (2%)
  other arithmetic  0.65 us (2%)
    pallas_call x1, Pallas kernels, on_device(): pl.pallas_call(xpart_kernel, out_shape=(jax.ShapeDtypeStruct((4 * layers,...  8.19 us
    pallas_call x1, Pallas kernels, on_device(): pl.pallas_call(step_kernel, out_shape=(plane,) * 4, in_specs=[smem] * 5 +...  7.36 us
    ppermute x1, starting transfers between devices, on_device(): lax.ppermute(fold, ('lat', 'lon'), [(last + x, last + n_lon - 1 - x) for...  4.21 us
    ppermute x1, starting transfers between devices, on_device(): lax.ppermute(bot, 'lat', [(i + 1, i) for i in range(n_lat - 1)])  4 us
    pallas_call x1, Pallas kernels, on_device(): pl.pallas_call(pack_kernel, out_shape=(row_tiles, row_tiles, row_tiles, c...  3.69 us
    ppermute x1, starting transfers between devices, on_device(): lax.ppermute(right, 'lon', [(i, (i + 1) % n_lon) for i in range(n_lon)])  1.8 us
    ppermute x1, starting transfers between devices, on_device(): lax.ppermute(top, 'lat', [(i, i + 1) for i in range(n_lat - 1)])  1.28 us
    unnamed x10, local copies, waits for them, and re-layouts  0.91 us
  transfers between devices with their start and end apart: 5, of which 0 were waited for; matrix products, arithmetic and copies ran while one was open for 2% of the time, Pallas kernels for 25%

profile of v8, /device:TPU:27, one launch (start us, length us, event | category | flops | bytes accessed | tf_op | source)
XLA Modules:
  0.0 32.9 jit_solution(2253960486609255925)
XLA Ops:
  0.6 3.7 %shard_map.138 = (f32[76,8,128]{2,1,0:T(8,128)}, f32[76,8,128]{2,1,0:T(8,128)}, f32[76,8,128]{2,1,0:T(8,128)}, f32[6,8,128]{2,1,0:T(8,128)}, f32[6,8,128]{2,1,0:T(8,128)}) custom-call(s32[1]{0:T(128)} %bitcast.1.last_ref, s32[8,128]{1,0:T(8,128)} %shore_ref.5, s32[8,128]{1,0:T(8,128)} %bottom_ref.5, f32[75,8,128]{2,1,0:T(8,128)} %t_ref.5, ...), custom_call_target="tpu_custom_call" | custom-call | tf_op jit(solution)/shard_map/pallas_call | solution.py:327
  4.3 1.8 %collective-permute-start.2 = (f32[6,8,128]{2,1,0:T(8,128)}, f32[6,8,128]{2,1,0:T(8,128)S(1)}, u32[]{:S(2)}, u32[]{:S(2)}) collective-permute-start(f32[6,8,128]{2,1,0:T(8,128)} %get-tuple-element.17), channel_id=1, source_target_pairs={{0,1},{1,2},{2,3},{3,0},{4,5},{5,6},{6,7},{7,4},{8,9},{9,10},{10,1... | collective-permute-start | bytes 73736 | tf_op jit(solution)/shard_map/ppermute | solution.py:336
  6.1 0.0 collective-permute-start.3
  6.1 1.3 %collective-permute-start = (f32[76,8,128]{2,1,0:T(8,128)}, f32[76,8,128]{2,1,0:T(8,128)S(1)}, u32[]{:S(2)}, u32[]{:S(2)}) collective-permute-start(f32[76,8,128]{2,1,0:T(8,128)} %get-tuple-element.14), channel_id=1, source_target_pairs={{0,4},{4,8},{8,12},{12,16},{16,20},{20,24},{24,28},{1,5},{5,9},{9,... | collective-permute-start | bytes 933896 | tf_op jit(solution)/shard_map/ppermute | solution.py:334
  7.4 4.0 %collective-permute-start.1 = (f32[76,8,128]{2,1,0:T(8,128)}, f32[76,8,128]{2,1,0:T(8,128)S(1)}, u32[]{:S(2)}, u32[]{:S(2)}) collective-permute-start(f32[76,8,128]{2,1,0:T(8,128)} %get-tuple-element.15), channel_id=1, source_target_pairs={{4,0},{8,4},{12,8},{16,12},{20,16},{24,20},{28,24},{5,1},{9,5},{13... | collective-permute-start | bytes 933896 | tf_op jit(solution)/shard_map/ppermute | solution.py:335
  11.4 0.0 collective-permute-done.2.west_ref
  11.4 0.0 copy-start.3
  11.5 0.0 collective-permute-done.3.east_ref
  11.5 0.0 copy-start.4
  11.5 4.2 %collective-permute-start.4 = (f32[76,8,128]{2,1,0:T(8,128)}, f32[76,8,128]{2,1,0:T(8,128)S(1)}, u32[]{:S(2)}, u32[]{:S(2)}) collective-permute-start(f32[76,8,128]{2,1,0:T(8,128)} %get-tuple-element.19), channel_id=1, source_target_pairs={{28,31},{29,30},{30,29},{31,28}} | collective-permute-start | bytes 933896 | tf_op jit(solution)/shard_map/ppermute | solution.py:340
  15.7 0.7 %pad_add_fusion.lat_ref = s32[2]{0:T(128)} fusion(s32[1]{0:T(128)} %constant.16.clone.1, s32[1]{0:T(128)} %bitcast), kind=kLoop, calls=%fused_computation | loop fusion | flops 2 | bytes 16 | tf_op jit(solution)/shard_map/stack | solution.py:321
  16.3 0.0 copy-done.3
  16.3 0.0 copy-done.4
  16.4 8.2 %shard_map.139 = (f32[300,8,128]{2,1,0:T(8,128)}, f32[75,8,128]{2,1,0:T(8,128)}) custom-call(f32[75]{0:T(128)} %constant.18.clone.h_ref, f32[75]{0:T(128)} %constant.20.clone.zmid_ref, s32[8,128]{1,0:T(8,128)} %shore_ref.5, s32[8,128]{1,0:T(8,128)} %bottom_ref.5, f32[75,8,128]{2,1,0:T(8,128)} %t_ref.5, f32[75,8,128]{2,1,0:T(8,128)} %s_ref.5, ...), custom_call_target="tpu_custom_call" | custom-call | tf_op jit(solution)/shard_map/pallas_call | solution.py:346
  24.5 0.0 collective-permute-done.south_ref
  24.6 0.0 copy-start
  24.6 0.0 collective-permute-done.1.north_ref
  24.6 0.0 copy-start.1
  24.6 0.0 collective-permute-done.4.fold_ref
  24.6 0.0 copy-start.2
  24.6 0.7 %copy-done = f32[76,8,128]{2,1,0:T(8,128)} copy-done((f32[76,8,128]{2,1,0:T(8,128)}, f32[76,8,128]{2,1,0:T(8,128)S(1)}, u32[]{:S(2)}) %copy-start) | copy-done | bytes 311320
  25.3 0.1 copy-done.1
  25.4 0.1 copy-done.2
  25.5 7.4 %shard_map.140 = (f32[75,8,128]{2,1,0:T(8,128)}, f32[75,8,128]{2,1,0:T(8,128)}, f32[75,8,128]{2,1,0:T(8,128)}, f32[75,8,128]{2,1,0:T(8,128)}) custom-call(s32[2]{0:T(128)} %pad_add_fusion.lat_ref, f32[75]{0:T(128)} %constant.18.clone.h_ref, f32[75]{0:T(128)} %constant.19.clone.inv_h_ref, f32[75]{0:T(128)} %constant.20.clone.zmid_ref, ...), custom_call_target="tpu_custom_call" | custom-call | tf_op jit(solution)/shard_map/pallas_call | solution.py:352
Async XLA Ops:
  4.3 7.1 %collective-permute-start.2 = (f32[6,8,128]{2,1,0:T(8,128)}, f32[6,8,128]{2,1,0:T(8,128)S(1)}, u32[]{:S(2)}, u32[]{:S(2)}) collective-permute-start(f32[6,8,128]{2,1,0:T(8,128)} %get-tuple-element.17), channel_id=1, source_target_pairs={{0,1},{1,2},{2,3},{3,0},{4,5},{5,6},{6,7},{7,4},{8,9},{9,10},{10,1... | collective-permute-start | bytes 73736 | tf_op jit(solution)/shard_map/ppermute | solution.py:336
  6.1 5.3 %collective-permute-start.3 = (f32[6,8,128]{2,1,0:T(8,128)}, f32[6,8,128]{2,1,0:T(8,128)S(1)}, u32[]{:S(2)}, u32[]{:S(2)}) collective-permute-start(f32[6,8,128]{2,1,0:T(8,128)} %get-tuple-element.18), channel_id=1, source_target_pairs={{1,0},{2,1},{3,2},{0,3},{5,4},{6,5},{7,6},{4,7},{9,8},{10,9},{11,1... | collective-permute-start | bytes 73736 | tf_op jit(solution)/shard_map/ppermute | solution.py:337
  6.1 18.4 %collective-permute-start = (f32[76,8,128]{2,1,0:T(8,128)}, f32[76,8,128]{2,1,0:T(8,128)S(1)}, u32[]{:S(2)}, u32[]{:S(2)}) collective-permute-start(f32[76,8,128]{2,1,0:T(8,128)} %get-tuple-element.14), channel_id=1, source_target_pairs={{0,4},{4,8},{8,12},{12,16},{16,20},{20,24},{24,28},{1,5},{5,9},{9,... | collective-permute-start | bytes 933896 | tf_op jit(solution)/shard_map/ppermute | solution.py:334
  7.4 17.1 %collective-permute-start.1 = (f32[76,8,128]{2,1,0:T(8,128)}, f32[76,8,128]{2,1,0:T(8,128)S(1)}, u32[]{:S(2)}, u32[]{:S(2)}) collective-permute-start(f32[76,8,128]{2,1,0:T(8,128)} %get-tuple-element.15), channel_id=1, source_target_pairs={{4,0},{8,4},{12,8},{16,12},{20,16},{24,20},{28,24},{5,1},{9,5},{13... | collective-permute-start | bytes 933896 | tf_op jit(solution)/shard_map/ppermute | solution.py:335
  11.4 4.9 %copy-start.3 = (f32[6,8,128]{2,1,0:T(8,128)}, f32[6,8,128]{2,1,0:T(8,128)S(1)}, u32[]{:S(2)}) copy-start(f32[6,8,128]{2,1,0:T(8,128)S(1)} %collective-permute-done.2.west_ref) | copy-start | bytes 73732
  11.5 4.9 %copy-start.4 = (f32[6,8,128]{2,1,0:T(8,128)}, f32[6,8,128]{2,1,0:T(8,128)S(1)}, u32[]{:S(2)}) copy-start(f32[6,8,128]{2,1,0:T(8,128)S(1)} %collective-permute-done.3.east_ref) | copy-start | bytes 73732
  11.5 13.1 %collective-permute-start.4 = (f32[76,8,128]{2,1,0:T(8,128)}, f32[76,8,128]{2,1,0:T(8,128)S(1)}, u32[]{:S(2)}, u32[]{:S(2)}) collective-permute-start(f32[76,8,128]{2,1,0:T(8,128)} %get-tuple-element.19), channel_id=1, source_target_pairs={{28,31},{29,30},{30,29},{31,28}} | collective-permute-start | bytes 933896 | tf_op jit(solution)/shard_map/ppermute | solution.py:340
  24.6 0.7 %copy-start = (f32[76,8,128]{2,1,0:T(8,128)}, f32[76,8,128]{2,1,0:T(8,128)S(1)}, u32[]{:S(2)}) copy-start(f32[76,8,128]{2,1,0:T(8,128)S(1)} %collective-permute-done.south_ref) | copy-start | bytes 933892
  24.6 0.8 %copy-start.1 = (f32[76,8,128]{2,1,0:T(8,128)}, f32[76,8,128]{2,1,0:T(8,128)S(1)}, u32[]{:S(2)}) copy-start(f32[76,8,128]{2,1,0:T(8,128)S(1)} %collective-permute-done.1.north_ref) | copy-start | bytes 933892
  24.6 0.9 %copy-start.2 = (f32[76,8,128]{2,1,0:T(8,128)}, f32[76,8,128]{2,1,0:T(8,128)S(1)}, u32[]{:S(2)}) copy-start(f32[76,8,128]{2,1,0:T(8,128)S(1)} %collective-permute-done.4.fold_ref) | copy-start | bytes 933892

commit v9 on v8

--- a/solution.py
+++ b/solution.py
@@ -27,11 +27,25 @@
     return -thermal * warmth * (1.0 + thermal_sq * warmth + depth_column) + haline * saltiness
 
 
-def face_flux(face_vel, before, here, after, beyond):
-    return face_vel * 0.5 * (here + after) - (
-        jnp.maximum(face_vel, 0.0) * (after - 2.0 * here + before)
-        + jnp.minimum(face_vel, 0.0) * (beyond - 2.0 * after + here)
-    ) * (1.0 / 6.0)
+def face_weights(face_vel):
+    return (
+        0.5 * face_vel,
+        jnp.maximum(face_vel, 0.0) * (1.0 / 6.0),
+        jnp.minimum(face_vel, 0.0) * (1.0 / 6.0),
+    )
+
+
+def flux_divergence(right_w, left_w, m2, m1, q0, p1, p2):
+    half_r, pos_r, neg_r = right_w
+    half_l, pos_l, neg_l = left_w
+    step_r = p1 - q0
+    step_l = q0 - m1
+    curv_0 = step_r - step_l
+    curv_p = (p2 - p1) - step_r
+    curv_m = step_l - (m1 - m2)
+    flux_r = half_r * (q0 + p1) - (pos_r * curv_0 + neg_r * curv_p)
+    flux_l = half_l * (m1 + q0) - (pos_l * curv_m + neg_l * curv_0)
+    return flux_r - flux_l
 
 
 def rolled(x, shift, axis):
@@ -41,7 +55,7 @@
 
 def pack_kernel(
     last_ref, shore_ref, bottom_ref, t_ref, s_ref, u_ref, v_ref,
-    top_ref, bot_ref, fold_ref, right_ref, left_ref,
+    top_ref, bot_ref, right_ref, left_ref,
 ):
     layers, rows, cols = t_ref.shape
     groups = layers // GROUP
@@ -95,7 +109,7 @@
             swapped, reverse, precision=lax.Precision.HIGHEST,
             preferred_element_type=jnp.float32,
         )
-        fold_ref[...] = flipped.reshape(layers + 1, rows, cols)
+        top_ref[...] = flipped.reshape(layers + 1, rows, cols)
 
 
 def xpart_kernel(
@@ -141,10 +155,12 @@
             xsh = {s: [xs(q[c], ex[c], s) for c in range(4)] for s in (-2, -1, 1, 2)}
             a_r = 0.5 * (q[2] + xsh[1][2]) * w0 * wxp
             a_l = 0.5 * (xsh[-1][2] + q[2]) * wxm * w0
+            w_r = face_weights(a_r)
+            w_l = face_weights(a_l)
             for c in range(4):
-                divx_ref[c * layers + k] = face_flux(
-                    a_r, xsh[-1][c], q[c], xsh[1][c], xsh[2][c]
-                ) - face_flux(a_l, xsh[-2][c], xsh[-1][c], q[c], xsh[1][c])
+                divx_ref[c * layers + k] = q[c] - courant * flux_divergence(
+                    w_r, w_l, xsh[-2][c], xsh[-1][c], q[c], xsh[1][c], xsh[2][c]
+                )
             load_xm = density(xsh[-1][0], xsh[-1][1], zmid) * wxm * h
             load_xp = density(xsh[1][0], xsh[1][1], zmid) * wxp * h
             cum_xm = cum_xm + load_xm
@@ -205,12 +221,12 @@
         ysh = {s: [ys(q[c], ey[c], s) for c in range(4)] for s in (-2, -1, 1, 2)}
         b_r = 0.5 * (q[3] + ysh[1][3]) * w0 * wyp
         b_l = 0.5 * (ysh[-1][3] + q[3]) * wym * w0
+        w_r = face_weights(b_r)
+        w_l = face_weights(b_l)
         adv = []
         for c in range(4):
-            div_y = face_flux(b_r, ysh[-1][c], q[c], ysh[1][c], ysh[2][c]) - face_flux(
-                b_l, ysh[-2][c], ysh[-1][c], q[c], ysh[1][c]
-            )
-            adv.append(q[c] - courant * (divx_ref[c * layers + k] + div_y))
+            div_y = flux_divergence(w_r, w_l, ysh[-2][c], ysh[-1][c], q[c], ysh[1][c], ysh[2][c])
+            adv.append(divx_ref[c * layers + k] - courant * div_y)
         load_ym = density(ysh[-1][0], ysh[-1][1], zmid) * wym * h
         load_yp = density(ysh[1][0], ysh[1][1], zmid) * wyp * h
         cum_ym = cum_ym + load_ym
@@ -324,11 +340,11 @@
     vmem = pl.BlockSpec(memory_space=pltpu.VMEM)
     row_tiles = jax.ShapeDtypeStruct((layers + 1, rows, cols), jnp.float32)
     col_tiles = jax.ShapeDtypeStruct((groups + 1, rows, cols), jnp.float32)
-    top, bot, fold, right, left = pl.pallas_call(
+    top, bot, right, left = pl.pallas_call(
         pack_kernel,
-        out_shape=(row_tiles, row_tiles, row_tiles, col_tiles, col_tiles),
+        out_shape=(row_tiles, row_tiles, col_tiles, col_tiles),
         in_specs=[smem] + [vmem] * 6,
-        out_specs=(vmem,) * 5,
+        out_specs=(vmem,) * 4,
     )(is_last, shoreline_indicator, bottom_layer_index, *fields)
 
     from_south = lax.ppermute(top, "lat", [(i, i + 1) for i in range(n_lat - 1)])
@@ -336,7 +352,7 @@
     from_west = lax.ppermute(right, "lon", [(i, (i + 1) % n_lon) for i in range(n_lon)])
     from_east = lax.ppermute(left, "lon", [((i + 1) % n_lon, i) for i in range(n_lon)])
     last = (n_lat - 1) * n_lon
-    fold, from_west, from_east = lax.optimization_barrier((fold, from_west, from_east))
+    fold, from_west, from_east = lax.optimization_barrier((top, from_west, from_east))
     from_fold = lax.ppermute(
         fold, ("lat", "lon"), [(last + x, last + n_lon - 1 - x) for x in range(n_lon)]
     )

time: 33.1 us -> 33.2 us (level)
  the two profiles are of different devices: /device:TPU:27 before, /device:TPU:0 now
where the time goes in v9:
time: 33.2 us; the launch traced here: 32.9 us
  Pallas kernels  18.5 us (56%)
  starting transfers between devices  9.2 us (28%)
  waiting for transfers between devices  2.98 us (9%)
  local copies, waits for them, and re-layouts  0.85 us (3%)
  between operations  0.71 us (2%)
  other arithmetic  0.65 us (2%)
    pallas_call x1, Pallas kernels, on_device(): pl.pallas_call(xpart_kernel, out_shape=(jax.ShapeDtypeStruct((4 * layers,...  8.22 us
    pallas_call x1, Pallas kernels, on_device(): pl.pallas_call(step_kernel, out_shape=(plane,) * 4, in_specs=[smem] * 5 +...  7.19 us
    ppermute x1, starting transfers between devices, on_device(): lax.ppermute(top, 'lat', [(i, i + 1) for i in range(n_lat - 1)])  4.77 us
    pallas_call x1, Pallas kernels, on_device(): pl.pallas_call(pack_kernel, out_shape=(row_tiles, row_tiles, col_tiles, c...  3.13 us
    ppermute x1, waiting for transfers between devices, on_device(): lax.ppermute(top, 'lat', [(i, i + 1) for i in range(n_lat - 1)])  2.97 us
    ppermute x1, starting transfers between devices, on_device(): lax.ppermute(left, 'lon', [((i + 1) % n_lon, i) for i in range(n_lon)])  2.01 us
    ppermute x1, starting transfers between devices, on_device(): lax.ppermute(bot, 'lat', [(i + 1, i) for i in range(n_lat - 1)])  1.28 us
    unnamed x10, local copies, waits for them, and re-layouts  0.85 us
  transfers between devices with their start and end apart: 5, of which 1 were waited for; matrix products, arithmetic and copies ran while one was open for 2% of the time, Pallas kernels for 25%

profile of v9, /device:TPU:0, one launch (start us, length us, event | category | flops | bytes accessed | tf_op | source)
XLA Modules:
  0.0 32.9 jit_solution(14948502815758410949)
XLA Ops:
  0.6 3.1 %shard_map.138 = (f32[76,8,128]{2,1,0:T(8,128)}, f32[76,8,128]{2,1,0:T(8,128)}, f32[6,8,128]{2,1,0:T(8,128)}, f32[6,8,128]{2,1,0:T(8,128)}) custom-call(s32[1]{0:T(128)} %bitcast.1.last_ref, s32[8,128]{1,0:T(8,128)} %shore_ref.5, s32[8,128]{1,0:T(8,128)} %bottom_ref.5, f32[75,8,128]{2,1,0:T(8,128)} %t_ref.5, f32[75,8,128]{2,1,0:T(8,128)} %s_ref.5, ...), custom_call_target="tpu_custom_call" | custom-call | tf_op jit(solution)/shard_map/pallas_call | solution.py:343
  3.8 0.5 %collective-permute-start.2 = (f32[6,8,128]{2,1,0:T(8,128)}, f32[6,8,128]{2,1,0:T(8,128)S(1)}, u32[]{:S(2)}, u32[]{:S(2)}) collective-permute-start(f32[6,8,128]{2,1,0:T(8,128)} %get-tuple-element.15), channel_id=1, source_target_pairs={{0,1},{1,2},{2,3},{3,0},{4,5},{5,6},{6,7},{7,4},{8,9},{9,10},{10,1... | collective-permute-start | bytes 73736 | tf_op jit(solution)/shard_map/ppermute | solution.py:352
  4.2 2.0 %collective-permute-start.3 = (f32[6,8,128]{2,1,0:T(8,128)}, f32[6,8,128]{2,1,0:T(8,128)S(1)}, u32[]{:S(2)}, u32[]{:S(2)}) collective-permute-start(f32[6,8,128]{2,1,0:T(8,128)} %get-tuple-element.16), channel_id=1, source_target_pairs={{1,0},{2,1},{3,2},{0,3},{5,4},{6,5},{7,6},{4,7},{9,8},{10,9},{11,1... | collective-permute-start | bytes 73736 | tf_op jit(solution)/shard_map/ppermute | solution.py:353
  6.2 1.3 %collective-permute-start.1 = (f32[76,8,128]{2,1,0:T(8,128)}, f32[76,8,128]{2,1,0:T(8,128)S(1)}, u32[]{:S(2)}, u32[]{:S(2)}) collective-permute-start(f32[76,8,128]{2,1,0:T(8,128)} %get-tuple-element.14), channel_id=1, source_target_pairs={{4,0},{8,4},{12,8},{16,12},{20,16},{24,20},{28,24},{5,1},{9,5},{13... | collective-permute-start | bytes 933896 | tf_op jit(solution)/shard_map/ppermute | solution.py:351
  7.5 4.8 %collective-permute-start = (f32[76,8,128]{2,1,0:T(8,128)}, f32[76,8,128]{2,1,0:T(8,128)S(1)}, u32[]{:S(2)}, u32[]{:S(2)}) collective-permute-start(f32[76,8,128]{2,1,0:T(8,128)} %get-tuple-element.17), channel_id=1, source_target_pairs={{0,4},{4,8},{8,12},{12,16},{16,20},{20,24},{24,28},{1,5},{5,9},{9,... | collective-permute-start | bytes 933896 | tf_op jit(solution)/shard_map/ppermute | solution.py:350
  12.3 0.0 collective-permute-done.2.west_ref
  12.3 0.0 copy-start.3
  12.3 0.0 collective-permute-done.3.east_ref
  12.3 0.0 copy-start.4
  12.3 0.7 %collective-permute-start.4 = (f32[76,8,128]{2,1,0:T(8,128)}, f32[76,8,128]{2,1,0:T(8,128)S(1)}, u32[]{:S(2)}, u32[]{:S(2)}) collective-permute-start(f32[76,8,128]{2,1,0:T(8,128)} %get-tuple-element.17), channel_id=1, source_target_pairs={{28,31},{29,30},{30,29},{31,28}} | collective-permute-start | bytes 933896 | tf_op jit(solution)/shard_map/ppermute | solution.py:356
  13.0 0.7 %pad_add_fusion.lat_ref = s32[2]{0:T(128)} fusion(s32[1]{0:T(128)} %constant.16.clone.1, s32[1]{0:T(128)} %bitcast), kind=kLoop, calls=%fused_computation | loop fusion | flops 2 | bytes 16 | tf_op jit(solution)/shard_map/stack | solution.py:337
  13.7 0.0 copy-done.3
  13.7 0.0 copy-done.4
  13.7 8.2 %shard_map.139 = (f32[300,8,128]{2,1,0:T(8,128)}, f32[75,8,128]{2,1,0:T(8,128)}) custom-call(f32[75]{0:T(128)} %constant.18.clone.h_ref, f32[75]{0:T(128)} %constant.20.clone.zmid_ref, s32[8,128]{1,0:T(8,128)} %shore_ref.5, s32[8,128]{1,0:T(8,128)} %bottom_ref.5, f32[75,8,128]{2,1,0:T(8,128)} %t_ref.5, f32[75,8,128]{2,1,0:T(8,128)} %s_ref.5, ...), custom_call_target="tpu_custom_call" | custom-call | tf_op jit(solution)/shard_map/pallas_call | solution.py:362
  21.9 0.0 collective-permute-done.1.north_ref
  21.9 0.0 copy-start
  21.9 3.0 %collective-permute-done.south_ref = f32[76,8,128]{2,1,0:T(8,128)S(1)} collective-permute-done((f32[76,8,128]{2,1,0:T(8,128)}, f32[76,8,128]{2,1,0:T(8,128)S(1)}, u32[]{:S(2)}, u32[]{:S(2)}) %collective-permute-start) | collective-permute-done | bytes 311328 | tf_op jit(solution)/shard_map/ppermute | solution.py:350
  24.9 0.0 copy-start.1
  24.9 0.0 collective-permute-done.4.fold_ref
  24.9 0.0 copy-start.2
  24.9 0.0 copy-done
  24.9 0.7 %copy-done.1 = f32[76,8,128]{2,1,0:T(8,128)} copy-done((f32[76,8,128]{2,1,0:T(8,128)}, f32[76,8,128]{2,1,0:T(8,128)S(1)}, u32[]{:S(2)}) %copy-start.1) | copy-done | bytes 311320
  25.6 0.1 copy-done.2
  25.7 7.2 %shard_map.140 = (f32[75,8,128]{2,1,0:T(8,128)}, f32[75,8,128]{2,1,0:T(8,128)}, f32[75,8,128]{2,1,0:T(8,128)}, f32[75,8,128]{2,1,0:T(8,128)}) custom-call(s32[2]{0:T(128)} %pad_add_fusion.lat_ref, f32[75]{0:T(128)} %constant.18.clone.h_ref, f32[75]{0:T(128)} %constant.19.clone.inv_h_ref, f32[75]{0:T(128)} %constant.20.clone.zmid_ref, ...), custom_call_target="tpu_custom_call" | custom-call | tf_op jit(solution)/shard_map/pallas_call | solution.py:368
Async XLA Ops:
  3.8 8.5 %collective-permute-start.2 = (f32[6,8,128]{2,1,0:T(8,128)}, f32[6,8,128]{2,1,0:T(8,128)S(1)}, u32[]{:S(2)}, u32[]{:S(2)}) collective-permute-start(f32[6,8,128]{2,1,0:T(8,128)} %get-tuple-element.15), channel_id=1, source_target_pairs={{0,1},{1,2},{2,3},{3,0},{4,5},{5,6},{6,7},{7,4},{8,9},{9,10},{10,1... | collective-permute-start | bytes 73736 | tf_op jit(solution)/shard_map/ppermute | solution.py:352
  4.2 8.1 %collective-permute-start.3 = (f32[6,8,128]{2,1,0:T(8,128)}, f32[6,8,128]{2,1,0:T(8,128)S(1)}, u32[]{:S(2)}, u32[]{:S(2)}) collective-permute-start(f32[6,8,128]{2,1,0:T(8,128)} %get-tuple-element.16), channel_id=1, source_target_pairs={{1,0},{2,1},{3,2},{0,3},{5,4},{6,5},{7,6},{4,7},{9,8},{10,9},{11,1... | collective-permute-start | bytes 73736 | tf_op jit(solution)/shard_map/ppermute | solution.py:353
  6.2 15.7 %collective-permute-start.1 = (f32[76,8,128]{2,1,0:T(8,128)}, f32[76,8,128]{2,1,0:T(8,128)S(1)}, u32[]{:S(2)}, u32[]{:S(2)}) collective-permute-start(f32[76,8,128]{2,1,0:T(8,128)} %get-tuple-element.14), channel_id=1, source_target_pairs={{4,0},{8,4},{12,8},{16,12},{20,16},{24,20},{28,24},{5,1},{9,5},{13... | collective-permute-start | bytes 933896 | tf_op jit(solution)/shard_map/ppermute | solution.py:351
  7.5 17.4 %collective-permute-start = (f32[76,8,128]{2,1,0:T(8,128)}, f32[76,8,128]{2,1,0:T(8,128)S(1)}, u32[]{:S(2)}, u32[]{:S(2)}) collective-permute-start(f32[76,8,128]{2,1,0:T(8,128)} %get-tuple-element.17), channel_id=1, source_target_pairs={{0,4},{4,8},{8,12},{12,16},{16,20},{20,24},{24,28},{1,5},{5,9},{9,... | collective-permute-start | bytes 933896 | tf_op jit(solution)/shard_map/ppermute | solution.py:350
  12.3 1.4 %copy-start.3 = (f32[6,8,128]{2,1,0:T(8,128)}, f32[6,8,128]{2,1,0:T(8,128)S(1)}, u32[]{:S(2)}) copy-start(f32[6,8,128]{2,1,0:T(8,128)S(1)} %collective-permute-done.2.west_ref) | copy-start | bytes 73732
  12.3 1.4 %copy-start.4 = (f32[6,8,128]{2,1,0:T(8,128)}, f32[6,8,128]{2,1,0:T(8,128)S(1)}, u32[]{:S(2)}) copy-start(f32[6,8,128]{2,1,0:T(8,128)S(1)} %collective-permute-done.3.east_ref) | copy-start | bytes 73732
  12.3 12.6 %collective-permute-start.4 = (f32[76,8,128]{2,1,0:T(8,128)}, f32[76,8,128]{2,1,0:T(8,128)S(1)}, u32[]{:S(2)}, u32[]{:S(2)}) collective-permute-start(f32[76,8,128]{2,1,0:T(8,128)} %get-tuple-element.17), channel_id=1, source_target_pairs={{28,31},{29,30},{30,29},{31,28}} | collective-permute-start | bytes 933896 | tf_op jit(solution)/shard_map/ppermute | solution.py:356
  21.9 3.0 %copy-start = (f32[76,8,128]{2,1,0:T(8,128)}, f32[76,8,128]{2,1,0:T(8,128)S(1)}, u32[]{:S(2)}) copy-start(f32[76,8,128]{2,1,0:T(8,128)S(1)} %collective-permute-done.1.north_ref) | copy-start | bytes 933892
  24.9 0.7 %copy-start.1 = (f32[76,8,128]{2,1,0:T(8,128)}, f32[76,8,128]{2,1,0:T(8,128)S(1)}, u32[]{:S(2)}) copy-start(f32[76,8,128]{2,1,0:T(8,128)S(1)} %collective-permute-done.south_ref) | copy-start | bytes 933892
  24.9 0.8 %copy-start.2 = (f32[76,8,128]{2,1,0:T(8,128)}, f32[76,8,128]{2,1,0:T(8,128)S(1)}, u32[]{:S(2)}) copy-start(f32[76,8,128]{2,1,0:T(8,128)S(1)} %collective-permute-done.4.fold_ref) | copy-start | bytes 933892

commit v10 on v9

--- a/solution.py
+++ b/solution.py
@@ -113,12 +113,16 @@
 
 
 def xpart_kernel(
-    h_ref, zmid_ref, shore_ref, bottom_ref, t_ref, s_ref, u_ref, v_ref, west_ref, east_ref,
-    divx_ref, gradx_ref,
+    lat_ref, h_ref, zmid_ref, shore_ref, bottom_ref, t_ref, s_ref, u_ref, v_ref,
+    west_ref, east_ref, divx_ref,
 ):
     layers, rows, cols = t_ref.shape
     groups = layers // GROUP
     lane = lax.broadcasted_iota(jnp.int32, (rows, cols), 1)
+    row = lax.broadcasted_iota(jnp.int32, (rows, cols), 0)
+    total_rows = rows * lat_ref[1]
+    row_ids = (lat_ref[0] * rows + row).astype(jnp.float32)
+    turning = coriolis * (2.0 * (row_ids + 0.5) / total_rows.astype(jnp.float32) - 1.0)
 
     def xs(v, e, s):
         if s == 1:
@@ -157,15 +161,21 @@
             a_l = 0.5 * (xsh[-1][2] + q[2]) * wxm * w0
             w_r = face_weights(a_r)
             w_l = face_weights(a_l)
-            for c in range(4):
-                divx_ref[c * layers + k] = q[c] - courant * flux_divergence(
+            part = [
+                q[c] - courant * flux_divergence(
                     w_r, w_l, xsh[-2][c], xsh[-1][c], q[c], xsh[1][c], xsh[2][c]
                 )
+                for c in range(4)
+            ]
             load_xm = density(xsh[-1][0], xsh[-1][1], zmid) * wxm * h
             load_xp = density(xsh[1][0], xsh[1][1], zmid) * wxp * h
             cum_xm = cum_xm + load_xm
             cum_xp = cum_xp + load_xp
-            gradx_ref[k] = 0.5 * ((cum_xp - 0.5 * load_xp) - (cum_xm - 0.5 * load_xm))
+            grad_x = 0.5 * ((cum_xp - 0.5 * load_xp) - (cum_xm - 0.5 * load_xm))
+            part[2] = part[2] + time_step * (turning * q[3] - gravity * grad_x)
+            part[3] = part[3] + time_step * (-turning * q[2])
+            for c in range(4):
+                divx_ref[c * layers + k] = part[c]
             carry = (cum_xm, cum_xp)
         return carry
 
@@ -175,7 +185,7 @@
 def step_kernel(
     lat_ref, h_ref, inv_h_ref, zmid_ref, inv_sp_ref,
     shore_ref, bottom_ref, flux_ref, t_ref, s_ref, u_ref, v_ref,
-    south_ref, north_ref, fold_ref, divx_ref, gradx_ref,
+    south_ref, north_ref, fold_ref, divx_ref,
     o0_ref, o1_ref, o2_ref, o3_ref,
     star_scr, r_scr, rs_scr,
 ):
@@ -201,9 +211,6 @@
     dep_lat = lat_edge(north_ref[layers] + fold_ref[layers], south_ref[layers], 0)
     dep_ym = ys(dep, dep_lat, -1)
     dep_yp = ys(dep, dep_lat, 1)
-    total_rows = rows * lat_ref[1]
-    row_ids = (lat_ref[0] * rows + row).astype(jnp.float32)
-    turning = coriolis * (2.0 * (row_ids + 0.5) / total_rows.astype(jnp.float32) - 1.0)
     zero = jnp.zeros((rows, cols), jnp.float32)
 
     def explicit(k, carry):
@@ -231,12 +238,11 @@
         load_yp = density(ysh[1][0], ysh[1][1], zmid) * wyp * h
         cum_ym = cum_ym + load_ym
         cum_yp = cum_yp + load_yp
-        grad_x = gradx_ref[k]
         grad_y = 0.5 * ((cum_yp - 0.5 * load_yp) - (cum_ym - 0.5 * load_ym))
         star0 = adv[0] * w0
         star1 = adv[1] * w0
-        star2 = (adv[2] + time_step * (turning * q[3] - gravity * grad_x)) * w0
-        star3 = (adv[3] + time_step * (-turning * q[2] - gravity * grad_y)) * w0
+        star2 = adv[2] * w0
+        star3 = (adv[3] - time_step * gravity * grad_y) * w0
         for c, val in enumerate((star0, star1, star2, star3)):
             star_scr[c * layers + k] = val
         rs_scr[k] = density(star0, star1, zmid)
@@ -359,16 +365,17 @@
 
     plane = jax.ShapeDtypeStruct((layers, rows, cols), jnp.float32)
     tables = level_tables(layers)
-    divx, gradx = pl.pallas_call(
+    divx = pl.pallas_call(
         xpart_kernel,
-        out_shape=(jax.ShapeDtypeStruct((4 * layers, rows, cols), jnp.float32), plane),
-        in_specs=[smem] * 2 + [vmem] * 8,
-        out_specs=(vmem,) * 2,
-    )(tables[0], tables[2], shoreline_indicator, bottom_layer_index, *fields, from_west, from_east)
+        out_shape=jax.ShapeDtypeStruct((4 * layers, rows, cols), jnp.float32),
+        in_specs=[smem] * 3 + [vmem] * 8,
+        out_specs=vmem,
+    )(lat_info, tables[0], tables[2], shoreline_indicator, bottom_layer_index, *fields,
+      from_west, from_east)
     outs = pl.pallas_call(
         step_kernel,
         out_shape=(plane,) * 4,
-        in_specs=[smem] * 5 + [vmem] * 12,
+        in_specs=[smem] * 5 + [vmem] * 11,
         out_specs=(vmem,) * 4,
         scratch_shapes=[
             pltpu.VMEM((4 * layers, rows, cols), jnp.float32),
@@ -378,7 +385,7 @@
     )(
         lat_info, *tables,
         shoreline_indicator, bottom_layer_index, boundary_fluxes, *fields,
-        from_south, from_north, from_fold, divx, gradx,
+        from_south, from_north, from_fold, divx,
     )
     return tuple(outs)
 

time: 33.2 us -> 33.6 us (1.012)
  local copies, waits for them, and re-layouts: 0.85 us -> 1.44 us
    unnamed x10, local copies, waits for them, and re-layouts: 0.85 us -> 1.44 us
  transfers between devices with their start and end apart: 5 -> 5, of which waited for: 1 -> 1; matrix products, arithmetic and copies ran while one was open for 2% -> 2% of each run, Pallas kernels for 25% -> 24%
where the time goes in v10:
time: 33.6 us; the launch traced here: 33.4 us
  Pallas kernels  18.3 us (54%)
  starting transfers between devices  9.2 us (27%)
  waiting for transfers between devices  3.15 us (9%)
  local copies, waits for them, and re-layouts  1.44 us (4%)
  between operations  0.7 us (2%)
  other arithmetic  0.62 us (2%)
    pallas_call x1, Pallas kernels, on_device(): pl.pallas_call(xpart_kernel, out_shape=jax.ShapeDtypeStruct((4 * layers,...  8.09 us
    pallas_call x1, Pallas kernels, on_device(): pl.pallas_call(step_kernel, out_shape=(plane,) * 4, in_specs=[smem] * 5 +...  7.05 us
    ppermute x1, starting transfers between devices, on_device(): lax.ppermute(top, 'lat', [(i, i + 1) for i in range(n_lat - 1)])  4.77 us
    pallas_call x1, Pallas kernels, on_device(): pl.pallas_call(pack_kernel, out_shape=(row_tiles, row_tiles, col_tiles, c...  3.14 us
    ppermute x1, waiting for transfers between devices, on_device(): lax.ppermute(top, 'lat', [(i, i + 1) for i in range(n_lat - 1)])  3.14 us
    ppermute x1, starting transfers between devices, on_device(): lax.ppermute(left, 'lon', [((i + 1) % n_lon, i) for i in range(n_lon)])  2.01 us
    unnamed x10, local copies, waits for them, and re-layouts  1.44 us
    ppermute x1, starting transfers between devices, on_device(): lax.ppermute(bot, 'lat', [(i + 1, i) for i in range(n_lat - 1)])  1.28 us
  transfers between devices with their start and end apart: 5, of which 1 were waited for; matrix products, arithmetic and copies ran while one was open for 2% of the time, Pallas kernels for 24%

profile of v10, /device:TPU:0, one launch (start us, length us, event | category | flops | bytes accessed | tf_op | source)
XLA Modules:
  0.0 33.4 jit_solution(6950258743514677710)
XLA Ops:
  0.6 3.1 %shard_map.138 = (f32[76,8,128]{2,1,0:T(8,128)}, f32[76,8,128]{2,1,0:T(8,128)}, f32[6,8,128]{2,1,0:T(8,128)}, f32[6,8,128]{2,1,0:T(8,128)}) custom-call(s32[1]{0:T(128)} %bitcast.1.last_ref, s32[8,128]{1,0:T(8,128)} %shore_ref.5, s32[8,128]{1,0:T(8,128)} %bottom_ref.5, f32[75,8,128]{2,1,0:T(8,128)} %t_ref.5, f32[75,8,128]{2,1,0:T(8,128)} %s_ref.5, ...), custom_call_target="tpu_custom_call" | custom-call | tf_op jit(solution)/shard_map/pallas_call | solution.py:349
  3.8 0.5 %collective-permute-start.2 = (f32[6,8,128]{2,1,0:T(8,128)}, f32[6,8,128]{2,1,0:T(8,128)S(1)}, u32[]{:S(2)}, u32[]{:S(2)}) collective-permute-start(f32[6,8,128]{2,1,0:T(8,128)} %get-tuple-element.13), channel_id=1, source_target_pairs={{0,1},{1,2},{2,3},{3,0},{4,5},{5,6},{6,7},{7,4},{8,9},{9,10},{10,1... | collective-permute-start | bytes 73736 | tf_op jit(solution)/shard_map/ppermute | solution.py:358
  4.2 2.0 %collective-permute-start.3 = (f32[6,8,128]{2,1,0:T(8,128)}, f32[6,8,128]{2,1,0:T(8,128)S(1)}, u32[]{:S(2)}, u32[]{:S(2)}) collective-permute-start(f32[6,8,128]{2,1,0:T(8,128)} %get-tuple-element.14), channel_id=1, source_target_pairs={{1,0},{2,1},{3,2},{0,3},{5,4},{6,5},{7,6},{4,7},{9,8},{10,9},{11,1... | collective-permute-start | bytes 73736 | tf_op jit(solution)/shard_map/ppermute | solution.py:359
  6.2 1.3 %collective-permute-start.1 = (f32[76,8,128]{2,1,0:T(8,128)}, f32[76,8,128]{2,1,0:T(8,128)S(1)}, u32[]{:S(2)}, u32[]{:S(2)}) collective-permute-start(f32[76,8,128]{2,1,0:T(8,128)} %get-tuple-element.12), channel_id=1, source_target_pairs={{4,0},{8,4},{12,8},{16,12},{20,16},{24,20},{28,24},{5,1},{9,5},{13... | collective-permute-start | bytes 933896 | tf_op jit(solution)/shard_map/ppermute | solution.py:357
  7.5 4.8 %collective-permute-start = (f32[76,8,128]{2,1,0:T(8,128)}, f32[76,8,128]{2,1,0:T(8,128)S(1)}, u32[]{:S(2)}, u32[]{:S(2)}) collective-permute-start(f32[76,8,128]{2,1,0:T(8,128)} %get-tuple-element.15), channel_id=1, source_target_pairs={{0,4},{4,8},{8,12},{12,16},{16,20},{20,24},{24,28},{1,5},{5,9},{9,... | collective-permute-start | bytes 933896 | tf_op jit(solution)/shard_map/ppermute | solution.py:356
  12.3 0.0 collective-permute-done.2.west_ref
  12.3 0.0 copy-start.3
  12.3 0.0 collective-permute-done.3.east_ref
  12.3 0.0 copy-start.4
  12.4 0.7 %collective-permute-start.4 = (f32[76,8,128]{2,1,0:T(8,128)}, f32[76,8,128]{2,1,0:T(8,128)S(1)}, u32[]{:S(2)}, u32[]{:S(2)}) collective-permute-start(f32[76,8,128]{2,1,0:T(8,128)} %get-tuple-element.15), channel_id=1, source_target_pairs={{28,31},{29,30},{30,29},{31,28}} | collective-permute-start | bytes 933896 | tf_op jit(solution)/shard_map/ppermute | solution.py:362
  13.0 0.6 %pad_add_fusion.lat_ref = s32[2]{0:T(128)} fusion(s32[1]{0:T(128)} %constant.16.clone.1, s32[1]{0:T(128)} %bitcast), kind=kLoop, calls=%fused_computation | loop fusion | flops 2 | bytes 16 | tf_op jit(solution)/shard_map/stack | solution.py:343
  13.7 0.0 copy-done.3
  13.7 0.0 copy-done.4
  13.7 8.1 %shard_map.139.divx_ref = f32[300,8,128]{2,1,0:T(8,128)} custom-call(s32[2]{0:T(128)} %pad_add_fusion.lat_ref, f32[75]{0:T(128)} %constant.18.clone.h_ref, f32[75]{0:T(128)} %constant.20.clone.zmid_ref, s32[8,128]{1,0:T(8,128)} %shore_ref.5, s32[8,128]{1,0:T(8,128)} %bottom_ref.5, f32[75,8,128]{2,1,0:T(8,128)} %t_ref.5, f32[75,8,128]{2,1,0:T(8,128)} %s_ref.5, ...), custom_call_target="tpu_custom_call" | custom-call | tf_op jit(solution)/shard_map/pallas_call | solution.py:368
  21.8 0.0 collective-permute-done.1.north_ref
  21.8 0.0 copy-start
  21.8 3.1 %collective-permute-done.south_ref = f32[76,8,128]{2,1,0:T(8,128)S(1)} collective-permute-done((f32[76,8,128]{2,1,0:T(8,128)}, f32[76,8,128]{2,1,0:T(8,128)S(1)}, u32[]{:S(2)}, u32[]{:S(2)}) %collective-permute-start) | collective-permute-done | bytes 311328 | tf_op jit(solution)/shard_map/ppermute | solution.py:356
  24.9 0.0 copy-start.1
  24.9 0.0 collective-permute-done.4.fold_ref
  24.9 0.0 copy-done
  24.9 0.7 %copy-done.1 = f32[76,8,128]{2,1,0:T(8,128)} copy-done((f32[76,8,128]{2,1,0:T(8,128)}, f32[76,8,128]{2,1,0:T(8,128)S(1)}, u32[]{:S(2)}) %copy-start.1) | copy-done | bytes 311320
  25.6 0.0 copy-start.2
  25.6 0.7 %copy-done.2 = f32[76,8,128]{2,1,0:T(8,128)} copy-done((f32[76,8,128]{2,1,0:T(8,128)}, f32[76,8,128]{2,1,0:T(8,128)S(1)}, u32[]{:S(2)}) %copy-start.2) | copy-done | bytes 311320
  26.3 7.1 %shard_map.140 = (f32[75,8,128]{2,1,0:T(8,128)}, f32[75,8,128]{2,1,0:T(8,128)}, f32[75,8,128]{2,1,0:T(8,128)}, f32[75,8,128]{2,1,0:T(8,128)}) custom-call(s32[2]{0:T(128)} %pad_add_fusion.lat_ref, f32[75]{0:T(128)} %constant.18.clone.h_ref, f32[75]{0:T(128)} %constant.19.clone.inv_h_ref, f32[75]{0:T(128)} %constant.20.clone.zmid_ref, ...), custom_call_target="tpu_custom_call" | custom-call | tf_op jit(solution)/shard_map/pallas_call | solution.py:375
Async XLA Ops:
  3.8 8.5 %collective-permute-start.2 = (f32[6,8,128]{2,1,0:T(8,128)}, f32[6,8,128]{2,1,0:T(8,128)S(1)}, u32[]{:S(2)}, u32[]{:S(2)}) collective-permute-start(f32[6,8,128]{2,1,0:T(8,128)} %get-tuple-element.13), channel_id=1, source_target_pairs={{0,1},{1,2},{2,3},{3,0},{4,5},{5,6},{6,7},{7,4},{8,9},{9,10},{10,1... | collective-permute-start | bytes 73736 | tf_op jit(solution)/shard_map/ppermute | solution.py:358
  4.2 8.1 %collective-permute-start.3 = (f32[6,8,128]{2,1,0:T(8,128)}, f32[6,8,128]{2,1,0:T(8,128)S(1)}, u32[]{:S(2)}, u32[]{:S(2)}) collective-permute-start(f32[6,8,128]{2,1,0:T(8,128)} %get-tuple-element.14), channel_id=1, source_target_pairs={{1,0},{2,1},{3,2},{0,3},{5,4},{6,5},{7,6},{4,7},{9,8},{10,9},{11,1... | collective-permute-start | bytes 73736 | tf_op jit(solution)/shard_map/ppermute | solution.py:359
  6.2 15.5 %collective-permute-start.1 = (f32[76,8,128]{2,1,0:T(8,128)}, f32[76,8,128]{2,1,0:T(8,128)S(1)}, u32[]{:S(2)}, u32[]{:S(2)}) collective-permute-start(f32[76,8,128]{2,1,0:T(8,128)} %get-tuple-element.12), channel_id=1, source_target_pairs={{4,0},{8,4},{12,8},{16,12},{20,16},{24,20},{28,24},{5,1},{9,5},{13... | collective-permute-start | bytes 933896 | tf_op jit(solution)/shard_map/ppermute | solution.py:357
  7.5 17.4 %collective-permute-start = (f32[76,8,128]{2,1,0:T(8,128)}, f32[76,8,128]{2,1,0:T(8,128)S(1)}, u32[]{:S(2)}, u32[]{:S(2)}) collective-permute-start(f32[76,8,128]{2,1,0:T(8,128)} %get-tuple-element.15), channel_id=1, source_target_pairs={{0,4},{4,8},{8,12},{12,16},{16,20},{20,24},{24,28},{1,5},{5,9},{9,... | collective-permute-start | bytes 933896 | tf_op jit(solution)/shard_map/ppermute | solution.py:356
  12.3 1.3 %copy-start.3 = (f32[6,8,128]{2,1,0:T(8,128)}, f32[6,8,128]{2,1,0:T(8,128)S(1)}, u32[]{:S(2)}) copy-start(f32[6,8,128]{2,1,0:T(8,128)S(1)} %collective-permute-done.2.west_ref) | copy-start | bytes 73732
  12.3 1.3 %copy-start.4 = (f32[6,8,128]{2,1,0:T(8,128)}, f32[6,8,128]{2,1,0:T(8,128)S(1)}, u32[]{:S(2)}) copy-start(f32[6,8,128]{2,1,0:T(8,128)S(1)} %collective-permute-done.3.east_ref) | copy-start | bytes 73732
  12.4 12.6 %collective-permute-start.4 = (f32[76,8,128]{2,1,0:T(8,128)}, f32[76,8,128]{2,1,0:T(8,128)S(1)}, u32[]{:S(2)}, u32[]{:S(2)}) collective-permute-start(f32[76,8,128]{2,1,0:T(8,128)} %get-tuple-element.15), channel_id=1, source_target_pairs={{28,31},{29,30},{30,29},{31,28}} | collective-permute-start | bytes 933896 | tf_op jit(solution)/shard_map/ppermute | solution.py:362
  21.8 3.2 %copy-start = (f32[76,8,128]{2,1,0:T(8,128)}, f32[76,8,128]{2,1,0:T(8,128)S(1)}, u32[]{:S(2)}) copy-start(f32[76,8,128]{2,1,0:T(8,128)S(1)} %collective-permute-done.1.north_ref) | copy-start | bytes 933892
  24.9 0.7 %copy-start.1 = (f32[76,8,128]{2,1,0:T(8,128)}, f32[76,8,128]{2,1,0:T(8,128)S(1)}, u32[]{:S(2)}) copy-start(f32[76,8,128]{2,1,0:T(8,128)S(1)} %collective-permute-done.south_ref) | copy-start | bytes 933892
  25.6 0.7 %copy-start.2 = (f32[76,8,128]{2,1,0:T(8,128)}, f32[76,8,128]{2,1,0:T(8,128)S(1)}, u32[]{:S(2)}) copy-start(f32[76,8,128]{2,1,0:T(8,128)S(1)} %collective-permute-done.4.fold_ref) | copy-start | bytes 933892

commit v11 on v9

--- a/solution.py
+++ b/solution.py
@@ -242,7 +242,7 @@
         rs_scr[k] = density(star0, star1, zmid)
         return (cum_ym, cum_yp)
 
-    lag = 2
+    lag = 3
     carry_e = lax.fori_loop(0, lag, explicit, (zero, zero))
 
     surface_scale = surface_gain * inv_h_ref[0]
@@ -287,7 +287,7 @@
         carry_e, carry_f = carry
         return (explicit(k, carry_e), forward(k - lag, carry_f))
 
-    _, carry_f = lax.fori_loop(lag, layers, fused, (carry_e, (zero,) * 7), unroll=3)
+    _, carry_f = lax.fori_loop(lag, layers, fused, (carry_e, (zero,) * 7), unroll=6)
     lax.fori_loop(layers - lag, layers, forward, carry_f)
 
     def backward(i, carry):

time: 33.2 us -> 32.8 us (0.988)
  Pallas kernels: 18.5 us -> 18.1 us
    pallas_call x1, Pallas kernels: 7.19 us -> 6.79 us  [on_device(): pl.pallas_call(step_kernel, out_shape=(plane,) * 4, in_specs=[smem] * 5 +...]
where the time goes in v11:
time: 32.8 us; the launch traced here: 32.5 us
  Pallas kernels  18.1 us (55%)
  starting transfers between devices  9.2 us (28%)
  waiting for transfers between devices  2.98 us (9%)
  local copies, waits for them, and re-layouts  0.85 us (3%)
  between operations  0.71 us (2%)
  other arithmetic  0.65 us (2%)
    pallas_call x1, Pallas kernels, on_device(): pl.pallas_call(xpart_kernel, out_shape=(jax.ShapeDtypeStruct((4 * layers,...  8.22 us
    pallas_call x1, Pallas kernels, on_device(): pl.pallas_call(step_kernel, out_shape=(plane,) * 4, in_specs=[smem] * 5 +...  6.79 us
    ppermute x1, starting transfers between devices, on_device(): lax.ppermute(top, 'lat', [(i, i + 1) for i in range(n_lat - 1)])  4.77 us
    pallas_call x1, Pallas kernels, on_device(): pl.pallas_call(pack_kernel, out_shape=(row_tiles, row_tiles, col_tiles, c...  3.13 us
    ppermute x1, waiting for transfers between devices, on_device(): lax.ppermute(top, 'lat', [(i, i + 1) for i in range(n_lat - 1)])  2.97 us
    ppermute x1, starting transfers between devices, on_device(): lax.ppermute(left, 'lon', [((i + 1) % n_lon, i) for i in range(n_lon)])  2.01 us
    ppermute x1, starting transfers between devices, on_device(): lax.ppermute(bot, 'lat', [(i + 1, i) for i in range(n_lat - 1)])  1.28 us
    unnamed x10, local copies, waits for them, and re-layouts  0.85 us
  transfers between devices with their start and end apart: 5, of which 1 were waited for; matrix products, arithmetic and copies ran while one was open for 2% of the time, Pallas kernels for 25%

profile of v11, /device:TPU:0, one launch (start us, length us, event | category | flops | bytes accessed | tf_op | source)
XLA Modules:
  0.0 32.5 jit_solution(1099303351155903362)
XLA Ops:
  0.6 3.1 %shard_map.138 = (f32[76,8,128]{2,1,0:T(8,128)}, f32[76,8,128]{2,1,0:T(8,128)}, f32[6,8,128]{2,1,0:T(8,128)}, f32[6,8,128]{2,1,0:T(8,128)}) custom-call(s32[1]{0:T(128)} %bitcast.1.last_ref, s32[8,128]{1,0:T(8,128)} %shore_ref.5, s32[8,128]{1,0:T(8,128)} %bottom_ref.5, f32[75,8,128]{2,1,0:T(8,128)} %t_ref.5, f32[75,8,128]{2,1,0:T(8,128)} %s_ref.5, ...), custom_call_target="tpu_custom_call" | custom-call | tf_op jit(solution)/shard_map/pallas_call | solution.py:343
  3.8 0.5 %collective-permute-start.2 = (f32[6,8,128]{2,1,0:T(8,128)}, f32[6,8,128]{2,1,0:T(8,128)S(1)}, u32[]{:S(2)}, u32[]{:S(2)}) collective-permute-start(f32[6,8,128]{2,1,0:T(8,128)} %get-tuple-element.15), channel_id=1, source_target_pairs={{0,1},{1,2},{2,3},{3,0},{4,5},{5,6},{6,7},{7,4},{8,9},{9,10},{10,1... | collective-permute-start | bytes 73736 | tf_op jit(solution)/shard_map/ppermute | solution.py:352
  4.2 2.0 %collective-permute-start.3 = (f32[6,8,128]{2,1,0:T(8,128)}, f32[6,8,128]{2,1,0:T(8,128)S(1)}, u32[]{:S(2)}, u32[]{:S(2)}) collective-permute-start(f32[6,8,128]{2,1,0:T(8,128)} %get-tuple-element.16), channel_id=1, source_target_pairs={{1,0},{2,1},{3,2},{0,3},{5,4},{6,5},{7,6},{4,7},{9,8},{10,9},{11,1... | collective-permute-start | bytes 73736 | tf_op jit(solution)/shard_map/ppermute | solution.py:353
  6.2 1.3 %collective-permute-start.1 = (f32[76,8,128]{2,1,0:T(8,128)}, f32[76,8,128]{2,1,0:T(8,128)S(1)}, u32[]{:S(2)}, u32[]{:S(2)}) collective-permute-start(f32[76,8,128]{2,1,0:T(8,128)} %get-tuple-element.14), channel_id=1, source_target_pairs={{4,0},{8,4},{12,8},{16,12},{20,16},{24,20},{28,24},{5,1},{9,5},{13... | collective-permute-start | bytes 933896 | tf_op jit(solution)/shard_map/ppermute | solution.py:351
  7.5 4.8 %collective-permute-start = (f32[76,8,128]{2,1,0:T(8,128)}, f32[76,8,128]{2,1,0:T(8,128)S(1)}, u32[]{:S(2)}, u32[]{:S(2)}) collective-permute-start(f32[76,8,128]{2,1,0:T(8,128)} %get-tuple-element.17), channel_id=1, source_target_pairs={{0,4},{4,8},{8,12},{12,16},{16,20},{20,24},{24,28},{1,5},{5,9},{9,... | collective-permute-start | bytes 933896 | tf_op jit(solution)/shard_map/ppermute | solution.py:350
  12.3 0.0 collective-permute-done.2.west_ref
  12.3 0.0 copy-start.3
  12.3 0.0 collective-permute-done.3.east_ref
  12.3 0.0 copy-start.4
  12.3 0.7 %collective-permute-start.4 = (f32[76,8,128]{2,1,0:T(8,128)}, f32[76,8,128]{2,1,0:T(8,128)S(1)}, u32[]{:S(2)}, u32[]{:S(2)}) collective-permute-start(f32[76,8,128]{2,1,0:T(8,128)} %get-tuple-element.17), channel_id=1, source_target_pairs={{28,31},{29,30},{30,29},{31,28}} | collective-permute-start | bytes 933896 | tf_op jit(solution)/shard_map/ppermute | solution.py:356
  13.0 0.7 %pad_add_fusion.lat_ref = s32[2]{0:T(128)} fusion(s32[1]{0:T(128)} %constant.16.clone.1, s32[1]{0:T(128)} %bitcast), kind=kLoop, calls=%fused_computation | loop fusion | flops 2 | bytes 16 | tf_op jit(solution)/shard_map/stack | solution.py:337
  13.7 0.0 copy-done.3
  13.7 0.0 copy-done.4
  13.7 8.2 %shard_map.139 = (f32[300,8,128]{2,1,0:T(8,128)}, f32[75,8,128]{2,1,0:T(8,128)}) custom-call(f32[75]{0:T(128)} %constant.18.clone.h_ref, f32[75]{0:T(128)} %constant.20.clone.zmid_ref, s32[8,128]{1,0:T(8,128)} %shore_ref.5, s32[8,128]{1,0:T(8,128)} %bottom_ref.5, f32[75,8,128]{2,1,0:T(8,128)} %t_ref.5, f32[75,8,128]{2,1,0:T(8,128)} %s_ref.5, ...), custom_call_target="tpu_custom_call" | custom-call | tf_op jit(solution)/shard_map/pallas_call | solution.py:362
  21.9 0.0 collective-permute-done.1.north_ref
  21.9 0.0 copy-start
  21.9 3.0 %collective-permute-done.south_ref = f32[76,8,128]{2,1,0:T(8,128)S(1)} collective-permute-done((f32[76,8,128]{2,1,0:T(8,128)}, f32[76,8,128]{2,1,0:T(8,128)S(1)}, u32[]{:S(2)}, u32[]{:S(2)}) %collective-permute-start) | collective-permute-done | bytes 311328 | tf_op jit(solution)/shard_map/ppermute | solution.py:350
  24.9 0.0 copy-start.1
  24.9 0.0 collective-permute-done.4.fold_ref
  24.9 0.0 copy-start.2
  24.9 0.0 copy-done
  24.9 0.7 %copy-done.1 = f32[76,8,128]{2,1,0:T(8,128)} copy-done((f32[76,8,128]{2,1,0:T(8,128)}, f32[76,8,128]{2,1,0:T(8,128)S(1)}, u32[]{:S(2)}) %copy-start.1) | copy-done | bytes 311320
  25.6 0.1 copy-done.2
  25.7 6.8 %shard_map.140 = (f32[75,8,128]{2,1,0:T(8,128)}, f32[75,8,128]{2,1,0:T(8,128)}, f32[75,8,128]{2,1,0:T(8,128)}, f32[75,8,128]{2,1,0:T(8,128)}) custom-call(s32[2]{0:T(128)} %pad_add_fusion.lat_ref, f32[75]{0:T(128)} %constant.18.clone.h_ref, f32[75]{0:T(128)} %constant.19.clone.inv_h_ref, f32[75]{0:T(128)} %constant.20.clone.zmid_ref, ...), custom_call_target="tpu_custom_call" | custom-call | tf_op jit(solution)/shard_map/pallas_call | solution.py:368
Async XLA Ops:
  3.8 8.5 %collective-permute-start.2 = (f32[6,8,128]{2,1,0:T(8,128)}, f32[6,8,128]{2,1,0:T(8,128)S(1)}, u32[]{:S(2)}, u32[]{:S(2)}) collective-permute-start(f32[6,8,128]{2,1,0:T(8,128)} %get-tuple-element.15), channel_id=1, source_target_pairs={{0,1},{1,2},{2,3},{3,0},{4,5},{5,6},{6,7},{7,4},{8,9},{9,10},{10,1... | collective-permute-start | bytes 73736 | tf_op jit(solution)/shard_map/ppermute | solution.py:352
  4.2 8.1 %collective-permute-start.3 = (f32[6,8,128]{2,1,0:T(8,128)}, f32[6,8,128]{2,1,0:T(8,128)S(1)}, u32[]{:S(2)}, u32[]{:S(2)}) collective-permute-start(f32[6,8,128]{2,1,0:T(8,128)} %get-tuple-element.16), channel_id=1, source_target_pairs={{1,0},{2,1},{3,2},{0,3},{5,4},{6,5},{7,6},{4,7},{9,8},{10,9},{11,1... | collective-permute-start | bytes 73736 | tf_op jit(solution)/shard_map/ppermute | solution.py:353
  6.2 15.7 %collective-permute-start.1 = (f32[76,8,128]{2,1,0:T(8,128)}, f32[76,8,128]{2,1,0:T(8,128)S(1)}, u32[]{:S(2)}, u32[]{:S(2)}) collective-permute-start(f32[76,8,128]{2,1,0:T(8,128)} %get-tuple-element.14), channel_id=1, source_target_pairs={{4,0},{8,4},{12,8},{16,12},{20,16},{24,20},{28,24},{5,1},{9,5},{13... | collective-permute-start | bytes 933896 | tf_op jit(solution)/shard_map/ppermute | solution.py:351
  7.5 17.4 %collective-permute-start = (f32[76,8,128]{2,1,0:T(8,128)}, f32[76,8,128]{2,1,0:T(8,128)S(1)}, u32[]{:S(2)}, u32[]{:S(2)}) collective-permute-start(f32[76,8,128]{2,1,0:T(8,128)} %get-tuple-element.17), channel_id=1, source_target_pairs={{0,4},{4,8},{8,12},{12,16},{16,20},{20,24},{24,28},{1,5},{5,9},{9,... | collective-permute-start | bytes 933896 | tf_op jit(solution)/shard_map/ppermute | solution.py:350
  12.3 1.4 %copy-start.3 = (f32[6,8,128]{2,1,0:T(8,128)}, f32[6,8,128]{2,1,0:T(8,128)S(1)}, u32[]{:S(2)}) copy-start(f32[6,8,128]{2,1,0:T(8,128)S(1)} %collective-permute-done.2.west_ref) | copy-start | bytes 73732
  12.3 1.4 %copy-start.4 = (f32[6,8,128]{2,1,0:T(8,128)}, f32[6,8,128]{2,1,0:T(8,128)S(1)}, u32[]{:S(2)}) copy-start(f32[6,8,128]{2,1,0:T(8,128)S(1)} %collective-permute-done.3.east_ref) | copy-start | bytes 73732
  12.3 12.6 %collective-permute-start.4 = (f32[76,8,128]{2,1,0:T(8,128)}, f32[76,8,128]{2,1,0:T(8,128)S(1)}, u32[]{:S(2)}, u32[]{:S(2)}) collective-permute-start(f32[76,8,128]{2,1,0:T(8,128)} %get-tuple-element.17), channel_id=1, source_target_pairs={{28,31},{29,30},{30,29},{31,28}} | collective-permute-start | bytes 933896 | tf_op jit(solution)/shard_map/ppermute | solution.py:356
  21.9 3.0 %copy-start = (f32[76,8,128]{2,1,0:T(8,128)}, f32[76,8,128]{2,1,0:T(8,128)S(1)}, u32[]{:S(2)}) copy-start(f32[76,8,128]{2,1,0:T(8,128)S(1)} %collective-permute-done.1.north_ref) | copy-start | bytes 933892
  24.9 0.7 %copy-start.1 = (f32[76,8,128]{2,1,0:T(8,128)}, f32[76,8,128]{2,1,0:T(8,128)S(1)}, u32[]{:S(2)}) copy-start(f32[76,8,128]{2,1,0:T(8,128)S(1)} %collective-permute-done.south_ref) | copy-start | bytes 933892
  24.9 0.8 %copy-start.2 = (f32[76,8,128]{2,1,0:T(8,128)}, f32[76,8,128]{2,1,0:T(8,128)S(1)}, u32[]{:S(2)}) copy-start(f32[76,8,128]{2,1,0:T(8,128)S(1)} %collective-permute-done.4.fold_ref) | copy-start | bytes 933892

commit v12 on v11

--- a/solution.py
+++ b/solution.py
@@ -54,11 +54,25 @@
 
 
 def pack_kernel(
-    last_ref, shore_ref, bottom_ref, t_ref, s_ref, u_ref, v_ref,
+    last_ref, shore_ref, bottom_ref, t_hbm, s_hbm, u_hbm, v_hbm,
     top_ref, bot_ref, right_ref, left_ref,
+    t_ref, s_ref, u_ref, v_ref, sems,
 ):
     layers, rows, cols = t_ref.shape
     groups = layers // GROUP
+
+    def chunk_copies(g):
+        span = pl.ds(g * GROUP, GROUP)
+        return [
+            pltpu.make_async_copy(src.at[span], dst.at[span], sems.at[g, i])
+            for i, (src, dst) in enumerate(
+                ((t_hbm, t_ref), (s_hbm, s_ref), (u_hbm, u_ref), (v_hbm, v_ref))
+            )
+        ]
+
+    for g in range(groups):
+        for copy in chunk_copies(g):
+            copy.start()
     lane = lax.broadcasted_iota(jnp.int32, (rows, cols), 1)
     row = lax.broadcasted_iota(jnp.int32, (rows, cols), 0)
     dep = (shore_ref[...] * bottom_ref[...]).astype(jnp.float32)
@@ -71,6 +85,8 @@
         return out
 
     def group_body(g, carry):
+        for copy in chunk_copies(g):
+            copy.wait()
         right = zero
         left = zero
         for j in range(GROUP):
@@ -343,8 +359,10 @@
     top, bot, right, left = pl.pallas_call(
         pack_kernel,
         out_shape=(row_tiles, row_tiles, col_tiles, col_tiles),
-        in_specs=[smem] + [vmem] * 6,
+        in_specs=[smem] + [vmem] * 2 + [pl.BlockSpec(memory_space=pl.ANY)] * 4,
         out_specs=(vmem,) * 4,
+        scratch_shapes=[pltpu.VMEM((layers, rows, cols), jnp.float32)] * 4
+        + [pltpu.SemaphoreType.DMA((groups, 4))],
     )(is_last, shoreline_indicator, bottom_layer_index, *fields)
 
     from_south = lax.ppermute(top, "lat", [(i, i + 1) for i in range(n_lat - 1)])

time: 32.8 us -> 33.4 us (1.018)
  Pallas kernels: 18.1 us -> 18.7 us
    pallas_call x1, Pallas kernels: 3.13 us -> 3.68 us  [on_device(): pl.pallas_call(pack_kernel, out_shape=(row_tiles, row_tiles, col_tiles, c...]
where the time goes in v12:
time: 33.4 us; the launch traced here: 33.1 us
  Pallas kernels  18.7 us (56%)
  starting transfers between devices  9.25 us (28%)
  waiting for transfers between devices  2.98 us (9%)
  local copies, waits for them, and re-layouts  0.85 us (3%)
  between operations  0.72 us (2%)
  other arithmetic  0.65 us (2%)
    pallas_call x1, Pallas kernels, on_device(): pl.pallas_call(xpart_kernel, out_shape=(jax.ShapeDtypeStruct((4 * layers,...  8.22 us
    pallas_call x1, Pallas kernels, on_device(): pl.pallas_call(step_kernel, out_shape=(plane,) * 4, in_specs=[smem] * 5 +...  6.79 us
    ppermute x1, starting transfers between devices, on_device(): lax.ppermute(top, 'lat', [(i, i + 1) for i in range(n_lat - 1)])  4.76 us
    pallas_call x1, Pallas kernels, on_device(): pl.pallas_call(pack_kernel, out_shape=(row_tiles, row_tiles, col_tiles, c...  3.68 us
    ppermute x1, waiting for transfers between devices, on_device(): lax.ppermute(top, 'lat', [(i, i + 1) for i in range(n_lat - 1)])  2.97 us
    ppermute x1, starting transfers between devices, on_device(): lax.ppermute(left, 'lon', [((i + 1) % n_lon, i) for i in range(n_lon)])  2.02 us
    ppermute x1, starting transfers between devices, on_device(): lax.ppermute(bot, 'lat', [(i + 1, i) for i in range(n_lat - 1)])  1.28 us
    unnamed x10, local copies, waits for them, and re-layouts  0.85 us
  transfers between devices with their start and end apart: 5, of which 1 were waited for; matrix products, arithmetic and copies ran while one was open for 2% of the time, Pallas kernels for 25%

profile of v12, /device:TPU:0, one launch (start us, length us, event | category | flops | bytes accessed | tf_op | source)
XLA Modules:
  0.0 33.1 jit_solution(16899584615886851894)
XLA Ops:
  0.6 3.7 %shard_map.138 = (f32[76,8,128]{2,1,0:T(8,128)}, f32[76,8,128]{2,1,0:T(8,128)}, f32[6,8,128]{2,1,0:T(8,128)}, f32[6,8,128]{2,1,0:T(8,128)}) custom-call(s32[1]{0:T(128)} %bitcast.1.last_ref, s32[8,128]{1,0:T(8,128)} %shore_ref.5, s32[8,128]{1,0:T(8,128)} %bottom_ref.5, f32[75,8,128]{2,1,0:T(8,128)} %t_ref.3, f32[75,8,128]{2,1,0:T(8,128)} %s_ref.3, ...), custom_call_target="tpu_custom_call" | custom-call | tf_op jit(solution)/shard_map/pallas_call | solution.py:359
  4.3 0.5 %collective-permute-start.2 = (f32[6,8,128]{2,1,0:T(8,128)}, f32[6,8,128]{2,1,0:T(8,128)S(1)}, u32[]{:S(2)}, u32[]{:S(2)}) collective-permute-start(f32[6,8,128]{2,1,0:T(8,128)} %get-tuple-element.15), channel_id=1, source_target_pairs={{0,1},{1,2},{2,3},{3,0},{4,5},{5,6},{6,7},{7,4},{8,9},{9,10},{10,1... | collective-permute-start | bytes 73736 | tf_op jit(solution)/shard_map/ppermute | solution.py:370
  4.8 2.0 %collective-permute-start.3 = (f32[6,8,128]{2,1,0:T(8,128)}, f32[6,8,128]{2,1,0:T(8,128)S(1)}, u32[]{:S(2)}, u32[]{:S(2)}) collective-permute-start(f32[6,8,128]{2,1,0:T(8,128)} %get-tuple-element.16), channel_id=1, source_target_pairs={{1,0},{2,1},{3,2},{0,3},{5,4},{6,5},{7,6},{4,7},{9,8},{10,9},{11,1... | collective-permute-start | bytes 73736 | tf_op jit(solution)/shard_map/ppermute | solution.py:371
  6.8 1.3 %collective-permute-start.1 = (f32[76,8,128]{2,1,0:T(8,128)}, f32[76,8,128]{2,1,0:T(8,128)S(1)}, u32[]{:S(2)}, u32[]{:S(2)}) collective-permute-start(f32[76,8,128]{2,1,0:T(8,128)} %get-tuple-element.14), channel_id=1, source_target_pairs={{4,0},{8,4},{12,8},{16,12},{20,16},{24,20},{28,24},{5,1},{9,5},{13... | collective-permute-start | bytes 933896 | tf_op jit(solution)/shard_map/ppermute | solution.py:369
  8.1 4.8 %collective-permute-start = (f32[76,8,128]{2,1,0:T(8,128)}, f32[76,8,128]{2,1,0:T(8,128)S(1)}, u32[]{:S(2)}, u32[]{:S(2)}) collective-permute-start(f32[76,8,128]{2,1,0:T(8,128)} %get-tuple-element.17), channel_id=1, source_target_pairs={{0,4},{4,8},{8,12},{12,16},{16,20},{20,24},{24,28},{1,5},{5,9},{9,... | collective-permute-start | bytes 933896 | tf_op jit(solution)/shard_map/ppermute | solution.py:368
  12.9 0.0 collective-permute-done.2.west_ref
  12.9 0.0 copy-start.3
  12.9 0.0 collective-permute-done.3.east_ref
  12.9 0.0 copy-start.4
  13.0 0.7 %collective-permute-start.4 = (f32[76,8,128]{2,1,0:T(8,128)}, f32[76,8,128]{2,1,0:T(8,128)S(1)}, u32[]{:S(2)}, u32[]{:S(2)}) collective-permute-start(f32[76,8,128]{2,1,0:T(8,128)} %get-tuple-element.17), channel_id=1, source_target_pairs={{28,31},{29,30},{30,29},{31,28}} | collective-permute-start | bytes 933896 | tf_op jit(solution)/shard_map/ppermute | solution.py:374
  13.6 0.7 %pad_add_fusion.lat_ref = s32[2]{0:T(128)} fusion(s32[1]{0:T(128)} %constant.16.clone.1, s32[1]{0:T(128)} %bitcast), kind=kLoop, calls=%fused_computation | loop fusion | flops 2 | bytes 16 | tf_op jit(solution)/shard_map/stack | solution.py:353
  14.3 0.0 copy-done.3
  14.3 0.0 copy-done.4
  14.3 8.2 %shard_map.139 = (f32[300,8,128]{2,1,0:T(8,128)}, f32[75,8,128]{2,1,0:T(8,128)}) custom-call(f32[75]{0:T(128)} %constant.18.clone.h_ref, f32[75]{0:T(128)} %constant.20.clone.zmid_ref, s32[8,128]{1,0:T(8,128)} %shore_ref.5, s32[8,128]{1,0:T(8,128)} %bottom_ref.5, f32[75,8,128]{2,1,0:T(8,128)} %t_ref.3, f32[75,8,128]{2,1,0:T(8,128)} %s_ref.3, ...), custom_call_target="tpu_custom_call" | custom-call | tf_op jit(solution)/shard_map/pallas_call | solution.py:380
  22.5 0.0 collective-permute-done.1.north_ref
  22.5 0.0 copy-start
  22.5 3.0 %collective-permute-done.south_ref = f32[76,8,128]{2,1,0:T(8,128)S(1)} collective-permute-done((f32[76,8,128]{2,1,0:T(8,128)}, f32[76,8,128]{2,1,0:T(8,128)S(1)}, u32[]{:S(2)}, u32[]{:S(2)}) %collective-permute-start) | collective-permute-done | bytes 311328 | tf_op jit(solution)/shard_map/ppermute | solution.py:368
  25.5 0.0 copy-start.1
  25.5 0.0 collective-permute-done.4.fold_ref
  25.5 0.0 copy-start.2
  25.5 0.0 copy-done
  25.5 0.7 %copy-done.1 = f32[76,8,128]{2,1,0:T(8,128)} copy-done((f32[76,8,128]{2,1,0:T(8,128)}, f32[76,8,128]{2,1,0:T(8,128)S(1)}, u32[]{:S(2)}) %copy-start.1) | copy-done | bytes 311320
  26.2 0.1 copy-done.2
  26.4 6.8 %shard_map.140 = (f32[75,8,128]{2,1,0:T(8,128)}, f32[75,8,128]{2,1,0:T(8,128)}, f32[75,8,128]{2,1,0:T(8,128)}, f32[75,8,128]{2,1,0:T(8,128)}) custom-call(s32[2]{0:T(128)} %pad_add_fusion.lat_ref, f32[75]{0:T(128)} %constant.18.clone.h_ref, f32[75]{0:T(128)} %constant.19.clone.inv_h_ref, f32[75]{0:T(128)} %constant.20.clone.zmid_ref, ...), custom_call_target="tpu_custom_call" | custom-call | tf_op jit(solution)/shard_map/pallas_call | solution.py:386
Async XLA Ops:
  4.3 8.6 %collective-permute-start.2 = (f32[6,8,128]{2,1,0:T(8,128)}, f32[6,8,128]{2,1,0:T(8,128)S(1)}, u32[]{:S(2)}, u32[]{:S(2)}) collective-permute-start(f32[6,8,128]{2,1,0:T(8,128)} %get-tuple-element.15), channel_id=1, source_target_pairs={{0,1},{1,2},{2,3},{3,0},{4,5},{5,6},{6,7},{7,4},{8,9},{9,10},{10,1... | collective-permute-start | bytes 73736 | tf_op jit(solution)/shard_map/ppermute | solution.py:370
  4.8 8.1 %collective-permute-start.3 = (f32[6,8,128]{2,1,0:T(8,128)}, f32[6,8,128]{2,1,0:T(8,128)S(1)}, u32[]{:S(2)}, u32[]{:S(2)}) collective-permute-start(f32[6,8,128]{2,1,0:T(8,128)} %get-tuple-element.16), channel_id=1, source_target_pairs={{1,0},{2,1},{3,2},{0,3},{5,4},{6,5},{7,6},{4,7},{9,8},{10,9},{11,1... | collective-permute-start | bytes 73736 | tf_op jit(solution)/shard_map/ppermute | solution.py:371
  6.8 15.7 %collective-permute-start.1 = (f32[76,8,128]{2,1,0:T(8,128)}, f32[76,8,128]{2,1,0:T(8,128)S(1)}, u32[]{:S(2)}, u32[]{:S(2)}) collective-permute-start(f32[76,8,128]{2,1,0:T(8,128)} %get-tuple-element.14), channel_id=1, source_target_pairs={{4,0},{8,4},{12,8},{16,12},{20,16},{24,20},{28,24},{5,1},{9,5},{13... | collective-permute-start | bytes 933896 | tf_op jit(solution)/shard_map/ppermute | solution.py:369
  8.1 17.4 %collective-permute-start = (f32[76,8,128]{2,1,0:T(8,128)}, f32[76,8,128]{2,1,0:T(8,128)S(1)}, u32[]{:S(2)}, u32[]{:S(2)}) collective-permute-start(f32[76,8,128]{2,1,0:T(8,128)} %get-tuple-element.17), channel_id=1, source_target_pairs={{0,4},{4,8},{8,12},{12,16},{16,20},{20,24},{24,28},{1,5},{5,9},{9,... | collective-permute-start | bytes 933896 | tf_op jit(solution)/shard_map/ppermute | solution.py:368
  12.9 1.4 %copy-start.3 = (f32[6,8,128]{2,1,0:T(8,128)}, f32[6,8,128]{2,1,0:T(8,128)S(1)}, u32[]{:S(2)}) copy-start(f32[6,8,128]{2,1,0:T(8,128)S(1)} %collective-permute-done.2.west_ref) | copy-start | bytes 73732
  12.9 1.4 %copy-start.4 = (f32[6,8,128]{2,1,0:T(8,128)}, f32[6,8,128]{2,1,0:T(8,128)S(1)}, u32[]{:S(2)}) copy-start(f32[6,8,128]{2,1,0:T(8,128)S(1)} %collective-permute-done.3.east_ref) | copy-start | bytes 73732
  13.0 12.6 %collective-permute-start.4 = (f32[76,8,128]{2,1,0:T(8,128)}, f32[76,8,128]{2,1,0:T(8,128)S(1)}, u32[]{:S(2)}, u32[]{:S(2)}) collective-permute-start(f32[76,8,128]{2,1,0:T(8,128)} %get-tuple-element.17), channel_id=1, source_target_pairs={{28,31},{29,30},{30,29},{31,28}} | collective-permute-start | bytes 933896 | tf_op jit(solution)/shard_map/ppermute | solution.py:374
  22.5 3.0 %copy-start = (f32[76,8,128]{2,1,0:T(8,128)}, f32[76,8,128]{2,1,0:T(8,128)S(1)}, u32[]{:S(2)}) copy-start(f32[76,8,128]{2,1,0:T(8,128)S(1)} %collective-permute-done.1.north_ref) | copy-start | bytes 933892
  25.5 0.7 %copy-start.1 = (f32[76,8,128]{2,1,0:T(8,128)}, f32[76,8,128]{2,1,0:T(8,128)S(1)}, u32[]{:S(2)}) copy-start(f32[76,8,128]{2,1,0:T(8,128)S(1)} %collective-permute-done.south_ref) | copy-start | bytes 933892
  25.5 0.8 %copy-start.2 = (f32[76,8,128]{2,1,0:T(8,128)}, f32[76,8,128]{2,1,0:T(8,128)S(1)}, u32[]{:S(2)}) copy-start(f32[76,8,128]{2,1,0:T(8,128)S(1)} %collective-permute-done.4.fold_ref) | copy-start | bytes 933892

commit v13 on v11

--- a/solution.py
+++ b/solution.py
@@ -364,6 +364,7 @@
         out_shape=(jax.ShapeDtypeStruct((4 * layers, rows, cols), jnp.float32), plane),
         in_specs=[smem] * 2 + [vmem] * 8,
         out_specs=(vmem,) * 2,
+        compiler_params=pltpu.CompilerParams(vmem_limit_bytes=16 * 1024 * 1024),
     )(tables[0], tables[2], shoreline_indicator, bottom_layer_index, *fields, from_west, from_east)
     outs = pl.pallas_call(
         step_kernel,
@@ -375,6 +376,7 @@
             pltpu.VMEM((2 * layers, rows, cols), jnp.float32),
             pltpu.VMEM((layers, rows, cols), jnp.float32),
         ],
+        compiler_params=pltpu.CompilerParams(vmem_limit_bytes=16 * 1024 * 1024),
     )(
         lat_info, *tables,
         shoreline_indicator, bottom_layer_index, boundary_fluxes, *fields,

time: 32.8 us -> 30.6 us (0.933)
  Pallas kernels: 18.1 us -> 14.9 us
  waiting for transfers between devices: 2.98 us -> 5.41 us
  local copies, waits for them, and re-layouts: 0.85 us -> 0.06 us
  other arithmetic: 0.65 us -> 0.08 us
    ppermute x1, waiting for transfers between devices: 2.97 us -> 5.4 us  [on_device(): lax.ppermute(top, 'lat', [(i, i + 1) for i in range(n_lat - 1)])]
    pallas_call x1, Pallas kernels: 8.22 us -> 6.33 us  [on_device(): pl.pallas_call(xpart_kernel, out_shape=(jax.ShapeDtypeStruct((4 * layers,...]
    pallas_call x1, Pallas kernels: 6.79 us -> 5.31 us  [on_device(): pl.pallas_call(step_kernel, out_shape=(plane,) * 4, in_specs=[smem] * 5 +...]
    unnamed x10 -> x22, local copies, waits for them, and re-layouts: 0.85 us -> 0.06 us
    another operation x1, other arithmetic: 0.65 us -> 0.08 us  [on_device(): lat_info = jnp.stack([lat_idx, jnp.int32(n_lat)])]
  transfers between devices with their start and end apart: 5 -> 5, of which waited for: 1 -> 1; matrix products, arithmetic and copies ran while one was open for 2% -> 0% of each run, Pallas kernels for 25% -> 21%
where the time goes in v13:
time: 30.6 us; the launch traced here: 30.4 us
  Pallas kernels  14.9 us (49%)
  starting transfers between devices  9.2 us (30%)
  waiting for transfers between devices  5.41 us (18%)
  between operations  0.83 us (3%)
    pallas_call x1, Pallas kernels, on_device(): pl.pallas_call(xpart_kernel, out_shape=(jax.ShapeDtypeStruct((4 * layers,...  6.33 us
    ppermute x1, waiting for transfers between devices, on_device(): lax.ppermute(top, 'lat', [(i, i + 1) for i in range(n_lat - 1)])  5.4 us
    pallas_call x1, Pallas kernels, on_device(): pl.pallas_call(step_kernel, out_shape=(plane,) * 4, in_specs=[smem] * 5 +...  5.31 us
    ppermute x1, starting transfers between devices, on_device(): lax.ppermute(top, 'lat', [(i, i + 1) for i in range(n_lat - 1)])  4.77 us
    pallas_call x1, Pallas kernels, on_device(): pl.pallas_call(pack_kernel, out_shape=(row_tiles, row_tiles, col_tiles, c...  3.21 us
    ppermute x1, starting transfers between devices, on_device(): lax.ppermute(left, 'lon', [((i + 1) % n_lon, i) for i in range(n_lon)])  2.01 us
    ppermute x1, starting transfers between devices, on_device(): lax.ppermute(bot, 'lat', [(i + 1, i) for i in range(n_lat - 1)])  1.28 us
    ppermute x1, starting transfers between devices, on_device(): lax.ppermute(fold, ('lat', 'lon'), [(last + x, last + n_lon - 1 - x) for...  0.68 us
  transfers between devices with their start and end apart: 5, of which 1 were waited for; matrix products, arithmetic and copies ran while one was open for 0% of the time, Pallas kernels for 21%

profile of v13, /device:TPU:0, one launch (start us, length us, event | category | flops | bytes accessed | tf_op | source)
XLA Modules:
  0.0 30.4 jit_solution(317964316192899280)
XLA Ops:
  0.6 0.0 copy-start.7
  0.6 0.0 copy-start.8
  0.7 0.0 copy-start.5
  0.7 0.0 copy-start.4
  0.7 0.0 copy-start.3
  0.7 0.0 copy-start.2
  0.7 0.0 copy-start.1
  0.7 0.0 copy-start
  0.7 0.0 copy-start.9
  0.7 0.0 copy-start.10
  0.8 3.2 %shard_map.138 = (f32[76,8,128]{2,1,0:T(8,128)}, f32[76,8,128]{2,1,0:T(8,128)}, f32[6,8,128]{2,1,0:T(8,128)}, f32[6,8,128]{2,1,0:T(8,128)}) custom-call(s32[1]{0:T(128)} %bitcast.1.last_ref, s32[8,128]{1,0:T(8,128)} %shore_ref.5, s32[8,128]{1,0:T(8,128)} %bottom_ref.5, f32[75,8,128]{2,1,0:T(8,128)} %t_ref.5, f32[75,8,128]{2,1,0:T(8,128)} %s_ref.5, ...), custom_call_target="tpu_custom_call" | custom-call | tf_op jit(solution)/shard_map/pallas_call | solution.py:343
  4.0 0.5 %collective-permute-start.2 = (f32[6,8,128]{2,1,0:T(8,128)}, f32[6,8,128]{2,1,0:T(8,128)S(1)}, u32[]{:S(2)}, u32[]{:S(2)}) collective-permute-start(f32[6,8,128]{2,1,0:T(8,128)} %get-tuple-element.15), channel_id=1, source_target_pairs={{0,1},{1,2},{2,3},{3,0},{4,5},{5,6},{6,7},{7,4},{8,9},{9,10},{10,1... | collective-permute-start | bytes 73736 | tf_op jit(solution)/shard_map/ppermute | solution.py:352
  4.4 2.0 %collective-permute-start.3 = (f32[6,8,128]{2,1,0:T(8,128)}, f32[6,8,128]{2,1,0:T(8,128)S(1)}, u32[]{:S(2)}, u32[]{:S(2)}) collective-permute-start(f32[6,8,128]{2,1,0:T(8,128)} %get-tuple-element.16), channel_id=1, source_target_pairs={{1,0},{2,1},{3,2},{0,3},{5,4},{6,5},{7,6},{4,7},{9,8},{10,9},{11,1... | collective-permute-start | bytes 73736 | tf_op jit(solution)/shard_map/ppermute | solution.py:353
  6.4 1.3 %collective-permute-start.1 = (f32[76,8,128]{2,1,0:T(8,128)}, f32[76,8,128]{2,1,0:T(8,128)S(1)}, u32[]{:S(2)}, u32[]{:S(2)}) collective-permute-start(f32[76,8,128]{2,1,0:T(8,128)} %get-tuple-element.14), channel_id=1, source_target_pairs={{4,0},{8,4},{12,8},{16,12},{20,16},{24,20},{28,24},{5,1},{9,5},{13... | collective-permute-start | bytes 933896 | tf_op jit(solution)/shard_map/ppermute | solution.py:351
  7.7 4.8 %collective-permute-start = (f32[76,8,128]{2,1,0:T(8,128)}, f32[76,8,128]{2,1,0:T(8,128)S(1)}, u32[]{:S(2)}, u32[]{:S(2)}) collective-permute-start(f32[76,8,128]{2,1,0:T(8,128)} %get-tuple-element.17), channel_id=1, source_target_pairs={{0,4},{4,8},{8,12},{12,16},{16,20},{20,24},{24,28},{1,5},{5,9},{9,... | collective-permute-start | bytes 933896 | tf_op jit(solution)/shard_map/ppermute | solution.py:350
  12.5 0.0 collective-permute-done.2.west_ref
  12.5 0.0 collective-permute-done.3.east_ref
  12.5 0.7 %collective-permute-start.4 = (f32[76,8,128]{2,1,0:T(8,128)}, f32[76,8,128]{2,1,0:T(8,128)S(1)}, u32[]{:S(2)}, u32[]{:S(2)}) collective-permute-start(f32[76,8,128]{2,1,0:T(8,128)} %get-tuple-element.17), channel_id=1, source_target_pairs={{28,31},{29,30},{30,29},{31,28}} | collective-permute-start | bytes 933896 | tf_op jit(solution)/shard_map/ppermute | solution.py:356
  13.2 0.1 pad_add_fusion.lat_ref
  13.3 6.3 %shard_map.139 = (f32[300,8,128]{2,1,0:T(8,128)S(1)}, f32[75,8,128]{2,1,0:T(8,128)S(1)}) custom-call(f32[75]{0:T(128)S(1)} %copy-done.8, f32[75]{0:T(128)S(1)} %copy-done.7, s32[8,128]{1,0:T(8,128)S(1)} %copy-done.4, s32[8,128]{1,0:T(8,128)S(1)} %copy-done.5, f32[75,8,128]{2,1,0:T(8,128)S(1)} %copy-done, f32[75,8,128]{2,1,0:T(8,128)S(1)} %copy-done.1, ...), custom_call_target="tpu_custom_call" | custom-call | tf_op jit(solution)/shard_map/pallas_call | solution.py:362
  19.7 0.0 collective-permute-done.1.north_ref
  19.7 5.4 %collective-permute-done.south_ref = f32[76,8,128]{2,1,0:T(8,128)S(1)} collective-permute-done((f32[76,8,128]{2,1,0:T(8,128)}, f32[76,8,128]{2,1,0:T(8,128)S(1)}, u32[]{:S(2)}, u32[]{:S(2)}) %collective-permute-start) | collective-permute-done | bytes 311328 | tf_op jit(solution)/shard_map/ppermute | solution.py:350
  25.1 0.0 collective-permute-done.4.fold_ref
  25.1 5.3 %shard_map.140 = (f32[75,8,128]{2,1,0:T(8,128)}, f32[75,8,128]{2,1,0:T(8,128)}, f32[75,8,128]{2,1,0:T(8,128)}, f32[75,8,128]{2,1,0:T(8,128)}) custom-call(s32[2]{0:T(128)S(1)} %pad_add_fusion.lat_ref, f32[75]{0:T(128)S(1)} %copy-done.8, f32[75]{0:T(128)S(1)} %copy-done.10, f32[75]{0:T(128)S(1)} %copy-done.7, f32[75]{0:T(128)S(1)} %copy-done.9, ...), custom_call_target="tpu_custom_call" | custom-call | tf_op jit(solution)/shard_map/pallas_call | solution.py:369
  (12 shorter events, 0.0 us)
Async XLA Ops:
  0.6 12.7 %copy-start.7 = (f32[75]{0:T(128)S(1)}, f32[75]{0:T(128)}, u32[]{:S(2)}) copy-start(f32[75]{0:T(128)} %constant.20.clone.zmid_ref) | copy-start | bytes 904
  0.6 12.7 %copy-start.8 = (f32[75]{0:T(128)S(1)}, f32[75]{0:T(128)}, u32[]{:S(2)}) copy-start(f32[75]{0:T(128)} %constant.18.clone.h_ref) | copy-start | bytes 904
  0.7 12.6 %copy-start.5 = (s32[8,128]{1,0:T(8,128)S(1)}, s32[8,128]{1,0:T(8,128)}, u32[]{:S(2)}) copy-start(s32[8,128]{1,0:T(8,128)} %bottom_ref.5) | copy-start | bytes 12292
  0.7 12.6 %copy-start.4 = (s32[8,128]{1,0:T(8,128)S(1)}, s32[8,128]{1,0:T(8,128)}, u32[]{:S(2)}) copy-start(s32[8,128]{1,0:T(8,128)} %shore_ref.5) | copy-start | bytes 12292
  0.7 12.6 %copy-start.3 = (f32[75,8,128]{2,1,0:T(8,128)S(1)}, f32[75,8,128]{2,1,0:T(8,128)}, u32[]{:S(2)}) copy-start(f32[75,8,128]{2,1,0:T(8,128)} %v_ref.5) | copy-start | bytes 921604
  0.7 12.6 %copy-start.2 = (f32[75,8,128]{2,1,0:T(8,128)S(1)}, f32[75,8,128]{2,1,0:T(8,128)}, u32[]{:S(2)}) copy-start(f32[75,8,128]{2,1,0:T(8,128)} %u_ref.5) | copy-start | bytes 921604
  0.7 12.6 %copy-start.1 = (f32[75,8,128]{2,1,0:T(8,128)S(1)}, f32[75,8,128]{2,1,0:T(8,128)}, u32[]{:S(2)}) copy-start(f32[75,8,128]{2,1,0:T(8,128)} %s_ref.5) | copy-start | bytes 921604
  0.7 12.6 %copy-start = (f32[75,8,128]{2,1,0:T(8,128)S(1)}, f32[75,8,128]{2,1,0:T(8,128)}, u32[]{:S(2)}) copy-start(f32[75,8,128]{2,1,0:T(8,128)} %t_ref.5) | copy-start | bytes 921604
  0.7 24.4 %copy-start.6 = (f32[4,8,128]{2,1,0:T(8,128)S(1)}, f32[4,8,128]{2,1,0:T(8,128)}, u32[]{:S(2)}) copy-start(f32[4,8,128]{2,1,0:T(8,128)} %flux_ref.1) | copy-start | bytes 49156
  0.7 24.4 %copy-start.9 = (f32[75]{0:T(128)S(1)}, f32[75]{0:T(128)}, u32[]{:S(2)}) copy-start(f32[75]{0:T(128)} %constant.21.clone.inv_sp_ref) | copy-start | bytes 904
  0.7 24.4 %copy-start.10 = (f32[75]{0:T(128)S(1)}, f32[75]{0:T(128)}, u32[]{:S(2)}) copy-start(f32[75]{0:T(128)} %constant.19.clone.inv_h_ref) | copy-start | bytes 904
  4.0 8.5 %collective-permute-start.2 = (f32[6,8,128]{2,1,0:T(8,128)}, f32[6,8,128]{2,1,0:T(8,128)S(1)}, u32[]{:S(2)}, u32[]{:S(2)}) collective-permute-start(f32[6,8,128]{2,1,0:T(8,128)} %get-tuple-element.15), channel_id=1, source_target_pairs={{0,1},{1,2},{2,3},{3,0},{4,5},{5,6},{6,7},{7,4},{8,9},{9,10},{10,1... | collective-permute-start | bytes 73736 | tf_op jit(solution)/shard_map/ppermute | solution.py:352
  4.4 8.1 %collective-permute-start.3 = (f32[6,8,128]{2,1,0:T(8,128)}, f32[6,8,128]{2,1,0:T(8,128)S(1)}, u32[]{:S(2)}, u32[]{:S(2)}) collective-permute-start(f32[6,8,128]{2,1,0:T(8,128)} %get-tuple-element.16), channel_id=1, source_target_pairs={{1,0},{2,1},{3,2},{0,3},{5,4},{6,5},{7,6},{4,7},{9,8},{10,9},{11,1... | collective-permute-start | bytes 73736 | tf_op jit(solution)/shard_map/ppermute | solution.py:353
  6.4 13.3 %collective-permute-start.1 = (f32[76,8,128]{2,1,0:T(8,128)}, f32[76,8,128]{2,1,0:T(8,128)S(1)}, u32[]{:S(2)}, u32[]{:S(2)}) collective-permute-start(f32[76,8,128]{2,1,0:T(8,128)} %get-tuple-element.14), channel_id=1, source_target_pairs={{4,0},{8,4},{12,8},{16,12},{20,16},{24,20},{28,24},{5,1},{9,5},{13... | collective-permute-start | bytes 933896 | tf_op jit(solution)/shard_map/ppermute | solution.py:351
  7.7 17.4 %collective-permute-start = (f32[76,8,128]{2,1,0:T(8,128)}, f32[76,8,128]{2,1,0:T(8,128)S(1)}, u32[]{:S(2)}, u32[]{:S(2)}) collective-permute-start(f32[76,8,128]{2,1,0:T(8,128)} %get-tuple-element.17), channel_id=1, source_target_pairs={{0,4},{4,8},{8,12},{12,16},{16,20},{20,24},{24,28},{1,5},{5,9},{9,... | collective-permute-start | bytes 933896 | tf_op jit(solution)/shard_map/ppermute | solution.py:350
  12.5 12.6 %collective-permute-start.4 = (f32[76,8,128]{2,1,0:T(8,128)}, f32[76,8,128]{2,1,0:T(8,128)S(1)}, u32[]{:S(2)}, u32[]{:S(2)}) collective-permute-start(f32[76,8,128]{2,1,0:T(8,128)} %get-tuple-element.17), channel_id=1, source_target_pairs={{28,31},{29,30},{30,29},{31,28}} | collective-permute-start | bytes 933896 | tf_op jit(solution)/shard_map/ppermute | solution.py:356

commit v14 on v13

--- a/solution.py
+++ b/solution.py
@@ -345,6 +345,7 @@
         out_shape=(row_tiles, row_tiles, col_tiles, col_tiles),
         in_specs=[smem] + [vmem] * 6,
         out_specs=(vmem,) * 4,
+        compiler_params=pltpu.CompilerParams(vmem_limit_bytes=16 * 1024 * 1024),
     )(is_last, shoreline_indicator, bottom_layer_index, *fields)
 
     from_south = lax.ppermute(top, "lat", [(i, i + 1) for i in range(n_lat - 1)])

time: 30.6 us -> 33.5 us (1.095)
  local copies, waits for them, and re-layouts: 0.06 us -> 5.3 us
  Pallas kernels: 14.9 us -> 12.6 us
    unnamed x22 -> x34, local copies, waits for them, and re-layouts: 0.06 us -> 5.3 us
    pallas_call x1, Pallas kernels: 3.21 us -> 1 us  [on_device(): pl.pallas_call(pack_kernel, out_shape=(row_tiles, row_tiles, col_tiles, c...]
  transfers between devices with their start and end apart: 5 -> 5, of which waited for: 1 -> 1; matrix products, arithmetic and copies ran while one was open for 0% -> 0% of each run, Pallas kernels for 21% -> 19%
where the time goes in v14:
time: 33.5 us; the launch traced here: 33.2 us
  Pallas kernels  12.6 us (38%)
  starting transfers between devices  9.25 us (28%)
  local copies, waits for them, and re-layouts  5.3 us (16%)
  waiting for transfers between devices  5.1 us (15%)
  between operations  0.82 us (2%)
    pallas_call x1, Pallas kernels, on_device(): pl.pallas_call(xpart_kernel, out_shape=(jax.ShapeDtypeStruct((4 * layers,...  6.33 us
    pallas_call x1, Pallas kernels, on_device(): pl.pallas_call(step_kernel, out_shape=(plane,) * 4, in_specs=[smem] * 5 +...  5.31 us
    unnamed x34, local copies, waits for them, and re-layouts  5.3 us
    ppermute x1, waiting for transfers between devices, on_device(): lax.ppermute(top, 'lat', [(i, i + 1) for i in range(n_lat - 1)])  5.09 us
    ppermute x1, starting transfers between devices, on_device(): lax.ppermute(top, 'lat', [(i, i + 1) for i in range(n_lat - 1)])  4.76 us
    ppermute x1, starting transfers between devices, on_device(): lax.ppermute(left, 'lon', [((i + 1) % n_lon, i) for i in range(n_lon)])  2.02 us
    ppermute x1, starting transfers between devices, on_device(): lax.ppermute(bot, 'lat', [(i + 1, i) for i in range(n_lat - 1)])  1.28 us
    pallas_call x1, Pallas kernels, on_device(): pl.pallas_call(pack_kernel, out_shape=(row_tiles, row_tiles, col_tiles, c...  1 us
  transfers between devices with their start and end apart: 5, of which 1 were waited for; matrix products, arithmetic and copies ran while one was open for 0% of the time, Pallas kernels for 19%

profile of v14, /device:TPU:0, one launch (start us, length us, event | category | flops | bytes accessed | tf_op | source)
XLA Modules:
  0.0 33.2 jit_solution(15439386830739599703)
XLA Ops:
  0.6 0.0 copy-start.13
  0.6 0.0 copy-start.14
  0.7 1.0 %copy-done = f32[75,8,128]{2,1,0:T(8,128)S(1)} copy-done((f32[75,8,128]{2,1,0:T(8,128)S(1)}, f32[75,8,128]{2,1,0:T(8,128)}, u32[]{:S(2)}) %copy-start) | copy-done | bytes 307224
  1.7 1.0 %copy-done.2 = f32[75,8,128]{2,1,0:T(8,128)S(1)} copy-done((f32[75,8,128]{2,1,0:T(8,128)S(1)}, f32[75,8,128]{2,1,0:T(8,128)}, u32[]{:S(2)}) %copy-start.2) | copy-done | bytes 307224
  2.6 1.0 %copy-done.4 = f32[75,8,128]{2,1,0:T(8,128)S(1)} copy-done((f32[75,8,128]{2,1,0:T(8,128)S(1)}, f32[75,8,128]{2,1,0:T(8,128)}, u32[]{:S(2)}) %copy-start.4) | copy-done | bytes 307224
  3.6 1.0 %copy-done.6 = f32[75,8,128]{2,1,0:T(8,128)S(1)} copy-done((f32[75,8,128]{2,1,0:T(8,128)S(1)}, f32[75,8,128]{2,1,0:T(8,128)}, u32[]{:S(2)}) %copy-start.6) | copy-done | bytes 307224
  4.6 0.7 %copy-done.8 = s32[8,128]{1,0:T(8,128)S(1)} copy-done((s32[8,128]{1,0:T(8,128)S(1)}, s32[8,128]{1,0:T(8,128)}, u32[]{:S(2)}) %copy-start.8) | copy-done | bytes 4120
  5.3 0.7 %copy-done.10 = s32[8,128]{1,0:T(8,128)S(1)} copy-done((s32[8,128]{1,0:T(8,128)S(1)}, s32[8,128]{1,0:T(8,128)}, u32[]{:S(2)}) %copy-start.10) | copy-done | bytes 4120
  6.0 0.0 copy-start.15
  6.0 0.0 copy-start.16
  6.0 1.0 %shard_map.138 = (f32[76,8,128]{2,1,0:T(8,128)S(1)}, f32[76,8,128]{2,1,0:T(8,128)S(1)}, f32[6,8,128]{2,1,0:T(8,128)S(1)}, f32[6,8,128]{2,1,0:T(8,128)S(1)}) custom-call(s32[1]{0:T(128)} %bitcast.1.last_ref, s32[8,128]{1,0:T(8,128)S(1)} %copy-done.8, s32[8,128]{1,0:T(8,128)S(1)} %copy-done.10, f32[75,8,128]{2,1,0:T(8,128)S(1)} %copy-done, ...), custom_call_target="tpu_custom_call" | custom-call | tf_op jit(solution)/shard_map/pallas_call | solution.py:343
  7.0 0.5 %collective-permute-start.2 = (f32[6,8,128]{2,1,0:T(8,128)S(1)}, f32[6,8,128]{2,1,0:T(8,128)S(1)}, u32[]{:S(2)}, u32[]{:S(2)}) collective-permute-start(f32[6,8,128]{2,1,0:T(8,128)S(1)} %get-tuple-element.15), channel_id=1, source_target_pairs={{0,1},{1,2},{2,3},{3,0},{4,5},{5,6},{6,7},{7,4},{8,9},{9,10},{10,1... | collective-permute-start | bytes 73736 | tf_op jit(solution)/shard_map/ppermute | solution.py:353
  7.5 2.0 %collective-permute-start.3 = (f32[6,8,128]{2,1,0:T(8,128)S(1)}, f32[6,8,128]{2,1,0:T(8,128)S(1)}, u32[]{:S(2)}, u32[]{:S(2)}) collective-permute-start(f32[6,8,128]{2,1,0:T(8,128)S(1)} %get-tuple-element.16), channel_id=1, source_target_pairs={{1,0},{2,1},{3,2},{0,3},{5,4},{6,5},{7,6},{4,7},{9,8},{10,9},{11,1... | collective-permute-start | bytes 73736 | tf_op jit(solution)/shard_map/ppermute | solution.py:354
  9.5 1.3 %collective-permute-start.1 = (f32[76,8,128]{2,1,0:T(8,128)S(1)}, f32[76,8,128]{2,1,0:T(8,128)S(1)}, u32[]{:S(2)}, u32[]{:S(2)}) collective-permute-start(f32[76,8,128]{2,1,0:T(8,128)S(1)} %get-tuple-element.14), channel_id=1, source_target_pairs={{4,0},{8,4},{12,8},{16,12},{20,16},{24,20},{28,24},{5,1},{9,5},{13... | collective-permute-start | bytes 933896 | tf_op jit(solution)/shard_map/ppermute | solution.py:352
  10.8 4.8 %collective-permute-start = (f32[76,8,128]{2,1,0:T(8,128)S(1)}, f32[76,8,128]{2,1,0:T(8,128)S(1)}, u32[]{:S(2)}, u32[]{:S(2)}) collective-permute-start(f32[76,8,128]{2,1,0:T(8,128)S(1)} %get-tuple-element.17), channel_id=1, source_target_pairs={{0,4},{4,8},{8,12},{12,16},{16,20},{20,24},{24,28},{1,5},{5,9},{9,... | collective-permute-start | bytes 933896 | tf_op jit(solution)/shard_map/ppermute | solution.py:351
  15.6 0.0 collective-permute-done.2.west_ref
  15.6 0.0 collective-permute-done.3.east_ref
  15.6 0.7 %collective-permute-start.4 = (f32[76,8,128]{2,1,0:T(8,128)S(1)}, f32[76,8,128]{2,1,0:T(8,128)S(1)}, u32[]{:S(2)}, u32[]{:S(2)}) collective-permute-start(f32[76,8,128]{2,1,0:T(8,128)S(1)} %get-tuple-element.17), channel_id=1, source_target_pairs={{28,31},{29,30},{30,29},{31,28}} | collective-permute-start | bytes 933896 | tf_op jit(solution)/shard_map/ppermute | solution.py:357
  16.3 0.1 pad_add_fusion.lat_ref
  16.4 6.3 %shard_map.139 = (f32[300,8,128]{2,1,0:T(8,128)S(1)}, f32[75,8,128]{2,1,0:T(8,128)S(1)}) custom-call(f32[75]{0:T(128)S(1)} %copy-done.14, f32[75]{0:T(128)S(1)} %copy-done.13, s32[8,128]{1,0:T(8,128)S(1)} %copy-done.9, s32[8,128]{1,0:T(8,128)S(1)} %copy-done.11, f32[75,8,128]{2,1,0:T(8,128)S(1)} %copy-done.1, f32[75,8,128]{2,1,0:T(8,128)S(1)} %copy-done.3, ...), custom_call_target="tpu_custom_call" | custom-call | tf_op jit(solution)/shard_map/pallas_call | solution.py:363
  22.8 0.0 collective-permute-done.1.north_ref
  22.8 5.1 %collective-permute-done.south_ref = f32[76,8,128]{2,1,0:T(8,128)S(1)} collective-permute-done((f32[76,8,128]{2,1,0:T(8,128)S(1)}, f32[76,8,128]{2,1,0:T(8,128)S(1)}, u32[]{:S(2)}, u32[]{:S(2)}) %collective-permute-start) | collective-permute-done | bytes 311328 | tf_op jit(solution)/shard_map/ppermute | solution.py:351
  27.9 0.0 collective-permute-done.4.fold_ref
  27.9 5.3 %shard_map.140 = (f32[75,8,128]{2,1,0:T(8,128)}, f32[75,8,128]{2,1,0:T(8,128)}, f32[75,8,128]{2,1,0:T(8,128)}, f32[75,8,128]{2,1,0:T(8,128)}) custom-call(s32[2]{0:T(128)S(1)} %pad_add_fusion.lat_ref, f32[75]{0:T(128)S(1)} %copy-done.14, f32[75]{0:T(128)S(1)} %copy-done.16, f32[75]{0:T(128)S(1)} %copy-done.13, f32[75]{0:T(128)S(1)} %copy-done.15, ...), custom_call_target="tpu_custom_call" | custom-call | tf_op jit(solution)/shard_map/pallas_call | solution.py:370
  (24 shorter events, 0.0 us)
Async XLA Ops:
  0.6 15.7 %copy-start.13 = (f32[75]{0:T(128)S(1)}, f32[75]{0:T(128)}, u32[]{:S(2)}) copy-start(f32[75]{0:T(128)} %constant.20.clone.zmid_ref) | copy-start | bytes 904
  0.6 15.7 %copy-start.14 = (f32[75]{0:T(128)S(1)}, f32[75]{0:T(128)}, u32[]{:S(2)}) copy-start(f32[75]{0:T(128)} %constant.18.clone.h_ref) | copy-start | bytes 904
  0.7 15.7 %copy-start.11 = (s32[8,128]{1,0:T(8,128)S(1)}, s32[8,128]{1,0:T(8,128)}, u32[]{:S(2)}) copy-start(s32[8,128]{1,0:T(8,128)} %bottom_ref.5) | copy-start | bytes 12292
  0.7 15.7 %copy-start.9 = (s32[8,128]{1,0:T(8,128)S(1)}, s32[8,128]{1,0:T(8,128)}, u32[]{:S(2)}) copy-start(s32[8,128]{1,0:T(8,128)} %shore_ref.5) | copy-start | bytes 12292
  0.7 1.0 %copy-start = (f32[75,8,128]{2,1,0:T(8,128)S(1)}, f32[75,8,128]{2,1,0:T(8,128)}, u32[]{:S(2)}) copy-start(f32[75,8,128]{2,1,0:T(8,128)} %t_ref.5) | copy-start | bytes 921604
  1.7 1.0 %copy-start.2 = (f32[75,8,128]{2,1,0:T(8,128)S(1)}, f32[75,8,128]{2,1,0:T(8,128)}, u32[]{:S(2)}) copy-start(f32[75,8,128]{2,1,0:T(8,128)} %s_ref.5) | copy-start | bytes 921604
  2.6 1.0 %copy-start.4 = (f32[75,8,128]{2,1,0:T(8,128)S(1)}, f32[75,8,128]{2,1,0:T(8,128)}, u32[]{:S(2)}) copy-start(f32[75,8,128]{2,1,0:T(8,128)} %u_ref.5) | copy-start | bytes 921604
  3.6 1.0 %copy-start.6 = (f32[75,8,128]{2,1,0:T(8,128)S(1)}, f32[75,8,128]{2,1,0:T(8,128)}, u32[]{:S(2)}) copy-start(f32[75,8,128]{2,1,0:T(8,128)} %v_ref.5) | copy-start | bytes 921604
  4.6 0.7 %copy-start.8 = (s32[8,128]{1,0:T(8,128)S(1)}, s32[8,128]{1,0:T(8,128)}, u32[]{:S(2)}) copy-start(s32[8,128]{1,0:T(8,128)} %shore_ref.5) | copy-start | bytes 12292
  5.3 0.7 %copy-start.10 = (s32[8,128]{1,0:T(8,128)S(1)}, s32[8,128]{1,0:T(8,128)}, u32[]{:S(2)}) copy-start(s32[8,128]{1,0:T(8,128)} %bottom_ref.5) | copy-start | bytes 12292
  5.9 10.4 %copy-start.1 = (f32[75,8,128]{2,1,0:T(8,128)S(1)}, f32[75,8,128]{2,1,0:T(8,128)}, u32[]{:S(2)}) copy-start(f32[75,8,128]{2,1,0:T(8,128)} %t_ref.5) | copy-start | bytes 921604
  5.9 10.4 %copy-start.3 = (f32[75,8,128]{2,1,0:T(8,128)S(1)}, f32[75,8,128]{2,1,0:T(8,128)}, u32[]{:S(2)}) copy-start(f32[75,8,128]{2,1,0:T(8,128)} %s_ref.5) | copy-start | bytes 921604
  5.9 10.5 %copy-start.5 = (f32[75,8,128]{2,1,0:T(8,128)S(1)}, f32[75,8,128]{2,1,0:T(8,128)}, u32[]{:S(2)}) copy-start(f32[75,8,128]{2,1,0:T(8,128)} %u_ref.5) | copy-start | bytes 921604
  5.9 10.5 %copy-start.7 = (f32[75,8,128]{2,1,0:T(8,128)S(1)}, f32[75,8,128]{2,1,0:T(8,128)}, u32[]{:S(2)}) copy-start(f32[75,8,128]{2,1,0:T(8,128)} %v_ref.5) | copy-start | bytes 921604
  6.0 21.9 %copy-start.12 = (f32[4,8,128]{2,1,0:T(8,128)S(1)}, f32[4,8,128]{2,1,0:T(8,128)}, u32[]{:S(2)}) copy-start(f32[4,8,128]{2,1,0:T(8,128)} %flux_ref.1) | copy-start | bytes 49156
  6.0 21.9 %copy-start.15 = (f32[75]{0:T(128)S(1)}, f32[75]{0:T(128)}, u32[]{:S(2)}) copy-start(f32[75]{0:T(128)} %constant.21.clone.inv_sp_ref) | copy-start | bytes 904
  6.0 21.9 %copy-start.16 = (f32[75]{0:T(128)S(1)}, f32[75]{0:T(128)}, u32[]{:S(2)}) copy-start(f32[75]{0:T(128)} %constant.19.clone.inv_h_ref) | copy-start | bytes 904
  7.0 8.6 %collective-permute-start.2 = (f32[6,8,128]{2,1,0:T(8,128)S(1)}, f32[6,8,128]{2,1,0:T(8,128)S(1)}, u32[]{:S(2)}, u32[]{:S(2)}) collective-permute-start(f32[6,8,128]{2,1,0:T(8,128)S(1)} %get-tuple-element.15), channel_id=1, source_target_pairs={{0,1},{1,2},{2,3},{3,0},{4,5},{5,6},{6,7},{7,4},{8,9},{9,10},{10,1... | collective-permute-start | bytes 73736 | tf_op jit(solution)/shard_map/ppermute | solution.py:353
  7.5 8.1 %collective-permute-start.3 = (f32[6,8,128]{2,1,0:T(8,128)S(1)}, f32[6,8,128]{2,1,0:T(8,128)S(1)}, u32[]{:S(2)}, u32[]{:S(2)}) collective-permute-start(f32[6,8,128]{2,1,0:T(8,128)S(1)} %get-tuple-element.16), channel_id=1, source_target_pairs={{1,0},{2,1},{3,2},{0,3},{5,4},{6,5},{7,6},{4,7},{9,8},{10,9},{11,1... | collective-permute-start | bytes 73736 | tf_op jit(solution)/shard_map/ppermute | solution.py:354
  9.5 13.2 %collective-permute-start.1 = (f32[76,8,128]{2,1,0:T(8,128)S(1)}, f32[76,8,128]{2,1,0:T(8,128)S(1)}, u32[]{:S(2)}, u32[]{:S(2)}) collective-permute-start(f32[76,8,128]{2,1,0:T(8,128)S(1)} %get-tuple-element.14), channel_id=1, source_target_pairs={{4,0},{8,4},{12,8},{16,12},{20,16},{24,20},{28,24},{5,1},{9,5},{13... | collective-permute-start | bytes 933896 | tf_op jit(solution)/shard_map/ppermute | solution.py:352
  10.8 17.1 %collective-permute-start = (f32[76,8,128]{2,1,0:T(8,128)S(1)}, f32[76,8,128]{2,1,0:T(8,128)S(1)}, u32[]{:S(2)}, u32[]{:S(2)}) collective-permute-start(f32[76,8,128]{2,1,0:T(8,128)S(1)} %get-tuple-element.17), channel_id=1, source_target_pairs={{0,4},{4,8},{8,12},{12,16},{16,20},{20,24},{24,28},{1,5},{5,9},{9,... | collective-permute-start | bytes 933896 | tf_op jit(solution)/shard_map/ppermute | solution.py:351
  15.6 12.3 %collective-permute-start.4 = (f32[76,8,128]{2,1,0:T(8,128)S(1)}, f32[76,8,128]{2,1,0:T(8,128)S(1)}, u32[]{:S(2)}, u32[]{:S(2)}) collective-permute-start(f32[76,8,128]{2,1,0:T(8,128)S(1)} %get-tuple-element.17), channel_id=1, source_target_pairs={{28,31},{29,30},{30,29},{31,28}} | collective-permute-start | bytes 933896 | tf_op jit(solution)/shard_map/ppermute | solution.py:357

commit v15 on v13

--- a/solution.py
+++ b/solution.py
@@ -57,8 +57,10 @@
     last_ref, shore_ref, bottom_ref, t_ref, s_ref, u_ref, v_ref,
     top_ref, bot_ref, right_ref, left_ref,
 ):
-    layers, rows, cols = t_ref.shape
+    layers = top_ref.shape[0] - 1
+    rows, cols = t_ref.shape[1], t_ref.shape[2]
     groups = layers // GROUP
+    g = pl.program_id(0)
     lane = lax.broadcasted_iota(jnp.int32, (rows, cols), 1)
     row = lax.broadcasted_iota(jnp.int32, (rows, cols), 0)
     dep = (shore_ref[...] * bottom_ref[...]).astype(jnp.float32)
@@ -76,7 +78,7 @@
         for j in range(GROUP):
             k = g * GROUP + j
             w = (k.astype(jnp.float32) < dep).astype(jnp.float32)
-            q = [r[k] * w for r in (t_ref, s_ref, u_ref, v_ref)]
+            q = [r[j] * w for r in (t_ref, s_ref, u_ref, v_ref)]
             top_ref[k] = pack_rows(q, rows - 2)
             bot_ref[k] = pack_rows(q, 0)
             for c in range(4):
@@ -88,13 +90,16 @@
         left_ref[g] = left
         return carry
 
-    lax.fori_loop(0, groups, group_body, 0)
-    top_ref[layers] = pack_rows([dep], rows - 2)
-    bot_ref[layers] = pack_rows([dep], 0)
-    right_ref[groups] = jnp.where(lane < 2, rolled(dep, 2, 1), zero)
-    left_ref[groups] = jnp.where(lane < 2, dep, zero)
-
-    @pl.when(last_ref[0] == 1)
+    group_body(g, 0)
+
+    @pl.when(g == groups - 1)
+    def _():
+        top_ref[layers] = pack_rows([dep], rows - 2)
+        bot_ref[layers] = pack_rows([dep], 0)
+        right_ref[groups] = jnp.where(lane < 2, rolled(dep, 2, 1), zero)
+        left_ref[groups] = jnp.where(lane < 2, dep, zero)
+
+    @pl.when(jnp.logical_and(g == groups - 1, last_ref[0] == 1))
     def _():
         tiles = top_ref[...].reshape((layers + 1) * rows, cols)
         tile_row = lax.broadcasted_iota(jnp.int32, tiles.shape, 0) % rows
@@ -340,11 +345,16 @@
     vmem = pl.BlockSpec(memory_space=pltpu.VMEM)
     row_tiles = jax.ShapeDtypeStruct((layers + 1, rows, cols), jnp.float32)
     col_tiles = jax.ShapeDtypeStruct((groups + 1, rows, cols), jnp.float32)
+    level_block = pl.BlockSpec((GROUP, rows, cols), lambda g: (g, 0, 0))
+    plane_block = pl.BlockSpec((rows, cols), lambda g: (0, 0))
+    row_block = pl.BlockSpec((layers + 1, rows, cols), lambda g: (0, 0, 0))
+    col_block = pl.BlockSpec((groups + 1, rows, cols), lambda g: (0, 0, 0))
     top, bot, right, left = pl.pallas_call(
         pack_kernel,
         out_shape=(row_tiles, row_tiles, col_tiles, col_tiles),
-        in_specs=[smem] + [vmem] * 6,
-        out_specs=(vmem,) * 4,
+        grid=(groups,),
+        in_specs=[smem, plane_block, plane_block] + [level_block] * 4,
+        out_specs=(row_block, row_block, col_block, col_block),
     )(is_last, shoreline_indicator, bottom_layer_index, *fields)
 
     from_south = lax.ppermute(top, "lat", [(i, i + 1) for i in range(n_lat - 1)])

time: 30.6 us -> 31.9 us (1.042)
  Pallas kernels: 14.9 us -> 16 us
    pallas_call x1, Pallas kernels: 3.21 us -> 4.38 us  [on_device(): pl.pallas_call(pack_kernel, out_shape=(row_tiles, row_tiles, col_tiles, c...]
  transfers between devices with their start and end apart: 5 -> 5, of which waited for: 1 -> 1; matrix products, arithmetic and copies ran while one was open for 0% -> 0% of each run, Pallas kernels for 21% -> 20%
where the time goes in v15:
time: 31.9 us; the launch traced here: 31.6 us
  Pallas kernels  16 us (50%)
  starting transfers between devices  9.25 us (29%)
  waiting for transfers between devices  5.41 us (17%)
  between operations  0.83 us (3%)
    pallas_call x1, Pallas kernels, on_device(): pl.pallas_call(xpart_kernel, out_shape=(jax.ShapeDtypeStruct((4 * layers,...  6.33 us
    ppermute x1, waiting for transfers between devices, on_device(): lax.ppermute(top, 'lat', [(i, i + 1) for i in range(n_lat - 1)])  5.4 us
    pallas_call x1, Pallas kernels, on_device(): pl.pallas_call(step_kernel, out_shape=(plane,) * 4, in_specs=[smem] * 5 +...  5.31 us
    ppermute x1, starting transfers between devices, on_device(): lax.ppermute(top, 'lat', [(i, i + 1) for i in range(n_lat - 1)])  4.76 us
    pallas_call x1, Pallas kernels, on_device(): pl.pallas_call(pack_kernel, out_shape=(row_tiles, row_tiles, col_tiles, c...  4.38 us
    ppermute x1, starting transfers between devices, on_device(): lax.ppermute(left, 'lon', [((i + 1) % n_lon, i) for i in range(n_lon)])  2.02 us
    ppermute x1, starting transfers between devices, on_device(): lax.ppermute(bot, 'lat', [(i + 1, i) for i in range(n_lat - 1)])  1.28 us
    ppermute x1, starting transfers between devices, on_device(): lax.ppermute(fold, ('lat', 'lon'), [(last + x, last + n_lon - 1 - x) for...  0.68 us
  transfers between devices with their start and end apart: 5, of which 1 were waited for; matrix products, arithmetic and copies ran while one was open for 0% of the time, Pallas kernels for 20%

profile of v15, /device:TPU:0, one launch (start us, length us, event | category | flops | bytes accessed | tf_op | source)
XLA Modules:
  0.0 31.6 jit_solution(12019086291326061562)
XLA Ops:
  0.6 0.0 copy-start.7
  0.6 0.0 copy-start.8
  0.7 0.0 copy-start.5
  0.7 0.0 copy-start.4
  0.7 0.0 copy-start.3
  0.7 0.0 copy-start.2
  0.7 0.0 copy-start.1
  0.7 0.0 copy-start.9
  0.7 0.0 copy-start.10
  0.8 4.4 %shard_map.138 = (f32[76,8,128]{2,1,0:T(8,128)}, f32[76,8,128]{2,1,0:T(8,128)}, f32[6,8,128]{2,1,0:T(8,128)}, f32[6,8,128]{2,1,0:T(8,128)}) custom-call(s32[1]{0:T(128)} %bitcast.1.last_ref, s32[8,128]{1,0:T(8,128)} %shore_ref.5, s32[8,128]{1,0:T(8,128)} %bottom_ref.5, f32[75,8,128]{2,1,0:T(8,128)} %t_ref.5, f32[75,8,128]{2,1,0:T(8,128)} %s_ref.5, ...), custom_call_target="tpu_custom_call" | custom-call | tf_op jit(solution)/shard_map/pallas_call | solution.py:352
  5.1 0.5 %collective-permute-start.2 = (f32[6,8,128]{2,1,0:T(8,128)}, f32[6,8,128]{2,1,0:T(8,128)S(1)}, u32[]{:S(2)}, u32[]{:S(2)}) collective-permute-start(f32[6,8,128]{2,1,0:T(8,128)} %get-tuple-element.15), channel_id=1, source_target_pairs={{0,1},{1,2},{2,3},{3,0},{4,5},{5,6},{6,7},{7,4},{8,9},{9,10},{10,1... | collective-permute-start | bytes 73736 | tf_op jit(solution)/shard_map/ppermute | solution.py:362
  5.6 2.0 %collective-permute-start.3 = (f32[6,8,128]{2,1,0:T(8,128)}, f32[6,8,128]{2,1,0:T(8,128)S(1)}, u32[]{:S(2)}, u32[]{:S(2)}) collective-permute-start(f32[6,8,128]{2,1,0:T(8,128)} %get-tuple-element.16), channel_id=1, source_target_pairs={{1,0},{2,1},{3,2},{0,3},{5,4},{6,5},{7,6},{4,7},{9,8},{10,9},{11,1... | collective-permute-start | bytes 73736 | tf_op jit(solution)/shard_map/ppermute | solution.py:363
  7.7 1.3 %collective-permute-start.1 = (f32[76,8,128]{2,1,0:T(8,128)}, f32[76,8,128]{2,1,0:T(8,128)S(1)}, u32[]{:S(2)}, u32[]{:S(2)}) collective-permute-start(f32[76,8,128]{2,1,0:T(8,128)} %get-tuple-element.14), channel_id=1, source_target_pairs={{4,0},{8,4},{12,8},{16,12},{20,16},{24,20},{28,24},{5,1},{9,5},{13... | collective-permute-start | bytes 933896 | tf_op jit(solution)/shard_map/ppermute | solution.py:361
  9.0 4.8 %collective-permute-start = (f32[76,8,128]{2,1,0:T(8,128)}, f32[76,8,128]{2,1,0:T(8,128)S(1)}, u32[]{:S(2)}, u32[]{:S(2)}) collective-permute-start(f32[76,8,128]{2,1,0:T(8,128)} %get-tuple-element.17), channel_id=1, source_target_pairs={{0,4},{4,8},{8,12},{12,16},{16,20},{20,24},{24,28},{1,5},{5,9},{9,... | collective-permute-start | bytes 933896 | tf_op jit(solution)/shard_map/ppermute | solution.py:360
  13.7 0.0 collective-permute-done.2.west_ref
  13.7 0.0 collective-permute-done.3.east_ref
  13.7 0.7 %collective-permute-start.4 = (f32[76,8,128]{2,1,0:T(8,128)}, f32[76,8,128]{2,1,0:T(8,128)S(1)}, u32[]{:S(2)}, u32[]{:S(2)}) collective-permute-start(f32[76,8,128]{2,1,0:T(8,128)} %get-tuple-element.17), channel_id=1, source_target_pairs={{28,31},{29,30},{30,29},{31,28}} | collective-permute-start | bytes 933896 | tf_op jit(solution)/shard_map/ppermute | solution.py:366
  14.4 0.1 pad_add_fusion.lat_ref
  14.5 0.0 copy-done.4
  14.6 6.3 %shard_map.139 = (f32[300,8,128]{2,1,0:T(8,128)S(1)}, f32[75,8,128]{2,1,0:T(8,128)S(1)}) custom-call(f32[75]{0:T(128)S(1)} %copy-done.8, f32[75]{0:T(128)S(1)} %copy-done.7, s32[8,128]{1,0:T(8,128)S(1)} %copy-done.4, s32[8,128]{1,0:T(8,128)S(1)} %copy-done.5, f32[75,8,128]{2,1,0:T(8,128)S(1)} %copy-done, f32[75,8,128]{2,1,0:T(8,128)S(1)} %copy-done.1, ...), custom_call_target="tpu_custom_call" | custom-call | tf_op jit(solution)/shard_map/pallas_call | solution.py:372
  20.9 0.0 collective-permute-done.1.north_ref
  20.9 5.4 %collective-permute-done.south_ref = f32[76,8,128]{2,1,0:T(8,128)S(1)} collective-permute-done((f32[76,8,128]{2,1,0:T(8,128)}, f32[76,8,128]{2,1,0:T(8,128)S(1)}, u32[]{:S(2)}, u32[]{:S(2)}) %collective-permute-start) | collective-permute-done | bytes 311328 | tf_op jit(solution)/shard_map/ppermute | solution.py:360
  26.3 0.0 collective-permute-done.4.fold_ref
  26.3 5.3 %shard_map.140 = (f32[75,8,128]{2,1,0:T(8,128)}, f32[75,8,128]{2,1,0:T(8,128)}, f32[75,8,128]{2,1,0:T(8,128)}, f32[75,8,128]{2,1,0:T(8,128)}) custom-call(s32[2]{0:T(128)S(1)} %pad_add_fusion.lat_ref, f32[75]{0:T(128)S(1)} %copy-done.8, f32[75]{0:T(128)S(1)} %copy-done.10, f32[75]{0:T(128)S(1)} %copy-done.7, f32[75]{0:T(128)S(1)} %copy-done.9, ...), custom_call_target="tpu_custom_call" | custom-call | tf_op jit(solution)/shard_map/pallas_call | solution.py:379
  (12 shorter events, 0.0 us)
Async XLA Ops:
  0.6 13.9 %copy-start.7 = (f32[75]{0:T(128)S(1)}, f32[75]{0:T(128)}, u32[]{:S(2)}) copy-start(f32[75]{0:T(128)} %constant.20.clone.zmid_ref) | copy-start | bytes 904
  0.6 13.9 %copy-start.8 = (f32[75]{0:T(128)S(1)}, f32[75]{0:T(128)}, u32[]{:S(2)}) copy-start(f32[75]{0:T(128)} %constant.18.clone.h_ref) | copy-start | bytes 904
  0.7 13.9 %copy-start.5 = (s32[8,128]{1,0:T(8,128)S(1)}, s32[8,128]{1,0:T(8,128)}, u32[]{:S(2)}) copy-start(s32[8,128]{1,0:T(8,128)} %bottom_ref.5) | copy-start | bytes 12292
  0.7 13.9 %copy-start.4 = (s32[8,128]{1,0:T(8,128)S(1)}, s32[8,128]{1,0:T(8,128)}, u32[]{:S(2)}) copy-start(s32[8,128]{1,0:T(8,128)} %shore_ref.5) | copy-start | bytes 12292
  0.7 13.9 %copy-start.3 = (f32[75,8,128]{2,1,0:T(8,128)S(1)}, f32[75,8,128]{2,1,0:T(8,128)}, u32[]{:S(2)}) copy-start(f32[75,8,128]{2,1,0:T(8,128)} %v_ref.5) | copy-start | bytes 921604
  0.7 13.9 %copy-start.2 = (f32[75,8,128]{2,1,0:T(8,128)S(1)}, f32[75,8,128]{2,1,0:T(8,128)}, u32[]{:S(2)}) copy-start(f32[75,8,128]{2,1,0:T(8,128)} %u_ref.5) | copy-start | bytes 921604
  0.7 13.9 %copy-start.1 = (f32[75,8,128]{2,1,0:T(8,128)S(1)}, f32[75,8,128]{2,1,0:T(8,128)}, u32[]{:S(2)}) copy-start(f32[75,8,128]{2,1,0:T(8,128)} %s_ref.5) | copy-start | bytes 921604
  0.7 13.9 %copy-start = (f32[75,8,128]{2,1,0:T(8,128)S(1)}, f32[75,8,128]{2,1,0:T(8,128)}, u32[]{:S(2)}) copy-start(f32[75,8,128]{2,1,0:T(8,128)} %t_ref.5) | copy-start | bytes 921604
  0.7 25.6 %copy-start.6 = (f32[4,8,128]{2,1,0:T(8,128)S(1)}, f32[4,8,128]{2,1,0:T(8,128)}, u32[]{:S(2)}) copy-start(f32[4,8,128]{2,1,0:T(8,128)} %flux_ref.1) | copy-start | bytes 49156
  0.7 25.6 %copy-start.9 = (f32[75]{0:T(128)S(1)}, f32[75]{0:T(128)}, u32[]{:S(2)}) copy-start(f32[75]{0:T(128)} %constant.21.clone.inv_sp_ref) | copy-start | bytes 904
  0.7 25.6 %copy-start.10 = (f32[75]{0:T(128)S(1)}, f32[75]{0:T(128)}, u32[]{:S(2)}) copy-start(f32[75]{0:T(128)} %constant.19.clone.inv_h_ref) | copy-start | bytes 904
  5.1 8.6 %collective-permute-start.2 = (f32[6,8,128]{2,1,0:T(8,128)}, f32[6,8,128]{2,1,0:T(8,128)S(1)}, u32[]{:S(2)}, u32[]{:S(2)}) collective-permute-start(f32[6,8,128]{2,1,0:T(8,128)} %get-tuple-element.15), channel_id=1, source_target_pairs={{0,1},{1,2},{2,3},{3,0},{4,5},{5,6},{6,7},{7,4},{8,9},{9,10},{10,1... | collective-permute-start | bytes 73736 | tf_op jit(solution)/shard_map/ppermute | solution.py:362
  5.6 8.1 %collective-permute-start.3 = (f32[6,8,128]{2,1,0:T(8,128)}, f32[6,8,128]{2,1,0:T(8,128)S(1)}, u32[]{:S(2)}, u32[]{:S(2)}) collective-permute-start(f32[6,8,128]{2,1,0:T(8,128)} %get-tuple-element.16), channel_id=1, source_target_pairs={{1,0},{2,1},{3,2},{0,3},{5,4},{6,5},{7,6},{4,7},{9,8},{10,9},{11,1... | collective-permute-start | bytes 73736 | tf_op jit(solution)/shard_map/ppermute | solution.py:363
  7.7 13.2 %collective-permute-start.1 = (f32[76,8,128]{2,1,0:T(8,128)}, f32[76,8,128]{2,1,0:T(8,128)S(1)}, u32[]{:S(2)}, u32[]{:S(2)}) collective-permute-start(f32[76,8,128]{2,1,0:T(8,128)} %get-tuple-element.14), channel_id=1, source_target_pairs={{4,0},{8,4},{12,8},{16,12},{20,16},{24,20},{28,24},{5,1},{9,5},{13... | collective-permute-start | bytes 933896 | tf_op jit(solution)/shard_map/ppermute | solution.py:361
  9.0 17.4 %collective-permute-start = (f32[76,8,128]{2,1,0:T(8,128)}, f32[76,8,128]{2,1,0:T(8,128)S(1)}, u32[]{:S(2)}, u32[]{:S(2)}) collective-permute-start(f32[76,8,128]{2,1,0:T(8,128)} %get-tuple-element.17), channel_id=1, source_target_pairs={{0,4},{4,8},{8,12},{12,16},{16,20},{20,24},{24,28},{1,5},{5,9},{9,... | collective-permute-start | bytes 933896 | tf_op jit(solution)/shard_map/ppermute | solution.py:360
  13.7 12.6 %collective-permute-start.4 = (f32[76,8,128]{2,1,0:T(8,128)}, f32[76,8,128]{2,1,0:T(8,128)S(1)}, u32[]{:S(2)}, u32[]{:S(2)}) collective-permute-start(f32[76,8,128]{2,1,0:T(8,128)} %get-tuple-element.17), channel_id=1, source_target_pairs={{28,31},{29,30},{30,29},{31,28}} | collective-permute-start | bytes 933896 | tf_op jit(solution)/shard_map/ppermute | solution.py:366

commit v16 on v10

--- a/solution.py
+++ b/solution.py
@@ -248,7 +248,7 @@
         rs_scr[k] = density(star0, star1, zmid)
         return (cum_ym, cum_yp)
 
-    lag = 2
+    lag = 3
     carry_e = lax.fori_loop(0, lag, explicit, (zero, zero))
 
     surface_scale = surface_gain * inv_h_ref[0]
@@ -293,7 +293,7 @@
         carry_e, carry_f = carry
         return (explicit(k, carry_e), forward(k - lag, carry_f))
 
-    _, carry_f = lax.fori_loop(lag, layers, fused, (carry_e, (zero,) * 7), unroll=3)
+    _, carry_f = lax.fori_loop(lag, layers, fused, (carry_e, (zero,) * 7), unroll=9)
     lax.fori_loop(layers - lag, layers, forward, carry_f)
 
     def backward(i, carry):
@@ -370,6 +370,7 @@
         out_shape=jax.ShapeDtypeStruct((4 * layers, rows, cols), jnp.float32),
         in_specs=[smem] * 3 + [vmem] * 8,
         out_specs=vmem,
+        compiler_params=pltpu.CompilerParams(vmem_limit_bytes=16 * 1024 * 1024),
     )(lat_info, tables[0], tables[2], shoreline_indicator, bottom_layer_index, *fields,
       from_west, from_east)
     outs = pl.pallas_call(
@@ -382,6 +383,7 @@
             pltpu.VMEM((2 * layers, rows, cols), jnp.float32),
             pltpu.VMEM((layers, rows, cols), jnp.float32),
         ],
+        compiler_params=pltpu.CompilerParams(vmem_limit_bytes=16 * 1024 * 1024),
     )(
         lat_info, *tables,
         shoreline_indicator, bottom_layer_index, boundary_fluxes, *fields,

time: 33.6 us -> 30.4 us (0.905)
  Pallas kernels: 18.3 us -> 14.6 us
  waiting for transfers between devices: 3.15 us -> 5.4 us
  local copies, waits for them, and re-layouts: 1.44 us -> 0.06 us
  other arithmetic: 0.62 us -> 0.08 us
    ppermute x1, waiting for transfers between devices: 3.14 us -> 5.39 us  [on_device(): lax.ppermute(top, 'lat', [(i, i + 1) for i in range(n_lat - 1)])]
    pallas_call x1, Pallas kernels: 7.05 us -> 5.09 us  [on_device(): pl.pallas_call(step_kernel, out_shape=(plane,) * 4, in_specs=[smem] * 5 +...]
    pallas_call x1, Pallas kernels: 8.09 us -> 6.31 us  [on_device(): pl.pallas_call(xpart_kernel, out_shape=jax.ShapeDtypeStruct((4 * layers,...]
    unnamed x10 -> x22, local copies, waits for them, and re-layouts: 1.44 us -> 0.06 us
    another operation x1, other arithmetic: 0.62 us -> 0.08 us  [on_device(): lat_info = jnp.stack([lat_idx, jnp.int32(n_lat)])]
  transfers between devices with their start and end apart: 5 -> 5, of which waited for: 1 -> 1; matrix products, arithmetic and copies ran while one was open for 2% -> 0% of each run, Pallas kernels for 24% -> 21%
where the time goes in v16:
time: 30.4 us; the launch traced here: 30.2 us
  Pallas kernels  14.6 us (48%)
  starting transfers between devices  9.2 us (30%)
  waiting for transfers between devices  5.4 us (18%)
  between operations  0.83 us (3%)
    pallas_call x1, Pallas kernels, on_device(): pl.pallas_call(xpart_kernel, out_shape=jax.ShapeDtypeStruct((4 * layers,...  6.31 us
    ppermute x1, waiting for transfers between devices, on_device(): lax.ppermute(top, 'lat', [(i, i + 1) for i in range(n_lat - 1)])  5.39 us
    pallas_call x1, Pallas kernels, on_device(): pl.pallas_call(step_kernel, out_shape=(plane,) * 4, in_specs=[smem] * 5 +...  5.09 us
    ppermute x1, starting transfers between devices, on_device(): lax.ppermute(top, 'lat', [(i, i + 1) for i in range(n_lat - 1)])  4.77 us
    pallas_call x1, Pallas kernels, on_device(): pl.pallas_call(pack_kernel, out_shape=(row_tiles, row_tiles, col_tiles, c...  3.22 us
    ppermute x1, starting transfers between devices, on_device(): lax.ppermute(left, 'lon', [((i + 1) % n_lon, i) for i in range(n_lon)])  2.01 us
    ppermute x1, starting transfers between devices, on_device(): lax.ppermute(bot, 'lat', [(i + 1, i) for i in range(n_lat - 1)])  1.28 us
    ppermute x1, starting transfers between devices, on_device(): lax.ppermute(fold, ('lat', 'lon'), [(last + x, last + n_lon - 1 - x) for...  0.68 us
  transfers between devices with their start and end apart: 5, of which 1 were waited for; matrix products, arithmetic and copies ran while one was open for 0% of the time, Pallas kernels for 21%

profile of v16, /device:TPU:0, one launch (start us, length us, event | category | flops | bytes accessed | tf_op | source)
XLA Modules:
  0.0 30.2 jit_solution(8290048852447506821)
XLA Ops:
  0.6 0.0 copy-start.7
  0.6 0.0 copy-start.8
  0.7 0.0 copy-start.5
  0.7 0.0 copy-start.4
  0.7 0.0 copy-start.3
  0.7 3.2 %shard_map.138 = (f32[76,8,128]{2,1,0:T(8,128)}, f32[76,8,128]{2,1,0:T(8,128)}, f32[6,8,128]{2,1,0:T(8,128)}, f32[6,8,128]{2,1,0:T(8,128)}) custom-call(s32[1]{0:T(128)} %bitcast.1.last_ref, s32[8,128]{1,0:T(8,128)} %shore_ref.5, s32[8,128]{1,0:T(8,128)} %bottom_ref.5, f32[75,8,128]{2,1,0:T(8,128)} %t_ref.5, f32[75,8,128]{2,1,0:T(8,128)} %s_ref.5, ...), custom_call_target="tpu_custom_call" | custom-call | tf_op jit(solution)/shard_map/pallas_call | solution.py:349
  3.9 0.5 %collective-permute-start.2 = (f32[6,8,128]{2,1,0:T(8,128)}, f32[6,8,128]{2,1,0:T(8,128)S(1)}, u32[]{:S(2)}, u32[]{:S(2)}) collective-permute-start(f32[6,8,128]{2,1,0:T(8,128)} %get-tuple-element.13), channel_id=1, source_target_pairs={{0,1},{1,2},{2,3},{3,0},{4,5},{5,6},{6,7},{7,4},{8,9},{9,10},{10,1... | collective-permute-start | bytes 73736 | tf_op jit(solution)/shard_map/ppermute | solution.py:358
  4.4 2.0 %collective-permute-start.3 = (f32[6,8,128]{2,1,0:T(8,128)}, f32[6,8,128]{2,1,0:T(8,128)S(1)}, u32[]{:S(2)}, u32[]{:S(2)}) collective-permute-start(f32[6,8,128]{2,1,0:T(8,128)} %get-tuple-element.14), channel_id=1, source_target_pairs={{1,0},{2,1},{3,2},{0,3},{5,4},{6,5},{7,6},{4,7},{9,8},{10,9},{11,1... | collective-permute-start | bytes 73736 | tf_op jit(solution)/shard_map/ppermute | solution.py:359
  6.4 1.3 %collective-permute-start.1 = (f32[76,8,128]{2,1,0:T(8,128)}, f32[76,8,128]{2,1,0:T(8,128)S(1)}, u32[]{:S(2)}, u32[]{:S(2)}) collective-permute-start(f32[76,8,128]{2,1,0:T(8,128)} %get-tuple-element.12), channel_id=1, source_target_pairs={{4,0},{8,4},{12,8},{16,12},{20,16},{24,20},{28,24},{5,1},{9,5},{13... | collective-permute-start | bytes 933896 | tf_op jit(solution)/shard_map/ppermute | solution.py:357
  7.7 4.8 %collective-permute-start = (f32[76,8,128]{2,1,0:T(8,128)}, f32[76,8,128]{2,1,0:T(8,128)S(1)}, u32[]{:S(2)}, u32[]{:S(2)}) collective-permute-start(f32[76,8,128]{2,1,0:T(8,128)} %get-tuple-element.15), channel_id=1, source_target_pairs={{0,4},{4,8},{8,12},{12,16},{16,20},{20,24},{24,28},{1,5},{5,9},{9,... | collective-permute-start | bytes 933896 | tf_op jit(solution)/shard_map/ppermute | solution.py:356
  12.5 0.0 collective-permute-done.2.west_ref
  12.5 0.0 collective-permute-done.3.east_ref
  12.5 0.7 %collective-permute-start.4 = (f32[76,8,128]{2,1,0:T(8,128)}, f32[76,8,128]{2,1,0:T(8,128)S(1)}, u32[]{:S(2)}, u32[]{:S(2)}) collective-permute-start(f32[76,8,128]{2,1,0:T(8,128)} %get-tuple-element.15), channel_id=1, source_target_pairs={{28,31},{29,30},{30,29},{31,28}} | collective-permute-start | bytes 933896 | tf_op jit(solution)/shard_map/ppermute | solution.py:362
  13.2 0.1 pad_add_fusion.lat_ref
  13.3 0.0 copy-done.8
  13.3 0.0 copy-start.6
  13.3 0.0 copy-start.9
  13.3 0.0 copy-start.10
  13.4 6.3 %shard_map.139.divx_ref = f32[300,8,128]{2,1,0:T(8,128)S(1)} custom-call(s32[2]{0:T(128)S(1)} %pad_add_fusion.lat_ref, f32[75]{0:T(128)S(1)} %copy-done.8, f32[75]{0:T(128)S(1)} %copy-done.7, s32[8,128]{1,0:T(8,128)S(1)} %copy-done.4, s32[8,128]{1,0:T(8,128)S(1)} %copy-done.5, f32[75,8,128]{2,1,0:T(8,128)S(1)} %copy-done, f32[75,8,128]{2,1,0:T(8,128)S(1)} %copy-done.1, ...), custom_call_target="tpu_custom_call" | custom-call | tf_op jit(solution)/shard_map/pallas_call | solution.py:368
  19.7 0.0 collective-permute-done.1.north_ref
  19.7 5.4 %collective-permute-done.south_ref = f32[76,8,128]{2,1,0:T(8,128)S(1)} collective-permute-done((f32[76,8,128]{2,1,0:T(8,128)}, f32[76,8,128]{2,1,0:T(8,128)S(1)}, u32[]{:S(2)}, u32[]{:S(2)}) %collective-permute-start) | collective-permute-done | bytes 311328 | tf_op jit(solution)/shard_map/ppermute | solution.py:356
  25.1 0.0 collective-permute-done.4.fold_ref
  25.1 0.0 copy-done.9
  25.1 5.1 %shard_map.140 = (f32[75,8,128]{2,1,0:T(8,128)}, f32[75,8,128]{2,1,0:T(8,128)}, f32[75,8,128]{2,1,0:T(8,128)}, f32[75,8,128]{2,1,0:T(8,128)}) custom-call(s32[2]{0:T(128)S(1)} %pad_add_fusion.lat_ref, f32[75]{0:T(128)S(1)} %copy-done.8, f32[75]{0:T(128)S(1)} %copy-done.10, f32[75]{0:T(128)S(1)} %copy-done.7, f32[75]{0:T(128)S(1)} %copy-done.9, ...), custom_call_target="tpu_custom_call" | custom-call | tf_op jit(solution)/shard_map/pallas_call | solution.py:376
  (12 shorter events, 0.0 us)
Async XLA Ops:
  0.6 12.6 %copy-start.7 = (f32[75]{0:T(128)S(1)}, f32[75]{0:T(128)}, u32[]{:S(2)}) copy-start(f32[75]{0:T(128)} %constant.20.clone.zmid_ref) | copy-start | bytes 904
  0.6 12.6 %copy-start.8 = (f32[75]{0:T(128)S(1)}, f32[75]{0:T(128)}, u32[]{:S(2)}) copy-start(f32[75]{0:T(128)} %constant.18.clone.h_ref) | copy-start | bytes 904
  0.7 12.6 %copy-start.5 = (s32[8,128]{1,0:T(8,128)S(1)}, s32[8,128]{1,0:T(8,128)}, u32[]{:S(2)}) copy-start(s32[8,128]{1,0:T(8,128)} %bottom_ref.5) | copy-start | bytes 12292
  0.7 12.6 %copy-start.4 = (s32[8,128]{1,0:T(8,128)S(1)}, s32[8,128]{1,0:T(8,128)}, u32[]{:S(2)}) copy-start(s32[8,128]{1,0:T(8,128)} %shore_ref.5) | copy-start | bytes 12292
  0.7 12.6 %copy-start.3 = (f32[75,8,128]{2,1,0:T(8,128)S(1)}, f32[75,8,128]{2,1,0:T(8,128)}, u32[]{:S(2)}) copy-start(f32[75,8,128]{2,1,0:T(8,128)} %v_ref.5) | copy-start | bytes 921604
  0.7 12.6 %copy-start.2 = (f32[75,8,128]{2,1,0:T(8,128)S(1)}, f32[75,8,128]{2,1,0:T(8,128)}, u32[]{:S(2)}) copy-start(f32[75,8,128]{2,1,0:T(8,128)} %u_ref.5) | copy-start | bytes 921604
  0.7 12.6 %copy-start.1 = (f32[75,8,128]{2,1,0:T(8,128)S(1)}, f32[75,8,128]{2,1,0:T(8,128)}, u32[]{:S(2)}) copy-start(f32[75,8,128]{2,1,0:T(8,128)} %s_ref.5) | copy-start | bytes 921604
  0.7 12.6 %copy-start = (f32[75,8,128]{2,1,0:T(8,128)S(1)}, f32[75,8,128]{2,1,0:T(8,128)}, u32[]{:S(2)}) copy-start(f32[75,8,128]{2,1,0:T(8,128)} %t_ref.5) | copy-start | bytes 921604
  3.9 8.5 %collective-permute-start.2 = (f32[6,8,128]{2,1,0:T(8,128)}, f32[6,8,128]{2,1,0:T(8,128)S(1)}, u32[]{:S(2)}, u32[]{:S(2)}) collective-permute-start(f32[6,8,128]{2,1,0:T(8,128)} %get-tuple-element.13), channel_id=1, source_target_pairs={{0,1},{1,2},{2,3},{3,0},{4,5},{5,6},{6,7},{7,4},{8,9},{9,10},{10,1... | collective-permute-start | bytes 73736 | tf_op jit(solution)/shard_map/ppermute | solution.py:358
  4.4 8.1 %collective-permute-start.3 = (f32[6,8,128]{2,1,0:T(8,128)}, f32[6,8,128]{2,1,0:T(8,128)S(1)}, u32[]{:S(2)}, u32[]{:S(2)}) collective-permute-start(f32[6,8,128]{2,1,0:T(8,128)} %get-tuple-element.14), channel_id=1, source_target_pairs={{1,0},{2,1},{3,2},{0,3},{5,4},{6,5},{7,6},{4,7},{9,8},{10,9},{11,1... | collective-permute-start | bytes 73736 | tf_op jit(solution)/shard_map/ppermute | solution.py:359
  6.4 13.3 %collective-permute-start.1 = (f32[76,8,128]{2,1,0:T(8,128)}, f32[76,8,128]{2,1,0:T(8,128)S(1)}, u32[]{:S(2)}, u32[]{:S(2)}) collective-permute-start(f32[76,8,128]{2,1,0:T(8,128)} %get-tuple-element.12), channel_id=1, source_target_pairs={{4,0},{8,4},{12,8},{16,12},{20,16},{24,20},{28,24},{5,1},{9,5},{13... | collective-permute-start | bytes 933896 | tf_op jit(solution)/shard_map/ppermute | solution.py:357
  7.7 17.4 %collective-permute-start = (f32[76,8,128]{2,1,0:T(8,128)}, f32[76,8,128]{2,1,0:T(8,128)S(1)}, u32[]{:S(2)}, u32[]{:S(2)}) collective-permute-start(f32[76,8,128]{2,1,0:T(8,128)} %get-tuple-element.15), channel_id=1, source_target_pairs={{0,4},{4,8},{8,12},{12,16},{16,20},{20,24},{24,28},{1,5},{5,9},{9,... | collective-permute-start | bytes 933896 | tf_op jit(solution)/shard_map/ppermute | solution.py:356
  12.5 12.6 %collective-permute-start.4 = (f32[76,8,128]{2,1,0:T(8,128)}, f32[76,8,128]{2,1,0:T(8,128)S(1)}, u32[]{:S(2)}, u32[]{:S(2)}) collective-permute-start(f32[76,8,128]{2,1,0:T(8,128)} %get-tuple-element.15), channel_id=1, source_target_pairs={{28,31},{29,30},{30,29},{31,28}} | collective-permute-start | bytes 933896 | tf_op jit(solution)/shard_map/ppermute | solution.py:362
  13.3 11.8 %copy-start.6 = (f32[4,8,128]{2,1,0:T(8,128)S(1)}, f32[4,8,128]{2,1,0:T(8,128)}, u32[]{:S(2)}) copy-start(f32[4,8,128]{2,1,0:T(8,128)} %flux_ref.1) | copy-start | bytes 49156
  13.3 11.7 %copy-start.9 = (f32[75]{0:T(128)S(1)}, f32[75]{0:T(128)}, u32[]{:S(2)}) copy-start(f32[75]{0:T(128)} %constant.21.clone.inv_sp_ref) | copy-start | bytes 904
  13.3 11.7 %copy-start.10 = (f32[75]{0:T(128)S(1)}, f32[75]{0:T(128)}, u32[]{:S(2)}) copy-start(f32[75]{0:T(128)} %constant.19.clone.inv_h_ref) | copy-start | bytes 904

commit v17 on v16

--- a/solution.py
+++ b/solution.py
@@ -186,8 +186,8 @@
     lat_ref, h_ref, inv_h_ref, zmid_ref, inv_sp_ref,
     shore_ref, bottom_ref, flux_ref, t_ref, s_ref, u_ref, v_ref,
     south_ref, north_ref, fold_ref, divx_ref,
-    o0_ref, o1_ref, o2_ref, o3_ref,
-    star_scr, r_scr, rs_scr,
+    o0_hbm, o1_hbm, o2_hbm, o3_hbm,
+    star_scr, r_scr, rs_scr, o0_ref, o1_ref, o2_ref, o3_ref, out_sems,
 ):
     layers = t_ref.shape[0]
     rows, cols = t_ref.shape[1], t_ref.shape[2]
@@ -311,7 +311,18 @@
         o3_ref[k] = x3
         return (x0, x1, x2, x3)
 
-    lax.fori_loop(0, layers, backward, (zero,) * 4, unroll=3)
+    pairs = ((o0_ref, o0_hbm), (o1_ref, o1_hbm), (o2_ref, o2_hbm), (o3_ref, o3_hbm))
+    writes = []
+    carry = (zero,) * 4
+    for chunk in range(groups):
+        carry = lax.fori_loop(chunk * GROUP, (chunk + 1) * GROUP, backward, carry, unroll=3)
+        span = pl.ds(layers - (chunk + 1) * GROUP, GROUP)
+        for c, (src, dst) in enumerate(pairs):
+            write = pltpu.make_async_copy(src.at[span], dst.at[span], out_sems.at[chunk, c])
+            write.start()
+            writes.append(write)
+    for write in writes:
+        write.wait()
 
 
 def level_tables(layers):
@@ -377,11 +388,13 @@
         step_kernel,
         out_shape=(plane,) * 4,
         in_specs=[smem] * 5 + [vmem] * 11,
-        out_specs=(vmem,) * 4,
+        out_specs=(pl.BlockSpec(memory_space=pl.ANY),) * 4,
         scratch_shapes=[
             pltpu.VMEM((4 * layers, rows, cols), jnp.float32),
             pltpu.VMEM((2 * layers, rows, cols), jnp.float32),
             pltpu.VMEM((layers, rows, cols), jnp.float32),
+        ] + [pltpu.VMEM((layers, rows, cols), jnp.float32)] * 4 + [
+            pltpu.SemaphoreType.DMA((groups, 4)),
         ],
         compiler_params=pltpu.CompilerParams(vmem_limit_bytes=16 * 1024 * 1024),
     )(

time: 30.4 us -> 30.2 us (level)
  no operation moved by 1% of the time
where the time goes in v17:
time: 30.2 us; the launch traced here: 30 us
  Pallas kernels  14.5 us (48%)
  starting transfers between devices  9.2 us (30%)
  waiting for transfers between devices  5.4 us (18%)
  between operations  0.83 us (3%)
    pallas_call x1, Pallas kernels, on_device(): pl.pallas_call(xpart_kernel, out_shape=jax.ShapeDtypeStruct((4 * layers,...  6.31 us
    ppermute x1, waiting for transfers between devices, on_device(): lax.ppermute(top, 'lat', [(i, i + 1) for i in range(n_lat - 1)])  5.39 us
    pallas_call x1, Pallas kernels, on_device(): pl.pallas_call(step_kernel, out_shape=(plane,) * 4, in_specs=[smem] * 5 +...  4.94 us
    ppermute x1, starting transfers between devices, on_device(): lax.ppermute(top, 'lat', [(i, i + 1) for i in range(n_lat - 1)])  4.77 us
    pallas_call x1, Pallas kernels, on_device(): pl.pallas_call(pack_kernel, out_shape=(row_tiles, row_tiles, col_tiles, c...  3.22 us
    ppermute x1, starting transfers between devices, on_device(): lax.ppermute(left, 'lon', [((i + 1) % n_lon, i) for i in range(n_lon)])  2.01 us
    ppermute x1, starting transfers between devices, on_device(): lax.ppermute(bot, 'lat', [(i + 1, i) for i in range(n_lat - 1)])  1.28 us
    ppermute x1, starting transfers between devices, on_device(): lax.ppermute(fold, ('lat', 'lon'), [(last + x, last + n_lon - 1 - x) for...  0.68 us
  transfers between devices with their start and end apart: 5, of which 1 were waited for; matrix products, arithmetic and copies ran while one was open for 0% of the time, Pallas kernels for 21%

profile of v17, /device:TPU:0, one launch (start us, length us, event | category | flops | bytes accessed | tf_op | source)
XLA Modules:
  0.0 30.0 jit_solution(16987725576194382688)
XLA Ops:
  0.6 0.0 copy-start.7
  0.6 0.0 copy-start.8
  0.7 0.0 copy-start.5
  0.7 0.0 copy-start.4
  0.7 0.0 copy-start.3
  0.7 3.2 %shard_map.138 = (f32[76,8,128]{2,1,0:T(8,128)}, f32[76,8,128]{2,1,0:T(8,128)}, f32[6,8,128]{2,1,0:T(8,128)}, f32[6,8,128]{2,1,0:T(8,128)}) custom-call(s32[1]{0:T(128)} %bitcast.1.last_ref, s32[8,128]{1,0:T(8,128)} %shore_ref.5, s32[8,128]{1,0:T(8,128)} %bottom_ref.5, f32[75,8,128]{2,1,0:T(8,128)} %t_ref.5, f32[75,8,128]{2,1,0:T(8,128)} %s_ref.5, ...), custom_call_target="tpu_custom_call" | custom-call | tf_op jit(solution)/shard_map/pallas_call | solution.py:360
  3.9 0.5 %collective-permute-start.2 = (f32[6,8,128]{2,1,0:T(8,128)}, f32[6,8,128]{2,1,0:T(8,128)S(1)}, u32[]{:S(2)}, u32[]{:S(2)}) collective-permute-start(f32[6,8,128]{2,1,0:T(8,128)} %get-tuple-element.13), channel_id=1, source_target_pairs={{0,1},{1,2},{2,3},{3,0},{4,5},{5,6},{6,7},{7,4},{8,9},{9,10},{10,1... | collective-permute-start | bytes 73736 | tf_op jit(solution)/shard_map/ppermute | solution.py:369
  4.4 2.0 %collective-permute-start.3 = (f32[6,8,128]{2,1,0:T(8,128)}, f32[6,8,128]{2,1,0:T(8,128)S(1)}, u32[]{:S(2)}, u32[]{:S(2)}) collective-permute-start(f32[6,8,128]{2,1,0:T(8,128)} %get-tuple-element.14), channel_id=1, source_target_pairs={{1,0},{2,1},{3,2},{0,3},{5,4},{6,5},{7,6},{4,7},{9,8},{10,9},{11,1... | collective-permute-start | bytes 73736 | tf_op jit(solution)/shard_map/ppermute | solution.py:370
  6.4 1.3 %collective-permute-start.1 = (f32[76,8,128]{2,1,0:T(8,128)}, f32[76,8,128]{2,1,0:T(8,128)S(1)}, u32[]{:S(2)}, u32[]{:S(2)}) collective-permute-start(f32[76,8,128]{2,1,0:T(8,128)} %get-tuple-element.12), channel_id=1, source_target_pairs={{4,0},{8,4},{12,8},{16,12},{20,16},{24,20},{28,24},{5,1},{9,5},{13... | collective-permute-start | bytes 933896 | tf_op jit(solution)/shard_map/ppermute | solution.py:368
  7.7 4.8 %collective-permute-start = (f32[76,8,128]{2,1,0:T(8,128)}, f32[76,8,128]{2,1,0:T(8,128)S(1)}, u32[]{:S(2)}, u32[]{:S(2)}) collective-permute-start(f32[76,8,128]{2,1,0:T(8,128)} %get-tuple-element.15), channel_id=1, source_target_pairs={{0,4},{4,8},{8,12},{12,16},{16,20},{20,24},{24,28},{1,5},{5,9},{9,... | collective-permute-start | bytes 933896 | tf_op jit(solution)/shard_map/ppermute | solution.py:367
  12.5 0.0 collective-permute-done.2.west_ref
  12.5 0.0 collective-permute-done.3.east_ref
  12.5 0.7 %collective-permute-start.4 = (f32[76,8,128]{2,1,0:T(8,128)}, f32[76,8,128]{2,1,0:T(8,128)S(1)}, u32[]{:S(2)}, u32[]{:S(2)}) collective-permute-start(f32[76,8,128]{2,1,0:T(8,128)} %get-tuple-element.15), channel_id=1, source_target_pairs={{28,31},{29,30},{30,29},{31,28}} | collective-permute-start | bytes 933896 | tf_op jit(solution)/shard_map/ppermute | solution.py:373
  13.2 0.1 pad_add_fusion.lat_ref
  13.3 0.0 copy-done.7
  13.3 0.0 copy-start.6
  13.3 0.0 copy-start.9
  13.3 0.0 copy-start.10
  13.4 6.3 %shard_map.139.divx_ref = f32[300,8,128]{2,1,0:T(8,128)S(1)} custom-call(s32[2]{0:T(128)S(1)} %pad_add_fusion.lat_ref, f32[75]{0:T(128)S(1)} %copy-done.8, f32[75]{0:T(128)S(1)} %copy-done.7, s32[8,128]{1,0:T(8,128)S(1)} %copy-done.4, s32[8,128]{1,0:T(8,128)S(1)} %copy-done.5, f32[75,8,128]{2,1,0:T(8,128)S(1)} %copy-done, f32[75,8,128]{2,1,0:T(8,128)S(1)} %copy-done.1, ...), custom_call_target="tpu_custom_call" | custom-call | tf_op jit(solution)/shard_map/pallas_call | solution.py:379
  19.7 0.0 collective-permute-done.1.north_ref
  19.7 5.4 %collective-permute-done.south_ref = f32[76,8,128]{2,1,0:T(8,128)S(1)} collective-permute-done((f32[76,8,128]{2,1,0:T(8,128)}, f32[76,8,128]{2,1,0:T(8,128)S(1)}, u32[]{:S(2)}, u32[]{:S(2)}) %collective-permute-start) | collective-permute-done | bytes 311328 | tf_op jit(solution)/shard_map/ppermute | solution.py:367
  25.1 0.0 collective-permute-done.4.fold_ref
  25.1 0.0 copy-done.6
  25.1 4.9 %shard_map.140 = (f32[75,8,128]{2,1,0:T(8,128)}, f32[75,8,128]{2,1,0:T(8,128)}, f32[75,8,128]{2,1,0:T(8,128)}, f32[75,8,128]{2,1,0:T(8,128)}) custom-call(s32[2]{0:T(128)S(1)} %pad_add_fusion.lat_ref, f32[75]{0:T(128)S(1)} %copy-done.8, f32[75]{0:T(128)S(1)} %copy-done.10, f32[75]{0:T(128)S(1)} %copy-done.7, f32[75]{0:T(128)S(1)} %copy-done.9, ...), custom_call_target="tpu_custom_call" | custom-call | tf_op jit(solution)/shard_map/pallas_call | solution.py:387
  (12 shorter events, 0.0 us)
Async XLA Ops:
  0.6 12.6 %copy-start.7 = (f32[75]{0:T(128)S(1)}, f32[75]{0:T(128)}, u32[]{:S(2)}) copy-start(f32[75]{0:T(128)} %constant.20.clone.zmid_ref) | copy-start | bytes 904
  0.6 12.6 %copy-start.8 = (f32[75]{0:T(128)S(1)}, f32[75]{0:T(128)}, u32[]{:S(2)}) copy-start(f32[75]{0:T(128)} %constant.18.clone.h_ref) | copy-start | bytes 904
  0.7 12.6 %copy-start.5 = (s32[8,128]{1,0:T(8,128)S(1)}, s32[8,128]{1,0:T(8,128)}, u32[]{:S(2)}) copy-start(s32[8,128]{1,0:T(8,128)} %bottom_ref.5) | copy-start | bytes 12292
  0.7 12.6 %copy-start.4 = (s32[8,128]{1,0:T(8,128)S(1)}, s32[8,128]{1,0:T(8,128)}, u32[]{:S(2)}) copy-start(s32[8,128]{1,0:T(8,128)} %shore_ref.5) | copy-start | bytes 12292
  0.7 12.6 %copy-start.3 = (f32[75,8,128]{2,1,0:T(8,128)S(1)}, f32[75,8,128]{2,1,0:T(8,128)}, u32[]{:S(2)}) copy-start(f32[75,8,128]{2,1,0:T(8,128)} %v_ref.5) | copy-start | bytes 921604
  0.7 12.6 %copy-start.2 = (f32[75,8,128]{2,1,0:T(8,128)S(1)}, f32[75,8,128]{2,1,0:T(8,128)}, u32[]{:S(2)}) copy-start(f32[75,8,128]{2,1,0:T(8,128)} %u_ref.5) | copy-start | bytes 921604
  0.7 12.6 %copy-start.1 = (f32[75,8,128]{2,1,0:T(8,128)S(1)}, f32[75,8,128]{2,1,0:T(8,128)}, u32[]{:S(2)}) copy-start(f32[75,8,128]{2,1,0:T(8,128)} %s_ref.5) | copy-start | bytes 921604
  0.7 12.6 %copy-start = (f32[75,8,128]{2,1,0:T(8,128)S(1)}, f32[75,8,128]{2,1,0:T(8,128)}, u32[]{:S(2)}) copy-start(f32[75,8,128]{2,1,0:T(8,128)} %t_ref.5) | copy-start | bytes 921604
  3.9 8.5 %collective-permute-start.2 = (f32[6,8,128]{2,1,0:T(8,128)}, f32[6,8,128]{2,1,0:T(8,128)S(1)}, u32[]{:S(2)}, u32[]{:S(2)}) collective-permute-start(f32[6,8,128]{2,1,0:T(8,128)} %get-tuple-element.13), channel_id=1, source_target_pairs={{0,1},{1,2},{2,3},{3,0},{4,5},{5,6},{6,7},{7,4},{8,9},{9,10},{10,1... | collective-permute-start | bytes 73736 | tf_op jit(solution)/shard_map/ppermute | solution.py:369
  4.4 8.1 %collective-permute-start.3 = (f32[6,8,128]{2,1,0:T(8,128)}, f32[6,8,128]{2,1,0:T(8,128)S(1)}, u32[]{:S(2)}, u32[]{:S(2)}) collective-permute-start(f32[6,8,128]{2,1,0:T(8,128)} %get-tuple-element.14), channel_id=1, source_target_pairs={{1,0},{2,1},{3,2},{0,3},{5,4},{6,5},{7,6},{4,7},{9,8},{10,9},{11,1... | collective-permute-start | bytes 73736 | tf_op jit(solution)/shard_map/ppermute | solution.py:370
  6.4 13.3 %collective-permute-start.1 = (f32[76,8,128]{2,1,0:T(8,128)}, f32[76,8,128]{2,1,0:T(8,128)S(1)}, u32[]{:S(2)}, u32[]{:S(2)}) collective-permute-start(f32[76,8,128]{2,1,0:T(8,128)} %get-tuple-element.12), channel_id=1, source_target_pairs={{4,0},{8,4},{12,8},{16,12},{20,16},{24,20},{28,24},{5,1},{9,5},{13... | collective-permute-start | bytes 933896 | tf_op jit(solution)/shard_map/ppermute | solution.py:368
  7.7 17.4 %collective-permute-start = (f32[76,8,128]{2,1,0:T(8,128)}, f32[76,8,128]{2,1,0:T(8,128)S(1)}, u32[]{:S(2)}, u32[]{:S(2)}) collective-permute-start(f32[76,8,128]{2,1,0:T(8,128)} %get-tuple-element.15), channel_id=1, source_target_pairs={{0,4},{4,8},{8,12},{12,16},{16,20},{20,24},{24,28},{1,5},{5,9},{9,... | collective-permute-start | bytes 933896 | tf_op jit(solution)/shard_map/ppermute | solution.py:367
  12.5 12.6 %collective-permute-start.4 = (f32[76,8,128]{2,1,0:T(8,128)}, f32[76,8,128]{2,1,0:T(8,128)S(1)}, u32[]{:S(2)}, u32[]{:S(2)}) collective-permute-start(f32[76,8,128]{2,1,0:T(8,128)} %get-tuple-element.15), channel_id=1, source_target_pairs={{28,31},{29,30},{30,29},{31,28}} | collective-permute-start | bytes 933896 | tf_op jit(solution)/shard_map/ppermute | solution.py:373
  13.3 11.8 %copy-start.6 = (f32[4,8,128]{2,1,0:T(8,128)S(1)}, f32[4,8,128]{2,1,0:T(8,128)}, u32[]{:S(2)}) copy-start(f32[4,8,128]{2,1,0:T(8,128)} %flux_ref.1) | copy-start | bytes 49156
  13.3 11.7 %copy-start.9 = (f32[75]{0:T(128)S(1)}, f32[75]{0:T(128)}, u32[]{:S(2)}) copy-start(f32[75]{0:T(128)} %constant.21.clone.inv_sp_ref) | copy-start | bytes 904
  13.3 11.7 %copy-start.10 = (f32[75]{0:T(128)S(1)}, f32[75]{0:T(128)}, u32[]{:S(2)}) copy-start(f32[75]{0:T(128)} %constant.19.clone.inv_h_ref) | copy-start | bytes 904

commit v18 on v17

--- a/solution.py
+++ b/solution.py
@@ -369,7 +369,7 @@
     from_west = lax.ppermute(right, "lon", [(i, (i + 1) % n_lon) for i in range(n_lon)])
     from_east = lax.ppermute(left, "lon", [((i + 1) % n_lon, i) for i in range(n_lon)])
     last = (n_lat - 1) * n_lon
-    fold, from_west, from_east = lax.optimization_barrier((top, from_west, from_east))
+    fold = top
     from_fold = lax.ppermute(
         fold, ("lat", "lon"), [(last + x, last + n_lon - 1 - x) for x in range(n_lon)]
     )

time: 30.2 us -> 30.6 us (1.013)
  the two profiles are of different devices: /device:TPU:0 before, /device:TPU:27 now
where the time goes in v18:
time: 30.6 us; the launch traced here: 30.4 us
  Pallas kernels  14.9 us (49%)
  starting transfers between devices  7.53 us (25%)
  waiting for transfers between devices  6.92 us (23%)
  between operations  0.83 us (3%)
    pallas_call x1, Pallas kernels, on_device(): pl.pallas_call(xpart_kernel, out_shape=jax.ShapeDtypeStruct((4 * layers,...  6.31 us
    ppermute x1, waiting for transfers between devices, on_device(): lax.ppermute(right, 'lon', [(i, (i + 1) % n_lon) for i in range(n_lon)])  5.68 us
    pallas_call x1, Pallas kernels, on_device(): pl.pallas_call(step_kernel, out_shape=(plane,) * 4, in_specs=[smem] * 5 +...  4.94 us
    ppermute x1, starting transfers between devices, on_device(): lax.ppermute(fold, ('lat', 'lon'), [(last + x, last + n_lon - 1 - x) for...  3.99 us
    pallas_call x1, Pallas kernels, on_device(): pl.pallas_call(pack_kernel, out_shape=(row_tiles, row_tiles, col_tiles, c...  3.69 us
    ppermute x1, starting transfers between devices, on_device(): lax.ppermute(bot, 'lat', [(i + 1, i) for i in range(n_lat - 1)])  1.69 us
    ppermute x1, starting transfers between devices, on_device(): lax.ppermute(top, 'lat', [(i, i + 1) for i in range(n_lat - 1)])  1.29 us
    ppermute x1, waiting for transfers between devices, on_device(): lax.ppermute(left, 'lon', [((i + 1) % n_lon, i) for i in range(n_lon)])  1.23 us
  transfers between devices with their start and end apart: 5, of which 2 were waited for; matrix products, arithmetic and copies ran while one was open for 0% of the time, Pallas kernels for 21%

profile of v18, /device:TPU:27, one launch (start us, length us, event | category | flops | bytes accessed | tf_op | source)
XLA Modules:
  0.0 30.4 jit_solution(16776244112778834327)
XLA Ops:
  0.6 0.0 copy-start.7
  0.6 0.0 copy-start.8
  0.7 0.0 copy-start.5
  0.7 0.0 copy-start.4
  0.7 0.0 copy-start.3
  0.7 0.0 copy-start.2
  0.7 0.0 copy-start.1
  0.7 0.0 copy-start
  0.7 3.7 %shard_map.138 = (f32[76,8,128]{2,1,0:T(8,128)}, f32[76,8,128]{2,1,0:T(8,128)}, f32[6,8,128]{2,1,0:T(8,128)}, f32[6,8,128]{2,1,0:T(8,128)}) custom-call(s32[1]{0:T(128)} %bitcast.1.last_ref, s32[8,128]{1,0:T(8,128)} %shore_ref.5, s32[8,128]{1,0:T(8,128)} %bottom_ref.5, f32[75,8,128]{2,1,0:T(8,128)} %t_ref.5, f32[75,8,128]{2,1,0:T(8,128)} %s_ref.5, ...), custom_call_target="tpu_custom_call" | custom-call | tf_op jit(solution)/shard_map/pallas_call | solution.py:360
  4.4 1.7 %collective-permute-start.1 = (f32[76,8,128]{2,1,0:T(8,128)}, f32[76,8,128]{2,1,0:T(8,128)S(1)}, u32[]{:S(2)}, u32[]{:S(2)}) collective-permute-start(f32[76,8,128]{2,1,0:T(8,128)} %get-tuple-element.9), channel_id=1, source_target_pairs={{4,0},{8,4},{12,8},{16,12},{20,16},{24,20},{28,24},{5,1},{9,5},{13... | collective-permute-start | bytes 933896 | tf_op jit(solution)/shard_map/ppermute | solution.py:368
  6.1 4.0 %collective-permute-start.2 = (f32[76,8,128]{2,1,0:T(8,128)}, f32[76,8,128]{2,1,0:T(8,128)S(1)}, u32[]{:S(2)}, u32[]{:S(2)}) collective-permute-start(f32[76,8,128]{2,1,0:T(8,128)} %get-tuple-element.8), channel_id=1, source_target_pairs={{28,31},{29,30},{30,29},{31,28}} | collective-permute-start | bytes 933896 | tf_op jit(solution)/shard_map/ppermute | solution.py:373
  10.1 1.3 %collective-permute-start = (f32[76,8,128]{2,1,0:T(8,128)}, f32[76,8,128]{2,1,0:T(8,128)S(1)}, u32[]{:S(2)}, u32[]{:S(2)}) collective-permute-start(f32[76,8,128]{2,1,0:T(8,128)} %get-tuple-element.8), channel_id=1, source_target_pairs={{0,4},{4,8},{8,12},{12,16},{16,20},{20,24},{24,28},{1,5},{5,9},{9,... | collective-permute-start | bytes 933896 | tf_op jit(solution)/shard_map/ppermute | solution.py:367
  11.4 0.1 collective-permute-start.3
  11.5 0.5 %collective-permute-start.4 = (f32[6,8,128]{2,1,0:T(8,128)}, f32[6,8,128]{2,1,0:T(8,128)S(1)}, u32[]{:S(2)}, u32[]{:S(2)}) collective-permute-start(f32[6,8,128]{2,1,0:T(8,128)} %get-tuple-element.11), channel_id=1, source_target_pairs={{1,0},{2,1},{3,2},{0,3},{5,4},{6,5},{7,6},{4,7},{9,8},{10,9},{11,1... | collective-permute-start | bytes 73736 | tf_op jit(solution)/shard_map/ppermute | solution.py:370
  12.0 0.1 pad_add_fusion.lat_ref
  12.1 5.7 %collective-permute-done.3.west_ref = f32[6,8,128]{2,1,0:T(8,128)S(1)} collective-permute-done((f32[6,8,128]{2,1,0:T(8,128)}, f32[6,8,128]{2,1,0:T(8,128)S(1)}, u32[]{:S(2)}, u32[]{:S(2)}) %collective-permute-start.3) | collective-permute-done | bytes 24608 | tf_op jit(solution)/shard_map/ppermute | solution.py:369
  17.7 1.2 %collective-permute-done.4.east_ref = f32[6,8,128]{2,1,0:T(8,128)S(1)} collective-permute-done((f32[6,8,128]{2,1,0:T(8,128)}, f32[6,8,128]{2,1,0:T(8,128)S(1)}, u32[]{:S(2)}, u32[]{:S(2)}) %collective-permute-start.4) | collective-permute-done | bytes 24608 | tf_op jit(solution)/shard_map/ppermute | solution.py:370
  19.0 0.0 copy-done.7
  19.0 0.0 copy-done.8
  19.0 6.3 %shard_map.139.divx_ref = f32[300,8,128]{2,1,0:T(8,128)S(1)} custom-call(s32[2]{0:T(128)S(1)} %pad_add_fusion.lat_ref, f32[75]{0:T(128)S(1)} %copy-done.8, f32[75]{0:T(128)S(1)} %copy-done.7, s32[8,128]{1,0:T(8,128)S(1)} %copy-done.4, s32[8,128]{1,0:T(8,128)S(1)} %copy-done.5, f32[75,8,128]{2,1,0:T(8,128)S(1)} %copy-done, f32[75,8,128]{2,1,0:T(8,128)S(1)} %copy-done.1, ...), custom_call_target="tpu_custom_call" | custom-call | tf_op jit(solution)/shard_map/pallas_call | solution.py:379
  25.3 0.0 collective-permute-done.1.north_ref
  25.4 0.0 collective-permute-done.2.fold_ref
  25.4 0.0 collective-permute-done.south_ref
  25.4 4.9 %shard_map.140 = (f32[75,8,128]{2,1,0:T(8,128)}, f32[75,8,128]{2,1,0:T(8,128)}, f32[75,8,128]{2,1,0:T(8,128)}, f32[75,8,128]{2,1,0:T(8,128)}) custom-call(s32[2]{0:T(128)S(1)} %pad_add_fusion.lat_ref, f32[75]{0:T(128)S(1)} %copy-done.8, f32[75]{0:T(128)S(1)} %copy-done.10, f32[75]{0:T(128)S(1)} %copy-done.7, f32[75]{0:T(128)S(1)} %copy-done.9, ...), custom_call_target="tpu_custom_call" | custom-call | tf_op jit(solution)/shard_map/pallas_call | solution.py:387
  (12 shorter events, 0.0 us)
Async XLA Ops:
  0.6 18.3 %copy-start.7 = (f32[75]{0:T(128)S(1)}, f32[75]{0:T(128)}, u32[]{:S(2)}) copy-start(f32[75]{0:T(128)} %constant.20.clone.zmid_ref) | copy-start | bytes 904
  0.6 18.3 %copy-start.8 = (f32[75]{0:T(128)S(1)}, f32[75]{0:T(128)}, u32[]{:S(2)}) copy-start(f32[75]{0:T(128)} %constant.18.clone.h_ref) | copy-start | bytes 904
  0.7 18.3 %copy-start.5 = (s32[8,128]{1,0:T(8,128)S(1)}, s32[8,128]{1,0:T(8,128)}, u32[]{:S(2)}) copy-start(s32[8,128]{1,0:T(8,128)} %bottom_ref.5) | copy-start | bytes 12292
  0.7 18.3 %copy-start.4 = (s32[8,128]{1,0:T(8,128)S(1)}, s32[8,128]{1,0:T(8,128)}, u32[]{:S(2)}) copy-start(s32[8,128]{1,0:T(8,128)} %shore_ref.5) | copy-start | bytes 12292
  0.7 18.3 %copy-start.3 = (f32[75,8,128]{2,1,0:T(8,128)S(1)}, f32[75,8,128]{2,1,0:T(8,128)}, u32[]{:S(2)}) copy-start(f32[75,8,128]{2,1,0:T(8,128)} %v_ref.5) | copy-start | bytes 921604
  0.7 18.3 %copy-start.2 = (f32[75,8,128]{2,1,0:T(8,128)S(1)}, f32[75,8,128]{2,1,0:T(8,128)}, u32[]{:S(2)}) copy-start(f32[75,8,128]{2,1,0:T(8,128)} %u_ref.5) | copy-start | bytes 921604
  0.7 18.3 %copy-start.1 = (f32[75,8,128]{2,1,0:T(8,128)S(1)}, f32[75,8,128]{2,1,0:T(8,128)}, u32[]{:S(2)}) copy-start(f32[75,8,128]{2,1,0:T(8,128)} %s_ref.5) | copy-start | bytes 921604
  0.7 18.3 %copy-start = (f32[75,8,128]{2,1,0:T(8,128)S(1)}, f32[75,8,128]{2,1,0:T(8,128)}, u32[]{:S(2)}) copy-start(f32[75,8,128]{2,1,0:T(8,128)} %t_ref.5) | copy-start | bytes 921604
  4.4 20.9 %collective-permute-start.1 = (f32[76,8,128]{2,1,0:T(8,128)}, f32[76,8,128]{2,1,0:T(8,128)S(1)}, u32[]{:S(2)}, u32[]{:S(2)}) collective-permute-start(f32[76,8,128]{2,1,0:T(8,128)} %get-tuple-element.9), channel_id=1, source_target_pairs={{4,0},{8,4},{12,8},{16,12},{20,16},{24,20},{28,24},{5,1},{9,5},{13... | collective-permute-start | bytes 933896 | tf_op jit(solution)/shard_map/ppermute | solution.py:368
  6.1 19.2 %collective-permute-start.2 = (f32[76,8,128]{2,1,0:T(8,128)}, f32[76,8,128]{2,1,0:T(8,128)S(1)}, u32[]{:S(2)}, u32[]{:S(2)}) collective-permute-start(f32[76,8,128]{2,1,0:T(8,128)} %get-tuple-element.8), channel_id=1, source_target_pairs={{28,31},{29,30},{30,29},{31,28}} | collective-permute-start | bytes 933896 | tf_op jit(solution)/shard_map/ppermute | solution.py:373
  10.1 15.3 %collective-permute-start = (f32[76,8,128]{2,1,0:T(8,128)}, f32[76,8,128]{2,1,0:T(8,128)S(1)}, u32[]{:S(2)}, u32[]{:S(2)}) collective-permute-start(f32[76,8,128]{2,1,0:T(8,128)} %get-tuple-element.8), channel_id=1, source_target_pairs={{0,4},{4,8},{8,12},{12,16},{16,20},{20,24},{24,28},{1,5},{5,9},{9,... | collective-permute-start | bytes 933896 | tf_op jit(solution)/shard_map/ppermute | solution.py:367
  11.4 6.3 %collective-permute-start.3 = (f32[6,8,128]{2,1,0:T(8,128)}, f32[6,8,128]{2,1,0:T(8,128)S(1)}, u32[]{:S(2)}, u32[]{:S(2)}) collective-permute-start(f32[6,8,128]{2,1,0:T(8,128)} %get-tuple-element.10), channel_id=1, source_target_pairs={{0,1},{1,2},{2,3},{3,0},{4,5},{5,6},{6,7},{7,4},{8,9},{9,10},{10,1... | collective-permute-start | bytes 73736 | tf_op jit(solution)/shard_map/ppermute | solution.py:369
  11.5 7.5 %collective-permute-start.4 = (f32[6,8,128]{2,1,0:T(8,128)}, f32[6,8,128]{2,1,0:T(8,128)S(1)}, u32[]{:S(2)}, u32[]{:S(2)}) collective-permute-start(f32[6,8,128]{2,1,0:T(8,128)} %get-tuple-element.11), channel_id=1, source_target_pairs={{1,0},{2,1},{3,2},{0,3},{5,4},{6,5},{7,6},{4,7},{9,8},{10,9},{11,1... | collective-permute-start | bytes 73736 | tf_op jit(solution)/shard_map/ppermute | solution.py:370
  12.1 13.3 %copy-start.6 = (f32[4,8,128]{2,1,0:T(8,128)S(1)}, f32[4,8,128]{2,1,0:T(8,128)}, u32[]{:S(2)}) copy-start(f32[4,8,128]{2,1,0:T(8,128)} %flux_ref.1) | copy-start | bytes 49156
  12.1 13.3 %copy-start.9 = (f32[75]{0:T(128)S(1)}, f32[75]{0:T(128)}, u32[]{:S(2)}) copy-start(f32[75]{0:T(128)} %constant.21.clone.inv_sp_ref) | copy-start | bytes 904
  12.1 13.3 %copy-start.10 = (f32[75]{0:T(128)S(1)}, f32[75]{0:T(128)}, u32[]{:S(2)}) copy-start(f32[75]{0:T(128)} %constant.19.clone.inv_h_ref) | copy-start | bytes 904

commit v19 on v17

--- a/solution.py
+++ b/solution.py
@@ -249,7 +249,7 @@
         return (cum_ym, cum_yp)
 
     lag = 3
-    carry_e = lax.fori_loop(0, lag, explicit, (zero, zero))
+    carry_e = lax.fori_loop(0, lag, explicit, (zero, zero), unroll=True)
 
     surface_scale = surface_gain * inv_h_ref[0]
     w_top = (0.0 < dep).astype(jnp.float32)
@@ -294,7 +294,7 @@
         return (explicit(k, carry_e), forward(k - lag, carry_f))
 
     _, carry_f = lax.fori_loop(lag, layers, fused, (carry_e, (zero,) * 7), unroll=9)
-    lax.fori_loop(layers - lag, layers, forward, carry_f)
+    lax.fori_loop(layers - lag, layers, forward, carry_f, unroll=True)
 
     def backward(i, carry):
         x0, x1, x2, x3 = carry
@@ -315,7 +315,7 @@
     writes = []
     carry = (zero,) * 4
     for chunk in range(groups):
-        carry = lax.fori_loop(chunk * GROUP, (chunk + 1) * GROUP, backward, carry, unroll=3)
+        carry = lax.fori_loop(chunk * GROUP, (chunk + 1) * GROUP, backward, carry, unroll=5)
         span = pl.ds(layers - (chunk + 1) * GROUP, GROUP)
         for c, (src, dst) in enumerate(pairs):
             write = pltpu.make_async_copy(src.at[span], dst.at[span], out_sems.at[chunk, c])

time: 30.2 us -> 30.1 us (level)
  no operation moved by 1% of the time
where the time goes in v19:
time: 30.1 us; the launch traced here: 29.9 us
  Pallas kernels  14.3 us (48%)
  starting transfers between devices  9.2 us (31%)
  waiting for transfers between devices  5.4 us (18%)
  between operations  0.83 us (3%)
    pallas_call x1, Pallas kernels, on_device(): pl.pallas_call(xpart_kernel, out_shape=jax.ShapeDtypeStruct((4 * layers,...  6.31 us
    ppermute x1, waiting for transfers between devices, on_device(): lax.ppermute(top, 'lat', [(i, i + 1) for i in range(n_lat - 1)])  5.39 us
    pallas_call x1, Pallas kernels, on_device(): pl.pallas_call(step_kernel, out_shape=(plane,) * 4, in_specs=[smem] * 5 +...  4.79 us
    ppermute x1, starting transfers between devices, on_device(): lax.ppermute(top, 'lat', [(i, i + 1) for i in range(n_lat - 1)])  4.77 us
    pallas_call x1, Pallas kernels, on_device(): pl.pallas_call(pack_kernel, out_shape=(row_tiles, row_tiles, col_tiles, c...  3.22 us
    ppermute x1, starting transfers between devices, on_device(): lax.ppermute(left, 'lon', [((i + 1) % n_lon, i) for i in range(n_lon)])  2.01 us
    ppermute x1, starting transfers between devices, on_device(): lax.ppermute(bot, 'lat', [(i + 1, i) for i in range(n_lat - 1)])  1.28 us
    ppermute x1, starting transfers between devices, on_device(): lax.ppermute(fold, ('lat', 'lon'), [(last + x, last + n_lon - 1 - x) for...  0.68 us
  transfers between devices with their start and end apart: 5, of which 1 were waited for; matrix products, arithmetic and copies ran while one was open for 0% of the time, Pallas kernels for 21%

profile of v19, /device:TPU:0, one launch (start us, length us, event | category | flops | bytes accessed | tf_op | source)
XLA Modules:
  0.0 29.9 jit_solution(941630050908855626)
XLA Ops:
  0.6 0.0 copy-start.7
  0.6 0.0 copy-start.8
  0.7 0.0 copy-start.5
  0.7 0.0 copy-start.4
  0.7 0.0 copy-start.3
  0.7 3.2 %shard_map.138 = (f32[76,8,128]{2,1,0:T(8,128)}, f32[76,8,128]{2,1,0:T(8,128)}, f32[6,8,128]{2,1,0:T(8,128)}, f32[6,8,128]{2,1,0:T(8,128)}) custom-call(s32[1]{0:T(128)} %bitcast.1.last_ref, s32[8,128]{1,0:T(8,128)} %shore_ref.5, s32[8,128]{1,0:T(8,128)} %bottom_ref.5, f32[75,8,128]{2,1,0:T(8,128)} %t_ref.5, f32[75,8,128]{2,1,0:T(8,128)} %s_ref.5, ...), custom_call_target="tpu_custom_call" | custom-call | tf_op jit(solution)/shard_map/pallas_call | solution.py:360
  3.9 0.5 %collective-permute-start.2 = (f32[6,8,128]{2,1,0:T(8,128)}, f32[6,8,128]{2,1,0:T(8,128)S(1)}, u32[]{:S(2)}, u32[]{:S(2)}) collective-permute-start(f32[6,8,128]{2,1,0:T(8,128)} %get-tuple-element.13), channel_id=1, source_target_pairs={{0,1},{1,2},{2,3},{3,0},{4,5},{5,6},{6,7},{7,4},{8,9},{9,10},{10,1... | collective-permute-start | bytes 73736 | tf_op jit(solution)/shard_map/ppermute | solution.py:369
  4.4 2.0 %collective-permute-start.3 = (f32[6,8,128]{2,1,0:T(8,128)}, f32[6,8,128]{2,1,0:T(8,128)S(1)}, u32[]{:S(2)}, u32[]{:S(2)}) collective-permute-start(f32[6,8,128]{2,1,0:T(8,128)} %get-tuple-element.14), channel_id=1, source_target_pairs={{1,0},{2,1},{3,2},{0,3},{5,4},{6,5},{7,6},{4,7},{9,8},{10,9},{11,1... | collective-permute-start | bytes 73736 | tf_op jit(solution)/shard_map/ppermute | solution.py:370
  6.4 1.3 %collective-permute-start.1 = (f32[76,8,128]{2,1,0:T(8,128)}, f32[76,8,128]{2,1,0:T(8,128)S(1)}, u32[]{:S(2)}, u32[]{:S(2)}) collective-permute-start(f32[76,8,128]{2,1,0:T(8,128)} %get-tuple-element.12), channel_id=1, source_target_pairs={{4,0},{8,4},{12,8},{16,12},{20,16},{24,20},{28,24},{5,1},{9,5},{13... | collective-permute-start | bytes 933896 | tf_op jit(solution)/shard_map/ppermute | solution.py:368
  7.7 4.8 %collective-permute-start = (f32[76,8,128]{2,1,0:T(8,128)}, f32[76,8,128]{2,1,0:T(8,128)S(1)}, u32[]{:S(2)}, u32[]{:S(2)}) collective-permute-start(f32[76,8,128]{2,1,0:T(8,128)} %get-tuple-element.15), channel_id=1, source_target_pairs={{0,4},{4,8},{8,12},{12,16},{16,20},{20,24},{24,28},{1,5},{5,9},{9,... | collective-permute-start | bytes 933896 | tf_op jit(solution)/shard_map/ppermute | solution.py:367
  12.5 0.0 collective-permute-done.2.west_ref
  12.5 0.0 collective-permute-done.3.east_ref
  12.5 0.7 %collective-permute-start.4 = (f32[76,8,128]{2,1,0:T(8,128)}, f32[76,8,128]{2,1,0:T(8,128)S(1)}, u32[]{:S(2)}, u32[]{:S(2)}) collective-permute-start(f32[76,8,128]{2,1,0:T(8,128)} %get-tuple-element.15), channel_id=1, source_target_pairs={{28,31},{29,30},{30,29},{31,28}} | collective-permute-start | bytes 933896 | tf_op jit(solution)/shard_map/ppermute | solution.py:373
  13.2 0.1 pad_add_fusion.lat_ref
  13.3 0.0 copy-done.7
  13.3 0.0 copy-start.6
  13.3 0.0 copy-start.9
  13.3 0.0 copy-start.10
  13.4 6.3 %shard_map.139.divx_ref = f32[300,8,128]{2,1,0:T(8,128)S(1)} custom-call(s32[2]{0:T(128)S(1)} %pad_add_fusion.lat_ref, f32[75]{0:T(128)S(1)} %copy-done.8, f32[75]{0:T(128)S(1)} %copy-done.7, s32[8,128]{1,0:T(8,128)S(1)} %copy-done.4, s32[8,128]{1,0:T(8,128)S(1)} %copy-done.5, f32[75,8,128]{2,1,0:T(8,128)S(1)} %copy-done, f32[75,8,128]{2,1,0:T(8,128)S(1)} %copy-done.1, ...), custom_call_target="tpu_custom_call" | custom-call | tf_op jit(solution)/shard_map/pallas_call | solution.py:379
  19.7 0.0 collective-permute-done.1.north_ref
  19.7 5.4 %collective-permute-done.south_ref = f32[76,8,128]{2,1,0:T(8,128)S(1)} collective-permute-done((f32[76,8,128]{2,1,0:T(8,128)}, f32[76,8,128]{2,1,0:T(8,128)S(1)}, u32[]{:S(2)}, u32[]{:S(2)}) %collective-permute-start) | collective-permute-done | bytes 311328 | tf_op jit(solution)/shard_map/ppermute | solution.py:367
  25.1 0.0 collective-permute-done.4.fold_ref
  25.1 0.0 copy-done.6
  25.1 4.8 %shard_map.140 = (f32[75,8,128]{2,1,0:T(8,128)}, f32[75,8,128]{2,1,0:T(8,128)}, f32[75,8,128]{2,1,0:T(8,128)}, f32[75,8,128]{2,1,0:T(8,128)}) custom-call(s32[2]{0:T(128)S(1)} %pad_add_fusion.lat_ref, f32[75]{0:T(128)S(1)} %copy-done.8, f32[75]{0:T(128)S(1)} %copy-done.10, f32[75]{0:T(128)S(1)} %copy-done.7, f32[75]{0:T(128)S(1)} %copy-done.9, ...), custom_call_target="tpu_custom_call" | custom-call | tf_op jit(solution)/shard_map/pallas_call | solution.py:387
  (12 shorter events, 0.0 us)
Async XLA Ops:
  0.6 12.6 %copy-start.7 = (f32[75]{0:T(128)S(1)}, f32[75]{0:T(128)}, u32[]{:S(2)}) copy-start(f32[75]{0:T(128)} %constant.20.clone.zmid_ref) | copy-start | bytes 904
  0.6 12.6 %copy-start.8 = (f32[75]{0:T(128)S(1)}, f32[75]{0:T(128)}, u32[]{:S(2)}) copy-start(f32[75]{0:T(128)} %constant.18.clone.h_ref) | copy-start | bytes 904
  0.7 12.6 %copy-start.5 = (s32[8,128]{1,0:T(8,128)S(1)}, s32[8,128]{1,0:T(8,128)}, u32[]{:S(2)}) copy-start(s32[8,128]{1,0:T(8,128)} %bottom_ref.5) | copy-start | bytes 12292
  0.7 12.6 %copy-start.4 = (s32[8,128]{1,0:T(8,128)S(1)}, s32[8,128]{1,0:T(8,128)}, u32[]{:S(2)}) copy-start(s32[8,128]{1,0:T(8,128)} %shore_ref.5) | copy-start | bytes 12292
  0.7 12.6 %copy-start.3 = (f32[75,8,128]{2,1,0:T(8,128)S(1)}, f32[75,8,128]{2,1,0:T(8,128)}, u32[]{:S(2)}) copy-start(f32[75,8,128]{2,1,0:T(8,128)} %v_ref.5) | copy-start | bytes 921604
  0.7 12.6 %copy-start.2 = (f32[75,8,128]{2,1,0:T(8,128)S(1)}, f32[75,8,128]{2,1,0:T(8,128)}, u32[]{:S(2)}) copy-start(f32[75,8,128]{2,1,0:T(8,128)} %u_ref.5) | copy-start | bytes 921604
  0.7 12.6 %copy-start.1 = (f32[75,8,128]{2,1,0:T(8,128)S(1)}, f32[75,8,128]{2,1,0:T(8,128)}, u32[]{:S(2)}) copy-start(f32[75,8,128]{2,1,0:T(8,128)} %s_ref.5) | copy-start | bytes 921604
  0.7 12.6 %copy-start = (f32[75,8,128]{2,1,0:T(8,128)S(1)}, f32[75,8,128]{2,1,0:T(8,128)}, u32[]{:S(2)}) copy-start(f32[75,8,128]{2,1,0:T(8,128)} %t_ref.5) | copy-start | bytes 921604
  3.9 8.5 %collective-permute-start.2 = (f32[6,8,128]{2,1,0:T(8,128)}, f32[6,8,128]{2,1,0:T(8,128)S(1)}, u32[]{:S(2)}, u32[]{:S(2)}) collective-permute-start(f32[6,8,128]{2,1,0:T(8,128)} %get-tuple-element.13), channel_id=1, source_target_pairs={{0,1},{1,2},{2,3},{3,0},{4,5},{5,6},{6,7},{7,4},{8,9},{9,10},{10,1... | collective-permute-start | bytes 73736 | tf_op jit(solution)/shard_map/ppermute | solution.py:369
  4.4 8.1 %collective-permute-start.3 = (f32[6,8,128]{2,1,0:T(8,128)}, f32[6,8,128]{2,1,0:T(8,128)S(1)}, u32[]{:S(2)}, u32[]{:S(2)}) collective-permute-start(f32[6,8,128]{2,1,0:T(8,128)} %get-tuple-element.14), channel_id=1, source_target_pairs={{1,0},{2,1},{3,2},{0,3},{5,4},{6,5},{7,6},{4,7},{9,8},{10,9},{11,1... | collective-permute-start | bytes 73736 | tf_op jit(solution)/shard_map/ppermute | solution.py:370
  6.4 13.3 %collective-permute-start.1 = (f32[76,8,128]{2,1,0:T(8,128)}, f32[76,8,128]{2,1,0:T(8,128)S(1)}, u32[]{:S(2)}, u32[]{:S(2)}) collective-permute-start(f32[76,8,128]{2,1,0:T(8,128)} %get-tuple-element.12), channel_id=1, source_target_pairs={{4,0},{8,4},{12,8},{16,12},{20,16},{24,20},{28,24},{5,1},{9,5},{13... | collective-permute-start | bytes 933896 | tf_op jit(solution)/shard_map/ppermute | solution.py:368
  7.7 17.4 %collective-permute-start = (f32[76,8,128]{2,1,0:T(8,128)}, f32[76,8,128]{2,1,0:T(8,128)S(1)}, u32[]{:S(2)}, u32[]{:S(2)}) collective-permute-start(f32[76,8,128]{2,1,0:T(8,128)} %get-tuple-element.15), channel_id=1, source_target_pairs={{0,4},{4,8},{8,12},{12,16},{16,20},{20,24},{24,28},{1,5},{5,9},{9,... | collective-permute-start | bytes 933896 | tf_op jit(solution)/shard_map/ppermute | solution.py:367
  12.5 12.6 %collective-permute-start.4 = (f32[76,8,128]{2,1,0:T(8,128)}, f32[76,8,128]{2,1,0:T(8,128)S(1)}, u32[]{:S(2)}, u32[]{:S(2)}) collective-permute-start(f32[76,8,128]{2,1,0:T(8,128)} %get-tuple-element.15), channel_id=1, source_target_pairs={{28,31},{29,30},{30,29},{31,28}} | collective-permute-start | bytes 933896 | tf_op jit(solution)/shard_map/ppermute | solution.py:373
  13.3 11.8 %copy-start.6 = (f32[4,8,128]{2,1,0:T(8,128)S(1)}, f32[4,8,128]{2,1,0:T(8,128)}, u32[]{:S(2)}) copy-start(f32[4,8,128]{2,1,0:T(8,128)} %flux_ref.1) | copy-start | bytes 49156
  13.3 11.7 %copy-start.9 = (f32[75]{0:T(128)S(1)}, f32[75]{0:T(128)}, u32[]{:S(2)}) copy-start(f32[75]{0:T(128)} %constant.21.clone.inv_sp_ref) | copy-start | bytes 904
  13.3 11.7 %copy-start.10 = (f32[75]{0:T(128)S(1)}, f32[75]{0:T(128)}, u32[]{:S(2)}) copy-start(f32[75]{0:T(128)} %constant.19.clone.inv_h_ref) | copy-start | bytes 904

commit v20 on v19

--- a/solution.py
+++ b/solution.py
@@ -293,7 +293,7 @@
         carry_e, carry_f = carry
         return (explicit(k, carry_e), forward(k - lag, carry_f))
 
-    _, carry_f = lax.fori_loop(lag, layers, fused, (carry_e, (zero,) * 7), unroll=9)
+    _, carry_f = lax.fori_loop(lag, layers, fused, (carry_e, (zero,) * 7), unroll=12)
     lax.fori_loop(layers - lag, layers, forward, carry_f, unroll=True)
 
     def backward(i, carry):

time: 30.1 us -> 30 us (level)
  no operation moved by 1% of the time
where the time goes in v20:
time: 30 us; the launch traced here: 29.8 us
  Pallas kernels  14.3 us (48%)
  starting transfers between devices  9.2 us (31%)
  waiting for transfers between devices  5.4 us (18%)
  between operations  0.83 us (3%)
    pallas_call x1, Pallas kernels, on_device(): pl.pallas_call(xpart_kernel, out_shape=jax.ShapeDtypeStruct((4 * layers,...  6.31 us
    ppermute x1, waiting for transfers between devices, on_device(): lax.ppermute(top, 'lat', [(i, i + 1) for i in range(n_lat - 1)])  5.39 us
    ppermute x1, starting transfers between devices, on_device(): lax.ppermute(top, 'lat', [(i, i + 1) for i in range(n_lat - 1)])  4.77 us
    pallas_call x1, Pallas kernels, on_device(): pl.pallas_call(step_kernel, out_shape=(plane,) * 4, in_specs=[smem] * 5 +...  4.73 us
    pallas_call x1, Pallas kernels, on_device(): pl.pallas_call(pack_kernel, out_shape=(row_tiles, row_tiles, col_tiles, c...  3.22 us
    ppermute x1, starting transfers between devices, on_device(): lax.ppermute(left, 'lon', [((i + 1) % n_lon, i) for i in range(n_lon)])  2.01 us
    ppermute x1, starting transfers between devices, on_device(): lax.ppermute(bot, 'lat', [(i + 1, i) for i in range(n_lat - 1)])  1.28 us
    ppermute x1, starting transfers between devices, on_device(): lax.ppermute(fold, ('lat', 'lon'), [(last + x, last + n_lon - 1 - x) for...  0.68 us
  transfers between devices with their start and end apart: 5, of which 1 were waited for; matrix products, arithmetic and copies ran while one was open for 0% of the time, Pallas kernels for 21%

profile of v20, /device:TPU:0, one launch (start us, length us, event | category | flops | bytes accessed | tf_op | source)
XLA Modules:
  0.0 29.8 jit_solution(7378279983741013062)
XLA Ops:
  0.6 0.0 copy-start.7
  0.6 0.0 copy-start.8
  0.7 0.0 copy-start.5
  0.7 0.0 copy-start.4
  0.7 0.0 copy-start.3
  0.7 3.2 %shard_map.138 = (f32[76,8,128]{2,1,0:T(8,128)}, f32[76,8,128]{2,1,0:T(8,128)}, f32[6,8,128]{2,1,0:T(8,128)}, f32[6,8,128]{2,1,0:T(8,128)}) custom-call(s32[1]{0:T(128)} %bitcast.1.last_ref, s32[8,128]{1,0:T(8,128)} %shore_ref.5, s32[8,128]{1,0:T(8,128)} %bottom_ref.5, f32[75,8,128]{2,1,0:T(8,128)} %t_ref.5, f32[75,8,128]{2,1,0:T(8,128)} %s_ref.5, ...), custom_call_target="tpu_custom_call" | custom-call | tf_op jit(solution)/shard_map/pallas_call | solution.py:360
  3.9 0.5 %collective-permute-start.2 = (f32[6,8,128]{2,1,0:T(8,128)}, f32[6,8,128]{2,1,0:T(8,128)S(1)}, u32[]{:S(2)}, u32[]{:S(2)}) collective-permute-start(f32[6,8,128]{2,1,0:T(8,128)} %get-tuple-element.13), channel_id=1, source_target_pairs={{0,1},{1,2},{2,3},{3,0},{4,5},{5,6},{6,7},{7,4},{8,9},{9,10},{10,1... | collective-permute-start | bytes 73736 | tf_op jit(solution)/shard_map/ppermute | solution.py:369
  4.4 2.0 %collective-permute-start.3 = (f32[6,8,128]{2,1,0:T(8,128)}, f32[6,8,128]{2,1,0:T(8,128)S(1)}, u32[]{:S(2)}, u32[]{:S(2)}) collective-permute-start(f32[6,8,128]{2,1,0:T(8,128)} %get-tuple-element.14), channel_id=1, source_target_pairs={{1,0},{2,1},{3,2},{0,3},{5,4},{6,5},{7,6},{4,7},{9,8},{10,9},{11,1... | collective-permute-start | bytes 73736 | tf_op jit(solution)/shard_map/ppermute | solution.py:370
  6.4 1.3 %collective-permute-start.1 = (f32[76,8,128]{2,1,0:T(8,128)}, f32[76,8,128]{2,1,0:T(8,128)S(1)}, u32[]{:S(2)}, u32[]{:S(2)}) collective-permute-start(f32[76,8,128]{2,1,0:T(8,128)} %get-tuple-element.12), channel_id=1, source_target_pairs={{4,0},{8,4},{12,8},{16,12},{20,16},{24,20},{28,24},{5,1},{9,5},{13... | collective-permute-start | bytes 933896 | tf_op jit(solution)/shard_map/ppermute | solution.py:368
  7.7 4.8 %collective-permute-start = (f32[76,8,128]{2,1,0:T(8,128)}, f32[76,8,128]{2,1,0:T(8,128)S(1)}, u32[]{:S(2)}, u32[]{:S(2)}) collective-permute-start(f32[76,8,128]{2,1,0:T(8,128)} %get-tuple-element.15), channel_id=1, source_target_pairs={{0,4},{4,8},{8,12},{12,16},{16,20},{20,24},{24,28},{1,5},{5,9},{9,... | collective-permute-start | bytes 933896 | tf_op jit(solution)/shard_map/ppermute | solution.py:367
  12.5 0.0 collective-permute-done.2.west_ref
  12.5 0.0 collective-permute-done.3.east_ref
  12.5 0.7 %collective-permute-start.4 = (f32[76,8,128]{2,1,0:T(8,128)}, f32[76,8,128]{2,1,0:T(8,128)S(1)}, u32[]{:S(2)}, u32[]{:S(2)}) collective-permute-start(f32[76,8,128]{2,1,0:T(8,128)} %get-tuple-element.15), channel_id=1, source_target_pairs={{28,31},{29,30},{30,29},{31,28}} | collective-permute-start | bytes 933896 | tf_op jit(solution)/shard_map/ppermute | solution.py:373
  13.2 0.1 pad_add_fusion.lat_ref
  13.3 0.0 copy-done.7
  13.3 0.0 copy-start.6
  13.3 0.0 copy-start.9
  13.3 0.0 copy-start.10
  13.4 6.3 %shard_map.139.divx_ref = f32[300,8,128]{2,1,0:T(8,128)S(1)} custom-call(s32[2]{0:T(128)S(1)} %pad_add_fusion.lat_ref, f32[75]{0:T(128)S(1)} %copy-done.8, f32[75]{0:T(128)S(1)} %copy-done.7, s32[8,128]{1,0:T(8,128)S(1)} %copy-done.4, s32[8,128]{1,0:T(8,128)S(1)} %copy-done.5, f32[75,8,128]{2,1,0:T(8,128)S(1)} %copy-done, f32[75,8,128]{2,1,0:T(8,128)S(1)} %copy-done.1, ...), custom_call_target="tpu_custom_call" | custom-call | tf_op jit(solution)/shard_map/pallas_call | solution.py:379
  19.7 0.0 collective-permute-done.1.north_ref
  19.7 5.4 %collective-permute-done.south_ref = f32[76,8,128]{2,1,0:T(8,128)S(1)} collective-permute-done((f32[76,8,128]{2,1,0:T(8,128)}, f32[76,8,128]{2,1,0:T(8,128)S(1)}, u32[]{:S(2)}, u32[]{:S(2)}) %collective-permute-start) | collective-permute-done | bytes 311328 | tf_op jit(solution)/shard_map/ppermute | solution.py:367
  25.1 0.0 collective-permute-done.4.fold_ref
  25.1 0.0 copy-done.6
  25.1 4.7 %shard_map.140 = (f32[75,8,128]{2,1,0:T(8,128)}, f32[75,8,128]{2,1,0:T(8,128)}, f32[75,8,128]{2,1,0:T(8,128)}, f32[75,8,128]{2,1,0:T(8,128)}) custom-call(s32[2]{0:T(128)S(1)} %pad_add_fusion.lat_ref, f32[75]{0:T(128)S(1)} %copy-done.8, f32[75]{0:T(128)S(1)} %copy-done.10, f32[75]{0:T(128)S(1)} %copy-done.7, f32[75]{0:T(128)S(1)} %copy-done.9, ...), custom_call_target="tpu_custom_call" | custom-call | tf_op jit(solution)/shard_map/pallas_call | solution.py:387
  (12 shorter events, 0.0 us)
Async XLA Ops:
  0.6 12.6 %copy-start.7 = (f32[75]{0:T(128)S(1)}, f32[75]{0:T(128)}, u32[]{:S(2)}) copy-start(f32[75]{0:T(128)} %constant.20.clone.zmid_ref) | copy-start | bytes 904
  0.6 12.6 %copy-start.8 = (f32[75]{0:T(128)S(1)}, f32[75]{0:T(128)}, u32[]{:S(2)}) copy-start(f32[75]{0:T(128)} %constant.18.clone.h_ref) | copy-start | bytes 904
  0.7 12.6 %copy-start.5 = (s32[8,128]{1,0:T(8,128)S(1)}, s32[8,128]{1,0:T(8,128)}, u32[]{:S(2)}) copy-start(s32[8,128]{1,0:T(8,128)} %bottom_ref.5) | copy-start | bytes 12292
  0.7 12.6 %copy-start.4 = (s32[8,128]{1,0:T(8,128)S(1)}, s32[8,128]{1,0:T(8,128)}, u32[]{:S(2)}) copy-start(s32[8,128]{1,0:T(8,128)} %shore_ref.5) | copy-start | bytes 12292
  0.7 12.6 %copy-start.3 = (f32[75,8,128]{2,1,0:T(8,128)S(1)}, f32[75,8,128]{2,1,0:T(8,128)}, u32[]{:S(2)}) copy-start(f32[75,8,128]{2,1,0:T(8,128)} %v_ref.5) | copy-start | bytes 921604
  0.7 12.6 %copy-start.2 = (f32[75,8,128]{2,1,0:T(8,128)S(1)}, f32[75,8,128]{2,1,0:T(8,128)}, u32[]{:S(2)}) copy-start(f32[75,8,128]{2,1,0:T(8,128)} %u_ref.5) | copy-start | bytes 921604
  0.7 12.6 %copy-start.1 = (f32[75,8,128]{2,1,0:T(8,128)S(1)}, f32[75,8,128]{2,1,0:T(8,128)}, u32[]{:S(2)}) copy-start(f32[75,8,128]{2,1,0:T(8,128)} %s_ref.5) | copy-start | bytes 921604
  0.7 12.6 %copy-start = (f32[75,8,128]{2,1,0:T(8,128)S(1)}, f32[75,8,128]{2,1,0:T(8,128)}, u32[]{:S(2)}) copy-start(f32[75,8,128]{2,1,0:T(8,128)} %t_ref.5) | copy-start | bytes 921604
  3.9 8.5 %collective-permute-start.2 = (f32[6,8,128]{2,1,0:T(8,128)}, f32[6,8,128]{2,1,0:T(8,128)S(1)}, u32[]{:S(2)}, u32[]{:S(2)}) collective-permute-start(f32[6,8,128]{2,1,0:T(8,128)} %get-tuple-element.13), channel_id=1, source_target_pairs={{0,1},{1,2},{2,3},{3,0},{4,5},{5,6},{6,7},{7,4},{8,9},{9,10},{10,1... | collective-permute-start | bytes 73736 | tf_op jit(solution)/shard_map/ppermute | solution.py:369
  4.4 8.1 %collective-permute-start.3 = (f32[6,8,128]{2,1,0:T(8,128)}, f32[6,8,128]{2,1,0:T(8,128)S(1)}, u32[]{:S(2)}, u32[]{:S(2)}) collective-permute-start(f32[6,8,128]{2,1,0:T(8,128)} %get-tuple-element.14), channel_id=1, source_target_pairs={{1,0},{2,1},{3,2},{0,3},{5,4},{6,5},{7,6},{4,7},{9,8},{10,9},{11,1... | collective-permute-start | bytes 73736 | tf_op jit(solution)/shard_map/ppermute | solution.py:370
  6.4 13.3 %collective-permute-start.1 = (f32[76,8,128]{2,1,0:T(8,128)}, f32[76,8,128]{2,1,0:T(8,128)S(1)}, u32[]{:S(2)}, u32[]{:S(2)}) collective-permute-start(f32[76,8,128]{2,1,0:T(8,128)} %get-tuple-element.12), channel_id=1, source_target_pairs={{4,0},{8,4},{12,8},{16,12},{20,16},{24,20},{28,24},{5,1},{9,5},{13... | collective-permute-start | bytes 933896 | tf_op jit(solution)/shard_map/ppermute | solution.py:368
  7.7 17.4 %collective-permute-start = (f32[76,8,128]{2,1,0:T(8,128)}, f32[76,8,128]{2,1,0:T(8,128)S(1)}, u32[]{:S(2)}, u32[]{:S(2)}) collective-permute-start(f32[76,8,128]{2,1,0:T(8,128)} %get-tuple-element.15), channel_id=1, source_target_pairs={{0,4},{4,8},{8,12},{12,16},{16,20},{20,24},{24,28},{1,5},{5,9},{9,... | collective-permute-start | bytes 933896 | tf_op jit(solution)/shard_map/ppermute | solution.py:367
  12.5 12.6 %collective-permute-start.4 = (f32[76,8,128]{2,1,0:T(8,128)}, f32[76,8,128]{2,1,0:T(8,128)S(1)}, u32[]{:S(2)}, u32[]{:S(2)}) collective-permute-start(f32[76,8,128]{2,1,0:T(8,128)} %get-tuple-element.15), channel_id=1, source_target_pairs={{28,31},{29,30},{30,29},{31,28}} | collective-permute-start | bytes 933896 | tf_op jit(solution)/shard_map/ppermute | solution.py:373
  13.3 11.8 %copy-start.6 = (f32[4,8,128]{2,1,0:T(8,128)S(1)}, f32[4,8,128]{2,1,0:T(8,128)}, u32[]{:S(2)}) copy-start(f32[4,8,128]{2,1,0:T(8,128)} %flux_ref.1) | copy-start | bytes 49156
  13.3 11.7 %copy-start.9 = (f32[75]{0:T(128)S(1)}, f32[75]{0:T(128)}, u32[]{:S(2)}) copy-start(f32[75]{0:T(128)} %constant.21.clone.inv_sp_ref) | copy-start | bytes 904
  13.3 11.7 %copy-start.10 = (f32[75]{0:T(128)S(1)}, f32[75]{0:T(128)}, u32[]{:S(2)}) copy-start(f32[75]{0:T(128)} %constant.19.clone.inv_h_ref) | copy-start | bytes 904

commit v21 on v19

--- a/solution.py
+++ b/solution.py
@@ -88,7 +88,7 @@
         left_ref[g] = left
         return carry
 
-    lax.fori_loop(0, groups, group_body, 0)
+    lax.fori_loop(0, groups, group_body, 0, unroll=True)
     top_ref[layers] = pack_rows([dep], rows - 2)
     bot_ref[layers] = pack_rows([dep], 0)
     right_ref[groups] = jnp.where(lane < 2, rolled(dep, 2, 1), zero)

time: 30.1 us -> 29.9 us (level)
  no operation moved by 1% of the time
where the time goes in v21:
time: 29.9 us; the launch traced here: 29.7 us
  Pallas kernels  14.1 us (47%)
  starting transfers between devices  9.2 us (31%)
  waiting for transfers between devices  5.4 us (18%)
  between operations  0.83 us (3%)
    pallas_call x1, Pallas kernels, on_device(): pl.pallas_call(xpart_kernel, out_shape=jax.ShapeDtypeStruct((4 * layers,...  6.31 us
    ppermute x1, waiting for transfers between devices, on_device(): lax.ppermute(top, 'lat', [(i, i + 1) for i in range(n_lat - 1)])  5.39 us
    pallas_call x1, Pallas kernels, on_device(): pl.pallas_call(step_kernel, out_shape=(plane,) * 4, in_specs=[smem] * 5 +...  4.79 us
    ppermute x1, starting transfers between devices, on_device(): lax.ppermute(top, 'lat', [(i, i + 1) for i in range(n_lat - 1)])  4.77 us
    pallas_call x1, Pallas kernels, on_device(): pl.pallas_call(pack_kernel, out_shape=(row_tiles, row_tiles, col_tiles, c...  3.01 us
    ppermute x1, starting transfers between devices, on_device(): lax.ppermute(left, 'lon', [((i + 1) % n_lon, i) for i in range(n_lon)])  2.01 us
    ppermute x1, starting transfers between devices, on_device(): lax.ppermute(bot, 'lat', [(i + 1, i) for i in range(n_lat - 1)])  1.28 us
    ppermute x1, starting transfers between devices, on_device(): lax.ppermute(fold, ('lat', 'lon'), [(last + x, last + n_lon - 1 - x) for...  0.68 us
  transfers between devices with their start and end apart: 5, of which 1 were waited for; matrix products, arithmetic and copies ran while one was open for 0% of the time, Pallas kernels for 21%

profile of v21, /device:TPU:0, one launch (start us, length us, event | category | flops | bytes accessed | tf_op | source)
XLA Modules:
  0.0 29.7 jit_solution(10601089357357038818)
XLA Ops:
  0.6 0.0 copy-start.7
  0.6 0.0 copy-start.8
  0.7 0.0 copy-start.5
  0.7 0.0 copy-start.4
  0.7 0.0 copy-start.3
  0.7 0.0 copy-start.2
  0.7 3.0 %shard_map.138 = (f32[76,8,128]{2,1,0:T(8,128)}, f32[76,8,128]{2,1,0:T(8,128)}, f32[6,8,128]{2,1,0:T(8,128)}, f32[6,8,128]{2,1,0:T(8,128)}) custom-call(s32[1]{0:T(128)} %bitcast.1.last_ref, s32[8,128]{1,0:T(8,128)} %shore_ref.5, s32[8,128]{1,0:T(8,128)} %bottom_ref.5, f32[75,8,128]{2,1,0:T(8,128)} %t_ref.5, f32[75,8,128]{2,1,0:T(8,128)} %s_ref.5, ...), custom_call_target="tpu_custom_call" | custom-call | tf_op jit(solution)/shard_map/pallas_call | solution.py:360
  3.7 0.5 %collective-permute-start.2 = (f32[6,8,128]{2,1,0:T(8,128)}, f32[6,8,128]{2,1,0:T(8,128)S(1)}, u32[]{:S(2)}, u32[]{:S(2)}) collective-permute-start(f32[6,8,128]{2,1,0:T(8,128)} %get-tuple-element.13), channel_id=1, source_target_pairs={{0,1},{1,2},{2,3},{3,0},{4,5},{5,6},{6,7},{7,4},{8,9},{9,10},{10,1... | collective-permute-start | bytes 73736 | tf_op jit(solution)/shard_map/ppermute | solution.py:369
  4.2 2.0 %collective-permute-start.3 = (f32[6,8,128]{2,1,0:T(8,128)}, f32[6,8,128]{2,1,0:T(8,128)S(1)}, u32[]{:S(2)}, u32[]{:S(2)}) collective-permute-start(f32[6,8,128]{2,1,0:T(8,128)} %get-tuple-element.14), channel_id=1, source_target_pairs={{1,0},{2,1},{3,2},{0,3},{5,4},{6,5},{7,6},{4,7},{9,8},{10,9},{11,1... | collective-permute-start | bytes 73736 | tf_op jit(solution)/shard_map/ppermute | solution.py:370
  6.2 1.3 %collective-permute-start.1 = (f32[76,8,128]{2,1,0:T(8,128)}, f32[76,8,128]{2,1,0:T(8,128)S(1)}, u32[]{:S(2)}, u32[]{:S(2)}) collective-permute-start(f32[76,8,128]{2,1,0:T(8,128)} %get-tuple-element.12), channel_id=1, source_target_pairs={{4,0},{8,4},{12,8},{16,12},{20,16},{24,20},{28,24},{5,1},{9,5},{13... | collective-permute-start | bytes 933896 | tf_op jit(solution)/shard_map/ppermute | solution.py:368
  7.5 4.8 %collective-permute-start = (f32[76,8,128]{2,1,0:T(8,128)}, f32[76,8,128]{2,1,0:T(8,128)S(1)}, u32[]{:S(2)}, u32[]{:S(2)}) collective-permute-start(f32[76,8,128]{2,1,0:T(8,128)} %get-tuple-element.15), channel_id=1, source_target_pairs={{0,4},{4,8},{8,12},{12,16},{16,20},{20,24},{24,28},{1,5},{5,9},{9,... | collective-permute-start | bytes 933896 | tf_op jit(solution)/shard_map/ppermute | solution.py:367
  12.3 0.0 collective-permute-done.2.west_ref
  12.3 0.0 collective-permute-done.3.east_ref
  12.3 0.7 %collective-permute-start.4 = (f32[76,8,128]{2,1,0:T(8,128)}, f32[76,8,128]{2,1,0:T(8,128)S(1)}, u32[]{:S(2)}, u32[]{:S(2)}) collective-permute-start(f32[76,8,128]{2,1,0:T(8,128)} %get-tuple-element.15), channel_id=1, source_target_pairs={{28,31},{29,30},{30,29},{31,28}} | collective-permute-start | bytes 933896 | tf_op jit(solution)/shard_map/ppermute | solution.py:373
  13.0 0.1 pad_add_fusion.lat_ref
  13.1 0.0 copy-done.4
  13.1 0.0 copy-start.6
  13.1 0.0 copy-start.9
  13.1 0.0 copy-start.10
  13.1 6.3 %shard_map.139.divx_ref = f32[300,8,128]{2,1,0:T(8,128)S(1)} custom-call(s32[2]{0:T(128)S(1)} %pad_add_fusion.lat_ref, f32[75]{0:T(128)S(1)} %copy-done.8, f32[75]{0:T(128)S(1)} %copy-done.7, s32[8,128]{1,0:T(8,128)S(1)} %copy-done.4, s32[8,128]{1,0:T(8,128)S(1)} %copy-done.5, f32[75,8,128]{2,1,0:T(8,128)S(1)} %copy-done, f32[75,8,128]{2,1,0:T(8,128)S(1)} %copy-done.1, ...), custom_call_target="tpu_custom_call" | custom-call | tf_op jit(solution)/shard_map/pallas_call | solution.py:379
  19.5 0.0 collective-permute-done.1.north_ref
  19.5 5.4 %collective-permute-done.south_ref = f32[76,8,128]{2,1,0:T(8,128)S(1)} collective-permute-done((f32[76,8,128]{2,1,0:T(8,128)}, f32[76,8,128]{2,1,0:T(8,128)S(1)}, u32[]{:S(2)}, u32[]{:S(2)}) %collective-permute-start) | collective-permute-done | bytes 311328 | tf_op jit(solution)/shard_map/ppermute | solution.py:367
  24.9 0.0 collective-permute-done.4.fold_ref
  24.9 4.8 %shard_map.140 = (f32[75,8,128]{2,1,0:T(8,128)}, f32[75,8,128]{2,1,0:T(8,128)}, f32[75,8,128]{2,1,0:T(8,128)}, f32[75,8,128]{2,1,0:T(8,128)}) custom-call(s32[2]{0:T(128)S(1)} %pad_add_fusion.lat_ref, f32[75]{0:T(128)S(1)} %copy-done.8, f32[75]{0:T(128)S(1)} %copy-done.10, f32[75]{0:T(128)S(1)} %copy-done.7, f32[75]{0:T(128)S(1)} %copy-done.9, ...), custom_call_target="tpu_custom_call" | custom-call | tf_op jit(solution)/shard_map/pallas_call | solution.py:387
  (12 shorter events, 0.0 us)
Async XLA Ops:
  0.6 12.4 %copy-start.7 = (f32[75]{0:T(128)S(1)}, f32[75]{0:T(128)}, u32[]{:S(2)}) copy-start(f32[75]{0:T(128)} %constant.20.clone.zmid_ref) | copy-start | bytes 904
  0.6 12.4 %copy-start.8 = (f32[75]{0:T(128)S(1)}, f32[75]{0:T(128)}, u32[]{:S(2)}) copy-start(f32[75]{0:T(128)} %constant.18.clone.h_ref) | copy-start | bytes 904
  0.7 12.4 %copy-start.5 = (s32[8,128]{1,0:T(8,128)S(1)}, s32[8,128]{1,0:T(8,128)}, u32[]{:S(2)}) copy-start(s32[8,128]{1,0:T(8,128)} %bottom_ref.5) | copy-start | bytes 12292
  0.7 12.4 %copy-start.4 = (s32[8,128]{1,0:T(8,128)S(1)}, s32[8,128]{1,0:T(8,128)}, u32[]{:S(2)}) copy-start(s32[8,128]{1,0:T(8,128)} %shore_ref.5) | copy-start | bytes 12292
  0.7 12.4 %copy-start.3 = (f32[75,8,128]{2,1,0:T(8,128)S(1)}, f32[75,8,128]{2,1,0:T(8,128)}, u32[]{:S(2)}) copy-start(f32[75,8,128]{2,1,0:T(8,128)} %v_ref.5) | copy-start | bytes 921604
  0.7 12.4 %copy-start.2 = (f32[75,8,128]{2,1,0:T(8,128)S(1)}, f32[75,8,128]{2,1,0:T(8,128)}, u32[]{:S(2)}) copy-start(f32[75,8,128]{2,1,0:T(8,128)} %u_ref.5) | copy-start | bytes 921604
  0.7 12.4 %copy-start.1 = (f32[75,8,128]{2,1,0:T(8,128)S(1)}, f32[75,8,128]{2,1,0:T(8,128)}, u32[]{:S(2)}) copy-start(f32[75,8,128]{2,1,0:T(8,128)} %s_ref.5) | copy-start | bytes 921604
  0.7 12.4 %copy-start = (f32[75,8,128]{2,1,0:T(8,128)S(1)}, f32[75,8,128]{2,1,0:T(8,128)}, u32[]{:S(2)}) copy-start(f32[75,8,128]{2,1,0:T(8,128)} %t_ref.5) | copy-start | bytes 921604
  3.7 8.5 %collective-permute-start.2 = (f32[6,8,128]{2,1,0:T(8,128)}, f32[6,8,128]{2,1,0:T(8,128)S(1)}, u32[]{:S(2)}, u32[]{:S(2)}) collective-permute-start(f32[6,8,128]{2,1,0:T(8,128)} %get-tuple-element.13), channel_id=1, source_target_pairs={{0,1},{1,2},{2,3},{3,0},{4,5},{5,6},{6,7},{7,4},{8,9},{9,10},{10,1... | collective-permute-start | bytes 73736 | tf_op jit(solution)/shard_map/ppermute | solution.py:369
  4.2 8.1 %collective-permute-start.3 = (f32[6,8,128]{2,1,0:T(8,128)}, f32[6,8,128]{2,1,0:T(8,128)S(1)}, u32[]{:S(2)}, u32[]{:S(2)}) collective-permute-start(f32[6,8,128]{2,1,0:T(8,128)} %get-tuple-element.14), channel_id=1, source_target_pairs={{1,0},{2,1},{3,2},{0,3},{5,4},{6,5},{7,6},{4,7},{9,8},{10,9},{11,1... | collective-permute-start | bytes 73736 | tf_op jit(solution)/shard_map/ppermute | solution.py:370
  6.2 13.3 %collective-permute-start.1 = (f32[76,8,128]{2,1,0:T(8,128)}, f32[76,8,128]{2,1,0:T(8,128)S(1)}, u32[]{:S(2)}, u32[]{:S(2)}) collective-permute-start(f32[76,8,128]{2,1,0:T(8,128)} %get-tuple-element.12), channel_id=1, source_target_pairs={{4,0},{8,4},{12,8},{16,12},{20,16},{24,20},{28,24},{5,1},{9,5},{13... | collective-permute-start | bytes 933896 | tf_op jit(solution)/shard_map/ppermute | solution.py:368
  7.5 17.4 %collective-permute-start = (f32[76,8,128]{2,1,0:T(8,128)}, f32[76,8,128]{2,1,0:T(8,128)S(1)}, u32[]{:S(2)}, u32[]{:S(2)}) collective-permute-start(f32[76,8,128]{2,1,0:T(8,128)} %get-tuple-element.15), channel_id=1, source_target_pairs={{0,4},{4,8},{8,12},{12,16},{16,20},{20,24},{24,28},{1,5},{5,9},{9,... | collective-permute-start | bytes 933896 | tf_op jit(solution)/shard_map/ppermute | solution.py:367
  12.3 12.6 %collective-permute-start.4 = (f32[76,8,128]{2,1,0:T(8,128)}, f32[76,8,128]{2,1,0:T(8,128)S(1)}, u32[]{:S(2)}, u32[]{:S(2)}) collective-permute-start(f32[76,8,128]{2,1,0:T(8,128)} %get-tuple-element.15), channel_id=1, source_target_pairs={{28,31},{29,30},{30,29},{31,28}} | collective-permute-start | bytes 933896 | tf_op jit(solution)/shard_map/ppermute | solution.py:373
  13.1 11.8 %copy-start.6 = (f32[4,8,128]{2,1,0:T(8,128)S(1)}, f32[4,8,128]{2,1,0:T(8,128)}, u32[]{:S(2)}) copy-start(f32[4,8,128]{2,1,0:T(8,128)} %flux_ref.1) | copy-start | bytes 49156
  13.1 11.7 %copy-start.9 = (f32[75]{0:T(128)S(1)}, f32[75]{0:T(128)}, u32[]{:S(2)}) copy-start(f32[75]{0:T(128)} %constant.21.clone.inv_sp_ref) | copy-start | bytes 904
  13.1 11.7 %copy-start.10 = (f32[75]{0:T(128)S(1)}, f32[75]{0:T(128)}, u32[]{:S(2)}) copy-start(f32[75]{0:T(128)} %constant.19.clone.inv_h_ref) | copy-start | bytes 904
